TPU v7x, 32 devices: a whole 2x2x4 slice. The times are simulated.
32 devices in a mesh: groups: 2 (over y), tile: 4 (over z), depth: 2 (over x), wave: 2 (over core).
Axes of the slice: x: 2, y: 2, z: 4, core: 2. Of those that a mesh axis runs over, the one named last changes fastest.
Arguments:
- incident: float32 [3, 2, 512, 256], P(None, None, ('groups', 'tile'), 'wave'), parts along dimension 2, may hold values from -6 to 6
- phase_shift: bfloat16 [8, 512, 256], P('depth', ('groups', 'tile'), 'wave'), parts along dimension 1, may hold values from -3.140625 to 3.140625
- absorption: bfloat16 [8, 512, 256], P('depth', ('groups', 'tile'), 'wave'), parts along dimension 1, may hold values from 0 to 0.059814453
- fir_taps: float32 [2, 33], replicated, may hold values from -0.6 to 0.6
Outputs:
- exit_waves: float32 [2, 3, 2, 512, 256], P('depth', None, None, ('groups', 'tile'), 'wave'), parts along dimension 3
There are 2 independent parts, one for each index of `groups`. A program takes and returns all parts, laid end to end along the dimension named above; an argument that names none is the same for every part. Nothing has to cross between parts.
All inputs are finite; a program needn't handle non-finite values.
Results may differ from a plain program's by a relative error of at most 0.0003.
Values may be sent and summed in bfloat16 or wider, within the bound.
No kernel may reach another device: no remote copies, remote signals or barrier semaphores. Data moves between devices by JAX's collectives and lax.ppermute only.
A program may use at most 64 MiB of HBM per device.

v0:
```python
import jax
import jax.numpy as jnp
from jax import lax
from jax.sharding import PartitionSpec as P

TAPS = 33
HALF = 16


def toeplitz(kernel, size, shift):
    outer = jnp.arange(size, dtype=jnp.int32)[:, None]
    inner = jnp.arange(size, dtype=jnp.int32)[None, :]
    offsets = inner - outer + shift
    band_real = jnp.zeros((size, size), jnp.float32)
    band_imag = jnp.zeros((size, size), jnp.float32)
    for tap in range(TAPS):
        hit = offsets == tap
        band_real = jnp.where(hit, kernel[0, tap], band_real)
        band_imag = jnp.where(hit, kernel[1, tap], band_imag)
    top = jnp.stack([band_real, -band_imag], axis=0)
    bottom = jnp.stack([band_imag, band_real], axis=0)
    return jnp.stack([top, bottom], axis=0)


def transmission(phase_part, absorb_part):
    amplitude = jnp.exp(-absorb_part.astype(jnp.float32))
    angle_part = phase_part.astype(jnp.float32)
    return jnp.stack([amplitude * jnp.cos(angle_part), amplitude * jnp.sin(angle_part)], axis=-3)


def modulate(field, trans):
    field_real = field[:, 0]
    field_imag = field[:, 1]
    return jnp.stack(
        [
            field_real * trans[0] - field_imag * trans[1],
            field_real * trans[1] + field_imag * trans[0],
        ],
        axis=1,
    )


def grow(stack, halo):
    tiles = lax.axis_size("tile")
    wave = lax.axis_index("wave")
    rows = stack.shape[-2]
    from_prev = lax.ppermute(stack[:, rows - halo:], "tile", [(i, i + 1) for i in range(tiles - 1)])
    from_next = lax.ppermute(stack[:, :halo], "tile", [(i + 1, i) for i in range(tiles - 1)])
    tall = jnp.concatenate([from_prev, stack, from_next], axis=-2)
    width = tall.shape[-1]
    edge = jnp.where(wave == 0, tall[..., width - halo:], tall[..., :halo])
    got = lax.ppermute(edge, "wave", [(0, 1), (1, 0)])
    joined = jnp.concatenate([got, tall, got], axis=-1)
    return lax.dynamic_slice_in_dim(joined, halo * (1 - wave), width + halo, axis=-1)


def per_device(incident, phase_shift, absorption, fir_taps):
    kernel = fir_taps / jnp.sqrt(jnp.sum(fir_taps * fir_taps) + 1e-06)
    depth_index = lax.axis_index("depth")
    depth_count = lax.axis_size("depth")
    wave = lax.axis_index("wave")
    slices = phase_shift.shape[0]
    rows, cols = incident.shape[2], incident.shape[3]
    reach = HALF * slices
    assert reach <= rows and reach <= cols

    trans_own = transmission(phase_shift, absorption)
    illum = incident.shape[0]
    grown = grow(
        jnp.concatenate([incident.reshape(2 * illum, rows, cols), trans_own.reshape(2 * slices, rows, cols)]),
        reach,
    )
    first_field = grown[: 2 * illum].reshape(illum, 2, rows + 2 * reach, cols + reach)
    trans_reg = grown[2 * illum:].reshape(slices, 2, rows + 2 * reach, cols + reach)
    width = cols + reach
    tall = rows + 2 * reach

    band = toeplitz(kernel, max(tall, width), HALF)
    col_band = band[:, :, :width, :width]
    row_bands = [
        band[:, :, HALF * (s + 1): tall - HALF * (s + 1), HALF * s: tall - HALF * s]
        for s in range(slices)
    ]

    def depth_section(field):
        current = field
        for s in range(slices):
            moved = modulate(current, trans_reg[s, :, HALF * s: tall - HALF * s])
            rows_done = jnp.einsum(
                "dcab,icbj->idaj", row_bands[s], moved, precision=lax.Precision.HIGHEST
            )
            current = jnp.einsum(
                "dcyj,icxj->idxy", col_band, rows_done, precision=lax.Precision.HIGHEST
            )
        return lax.dynamic_slice_in_dim(current, reach * wave, cols, axis=-1)

    exits = jnp.zeros(incident.shape, jnp.float32)
    carried = None
    for step in range(depth_count):
        if step == 0:
            field = first_field
        else:
            field = grow(carried.reshape(2 * illum, rows, cols), reach).reshape(
                illum, 2, tall, width
            )
        result = depth_section(field)
        exits = jnp.where(depth_index == step, result, exits)
        if step + 1 < depth_count:
            carried = lax.ppermute(
                result, "depth", [(i, i + 1) for i in range(depth_count - 1)]
            )
    return exits[None]


def solution(mesh):
    return jax.shard_map(
        per_device,
        mesh=mesh,
        in_specs=(
            P(None, None, ("groups", "tile"), "wave"),
            P("depth", ("groups", "tile"), "wave"),
            P("depth", ("groups", "tile"), "wave"),
            P(),
        ),
        out_specs=P("depth", None, None, ("groups", "tile"), "wave"),
        check_vma=False,
    )
```

profile of v0, /device:TPU:15, one launch (start us, length us, event | category | flops | bytes accessed | tf_op | source)
XLA Modules:
  0.0 148.5 jit_solution(8467516093745068936)
XLA Ops:
  0.0 1.4 fusion.66
  2.4 3.2 %collective-permute-start = (f32[14,64,128]{2,1,0:T(8,128)S(1)}, f32[14,64,128]{2,1,0:T(8,128)S(1)}, u32[]{:S(2)}, u32[]{:S(2)}) collective-permute-start(f32[14,64,128]{2,1,0:T(8,128)S(1)} %pad_maximum_fusion.3), channel_id=1, source_target_pairs={{0,4},{4,8},{8,12},{1,5},{5,9},{9,13},{2,6},{6,10},{10,14},{3,7},{... | collective-permute-start | bytes 1376264 | tf_op jit(solution)/shard_map/ppermute | solution.py:47
  5.6 2.1 %collective-permute-start.1 = (f32[14,64,128]{2,1,0:T(8,128)S(1)}, f32[14,64,128]{2,1,0:T(8,128)S(1)}, u32[]{:S(2)}, u32[]{:S(2)}) collective-permute-start(f32[14,64,128]{2,1,0:T(8,128)S(1)} %pad_maximum_fusion.3), channel_id=1, source_target_pairs={{4,0},{8,4},{12,8},{5,1},{9,5},{13,9},{6,2},{10,6},{14,10},{7,3},{... | collective-permute-start | bytes 1376264 | tf_op jit(solution)/shard_map/ppermute | solution.py:48
  10.5 5.2 %collective-permute-done = f32[14,64,128]{2,1,0:T(8,128)S(1)} collective-permute-done((f32[14,64,128]{2,1,0:T(8,128)S(1)}, f32[14,64,128]{2,1,0:T(8,128)S(1)}, u32[]{:S(2)}, u32[]{:S(2)}) %collective-permute-start) | collective-permute-done | bytes 458784 | tf_op jit(solution)/shard_map/ppermute | solution.py:47
  15.7 2.9 %collective-permute-done.1 = f32[14,64,128]{2,1,0:T(8,128)S(1)} collective-permute-done((f32[14,64,128]{2,1,0:T(8,128)S(1)}, f32[14,64,128]{2,1,0:T(8,128)S(1)}, u32[]{:S(2)}, u32[]{:S(2)}) %collective-permute-start.1) | collective-permute-done | bytes 458784 | tf_op jit(solution)/shard_map/ppermute | solution.py:48
  19.1 1.5 copy.11
  20.6 1.9 %collective-permute-start.2 = (f32[14,192,64]{1,2,0:T(8,128)}, f32[14,192,64]{1,2,0:T(8,128)}, u32[]{:S(2)}, u32[]{:S(2)}) collective-permute-start(f32[14,192,64]{1,2,0:T(8,128)} %copy.11), channel_id=1, source_target_pairs={{0,1},{1,0},{2,3},{3,2},{4,5},{5,4},{6,7},{7,6},{8,9},{9,8},{10,11... | collective-permute-start | bytes 2064392 | tf_op jit(solution)/shard_map/ppermute | solution.py:52
  23.9 20.7 %select_select_fusion = f32[1,192,192]{2,1,0:T(8,128)S(1)} fusion(f32[]{:T(128)} %bitcast.75, f32[]{:T(128)} %bitcast.74, f32[]{:T(128)} %bitcast.73, f32[]{:T(128)} %bitcast.72, f32[]{:T(128)} %bitcast.71, f32[]{:T(128)} %bitcast.70, f32[]{:T(128)} %bitcast.69, f32[]{:T(128)} %bitcast.68, f32[]{:T(128)} %bitcast.67, f32[]{:T(128)} %bitcast.66, f32[]{:T(128)} %bitcast.65, ...), kind=kLoop, calls=%fused_computation.99 | loop fusion | flops 2506752 | bytes 147588 | tf_op jit(solution)/shard_map/jit(_where)/select_n | solution.py:19
  44.5 20.7 %select_select_fusion.1 = f32[1,192,192]{2,1,0:T(8,128)S(1)} fusion(f32[]{:T(128)} %bitcast.42, f32[]{:T(128)} %bitcast.41, f32[]{:T(128)} %bitcast.40, f32[]{:T(128)} %bitcast.39, f32[]{:T(128)} %bitcast.38, f32[]{:T(128)} %bitcast.37, f32[]{:T(128)} %bitcast.36, f32[]{:T(128)} %bitcast.35, f32[]{:T(128)} %bitcast.34, f32[]{:T(128)} %bitcast.33, ...), kind=kLoop, calls=%fused_computation.100 | loop fusion | flops 2506752 | bytes 147588 | tf_op jit(solution)/shard_map/jit(_where)/select_n | solution.py:18
  65.2 20.7 %fusion.71 = f32[1,192,192]{2,1,0:T(8,128)S(1)} fusion(f32[]{:T(128)} %bitcast.75, f32[]{:T(128)} %bitcast.74, f32[]{:T(128)} %bitcast.73, f32[]{:T(128)} %bitcast.72, f32[]{:T(128)} %bitcast.71, f32[]{:T(128)} %bitcast.70, f32[]{:T(128)} %bitcast.69, f32[]{:T(128)} %bitcast.68, f32[]{:T(128)} %bitcast.67, f32[]{:T(128)} %bitcast.66, f32[]{:T(128)} %bitcast.65, ...), kind=kLoop, calls=%fused_computation.150 | loop fusion | flops 2543616 | bytes 147588 | tf_op jit(solution)/shard_map/neg | solution.py:20
  86.0 1.6 %copy.12 = f32[14,192,64]{2,1,0:T(8,128)S(1)} copy(f32[14,192,64]{1,2,0:T(8,128)} %collective-permute-done.2) | data formatting | bytes 1376256 | tf_op jit(solution)/shard_map/ppermute | solution.py:52
  87.6 2.3 %dynamic-slice_maximum_fusion = f32[14,192,192]{2,1,0:T(8,128)S(1)} fusion(s32[]{:T(128)S(6)} %select_n.835, f32[14,192,64]{2,1,0:T(8,128)S(1)} %copy.12, f32[14,64,128]{2,1,0:T(8,128)S(1)} %collective-permute-done.1, f32[8,64,128]{2,1,0:T(8,128)S(1)} %bitcast.295, f32[6,64,128]{2,1,0:T(8,128)S(1)} %bitcast.301, f32[14,64,128]{2,1,0:T(8,128)S(1)} %collective-permute-done), kind=kLoop, calls=%fused_computation | loop fusion | flops 2580480 | bytes 4128772 | tf_op jit(solution)/shard_map/concatenate | solution.py:53
  90.0 1.5 %copy-done = f32[14,192,192]{2,1,0:T(8,128)} copy-done((f32[14,192,192]{2,1,0:T(8,128)}, f32[14,192,192]{2,1,0:T(8,128)S(1)}, u32[]{:S(2)}) %copy-start) | copy-done | bytes 2064408
  91.7 1.3 slice-done
  93.2 1.8 %convolution_bitcast_fusion.3 = f32[3,2,160,192,1]{3,2,1,4,0:T(8,128)S(1)} fusion(f32[3,1,192,192]{3,2,1,0:T(8,128)S(1)} %get-tuple-element.16, f32[3,1,192,192]{3,2,1,0:T(8,128)S(1)} %get-tuple-element.15, f32[1,2,192,192]{3,2,1,0:T(8,128)S(1)} %get-tuple-element.30, f32[1,2,192,192]{3,2,1,0:T(8,128)S(1)} %get-tuple-element.29), kind=kOutput, calls=%fused_computation.24 | convolution fusion | flops 849690624 | bytes 2211840 | tf_op jit(solution)/shard_map/dcab,icbj->idaj/dot_general | solution.py:89
  95.0 1.7 %convolution_bitcast_fusion.2 = f32[3,2,160,192]{3,2,1,0:T(8,128)S(1)} fusion(f32[3,2,160,192,1]{3,2,1,4,0:T(8,128)S(1)} %convolution_bitcast_fusion.3, f32[1,2,192,192]{3,2,1,0:T(8,128)S(1)} %get-tuple-element.29, f32[1,2,192,192]{3,2,1,0:T(8,128)S(1)} %get-tuple-element.30), kind=kOutput, calls=%fused_computation.23 | convolution fusion | flops 849494016 | bytes 2064384 | tf_op jit(solution)/shard_map/dcyj,icxj->idxy/dot_general | solution.py:92
  96.9 2.5 %convolution_bitcast_fusion.11 = f32[3,2,128,192,1]{2,3,1,4,0:T(8,128)S(1)} fusion(f32[3,1,160,192]{3,2,1,0:T(8,128)S(1)} %get-tuple-element.20, f32[3,1,160,192]{3,2,1,0:T(8,128)S(1)} %get-tuple-element.19, f32[1,2,192,192]{3,2,1,0:T(8,128)S(1)} %get-tuple-element.30, f32[1,2,192,192]{3,2,1,0:T(8,128)S(1)} %get-tuple-element.29), kind=kOutput, calls=%fused_computation.32 | convolution fusion | flops 566497280 | bytes 1916928 | tf_op jit(solution)/shard_map/dcab,icbj->idaj/dot_general | solution.py:89
  99.4 1.5 %convolution_bitcast_fusion.10 = f32[3,2,128,192]{2,3,1,0:T(8,128)S(1)} fusion(f32[3,2,128,192,1]{2,3,1,4,0:T(8,128)S(1)} %convolution_bitcast_fusion.11, f32[1,2,192,192]{3,2,1,0:T(8,128)S(1)} %get-tuple-element.29, f32[1,2,192,192]{3,2,1,0:T(8,128)S(1)} %get-tuple-element.30), kind=kOutput, calls=%fused_computation.31 | convolution fusion | flops 679624704 | bytes 1769472 | tf_op jit(solution)/shard_map/dcyj,icxj->idxy/dot_general | solution.py:92
  102.0 2.4 %convolution_bitcast_fusion.8 = f32[3,2,96,192]{3,2,1,0:T(8,128)S(1)} fusion(f32[3,2,96,192,1]{2,3,1,4,0:T(8,128)S(1)} %convolution_bitcast_fusion.9, f32[1,2,192,192]{3,2,1,0:T(8,128)S(1)} %get-tuple-element.29, f32[1,2,192,192]{3,2,1,0:T(8,128)S(1)} %get-tuple-element.30), kind=kOutput, calls=%fused_computation.29 | convolution fusion | flops 509755392 | bytes 1474560 | tf_op jit(solution)/shard_map/dcyj,icxj->idxy/dot_general | solution.py:92
  107.4 7.1 %collective-permute-done.3 = f32[3,2,64,128]{3,2,1,0:T(8,128)S(1)} collective-permute-done((f32[3,2,64,128]{3,2,1,0:T(8,128)S(1)}, f32[3,2,64,128]{3,2,1,0:T(8,128)S(1)}, u32[]{:S(2)}, u32[]{:S(2)}) %collective-permute-start.3) | collective-permute-done | bytes 196640 | tf_op jit(solution)/shard_map/ppermute | solution.py:109
  114.7 3.2 %collective-permute-start.4 = (f32[6,64,128]{1,2,0:T(8,128)S(1)}, f32[6,64,128]{1,2,0:T(8,128)S(1)}, u32[]{:S(2)}, u32[]{:S(2)}) collective-permute-start(f32[6,64,128]{1,2,0:T(8,128)S(1)} %copy.18), channel_id=1, source_target_pairs={{0,4},{4,8},{8,12},{1,5},{5,9},{9,13},{2,6},{6,10},{10,14},{3,7},{... | collective-permute-start | bytes 589832 | tf_op jit(solution)/shard_map/ppermute | solution.py:47
  117.9 2.1 %collective-permute-start.5 = (f32[6,64,128]{1,2,0:T(8,128)S(1)}, f32[6,64,128]{1,2,0:T(8,128)S(1)}, u32[]{:S(2)}, u32[]{:S(2)}) collective-permute-start(f32[6,64,128]{1,2,0:T(8,128)S(1)} %copy.18), channel_id=1, source_target_pairs={{4,0},{8,4},{12,8},{5,1},{9,5},{13,9},{6,2},{10,6},{14,10},{7,3},{... | collective-permute-start | bytes 589832 | tf_op jit(solution)/shard_map/ppermute | solution.py:48
  120.0 6.4 %collective-permute-done.4 = f32[6,64,128]{1,2,0:T(8,128)S(1)} collective-permute-done((f32[6,64,128]{1,2,0:T(8,128)S(1)}, f32[6,64,128]{1,2,0:T(8,128)S(1)}, u32[]{:S(2)}, u32[]{:S(2)}) %collective-permute-start.4) | collective-permute-done | bytes 196640 | tf_op jit(solution)/shard_map/ppermute | solution.py:47
  126.4 2.9 %collective-permute-done.5 = f32[6,64,128]{1,2,0:T(8,128)S(1)} collective-permute-done((f32[6,64,128]{1,2,0:T(8,128)S(1)}, f32[6,64,128]{1,2,0:T(8,128)S(1)}, u32[]{:S(2)}, u32[]{:S(2)}) %collective-permute-start.5) | collective-permute-done | bytes 196640 | tf_op jit(solution)/shard_map/ppermute | solution.py:48
  129.7 2.0 %collective-permute-start.6 = (f32[6,192,64]{1,2,0:T(8,128)S(1)}, f32[6,192,64]{1,2,0:T(8,128)}, u32[]{:S(2)}, u32[]{:S(2)}) collective-permute-start(f32[6,192,64]{1,2,0:T(8,128)S(1)} %slice_select_fusion.1), channel_id=1, source_target_pairs={{0,1},{1,0},{2,3},{3,2},{4,5},{5,4},{6,7},{7,6},{8,9},{9,8},{10,11... | collective-permute-start | bytes 884744 | tf_op jit(solution)/shard_map/ppermute | solution.py:52
  131.7 1.5 collective-permute-done.6
  133.2 1.4 fusion.1
  135.2 1.8 %convolution_bitcast_fusion.1 = f32[3,2,160,192,1]{3,2,1,4,0:T(8,128)S(1)} fusion(f32[3,1,192,192]{3,2,1,0:T(8,128)S(1)} %get-tuple-element.8, f32[3,1,192,192]{3,2,1,0:T(8,128)S(1)} %get-tuple-element.7, f32[1,2,192,192]{3,2,1,0:T(8,128)S(1)} %get-tuple-element.30, f32[1,2,192,192]{3,2,1,0:T(8,128)S(1)} %get-tuple-element.29), kind=kOutput, calls=%fused_computation.22 | convolution fusion | flops 849690624 | bytes 2211840 | tf_op jit(solution)/shard_map/dcab,icbj->idaj/dot_general | solution.py:89
  137.1 1.7 %convolution_bitcast_fusion = f32[3,2,160,192]{3,2,1,0:T(8,128)S(1)} fusion(f32[3,2,160,192,1]{3,2,1,4,0:T(8,128)S(1)} %convolution_bitcast_fusion.1, f32[1,2,192,192]{3,2,1,0:T(8,128)S(1)} %get-tuple-element.29, f32[1,2,192,192]{3,2,1,0:T(8,128)S(1)} %get-tuple-element.30), kind=kOutput, calls=%fused_computation.21 | convolution fusion | flops 849494016 | bytes 2064384 | tf_op jit(solution)/shard_map/dcyj,icxj->idxy/dot_general | solution.py:92
  139.0 2.5 %convolution_bitcast_fusion.7 = f32[3,2,128,192,1]{2,3,1,4,0:T(8,128)S(1)} fusion(f32[3,1,160,192]{3,2,1,0:T(8,128)S(1)} %get-tuple-element.18, f32[3,1,160,192]{3,2,1,0:T(8,128)S(1)} %get-tuple-element.17, f32[1,2,192,192]{3,2,1,0:T(8,128)S(1)} %get-tuple-element.30, f32[1,2,192,192]{3,2,1,0:T(8,128)S(1)} %get-tuple-element.29), kind=kOutput, calls=%fused_computation.28 | convolution fusion | flops 566497280 | bytes 1916928 | tf_op jit(solution)/shard_map/dcab,icbj->idaj/dot_general | solution.py:89
  141.5 1.3 convolution_bitcast_fusion.6
  143.7 2.4 %convolution_bitcast_fusion.4 = f32[3,2,96,192]{3,2,1,0:T(8,128)S(1)} fusion(f32[3,2,96,192,1]{2,3,1,4,0:T(8,128)S(1)} %convolution_bitcast_fusion.5, f32[1,2,192,192]{3,2,1,0:T(8,128)S(1)} %get-tuple-element.29, f32[1,2,192,192]{3,2,1,0:T(8,128)S(1)} %get-tuple-element.30), kind=kOutput, calls=%fused_computation.25 | convolution fusion | flops 509755392 | bytes 1474560 | tf_op jit(solution)/shard_map/dcyj,icxj->idxy/dot_general | solution.py:92
  (74 shorter events, 13.8 us)
Async XLA Ops:
  0.0 18.6 %copy-start.1 = (f32[3,2,64,128]{3,2,1,0:T(8,128)S(1)}, f32[3,2,64,128]{3,2,1,0:T(8,128)}, u32[]{:S(2)}) copy-start(f32[3,2,64,128]{3,2,1,0:T(8,128)} %param.4) | copy-start | bytes 589828
  0.0 7.7 %copy-start.16 = (f32[2,33]{1,0:T(2,128)S(1)}, f32[2,33]{1,0:T(2,128)}, u32[]{:S(2)}) copy-start(f32[2,33]{1,0:T(2,128)} %param.7) | copy-start | bytes 796
  2.4 13.3 %collective-permute-start = (f32[14,64,128]{2,1,0:T(8,128)S(1)}, f32[14,64,128]{2,1,0:T(8,128)S(1)}, u32[]{:S(2)}, u32[]{:S(2)}) collective-permute-start(f32[14,64,128]{2,1,0:T(8,128)S(1)} %pad_maximum_fusion.3), channel_id=1, source_target_pairs={{0,4},{4,8},{8,12},{1,5},{5,9},{9,13},{2,6},{6,10},{10,14},{3,7},{... | collective-permute-start | bytes 1376264 | tf_op jit(solution)/shard_map/ppermute | solution.py:47
  5.6 13.0 %collective-permute-start.1 = (f32[14,64,128]{2,1,0:T(8,128)S(1)}, f32[14,64,128]{2,1,0:T(8,128)S(1)}, u32[]{:S(2)}, u32[]{:S(2)}) collective-permute-start(f32[14,64,128]{2,1,0:T(8,128)S(1)} %pad_maximum_fusion.3), channel_id=1, source_target_pairs={{4,0},{8,4},{12,8},{5,1},{9,5},{13,9},{6,2},{10,6},{14,10},{7,3},{... | collective-permute-start | bytes 1376264 | tf_op jit(solution)/shard_map/ppermute | solution.py:48
  20.6 65.4 %collective-permute-start.2 = (f32[14,192,64]{1,2,0:T(8,128)}, f32[14,192,64]{1,2,0:T(8,128)}, u32[]{:S(2)}, u32[]{:S(2)}) collective-permute-start(f32[14,192,64]{1,2,0:T(8,128)} %copy.11), channel_id=1, source_target_pairs={{0,1},{1,0},{2,3},{3,2},{4,5},{5,4},{6,7},{7,6},{8,9},{9,8},{10,11... | collective-permute-start | bytes 2064392 | tf_op jit(solution)/shard_map/ppermute | solution.py:52
  89.9 1.5 %copy-start = (f32[14,192,192]{2,1,0:T(8,128)}, f32[14,192,192]{2,1,0:T(8,128)S(1)}, u32[]{:S(2)}) copy-start(f32[14,192,192]{2,1,0:T(8,128)S(1)} %dynamic-slice_maximum_fusion) | copy-start | bytes 6193156
  91.6 1.5 slice-start
  91.6 5.1 %copy-start.4 = (f32[160,192]{1,0:T(8,128)}, f32[160,192]{1,0:T(8,128)S(1)}, u32[]{:S(2)}) copy-start(f32[160,192]{1,0:T(8,128)S(1)} %get-tuple-element.13) | copy-start | bytes 368644
  91.6 5.1 %copy-start.6 = (f32[160,192]{1,0:T(8,128)}, f32[160,192]{1,0:T(8,128)S(1)}, u32[]{:S(2)}) copy-start(f32[160,192]{1,0:T(8,128)S(1)} %get-tuple-element.14) | copy-start | bytes 368644
  91.7 12.7 %copy-start.12 = (f32[96,192]{1,0:T(8,128)}, f32[96,192]{1,0:T(8,128)S(1)}, u32[]{:S(2)}) copy-start(f32[96,192]{1,0:T(8,128)S(1)} %get-tuple-element.9) | copy-start | bytes 221188
  91.7 12.7 %copy-start.14 = (f32[96,192]{1,0:T(8,128)}, f32[96,192]{1,0:T(8,128)S(1)}, u32[]{:S(2)}) copy-start(f32[96,192]{1,0:T(8,128)S(1)} %get-tuple-element.10) | copy-start | bytes 221188
  101.0 0.9 copy-start.8
  101.1 0.8 copy-start.10
  105.9 20.5 %copy-start.2 = (f32[3,64,2,192]{3,1,2,0:T(8,128)}, f32[3,64,2,192]{3,1,2,0:T(8,128)S(1)}, u32[]{:S(2)}) copy-start(f32[3,64,2,192]{3,1,2,0:T(8,128)S(1)} %convolution_bitcast_fusion.14) | copy-start | bytes 884740
  106.1 8.4 %collective-permute-start.3 = (f32[3,2,64,128]{3,2,1,0:T(8,128)S(1)}, f32[3,2,64,128]{3,2,1,0:T(8,128)S(1)}, u32[]{:S(2)}, u32[]{:S(2)}) collective-permute-start(f32[3,2,64,128]{3,2,1,0:T(8,128)S(1)} %dynamic-slice_bitcast_fusion), channel_id=1, source_target_pairs={{0,2},{1,3},{4,6},{5,7},{8,10},{9,11},{12,14},{13,15},{16,18},{17,... | collective-permute-start | bytes 589832 | tf_op jit(solution)/shard_map/ppermute | solution.py:109
  114.7 11.8 %collective-permute-start.4 = (f32[6,64,128]{1,2,0:T(8,128)S(1)}, f32[6,64,128]{1,2,0:T(8,128)S(1)}, u32[]{:S(2)}, u32[]{:S(2)}) collective-permute-start(f32[6,64,128]{1,2,0:T(8,128)S(1)} %copy.18), channel_id=1, source_target_pairs={{0,4},{4,8},{8,12},{1,5},{5,9},{9,13},{2,6},{6,10},{10,14},{3,7},{... | collective-permute-start | bytes 589832 | tf_op jit(solution)/shard_map/ppermute | solution.py:47
  117.9 11.4 %collective-permute-start.5 = (f32[6,64,128]{1,2,0:T(8,128)S(1)}, f32[6,64,128]{1,2,0:T(8,128)S(1)}, u32[]{:S(2)}, u32[]{:S(2)}) collective-permute-start(f32[6,64,128]{1,2,0:T(8,128)S(1)} %copy.18), channel_id=1, source_target_pairs={{4,0},{8,4},{12,8},{5,1},{9,5},{13,9},{6,2},{10,6},{14,10},{7,3},{... | collective-permute-start | bytes 589832 | tf_op jit(solution)/shard_map/ppermute | solution.py:48
  129.7 3.5 %collective-permute-start.6 = (f32[6,192,64]{1,2,0:T(8,128)S(1)}, f32[6,192,64]{1,2,0:T(8,128)}, u32[]{:S(2)}, u32[]{:S(2)}) collective-permute-start(f32[6,192,64]{1,2,0:T(8,128)S(1)} %slice_select_fusion.1), channel_id=1, source_target_pairs={{0,1},{1,0},{2,3},{3,2},{4,5},{5,4},{6,7},{7,6},{8,9},{9,8},{10,11... | collective-permute-start | bytes 884744 | tf_op jit(solution)/shard_map/ppermute | solution.py:52
  137.0 1.8 %copy-start.5 = (f32[160,192]{1,0:T(8,128)S(1)}, f32[160,192]{1,0:T(8,128)}, u32[]{:S(2)}) copy-start(f32[160,192]{1,0:T(8,128)} %copy-done.4) | copy-start | bytes 368644
  137.1 1.8 %copy-start.7 = (f32[160,192]{1,0:T(8,128)S(1)}, f32[160,192]{1,0:T(8,128)}, u32[]{:S(2)}) copy-start(f32[160,192]{1,0:T(8,128)} %copy-done.6) | copy-start | bytes 368644
  141.5 1.4 copy-start.9
  141.5 1.4 copy-start.11
  143.6 2.4 %copy-start.13 = (f32[96,192]{1,0:T(8,128)S(1)}, f32[96,192]{1,0:T(8,128)}, u32[]{:S(2)}) copy-start(f32[96,192]{1,0:T(8,128)} %copy-done.12) | copy-start | bytes 221188
  143.6 2.4 %copy-start.15 = (f32[96,192]{1,0:T(8,128)S(1)}, f32[96,192]{1,0:T(8,128)}, u32[]{:S(2)}) copy-start(f32[96,192]{1,0:T(8,128)} %copy-done.14) | copy-start | bytes 221188
  146.1 1.5 copy-start.3
where the time goes:
time: 150 us; the launch traced here: 148 us
  other arithmetic  71.3 us (48%)
  waiting for transfers between devices  26 us (17%)
  matrix products  24 us (16%)
  starting transfers between devices  15.8 us (11%)
  local copies, waits for them, and re-layouts  9.92 us (7%)
    select_n x1, other arithmetic, toeplitz(): band_real = jnp.where(hit, kernel[0, tap], band_real)  20.7 us
    neg x1, other arithmetic, toeplitz(): top = jnp.stack([band_real, -band_imag], axis=0)  20.7 us
    select_n x1, other arithmetic, toeplitz(): band_imag = jnp.where(hit, kernel[1, tap], band_imag)  20.7 us
    dot_general x8, matrix products, depth_section(): jnp.einsum('dcyj,icxj->idxy', col_band, rows_done, precision=lax.Precisio...  12.7 us
    ppermute x2, waiting for transfers between devices, grow(): lax.ppermute(stack[:, rows - halo:], 'tile', [(i, i + 1) for i in range(t...  11.6 us
    dot_general x8, matrix products, depth_section(): jnp.einsum('dcab,icbj->idaj', row_bands[s], moved, precision=lax.Precisio...  11.3 us
    ppermute x1, waiting for transfers between devices, per_device(): lax.ppermute(result, 'depth', [(i, i + 1) for i in range(depth_count - 1)])  7.13 us
    ppermute x2, starting transfers between devices, grow(): lax.ppermute(stack[:, rows - halo:], 'tile', [(i, i + 1) for i in range(t...  6.41 us
  transfers between devices with their start and end apart: 7, of which 6 were waited for; matrix products, arithmetic and copies ran while one was open for 44% of the time, Pallas kernels for 0%

commit v1 on v0

--- a/solution.py
+++ b/solution.py
@@ -8,15 +8,12 @@
 
 
 def toeplitz(kernel, size, shift):
-    outer = jnp.arange(size, dtype=jnp.int32)[:, None]
-    inner = jnp.arange(size, dtype=jnp.int32)[None, :]
-    offsets = inner - outer + shift
-    band_real = jnp.zeros((size, size), jnp.float32)
-    band_imag = jnp.zeros((size, size), jnp.float32)
-    for tap in range(TAPS):
-        hit = offsets == tap
-        band_real = jnp.where(hit, kernel[0, tap], band_real)
-        band_imag = jnp.where(hit, kernel[1, tap], band_imag)
+    period = 2 * size
+    gap = jnp.zeros((2, period - TAPS), jnp.float32)
+    base = jnp.concatenate([kernel[:, shift:], gap, kernel[:, :shift]], axis=1)
+    rolled = jnp.tile(base, (1, size))[:, : size * (period - 1)]
+    bands = rolled.reshape(2, size, period - 1)[:, :, :size]
+    band_real, band_imag = bands[0], bands[1]
     top = jnp.stack([band_real, -band_imag], axis=0)
     bottom = jnp.stack([band_imag, band_real], axis=0)
     return jnp.stack([top, bottom], axis=0)

time: 150 us -> 87.4 us (0.58)
  other arithmetic: 71.3 us -> 9.42 us
    select_n x2 -> x0, other arithmetic: 41.4 us -> none  [the longest x1 20.7 us: toeplitz(): band_real = jnp.where(hit, kernel[0, tap], band_real)]
    neg x1 -> x0, other arithmetic: 20.7 us -> none  [toeplitz(): top = jnp.stack([band_real, -band_imag], axis=0)]
    slice x4 -> x2, local copies, waits for them, and re-layouts: 2.87 us -> 0.11 us  [the longest x1 0.07 us: toeplitz(): base = jnp.concatenate([kernel[:, shift:], gap, kernel[:, :shift]], axis=1)]
  transfers between devices with their start and end apart: 7 -> 7, of which waited for: 6 -> 7; matrix products, arithmetic and copies ran while one was open for 44% -> 3% of each run, Pallas kernels for 0% -> 0%
where the time goes in v1:
time: 87.4 us; the launch traced here: 86.9 us
  waiting for transfers between devices  27.3 us (31%)
  matrix products  24 us (27%)
  starting transfers between devices  16.2 us (19%)
  other arithmetic  9.42 us (11%)
  local copies, waits for them, and re-layouts  8.54 us (10%)
  between operations  1.35 us (2%)
    dot_general x8, matrix products, depth_section(): jnp.einsum('dcyj,icxj->idxy', col_band, rows_done, precision=lax.Precisio...  12.7 us
    ppermute x2, waiting for transfers between devices, grow(): lax.ppermute(stack[:, rows - halo:], 'tile', [(i, i + 1) for i in range(t...  12.5 us
    dot_general x8, matrix products, depth_section(): jnp.einsum('dcab,icbj->idaj', row_bands[s], moved, precision=lax.Precisio...  11.3 us
    ppermute x1, waiting for transfers between devices, per_device(): lax.ppermute(result, 'depth', [(i, i + 1) for i in range(depth_count - 1)])  6.71 us
    ppermute x2, starting transfers between devices, grow(): lax.ppermute(stack[:, rows - halo:], 'tile', [(i, i + 1) for i in range(t...  6.41 us
    ppermute x2, waiting for transfers between devices, grow(): lax.ppermute(stack[:, :halo], 'tile', [(i + 1, i) for i in range(tiles -...  5.82 us
    ppermute x2, starting transfers between devices, grow(): got = lax.ppermute(edge, 'wave', [(0, 1), (1, 0)])  4.33 us
    ppermute x2, starting transfers between devices, grow(): lax.ppermute(stack[:, :halo], 'tile', [(i + 1, i) for i in range(tiles -...  4.2 us
  transfers between devices with their start and end apart: 7, of which 7 were waited for; matrix products, arithmetic and copies ran while one was open for 3% of the time, Pallas kernels for 0%

profile of v1, /device:TPU:15, one launch (start us, length us, event | category | flops | bytes accessed | tf_op | source)
XLA Modules:
  0.0 86.9 jit_solution(13392988578434198909)
XLA Ops:
  0.0 1.4 %fusion.33 = (f32[4,1,64,128]{3,2,1,0:T(8,128)S(1)}, f32[4,1,64,128]{3,2,1,0:T(8,128)S(1)}) fusion(bf16[4,64,128]{2,1,0:T(8,128)(2,1)} %param.5, bf16[4,64,128]{2,1,0:T(8,128)(2,1)} %param.6), kind=kLoop, calls=%fused_computation.105 | loop fusion | flops 163840 | bytes 393216 | tf_op jit(solution)/shard_map/stack | solution.py:25
  1.4 1.0 %pad_maximum_fusion.3 = f32[14,64,128]{2,1,0:T(8,128)S(1)} fusion(f32[8,64,128]{2,1,0:T(8,128)S(1)} %bitcast.231, f32[6,64,128]{2,1,0:T(8,128)} %bitcast.238), kind=kLoop, calls=%fused_computation.79 | loop fusion | flops 114688 | bytes 917504 | tf_op jit(solution)/shard_map/concatenate | solution.py:67
  2.4 3.2 %collective-permute-start = (f32[14,64,128]{2,1,0:T(8,128)S(1)}, f32[14,64,128]{2,1,0:T(8,128)S(1)}, u32[]{:S(2)}, u32[]{:S(2)}) collective-permute-start(f32[14,64,128]{2,1,0:T(8,128)S(1)} %pad_maximum_fusion.3), channel_id=1, source_target_pairs={{0,4},{4,8},{8,12},{1,5},{5,9},{9,13},{2,6},{6,10},{10,14},{3,7},{... | collective-permute-start | bytes 1376264 | tf_op jit(solution)/shard_map/ppermute | solution.py:44
  5.6 2.1 %collective-permute-start.1 = (f32[14,64,128]{2,1,0:T(8,128)S(1)}, f32[14,64,128]{2,1,0:T(8,128)S(1)}, u32[]{:S(2)}, u32[]{:S(2)}) collective-permute-start(f32[14,64,128]{2,1,0:T(8,128)S(1)} %pad_maximum_fusion.3), channel_id=1, source_target_pairs={{4,0},{8,4},{12,8},{5,1},{9,5},{13,9},{6,2},{10,6},{14,10},{7,3},{... | collective-permute-start | bytes 1376264 | tf_op jit(solution)/shard_map/ppermute | solution.py:45
  9.2 6.5 %collective-permute-done = f32[14,64,128]{2,1,0:T(8,128)S(1)} collective-permute-done((f32[14,64,128]{2,1,0:T(8,128)S(1)}, f32[14,64,128]{2,1,0:T(8,128)S(1)}, u32[]{:S(2)}, u32[]{:S(2)}) %collective-permute-start) | collective-permute-done | bytes 458784 | tf_op jit(solution)/shard_map/ppermute | solution.py:44
  15.7 2.9 %collective-permute-done.1 = f32[14,64,128]{2,1,0:T(8,128)S(1)} collective-permute-done((f32[14,64,128]{2,1,0:T(8,128)S(1)}, f32[14,64,128]{2,1,0:T(8,128)S(1)}, u32[]{:S(2)}, u32[]{:S(2)}) %collective-permute-start.1) | collective-permute-done | bytes 458784 | tf_op jit(solution)/shard_map/ppermute | solution.py:45
  19.1 1.5 %copy.11 = f32[14,192,64]{1,2,0:T(8,128)} copy(f32[14,192,64]{2,1,0:T(8,128)S(1)} %slice_select_fusion) | data formatting | bytes 1376256 | tf_op jit(solution)/shard_map/jit(_where)/select_n | solution.py:48
  20.6 1.9 %collective-permute-start.2 = (f32[14,192,64]{1,2,0:T(8,128)}, f32[14,192,64]{1,2,0:T(8,128)}, u32[]{:S(2)}, u32[]{:S(2)}) collective-permute-start(f32[14,192,64]{1,2,0:T(8,128)} %copy.11), channel_id=1, source_target_pairs={{0,1},{1,0},{2,3},{3,2},{4,5},{5,4},{6,7},{7,6},{8,9},{9,8},{10,11... | collective-permute-start | bytes 2064392 | tf_op jit(solution)/shard_map/ppermute | solution.py:49
  24.9 1.6 %copy.12 = f32[14,192,64]{2,1,0:T(8,128)S(1)} copy(f32[14,192,64]{1,2,0:T(8,128)} %collective-permute-done.2) | data formatting | bytes 1376256 | tf_op jit(solution)/shard_map/ppermute | solution.py:49
  26.5 2.3 %dynamic-slice_maximum_fusion = f32[14,192,192]{2,1,0:T(8,128)S(1)} fusion(s32[]{:T(128)S(6)} %select_n.42, f32[14,192,64]{2,1,0:T(8,128)S(1)} %copy.12, f32[14,64,128]{2,1,0:T(8,128)S(1)} %collective-permute-done.1, f32[8,64,128]{2,1,0:T(8,128)S(1)} %bitcast.233, f32[6,64,128]{2,1,0:T(8,128)S(1)} %bitcast.240, f32[14,64,128]{2,1,0:T(8,128)S(1)} %collective-permute-done), kind=kLoop, calls=%fused_computation | loop fusion | flops 2580480 | bytes 4128772 | tf_op jit(solution)/shard_map/concatenate | solution.py:50
  28.9 1.5 %copy-done = f32[14,192,192]{2,1,0:T(8,128)} copy-done((f32[14,192,192]{2,1,0:T(8,128)}, f32[14,192,192]{2,1,0:T(8,128)S(1)}, u32[]{:S(2)}) %copy-start) | copy-done | bytes 2064408
  30.6 1.3 %slice-done = f32[6,192,192]{2,1,0:T(8,128)S(1)} async-done(((f32[14,192,192]{2,1,0:T(8,128)}), f32[6,192,192]{2,1,0:T(8,128)S(1)}, s32[]{:S(2)}) %slice-start) | async-done | bytes 884760 | tf_op jit(solution)/shard_map/slice | solution.py:70
  32.0 1.8 %convolution_bitcast_fusion.3 = f32[3,2,160,192,1]{3,2,1,4,0:T(8,128)S(1)} fusion(f32[3,1,192,192]{3,2,1,0:T(8,128)S(1)} %get-tuple-element.16, f32[3,1,192,192]{3,2,1,0:T(8,128)S(1)} %get-tuple-element.15, f32[1,2,192,192]{3,2,1,0:T(8,128)S(1)} %get-tuple-element.33, f32[1,2,192,192]{3,2,1,0:T(8,128)S(1)} %get-tuple-element.32), kind=kOutput, calls=%fused_computation.24 | convolution fusion | flops 849690624 | bytes 2211840 | tf_op jit(solution)/shard_map/dcab,icbj->idaj/dot_general | solution.py:86
  33.9 1.7 %convolution_bitcast_fusion.2 = f32[3,2,160,192]{3,2,1,0:T(8,128)S(1)} fusion(f32[3,2,160,192,1]{3,2,1,4,0:T(8,128)S(1)} %convolution_bitcast_fusion.3, f32[1,2,192,192]{3,2,1,0:T(8,128)S(1)} %get-tuple-element.32, f32[1,2,192,192]{3,2,1,0:T(8,128)S(1)} %get-tuple-element.33), kind=kOutput, calls=%fused_computation.23 | convolution fusion | flops 849494016 | bytes 2064384 | tf_op jit(solution)/shard_map/dcyj,icxj->idxy/dot_general | solution.py:89
  35.8 2.5 %convolution_bitcast_fusion.11 = f32[3,2,128,192,1]{2,3,1,4,0:T(8,128)S(1)} fusion(f32[3,1,160,192]{3,2,1,0:T(8,128)S(1)} %get-tuple-element.20, f32[3,1,160,192]{3,2,1,0:T(8,128)S(1)} %get-tuple-element.19, f32[1,2,192,192]{3,2,1,0:T(8,128)S(1)} %get-tuple-element.33, f32[1,2,192,192]{3,2,1,0:T(8,128)S(1)} %get-tuple-element.32), kind=kOutput, calls=%fused_computation.32 | convolution fusion | flops 566497280 | bytes 1916928 | tf_op jit(solution)/shard_map/dcab,icbj->idaj/dot_general | solution.py:86
  38.3 1.5 %convolution_bitcast_fusion.10 = f32[3,2,128,192]{2,3,1,0:T(8,128)S(1)} fusion(f32[3,2,128,192,1]{2,3,1,4,0:T(8,128)S(1)} %convolution_bitcast_fusion.11, f32[1,2,192,192]{3,2,1,0:T(8,128)S(1)} %get-tuple-element.32, f32[1,2,192,192]{3,2,1,0:T(8,128)S(1)} %get-tuple-element.33), kind=kOutput, calls=%fused_computation.31 | convolution fusion | flops 679624704 | bytes 1769472 | tf_op jit(solution)/shard_map/dcyj,icxj->idxy/dot_general | solution.py:89
  40.8 2.4 %convolution_bitcast_fusion.8 = f32[3,2,96,192]{3,2,1,0:T(8,128)S(1)} fusion(f32[3,2,96,192,1]{2,3,1,4,0:T(8,128)S(1)} %convolution_bitcast_fusion.9, f32[1,2,192,192]{3,2,1,0:T(8,128)S(1)} %get-tuple-element.32, f32[1,2,192,192]{3,2,1,0:T(8,128)S(1)} %get-tuple-element.33), kind=kOutput, calls=%fused_computation.29 | convolution fusion | flops 509755392 | bytes 1474560 | tf_op jit(solution)/shard_map/dcyj,icxj->idxy/dot_general | solution.py:89
  44.9 1.3 %collective-permute-start.3 = (f32[3,2,64,128]{3,2,1,0:T(8,128)S(1)}, f32[3,2,64,128]{3,2,1,0:T(8,128)S(1)}, u32[]{:S(2)}, u32[]{:S(2)}) collective-permute-start(f32[3,2,64,128]{3,2,1,0:T(8,128)S(1)} %dynamic-slice_bitcast_fusion), channel_id=1, source_target_pairs={{0,2},{1,3},{4,6},{5,7},{8,10},{9,11},{12,14},{13,15},{16,18},{17,... | collective-permute-start | bytes 589832 | tf_op jit(solution)/shard_map/ppermute | solution.py:106
  46.2 6.7 %collective-permute-done.3 = f32[3,2,64,128]{3,2,1,0:T(8,128)S(1)} collective-permute-done((f32[3,2,64,128]{3,2,1,0:T(8,128)S(1)}, f32[3,2,64,128]{3,2,1,0:T(8,128)S(1)}, u32[]{:S(2)}, u32[]{:S(2)}) %collective-permute-start.3) | collective-permute-done | bytes 196640 | tf_op jit(solution)/shard_map/ppermute | solution.py:106
  53.1 3.2 %collective-permute-start.4 = (f32[6,64,128]{1,2,0:T(8,128)S(1)}, f32[6,64,128]{1,2,0:T(8,128)S(1)}, u32[]{:S(2)}, u32[]{:S(2)}) collective-permute-start(f32[6,64,128]{1,2,0:T(8,128)S(1)} %copy.18), channel_id=1, source_target_pairs={{0,4},{4,8},{8,12},{1,5},{5,9},{9,13},{2,6},{6,10},{10,14},{3,7},{... | collective-permute-start | bytes 589832 | tf_op jit(solution)/shard_map/ppermute | solution.py:44
  56.3 2.1 %collective-permute-start.5 = (f32[6,64,128]{1,2,0:T(8,128)S(1)}, f32[6,64,128]{1,2,0:T(8,128)S(1)}, u32[]{:S(2)}, u32[]{:S(2)}) collective-permute-start(f32[6,64,128]{1,2,0:T(8,128)S(1)} %copy.18), channel_id=1, source_target_pairs={{4,0},{8,4},{12,8},{5,1},{9,5},{13,9},{6,2},{10,6},{14,10},{7,3},{... | collective-permute-start | bytes 589832 | tf_op jit(solution)/shard_map/ppermute | solution.py:45
  58.4 6.0 %collective-permute-done.4 = f32[6,64,128]{1,2,0:T(8,128)S(1)} collective-permute-done((f32[6,64,128]{1,2,0:T(8,128)S(1)}, f32[6,64,128]{1,2,0:T(8,128)S(1)}, u32[]{:S(2)}, u32[]{:S(2)}) %collective-permute-start.4) | collective-permute-done | bytes 196640 | tf_op jit(solution)/shard_map/ppermute | solution.py:44
  64.4 2.9 %collective-permute-done.5 = f32[6,64,128]{1,2,0:T(8,128)S(1)} collective-permute-done((f32[6,64,128]{1,2,0:T(8,128)S(1)}, f32[6,64,128]{1,2,0:T(8,128)S(1)}, u32[]{:S(2)}, u32[]{:S(2)}) %collective-permute-start.5) | collective-permute-done | bytes 196640 | tf_op jit(solution)/shard_map/ppermute | solution.py:45
  67.7 2.5 %collective-permute-start.6 = (f32[6,192,64]{1,2,0:T(8,128)S(1)}, f32[6,192,64]{1,2,0:T(8,128)}, u32[]{:S(2)}, u32[]{:S(2)}) collective-permute-start(f32[6,192,64]{1,2,0:T(8,128)S(1)} %slice_select_fusion.1), channel_id=1, source_target_pairs={{0,1},{1,0},{2,3},{3,2},{4,5},{5,4},{6,7},{7,6},{8,9},{9,8},{10,11... | collective-permute-start | bytes 884744 | tf_op jit(solution)/shard_map/ppermute | solution.py:49
  70.1 1.5 %collective-permute-done.6 = f32[6,192,64]{1,2,0:T(8,128)} collective-permute-done((f32[6,192,64]{1,2,0:T(8,128)S(1)}, f32[6,192,64]{1,2,0:T(8,128)}, u32[]{:S(2)}, u32[]{:S(2)}) %collective-permute-start.6) | collective-permute-done | bytes 294944 | tf_op jit(solution)/shard_map/ppermute | solution.py:49
  71.6 1.4 %fusion.1 = f32[6,192,192]{1,2,0:T(8,128)S(1)} fusion(s32[]{:T(128)S(6)} %select_n.42, f32[6,192,64]{1,2,0:T(8,128)} %collective-permute-done.6, f32[6,64,128]{1,2,0:T(8,128)S(1)} %collective-permute-done.4, f32[6,64,128]{1,2,0:T(8,128)S(1)} %copy.18, f32[6,64,128]{1,2,0:T(8,128)S(1)} %collective-permute-done.5), kind=kLoop, calls=%fused_computation.38 | loop fusion | flops 884736 | bytes 1769476 | tf_op jit(solution)/shard_map/concatenate | solution.py:50
  73.6 1.8 %convolution_bitcast_fusion.1 = f32[3,2,160,192,1]{3,2,1,4,0:T(8,128)S(1)} fusion(f32[3,1,192,192]{3,2,1,0:T(8,128)S(1)} %get-tuple-element.8, f32[3,1,192,192]{3,2,1,0:T(8,128)S(1)} %get-tuple-element.7, f32[1,2,192,192]{3,2,1,0:T(8,128)S(1)} %get-tuple-element.33, f32[1,2,192,192]{3,2,1,0:T(8,128)S(1)} %get-tuple-element.32), kind=kOutput, calls=%fused_computation.22 | convolution fusion | flops 849690624 | bytes 2211840 | tf_op jit(solution)/shard_map/dcab,icbj->idaj/dot_general | solution.py:86
  75.5 1.7 %convolution_bitcast_fusion = f32[3,2,160,192]{3,2,1,0:T(8,128)S(1)} fusion(f32[3,2,160,192,1]{3,2,1,4,0:T(8,128)S(1)} %convolution_bitcast_fusion.1, f32[1,2,192,192]{3,2,1,0:T(8,128)S(1)} %get-tuple-element.32, f32[1,2,192,192]{3,2,1,0:T(8,128)S(1)} %get-tuple-element.33), kind=kOutput, calls=%fused_computation.21 | convolution fusion | flops 849494016 | bytes 2064384 | tf_op jit(solution)/shard_map/dcyj,icxj->idxy/dot_general | solution.py:89
  77.4 2.5 %convolution_bitcast_fusion.7 = f32[3,2,128,192,1]{2,3,1,4,0:T(8,128)S(1)} fusion(f32[3,1,160,192]{3,2,1,0:T(8,128)S(1)} %get-tuple-element.18, f32[3,1,160,192]{3,2,1,0:T(8,128)S(1)} %get-tuple-element.17, f32[1,2,192,192]{3,2,1,0:T(8,128)S(1)} %get-tuple-element.33, f32[1,2,192,192]{3,2,1,0:T(8,128)S(1)} %get-tuple-element.32), kind=kOutput, calls=%fused_computation.28 | convolution fusion | flops 566497280 | bytes 1916928 | tf_op jit(solution)/shard_map/dcab,icbj->idaj/dot_general | solution.py:86
  79.9 1.3 %convolution_bitcast_fusion.6 = f32[3,2,128,192]{2,3,1,0:T(8,128)S(1)} fusion(f32[3,2,128,192,1]{2,3,1,4,0:T(8,128)S(1)} %convolution_bitcast_fusion.7, f32[1,2,192,192]{3,2,1,0:T(8,128)S(1)} %get-tuple-element.32, f32[1,2,192,192]{3,2,1,0:T(8,128)S(1)} %get-tuple-element.33), kind=kOutput, calls=%fused_computation.27 | convolution fusion | flops 679624704 | bytes 1769472 | tf_op jit(solution)/shard_map/dcyj,icxj->idxy/dot_general | solution.py:89
  82.1 2.4 %convolution_bitcast_fusion.4 = f32[3,2,96,192]{3,2,1,0:T(8,128)S(1)} fusion(f32[3,2,96,192,1]{2,3,1,4,0:T(8,128)S(1)} %convolution_bitcast_fusion.5, f32[1,2,192,192]{3,2,1,0:T(8,128)S(1)} %get-tuple-element.32, f32[1,2,192,192]{3,2,1,0:T(8,128)S(1)} %get-tuple-element.33), kind=kOutput, calls=%fused_computation.25 | convolution fusion | flops 509755392 | bytes 1474560 | tf_op jit(solution)/shard_map/dcyj,icxj->idxy/dot_general | solution.py:89
  86.0 0.9 fusion.29
  (76 shorter events, 10.3 us)
Async XLA Ops:
  0.0 18.6 %copy-start.1 = (f32[3,2,64,128]{3,2,1,0:T(8,128)S(1)}, f32[3,2,64,128]{3,2,1,0:T(8,128)}, u32[]{:S(2)}) copy-start(f32[3,2,64,128]{3,2,1,0:T(8,128)} %param.4) | copy-start | bytes 589828
  0.0 7.7 %copy-start.16 = (f32[2,33]{1,0:T(2,128)S(1)}, f32[2,33]{1,0:T(2,128)}, u32[]{:S(2)}) copy-start(f32[2,33]{1,0:T(2,128)} %param.7) | copy-start | bytes 796
  2.4 13.3 %collective-permute-start = (f32[14,64,128]{2,1,0:T(8,128)S(1)}, f32[14,64,128]{2,1,0:T(8,128)S(1)}, u32[]{:S(2)}, u32[]{:S(2)}) collective-permute-start(f32[14,64,128]{2,1,0:T(8,128)S(1)} %pad_maximum_fusion.3), channel_id=1, source_target_pairs={{0,4},{4,8},{8,12},{1,5},{5,9},{9,13},{2,6},{6,10},{10,14},{3,7},{... | collective-permute-start | bytes 1376264 | tf_op jit(solution)/shard_map/ppermute | solution.py:44
  5.6 13.0 %collective-permute-start.1 = (f32[14,64,128]{2,1,0:T(8,128)S(1)}, f32[14,64,128]{2,1,0:T(8,128)S(1)}, u32[]{:S(2)}, u32[]{:S(2)}) collective-permute-start(f32[14,64,128]{2,1,0:T(8,128)S(1)} %pad_maximum_fusion.3), channel_id=1, source_target_pairs={{4,0},{8,4},{12,8},{5,1},{9,5},{13,9},{6,2},{10,6},{14,10},{7,3},{... | collective-permute-start | bytes 1376264 | tf_op jit(solution)/shard_map/ppermute | solution.py:45
  20.6 4.3 %collective-permute-start.2 = (f32[14,192,64]{1,2,0:T(8,128)}, f32[14,192,64]{1,2,0:T(8,128)}, u32[]{:S(2)}, u32[]{:S(2)}) collective-permute-start(f32[14,192,64]{1,2,0:T(8,128)} %copy.11), channel_id=1, source_target_pairs={{0,1},{1,0},{2,3},{3,2},{4,5},{5,4},{6,7},{7,6},{8,9},{9,8},{10,11... | collective-permute-start | bytes 2064392 | tf_op jit(solution)/shard_map/ppermute | solution.py:49
  28.8 1.5 %copy-start = (f32[14,192,192]{2,1,0:T(8,128)}, f32[14,192,192]{2,1,0:T(8,128)S(1)}, u32[]{:S(2)}) copy-start(f32[14,192,192]{2,1,0:T(8,128)S(1)} %dynamic-slice_maximum_fusion) | copy-start | bytes 6193156
  30.4 1.5 %slice-start = ((f32[14,192,192]{2,1,0:T(8,128)}), f32[6,192,192]{2,1,0:T(8,128)S(1)}, s32[]{:S(2)}) async-start(f32[14,192,192]{2,1,0:T(8,128)} %copy-done), calls=%async_computation | async-start | bytes 2359296 | tf_op jit(solution)/shard_map/slice | solution.py:70
  30.5 5.1 %copy-start.4 = (f32[160,192]{1,0:T(8,128)}, f32[160,192]{1,0:T(8,128)S(1)}, u32[]{:S(2)}) copy-start(f32[160,192]{1,0:T(8,128)S(1)} %get-tuple-element.13) | copy-start | bytes 368644
  30.5 5.1 %copy-start.6 = (f32[160,192]{1,0:T(8,128)}, f32[160,192]{1,0:T(8,128)S(1)}, u32[]{:S(2)}) copy-start(f32[160,192]{1,0:T(8,128)S(1)} %get-tuple-element.14) | copy-start | bytes 368644
  30.6 12.7 %copy-start.12 = (f32[96,192]{1,0:T(8,128)}, f32[96,192]{1,0:T(8,128)S(1)}, u32[]{:S(2)}) copy-start(f32[96,192]{1,0:T(8,128)S(1)} %get-tuple-element.9) | copy-start | bytes 221188
  30.6 12.7 %copy-start.14 = (f32[96,192]{1,0:T(8,128)}, f32[96,192]{1,0:T(8,128)S(1)}, u32[]{:S(2)}) copy-start(f32[96,192]{1,0:T(8,128)S(1)} %get-tuple-element.10) | copy-start | bytes 221188
  39.9 0.9 %copy-start.8 = (f32[128,192]{0,1:T(8,128)}, f32[128,192]{0,1:T(8,128)S(1)}, u32[]{:S(2)}) copy-start(f32[128,192]{0,1:T(8,128)S(1)} %copy.15) | copy-start | bytes 294916
  40.0 0.8 copy-start.10
  44.8 19.6 %copy-start.2 = (f32[3,64,2,192]{3,1,2,0:T(8,128)}, f32[3,64,2,192]{3,1,2,0:T(8,128)S(1)}, u32[]{:S(2)}) copy-start(f32[3,64,2,192]{3,1,2,0:T(8,128)S(1)} %convolution_bitcast_fusion.14) | copy-start | bytes 884740
  44.9 8.0 %collective-permute-start.3 = (f32[3,2,64,128]{3,2,1,0:T(8,128)S(1)}, f32[3,2,64,128]{3,2,1,0:T(8,128)S(1)}, u32[]{:S(2)}, u32[]{:S(2)}) collective-permute-start(f32[3,2,64,128]{3,2,1,0:T(8,128)S(1)} %dynamic-slice_bitcast_fusion), channel_id=1, source_target_pairs={{0,2},{1,3},{4,6},{5,7},{8,10},{9,11},{12,14},{13,15},{16,18},{17,... | collective-permute-start | bytes 589832 | tf_op jit(solution)/shard_map/ppermute | solution.py:106
  53.1 11.3 %collective-permute-start.4 = (f32[6,64,128]{1,2,0:T(8,128)S(1)}, f32[6,64,128]{1,2,0:T(8,128)S(1)}, u32[]{:S(2)}, u32[]{:S(2)}) collective-permute-start(f32[6,64,128]{1,2,0:T(8,128)S(1)} %copy.18), channel_id=1, source_target_pairs={{0,4},{4,8},{8,12},{1,5},{5,9},{9,13},{2,6},{6,10},{10,14},{3,7},{... | collective-permute-start | bytes 589832 | tf_op jit(solution)/shard_map/ppermute | solution.py:44
  56.3 11.0 %collective-permute-start.5 = (f32[6,64,128]{1,2,0:T(8,128)S(1)}, f32[6,64,128]{1,2,0:T(8,128)S(1)}, u32[]{:S(2)}, u32[]{:S(2)}) collective-permute-start(f32[6,64,128]{1,2,0:T(8,128)S(1)} %copy.18), channel_id=1, source_target_pairs={{4,0},{8,4},{12,8},{5,1},{9,5},{13,9},{6,2},{10,6},{14,10},{7,3},{... | collective-permute-start | bytes 589832 | tf_op jit(solution)/shard_map/ppermute | solution.py:45
  67.7 3.9 %collective-permute-start.6 = (f32[6,192,64]{1,2,0:T(8,128)S(1)}, f32[6,192,64]{1,2,0:T(8,128)}, u32[]{:S(2)}, u32[]{:S(2)}) collective-permute-start(f32[6,192,64]{1,2,0:T(8,128)S(1)} %slice_select_fusion.1), channel_id=1, source_target_pairs={{0,1},{1,0},{2,3},{3,2},{4,5},{5,4},{6,7},{7,6},{8,9},{9,8},{10,11... | collective-permute-start | bytes 884744 | tf_op jit(solution)/shard_map/ppermute | solution.py:49
  75.5 1.8 %copy-start.5 = (f32[160,192]{1,0:T(8,128)S(1)}, f32[160,192]{1,0:T(8,128)}, u32[]{:S(2)}) copy-start(f32[160,192]{1,0:T(8,128)} %copy-done.4) | copy-start | bytes 368644
  75.5 1.8 %copy-start.7 = (f32[160,192]{1,0:T(8,128)S(1)}, f32[160,192]{1,0:T(8,128)}, u32[]{:S(2)}) copy-start(f32[160,192]{1,0:T(8,128)} %copy-done.6) | copy-start | bytes 368644
  79.9 1.4 %copy-start.9 = (f32[128,192]{0,1:T(8,128)S(1)}, f32[128,192]{0,1:T(8,128)}, u32[]{:S(2)}) copy-start(f32[128,192]{0,1:T(8,128)} %copy-done.8) | copy-start | bytes 294916
  79.9 1.4 %copy-start.11 = (f32[128,192]{0,1:T(8,128)S(1)}, f32[128,192]{0,1:T(8,128)}, u32[]{:S(2)}) copy-start(f32[128,192]{0,1:T(8,128)} %copy-done.10) | copy-start | bytes 294916
  82.1 2.4 %copy-start.13 = (f32[96,192]{1,0:T(8,128)S(1)}, f32[96,192]{1,0:T(8,128)}, u32[]{:S(2)}) copy-start(f32[96,192]{1,0:T(8,128)} %copy-done.12) | copy-start | bytes 221188
  82.1 2.4 %copy-start.15 = (f32[96,192]{1,0:T(8,128)S(1)}, f32[96,192]{1,0:T(8,128)}, u32[]{:S(2)}) copy-start(f32[96,192]{1,0:T(8,128)} %copy-done.14) | copy-start | bytes 221188
  84.5 1.5 %copy-start.3 = (f32[3,64,2,192]{3,1,2,0:T(8,128)S(1)}, f32[3,64,2,192]{3,1,2,0:T(8,128)}, u32[]{:S(2)}) copy-start(f32[3,64,2,192]{3,1,2,0:T(8,128)} %copy-done.2) | copy-start | bytes 884740

commit v2 on v1

--- a/solution.py
+++ b/solution.py
@@ -84,10 +84,10 @@
         for s in range(slices):
             moved = modulate(current, trans_reg[s, :, HALF * s: tall - HALF * s])
             rows_done = jnp.einsum(
-                "dcab,icbj->idaj", row_bands[s], moved, precision=lax.Precision.HIGHEST
+                "dcab,icbj->idaj", row_bands[s], moved, precision=lax.Precision.HIGH
             )
             current = jnp.einsum(
-                "dcyj,icxj->idxy", col_band, rows_done, precision=lax.Precision.HIGHEST
+                "dcyj,icxj->idxy", col_band, rows_done, precision=lax.Precision.HIGH
             )
         return lax.dynamic_slice_in_dim(current, reach * wave, cols, axis=-1)
 

time: 87.4 us -> 77.5 us (0.89)
  matrix products: 24 us -> 13.8 us
    dot_general x8, matrix products: 12.7 us -> 7.15 us  [depth_section(): jnp.einsum('dcyj,icxj->idxy', col_band, rows_done, precision=lax.Precisio...]
    dot_general x8, matrix products: 11.3 us -> 6.66 us  [depth_section(): jnp.einsum('dcab,icbj->idaj', row_bands[s], moved, precision=lax.Precisio...]
where the time goes in v2:
time: 77.5 us; the launch traced here: 76.9 us
  waiting for transfers between devices  27.3 us (35%)
  starting transfers between devices  16.2 us (21%)
  matrix products  13.8 us (18%)
  other arithmetic  9.41 us (12%)
  local copies, waits for them, and re-layouts  8.78 us (11%)
  between operations  1.31 us (2%)
    ppermute x2, waiting for transfers between devices, grow(): lax.ppermute(stack[:, rows - halo:], 'tile', [(i, i + 1) for i in range(t...  12.5 us
    dot_general x8, matrix products, depth_section(): jnp.einsum('dcyj,icxj->idxy', col_band, rows_done, precision=lax.Precisio...  7.15 us
    ppermute x1, waiting for transfers between devices, per_device(): lax.ppermute(result, 'depth', [(i, i + 1) for i in range(depth_count - 1)])  6.71 us
    dot_general x8, matrix products, depth_section(): jnp.einsum('dcab,icbj->idaj', row_bands[s], moved, precision=lax.Precisio...  6.66 us
    ppermute x2, starting transfers between devices, grow(): lax.ppermute(stack[:, rows - halo:], 'tile', [(i, i + 1) for i in range(t...  6.41 us
    ppermute x2, waiting for transfers between devices, grow(): lax.ppermute(stack[:, :halo], 'tile', [(i + 1, i) for i in range(tiles -...  5.82 us
    ppermute x2, starting transfers between devices, grow(): got = lax.ppermute(edge, 'wave', [(0, 1), (1, 0)])  4.33 us
    ppermute x2, starting transfers between devices, grow(): lax.ppermute(stack[:, :halo], 'tile', [(i + 1, i) for i in range(tiles -...  4.2 us
  transfers between devices with their start and end apart: 7, of which 7 were waited for; matrix products, arithmetic and copies ran while one was open for 3% of the time, Pallas kernels for 0%

profile of v2, /device:TPU:15, one launch (start us, length us, event | category | flops | bytes accessed | tf_op | source)
XLA Modules:
  0.0 76.9 jit_solution(14996855647425843769)
XLA Ops:
  0.0 1.4 %fusion.33 = (f32[4,1,64,128]{3,2,1,0:T(8,128)S(1)}, f32[4,1,64,128]{3,2,1,0:T(8,128)S(1)}) fusion(bf16[4,64,128]{2,1,0:T(8,128)(2,1)} %param.5, bf16[4,64,128]{2,1,0:T(8,128)(2,1)} %param.6), kind=kLoop, calls=%fused_computation.105 | loop fusion | flops 163840 | bytes 393216 | tf_op jit(solution)/shard_map/stack | solution.py:25
  1.4 1.0 %pad_maximum_fusion.3 = f32[14,64,128]{2,1,0:T(8,128)S(1)} fusion(f32[8,64,128]{2,1,0:T(8,128)S(1)} %bitcast.231, f32[6,64,128]{2,1,0:T(8,128)} %bitcast.238), kind=kLoop, calls=%fused_computation.79 | loop fusion | flops 114688 | bytes 917504 | tf_op jit(solution)/shard_map/concatenate | solution.py:67
  2.4 3.2 %collective-permute-start = (f32[14,64,128]{2,1,0:T(8,128)S(1)}, f32[14,64,128]{2,1,0:T(8,128)S(1)}, u32[]{:S(2)}, u32[]{:S(2)}) collective-permute-start(f32[14,64,128]{2,1,0:T(8,128)S(1)} %pad_maximum_fusion.3), channel_id=1, source_target_pairs={{0,4},{4,8},{8,12},{1,5},{5,9},{9,13},{2,6},{6,10},{10,14},{3,7},{... | collective-permute-start | bytes 1376264 | tf_op jit(solution)/shard_map/ppermute | solution.py:44
  5.6 2.1 %collective-permute-start.1 = (f32[14,64,128]{2,1,0:T(8,128)S(1)}, f32[14,64,128]{2,1,0:T(8,128)S(1)}, u32[]{:S(2)}, u32[]{:S(2)}) collective-permute-start(f32[14,64,128]{2,1,0:T(8,128)S(1)} %pad_maximum_fusion.3), channel_id=1, source_target_pairs={{4,0},{8,4},{12,8},{5,1},{9,5},{13,9},{6,2},{10,6},{14,10},{7,3},{... | collective-permute-start | bytes 1376264 | tf_op jit(solution)/shard_map/ppermute | solution.py:45
  9.2 6.5 %collective-permute-done = f32[14,64,128]{2,1,0:T(8,128)S(1)} collective-permute-done((f32[14,64,128]{2,1,0:T(8,128)S(1)}, f32[14,64,128]{2,1,0:T(8,128)S(1)}, u32[]{:S(2)}, u32[]{:S(2)}) %collective-permute-start) | collective-permute-done | bytes 458784 | tf_op jit(solution)/shard_map/ppermute | solution.py:44
  15.7 2.9 %collective-permute-done.1 = f32[14,64,128]{2,1,0:T(8,128)S(1)} collective-permute-done((f32[14,64,128]{2,1,0:T(8,128)S(1)}, f32[14,64,128]{2,1,0:T(8,128)S(1)}, u32[]{:S(2)}, u32[]{:S(2)}) %collective-permute-start.1) | collective-permute-done | bytes 458784 | tf_op jit(solution)/shard_map/ppermute | solution.py:45
  19.1 1.5 %copy.11 = f32[14,192,64]{1,2,0:T(8,128)} copy(f32[14,192,64]{2,1,0:T(8,128)S(1)} %slice_select_fusion) | data formatting | bytes 1376256 | tf_op jit(solution)/shard_map/jit(_where)/select_n | solution.py:48
  20.6 1.9 %collective-permute-start.2 = (f32[14,192,64]{1,2,0:T(8,128)}, f32[14,192,64]{1,2,0:T(8,128)}, u32[]{:S(2)}, u32[]{:S(2)}) collective-permute-start(f32[14,192,64]{1,2,0:T(8,128)} %copy.11), channel_id=1, source_target_pairs={{0,1},{1,0},{2,3},{3,2},{4,5},{5,4},{6,7},{7,6},{8,9},{9,8},{10,11... | collective-permute-start | bytes 2064392 | tf_op jit(solution)/shard_map/ppermute | solution.py:49
  23.1 0.8 %reshape.43 = f32[2,192,383]{2,1,0:T(8,128)S(1)} reshape(f32[2,73536]{1,0:T(2,128)S(1)} %slice.215) | data formatting | bytes 1176576 | tf_op jit(solution)/shard_map/reshape | solution.py:15
  24.0 0.8 %collective-permute-done.2 = f32[14,192,64]{1,2,0:T(8,128)} collective-permute-done((f32[14,192,64]{1,2,0:T(8,128)}, f32[14,192,64]{1,2,0:T(8,128)}, u32[]{:S(2)}, u32[]{:S(2)}) %collective-permute-start.2) | collective-permute-done | bytes 688160 | tf_op jit(solution)/shard_map/ppermute | solution.py:49
  24.9 1.6 %copy.12 = f32[14,192,64]{2,1,0:T(8,128)S(1)} copy(f32[14,192,64]{1,2,0:T(8,128)} %collective-permute-done.2) | data formatting | bytes 1376256 | tf_op jit(solution)/shard_map/ppermute | solution.py:49
  26.5 2.3 %dynamic-slice_maximum_fusion = f32[14,192,192]{2,1,0:T(8,128)S(1)} fusion(s32[]{:T(128)S(6)} %select_n.42, f32[14,192,64]{2,1,0:T(8,128)S(1)} %copy.12, f32[14,64,128]{2,1,0:T(8,128)S(1)} %collective-permute-done.1, f32[8,64,128]{2,1,0:T(8,128)S(1)} %bitcast.233, f32[6,64,128]{2,1,0:T(8,128)S(1)} %bitcast.240, f32[14,64,128]{2,1,0:T(8,128)S(1)} %collective-permute-done), kind=kLoop, calls=%fused_computation | loop fusion | flops 2580480 | bytes 4128772 | tf_op jit(solution)/shard_map/concatenate | solution.py:50
  28.9 1.5 %copy-done = f32[14,192,192]{2,1,0:T(8,128)} copy-done((f32[14,192,192]{2,1,0:T(8,128)}, f32[14,192,192]{2,1,0:T(8,128)S(1)}, u32[]{:S(2)}) %copy-start) | copy-done | bytes 2064408
  30.6 1.3 %slice-done = f32[6,192,192]{2,1,0:T(8,128)S(1)} async-done(((f32[14,192,192]{2,1,0:T(8,128)}), f32[6,192,192]{2,1,0:T(8,128)S(1)}, s32[]{:S(2)}) %slice-start) | async-done | bytes 884760 | tf_op jit(solution)/shard_map/slice | solution.py:70
  32.0 1.0 %convolution_bitcast_fusion.3 = f32[3,2,160,192,1]{3,2,1,4,0:T(8,128)S(1)} fusion(f32[3,1,192,192]{3,2,1,0:T(8,128)S(1)} %get-tuple-element.16, f32[3,1,192,192]{3,2,1,0:T(8,128)S(1)} %get-tuple-element.15, f32[1,2,192,192]{3,2,1,0:T(8,128)S(1)} %get-tuple-element.33, f32[1,2,192,192]{3,2,1,0:T(8,128)S(1)} %get-tuple-element.32), kind=kOutput, calls=%fused_computation.24 | convolution fusion | flops 425017344 | bytes 2211840 | tf_op jit(solution)/shard_map/dcab,icbj->idaj/dot_general | solution.py:86
  33.0 1.0 %convolution_bitcast_fusion.2 = f32[3,2,160,192]{3,2,1,0:T(8,128)S(1)} fusion(f32[3,2,160,192,1]{3,2,1,4,0:T(8,128)S(1)} %convolution_bitcast_fusion.3, f32[1,2,192,192]{3,2,1,0:T(8,128)S(1)} %get-tuple-element.32, f32[1,2,192,192]{3,2,1,0:T(8,128)S(1)} %get-tuple-element.33), kind=kOutput, calls=%fused_computation.23 | convolution fusion | flops 424820736 | bytes 2064384 | tf_op jit(solution)/shard_map/dcyj,icxj->idxy/dot_general | solution.py:89
  34.2 1.4 %convolution_bitcast_fusion.11 = f32[3,2,128,192,1]{2,3,1,4,0:T(8,128)S(1)} fusion(f32[3,1,160,192]{3,2,1,0:T(8,128)S(1)} %get-tuple-element.20, f32[3,1,160,192]{3,2,1,0:T(8,128)S(1)} %get-tuple-element.19, f32[1,2,192,192]{3,2,1,0:T(8,128)S(1)} %get-tuple-element.33, f32[1,2,192,192]{3,2,1,0:T(8,128)S(1)} %get-tuple-element.32), kind=kOutput, calls=%fused_computation.32 | convolution fusion | flops 283381760 | bytes 1916928 | tf_op jit(solution)/shard_map/dcab,icbj->idaj/dot_general | solution.py:86
  37.2 1.3 %convolution_bitcast_fusion.8 = f32[3,2,96,192]{3,2,1,0:T(8,128)S(1)} fusion(f32[3,2,96,192,1]{2,3,1,4,0:T(8,128)S(1)} %convolution_bitcast_fusion.9, f32[1,2,192,192]{3,2,1,0:T(8,128)S(1)} %get-tuple-element.32, f32[1,2,192,192]{3,2,1,0:T(8,128)S(1)} %get-tuple-element.33), kind=kOutput, calls=%fused_computation.29 | convolution fusion | flops 254951424 | bytes 1474560 | tf_op jit(solution)/shard_map/dcyj,icxj->idxy/dot_general | solution.py:89
  39.8 1.3 %collective-permute-start.3 = (f32[3,2,64,128]{3,2,1,0:T(8,128)S(1)}, f32[3,2,64,128]{3,2,1,0:T(8,128)S(1)}, u32[]{:S(2)}, u32[]{:S(2)}) collective-permute-start(f32[3,2,64,128]{3,2,1,0:T(8,128)S(1)} %dynamic-slice_bitcast_fusion), channel_id=1, source_target_pairs={{0,2},{1,3},{4,6},{5,7},{8,10},{9,11},{12,14},{13,15},{16,18},{17,... | collective-permute-start | bytes 589832 | tf_op jit(solution)/shard_map/ppermute | solution.py:106
  41.1 6.7 %collective-permute-done.3 = f32[3,2,64,128]{3,2,1,0:T(8,128)S(1)} collective-permute-done((f32[3,2,64,128]{3,2,1,0:T(8,128)S(1)}, f32[3,2,64,128]{3,2,1,0:T(8,128)S(1)}, u32[]{:S(2)}, u32[]{:S(2)}) %collective-permute-start.3) | collective-permute-done | bytes 196640 | tf_op jit(solution)/shard_map/ppermute | solution.py:106
  48.0 3.2 %collective-permute-start.4 = (f32[6,64,128]{1,2,0:T(8,128)S(1)}, f32[6,64,128]{1,2,0:T(8,128)S(1)}, u32[]{:S(2)}, u32[]{:S(2)}) collective-permute-start(f32[6,64,128]{1,2,0:T(8,128)S(1)} %copy.18), channel_id=1, source_target_pairs={{0,4},{4,8},{8,12},{1,5},{5,9},{9,13},{2,6},{6,10},{10,14},{3,7},{... | collective-permute-start | bytes 589832 | tf_op jit(solution)/shard_map/ppermute | solution.py:44
  51.2 2.1 %collective-permute-start.5 = (f32[6,64,128]{1,2,0:T(8,128)S(1)}, f32[6,64,128]{1,2,0:T(8,128)S(1)}, u32[]{:S(2)}, u32[]{:S(2)}) collective-permute-start(f32[6,64,128]{1,2,0:T(8,128)S(1)} %copy.18), channel_id=1, source_target_pairs={{4,0},{8,4},{12,8},{5,1},{9,5},{13,9},{6,2},{10,6},{14,10},{7,3},{... | collective-permute-start | bytes 589832 | tf_op jit(solution)/shard_map/ppermute | solution.py:45
  53.3 6.0 %collective-permute-done.4 = f32[6,64,128]{1,2,0:T(8,128)S(1)} collective-permute-done((f32[6,64,128]{1,2,0:T(8,128)S(1)}, f32[6,64,128]{1,2,0:T(8,128)S(1)}, u32[]{:S(2)}, u32[]{:S(2)}) %collective-permute-start.4) | collective-permute-done | bytes 196640 | tf_op jit(solution)/shard_map/ppermute | solution.py:44
  59.3 2.9 %collective-permute-done.5 = f32[6,64,128]{1,2,0:T(8,128)S(1)} collective-permute-done((f32[6,64,128]{1,2,0:T(8,128)S(1)}, f32[6,64,128]{1,2,0:T(8,128)S(1)}, u32[]{:S(2)}, u32[]{:S(2)}) %collective-permute-start.5) | collective-permute-done | bytes 196640 | tf_op jit(solution)/shard_map/ppermute | solution.py:45
  62.6 2.5 %collective-permute-start.6 = (f32[6,192,64]{1,2,0:T(8,128)S(1)}, f32[6,192,64]{1,2,0:T(8,128)}, u32[]{:S(2)}, u32[]{:S(2)}) collective-permute-start(f32[6,192,64]{1,2,0:T(8,128)S(1)} %slice_select_fusion.1), channel_id=1, source_target_pairs={{0,1},{1,0},{2,3},{3,2},{4,5},{5,4},{6,7},{7,6},{8,9},{9,8},{10,11... | collective-permute-start | bytes 884744 | tf_op jit(solution)/shard_map/ppermute | solution.py:49
  65.1 1.5 %collective-permute-done.6 = f32[6,192,64]{1,2,0:T(8,128)} collective-permute-done((f32[6,192,64]{1,2,0:T(8,128)S(1)}, f32[6,192,64]{1,2,0:T(8,128)}, u32[]{:S(2)}, u32[]{:S(2)}) %collective-permute-start.6) | collective-permute-done | bytes 294944 | tf_op jit(solution)/shard_map/ppermute | solution.py:49
  66.5 1.4 %fusion.1 = f32[6,192,192]{1,2,0:T(8,128)S(1)} fusion(s32[]{:T(128)S(6)} %select_n.42, f32[6,192,64]{1,2,0:T(8,128)} %collective-permute-done.6, f32[6,64,128]{1,2,0:T(8,128)S(1)} %collective-permute-done.4, f32[6,64,128]{1,2,0:T(8,128)S(1)} %copy.18, f32[6,64,128]{1,2,0:T(8,128)S(1)} %collective-permute-done.5), kind=kLoop, calls=%fused_computation.38 | loop fusion | flops 884736 | bytes 1769476 | tf_op jit(solution)/shard_map/concatenate | solution.py:50
  68.6 1.0 %convolution_bitcast_fusion.1 = f32[3,2,160,192,1]{3,2,1,4,0:T(8,128)S(1)} fusion(f32[3,1,192,192]{3,2,1,0:T(8,128)S(1)} %get-tuple-element.8, f32[3,1,192,192]{3,2,1,0:T(8,128)S(1)} %get-tuple-element.7, f32[1,2,192,192]{3,2,1,0:T(8,128)S(1)} %get-tuple-element.33, f32[1,2,192,192]{3,2,1,0:T(8,128)S(1)} %get-tuple-element.32), kind=kOutput, calls=%fused_computation.22 | convolution fusion | flops 425017344 | bytes 2211840 | tf_op jit(solution)/shard_map/dcab,icbj->idaj/dot_general | solution.py:86
  69.6 0.9 %convolution_bitcast_fusion = f32[3,2,160,192]{3,2,1,0:T(8,128)S(1)} fusion(f32[3,2,160,192,1]{3,2,1,4,0:T(8,128)S(1)} %convolution_bitcast_fusion.1, f32[1,2,192,192]{3,2,1,0:T(8,128)S(1)} %get-tuple-element.32, f32[1,2,192,192]{3,2,1,0:T(8,128)S(1)} %get-tuple-element.33), kind=kOutput, calls=%fused_computation.21 | convolution fusion | flops 424820736 | bytes 2064384 | tf_op jit(solution)/shard_map/dcyj,icxj->idxy/dot_general | solution.py:89
  70.7 1.4 %convolution_bitcast_fusion.7 = f32[3,2,128,192,1]{2,3,1,4,0:T(8,128)S(1)} fusion(f32[3,1,160,192]{3,2,1,0:T(8,128)S(1)} %get-tuple-element.18, f32[3,1,160,192]{3,2,1,0:T(8,128)S(1)} %get-tuple-element.17, f32[1,2,192,192]{3,2,1,0:T(8,128)S(1)} %get-tuple-element.33, f32[1,2,192,192]{3,2,1,0:T(8,128)S(1)} %get-tuple-element.32), kind=kOutput, calls=%fused_computation.28 | convolution fusion | flops 283381760 | bytes 1916928 | tf_op jit(solution)/shard_map/dcab,icbj->idaj/dot_general | solution.py:86
  73.7 1.3 %convolution_bitcast_fusion.4 = f32[3,2,96,192]{3,2,1,0:T(8,128)S(1)} fusion(f32[3,2,96,192,1]{2,3,1,4,0:T(8,128)S(1)} %convolution_bitcast_fusion.5, f32[1,2,192,192]{3,2,1,0:T(8,128)S(1)} %get-tuple-element.32, f32[1,2,192,192]{3,2,1,0:T(8,128)S(1)} %get-tuple-element.33), kind=kOutput, calls=%fused_computation.25 | convolution fusion | flops 254951424 | bytes 1474560 | tf_op jit(solution)/shard_map/dcyj,icxj->idxy/dot_general | solution.py:89
  76.0 0.8 %fusion.29 = f32[1,3,2,64,128]{4,3,2,1,0:T(8,128)} fusion(f32[3,64,2,192]{3,1,2,0:T(8,128)S(1)} %convolution_bitcast_fusion.12, s32[]{:T(128)S(6)} %select_n.43, pred[]{:T(512)S(6)} %eq.12, pred[]{:T(512)S(6)} %eq.10, f32[3,64,2,192]{3,1,2,0:T(8,128)S(1)} %copy-done.3), kind=kLoop, calls=%fused_computation.98 | loop fusion | flops 98304 | bytes 589830 | tf_op jit(solution)/shard_map/broadcast_in_dim | solution.py:109
  (76 shorter events, 9.1 us)
Async XLA Ops:
  0.0 18.6 %copy-start.1 = (f32[3,2,64,128]{3,2,1,0:T(8,128)S(1)}, f32[3,2,64,128]{3,2,1,0:T(8,128)}, u32[]{:S(2)}) copy-start(f32[3,2,64,128]{3,2,1,0:T(8,128)} %param.4) | copy-start | bytes 589828
  0.0 7.7 %copy-start.16 = (f32[2,33]{1,0:T(2,128)S(1)}, f32[2,33]{1,0:T(2,128)}, u32[]{:S(2)}) copy-start(f32[2,33]{1,0:T(2,128)} %param.7) | copy-start | bytes 796
  2.4 13.3 %collective-permute-start = (f32[14,64,128]{2,1,0:T(8,128)S(1)}, f32[14,64,128]{2,1,0:T(8,128)S(1)}, u32[]{:S(2)}, u32[]{:S(2)}) collective-permute-start(f32[14,64,128]{2,1,0:T(8,128)S(1)} %pad_maximum_fusion.3), channel_id=1, source_target_pairs={{0,4},{4,8},{8,12},{1,5},{5,9},{9,13},{2,6},{6,10},{10,14},{3,7},{... | collective-permute-start | bytes 1376264 | tf_op jit(solution)/shard_map/ppermute | solution.py:44
  5.6 13.0 %collective-permute-start.1 = (f32[14,64,128]{2,1,0:T(8,128)S(1)}, f32[14,64,128]{2,1,0:T(8,128)S(1)}, u32[]{:S(2)}, u32[]{:S(2)}) collective-permute-start(f32[14,64,128]{2,1,0:T(8,128)S(1)} %pad_maximum_fusion.3), channel_id=1, source_target_pairs={{4,0},{8,4},{12,8},{5,1},{9,5},{13,9},{6,2},{10,6},{14,10},{7,3},{... | collective-permute-start | bytes 1376264 | tf_op jit(solution)/shard_map/ppermute | solution.py:45
  20.6 4.3 %collective-permute-start.2 = (f32[14,192,64]{1,2,0:T(8,128)}, f32[14,192,64]{1,2,0:T(8,128)}, u32[]{:S(2)}, u32[]{:S(2)}) collective-permute-start(f32[14,192,64]{1,2,0:T(8,128)} %copy.11), channel_id=1, source_target_pairs={{0,1},{1,0},{2,3},{3,2},{4,5},{5,4},{6,7},{7,6},{8,9},{9,8},{10,11... | collective-permute-start | bytes 2064392 | tf_op jit(solution)/shard_map/ppermute | solution.py:49
  28.8 1.5 %copy-start = (f32[14,192,192]{2,1,0:T(8,128)}, f32[14,192,192]{2,1,0:T(8,128)S(1)}, u32[]{:S(2)}) copy-start(f32[14,192,192]{2,1,0:T(8,128)S(1)} %dynamic-slice_maximum_fusion) | copy-start | bytes 6193156
  30.4 1.5 %slice-start = ((f32[14,192,192]{2,1,0:T(8,128)}), f32[6,192,192]{2,1,0:T(8,128)S(1)}, s32[]{:S(2)}) async-start(f32[14,192,192]{2,1,0:T(8,128)} %copy-done), calls=%async_computation | async-start | bytes 2359296 | tf_op jit(solution)/shard_map/slice | solution.py:70
  30.5 3.5 %copy-start.4 = (f32[160,192]{1,0:T(8,128)}, f32[160,192]{1,0:T(8,128)S(1)}, u32[]{:S(2)}) copy-start(f32[160,192]{1,0:T(8,128)S(1)} %get-tuple-element.13) | copy-start | bytes 368644
  30.5 3.5 %copy-start.6 = (f32[160,192]{1,0:T(8,128)}, f32[160,192]{1,0:T(8,128)S(1)}, u32[]{:S(2)}) copy-start(f32[160,192]{1,0:T(8,128)S(1)} %get-tuple-element.14) | copy-start | bytes 368644
  30.6 7.9 %copy-start.12 = (f32[96,192]{1,0:T(8,128)}, f32[96,192]{1,0:T(8,128)S(1)}, u32[]{:S(2)}) copy-start(f32[96,192]{1,0:T(8,128)S(1)} %get-tuple-element.9) | copy-start | bytes 221188
  30.6 7.9 %copy-start.14 = (f32[96,192]{1,0:T(8,128)}, f32[96,192]{1,0:T(8,128)S(1)}, u32[]{:S(2)}) copy-start(f32[96,192]{1,0:T(8,128)S(1)} %get-tuple-element.10) | copy-start | bytes 221188
  36.4 0.7 copy-start.8
  36.5 0.6 copy-start.10
  39.7 19.6 %copy-start.2 = (f32[3,64,2,192]{3,1,2,0:T(8,128)}, f32[3,64,2,192]{3,1,2,0:T(8,128)S(1)}, u32[]{:S(2)}) copy-start(f32[3,64,2,192]{3,1,2,0:T(8,128)S(1)} %convolution_bitcast_fusion.14) | copy-start | bytes 884740
  39.8 8.0 %collective-permute-start.3 = (f32[3,2,64,128]{3,2,1,0:T(8,128)S(1)}, f32[3,2,64,128]{3,2,1,0:T(8,128)S(1)}, u32[]{:S(2)}, u32[]{:S(2)}) collective-permute-start(f32[3,2,64,128]{3,2,1,0:T(8,128)S(1)} %dynamic-slice_bitcast_fusion), channel_id=1, source_target_pairs={{0,2},{1,3},{4,6},{5,7},{8,10},{9,11},{12,14},{13,15},{16,18},{17,... | collective-permute-start | bytes 589832 | tf_op jit(solution)/shard_map/ppermute | solution.py:106
  48.0 11.3 %collective-permute-start.4 = (f32[6,64,128]{1,2,0:T(8,128)S(1)}, f32[6,64,128]{1,2,0:T(8,128)S(1)}, u32[]{:S(2)}, u32[]{:S(2)}) collective-permute-start(f32[6,64,128]{1,2,0:T(8,128)S(1)} %copy.18), channel_id=1, source_target_pairs={{0,4},{4,8},{8,12},{1,5},{5,9},{9,13},{2,6},{6,10},{10,14},{3,7},{... | collective-permute-start | bytes 589832 | tf_op jit(solution)/shard_map/ppermute | solution.py:44
  51.2 11.0 %collective-permute-start.5 = (f32[6,64,128]{1,2,0:T(8,128)S(1)}, f32[6,64,128]{1,2,0:T(8,128)S(1)}, u32[]{:S(2)}, u32[]{:S(2)}) collective-permute-start(f32[6,64,128]{1,2,0:T(8,128)S(1)} %copy.18), channel_id=1, source_target_pairs={{4,0},{8,4},{12,8},{5,1},{9,5},{13,9},{6,2},{10,6},{14,10},{7,3},{... | collective-permute-start | bytes 589832 | tf_op jit(solution)/shard_map/ppermute | solution.py:45
  62.6 3.9 %collective-permute-start.6 = (f32[6,192,64]{1,2,0:T(8,128)S(1)}, f32[6,192,64]{1,2,0:T(8,128)}, u32[]{:S(2)}, u32[]{:S(2)}) collective-permute-start(f32[6,192,64]{1,2,0:T(8,128)S(1)} %slice_select_fusion.1), channel_id=1, source_target_pairs={{0,1},{1,0},{2,3},{3,2},{4,5},{5,4},{6,7},{7,6},{8,9},{9,8},{10,11... | collective-permute-start | bytes 884744 | tf_op jit(solution)/shard_map/ppermute | solution.py:49
  69.6 1.0 %copy-start.5 = (f32[160,192]{1,0:T(8,128)S(1)}, f32[160,192]{1,0:T(8,128)}, u32[]{:S(2)}) copy-start(f32[160,192]{1,0:T(8,128)} %copy-done.4) | copy-start | bytes 368644
  69.6 1.0 %copy-start.7 = (f32[160,192]{1,0:T(8,128)S(1)}, f32[160,192]{1,0:T(8,128)}, u32[]{:S(2)}) copy-start(f32[160,192]{1,0:T(8,128)} %copy-done.6) | copy-start | bytes 368644
  72.1 0.9 %copy-start.9 = (f32[128,192]{0,1:T(8,128)S(1)}, f32[128,192]{0,1:T(8,128)}, u32[]{:S(2)}) copy-start(f32[128,192]{0,1:T(8,128)} %copy-done.8) | copy-start | bytes 294916
  72.1 0.9 %copy-start.11 = (f32[128,192]{0,1:T(8,128)S(1)}, f32[128,192]{0,1:T(8,128)}, u32[]{:S(2)}) copy-start(f32[128,192]{0,1:T(8,128)} %copy-done.10) | copy-start | bytes 294916
  73.6 1.3 %copy-start.13 = (f32[96,192]{1,0:T(8,128)S(1)}, f32[96,192]{1,0:T(8,128)}, u32[]{:S(2)}) copy-start(f32[96,192]{1,0:T(8,128)} %copy-done.12) | copy-start | bytes 221188
  73.6 1.3 %copy-start.15 = (f32[96,192]{1,0:T(8,128)S(1)}, f32[96,192]{1,0:T(8,128)}, u32[]{:S(2)}) copy-start(f32[96,192]{1,0:T(8,128)} %copy-done.14) | copy-start | bytes 221188
  75.0 1.0 %copy-start.3 = (f32[3,64,2,192]{3,1,2,0:T(8,128)S(1)}, f32[3,64,2,192]{3,1,2,0:T(8,128)}, u32[]{:S(2)}) copy-start(f32[3,64,2,192]{3,1,2,0:T(8,128)} %copy-done.2) | copy-start | bytes 884740

commit v3 on v2

--- a/solution.py
+++ b/solution.py
@@ -37,18 +37,22 @@
     )
 
 
-def grow(stack, halo):
+def grow(stack, halo, splits):
     tiles = lax.axis_size("tile")
     wave = lax.axis_index("wave")
-    rows = stack.shape[-2]
+    rows, cols = stack.shape[-2], stack.shape[-1]
     from_prev = lax.ppermute(stack[:, rows - halo:], "tile", [(i, i + 1) for i in range(tiles - 1)])
     from_next = lax.ppermute(stack[:, :halo], "tile", [(i + 1, i) for i in range(tiles - 1)])
     tall = jnp.concatenate([from_prev, stack, from_next], axis=-2)
-    width = tall.shape[-1]
-    edge = jnp.where(wave == 0, tall[..., width - halo:], tall[..., :halo])
-    got = lax.ppermute(edge, "wave", [(0, 1), (1, 0)])
-    joined = jnp.concatenate([got, tall, got], axis=-1)
-    return lax.dynamic_slice_in_dim(joined, halo * (1 - wave), width + halo, axis=-1)
+    got = lax.ppermute(tall, "wave", [(0, 1), (1, 0)])
+    out, start = [], 0
+    for size in splits:
+        own, other = tall[start:start + size], got[start:start + size]
+        start += size
+        left = jnp.concatenate([own, other[..., :halo]], axis=-1)
+        right = jnp.concatenate([other[..., cols - halo:], own], axis=-1)
+        out.append(jnp.where(wave == 0, left, right))
+    return out
 
 
 def per_device(incident, phase_shift, absorption, fir_taps):
@@ -63,12 +67,13 @@
 
     trans_own = transmission(phase_shift, absorption)
     illum = incident.shape[0]
-    grown = grow(
+    field_grown, trans_grown = grow(
         jnp.concatenate([incident.reshape(2 * illum, rows, cols), trans_own.reshape(2 * slices, rows, cols)]),
         reach,
+        (2 * illum, 2 * slices),
     )
-    first_field = grown[: 2 * illum].reshape(illum, 2, rows + 2 * reach, cols + reach)
-    trans_reg = grown[2 * illum:].reshape(slices, 2, rows + 2 * reach, cols + reach)
+    first_field = field_grown.reshape(illum, 2, rows + 2 * reach, cols + reach)
+    trans_reg = trans_grown.reshape(slices, 2, rows + 2 * reach, cols + reach)
     width = cols + reach
     tall = rows + 2 * reach
 
@@ -97,7 +102,7 @@
         if step == 0:
             field = first_field
         else:
-            field = grow(carried.reshape(2 * illum, rows, cols), reach).reshape(
+            field = grow(carried.reshape(2 * illum, rows, cols), reach, (2 * illum,))[0].reshape(
                 illum, 2, tall, width
             )
         result = depth_section(field)

time: 77.5 us -> 64.2 us (0.83)
  local copies, waits for them, and re-layouts: 8.78 us -> 3.55 us
  waiting for transfers between devices: 27.3 us -> 22.6 us
  matrix products: 13.8 us -> 12.3 us
  other arithmetic: 9.41 us -> 8.52 us
    ppermute x2, waiting for transfers between devices: 12.5 us -> 3.7 us  [grow(): lax.ppermute(stack[:, rows - halo:], 'tile', [(i, i + 1) for i in range(t...]
    ppermute x2, waiting for transfers between devices: 5.82 us -> 9.99 us  [grow(): lax.ppermute(stack[:, :halo], 'tile', [(i + 1, i) for i in range(tiles -...]
    concatenate x2 -> x0, other arithmetic: 3.76 us -> none  [grow(): joined = jnp.concatenate([got, tall, got], axis=-1)]
    unnamed x36 -> x6, local copies, waits for them, and re-layouts: 2.27 us -> 0.51 us
    ppermute x1 -> x0, local copies, waits for them, and re-layouts: 1.59 us -> none  [grow(): got = lax.ppermute(edge, 'wave', [(0, 1), (1, 0)])]
    select_n x1 -> x0, local copies, waits for them, and re-layouts: 1.45 us -> none  [grow(): edge = jnp.where(wave == 0, tall[..., width - halo:], tall[..., :halo])]
    dot_general x8, matrix products: 7.15 us -> 5.71 us  [depth_section(): jnp.einsum('dcyj,icxj->idxy', col_band, rows_done, precision=lax.Precisio...]
    select_n x2 -> x4, other arithmetic: 0.47 us -> 1.73 us  [grow(): out.append(jnp.where(wave == 0, left, right))]
  transfers between devices with their start and end apart: 7 -> 7, of which waited for: 7 -> 6; matrix products, arithmetic and copies ran while one was open for 3% -> 7% of each run, Pallas kernels for 0% -> 0%
where the time goes in v3:
time: 64.2 us; the launch traced here: 63.7 us
  waiting for transfers between devices  22.6 us (35%)
  starting transfers between devices  15.7 us (24%)
  matrix products  12.3 us (19%)
  other arithmetic  8.52 us (13%)
  local copies, waits for them, and re-layouts  3.55 us (6%)
  between operations  1.1 us (2%)
    ppermute x2, waiting for transfers between devices, grow(): lax.ppermute(stack[:, :halo], 'tile', [(i + 1, i) for i in range(tiles -...  9.99 us
    ppermute x1, waiting for transfers between devices, per_device(): lax.ppermute(result, 'depth', [(i, i + 1) for i in range(depth_count - 1)])  7.08 us
    ppermute x2, starting transfers between devices, grow(): lax.ppermute(stack[:, rows - halo:], 'tile', [(i, i + 1) for i in range(t...  6.75 us
    dot_general x8, matrix products, depth_section(): jnp.einsum('dcab,icbj->idaj', row_bands[s], moved, precision=lax.Precisio...  6.55 us
    dot_general x8, matrix products, depth_section(): jnp.einsum('dcyj,icxj->idxy', col_band, rows_done, precision=lax.Precisio...  5.71 us
    ppermute x2, starting transfers between devices, grow(): lax.ppermute(stack[:, :halo], 'tile', [(i + 1, i) for i in range(tiles -...  3.99 us
    ppermute x2, waiting for transfers between devices, grow(): lax.ppermute(stack[:, rows - halo:], 'tile', [(i, i + 1) for i in range(t...  3.7 us
    ppermute x2, starting transfers between devices, grow(): got = lax.ppermute(tall, 'wave', [(0, 1), (1, 0)])  3.65 us
  transfers between devices with their start and end apart: 7, of which 6 were waited for; matrix products, arithmetic and copies ran while one was open for 7% of the time, Pallas kernels for 0%

profile of v3, /device:TPU:15, one launch (start us, length us, event | category | flops | bytes accessed | tf_op | source)
XLA Modules:
  0.0 63.7 jit_solution(14368910939393881599)
XLA Ops:
  0.0 1.4 %fusion.29 = (f32[4,1,64,128]{3,2,1,0:T(8,128)S(1)}, f32[4,1,64,128]{3,2,1,0:T(8,128)S(1)}) fusion(bf16[4,64,128]{2,1,0:T(8,128)(2,1)} %param.5, bf16[4,64,128]{2,1,0:T(8,128)(2,1)} %param.6), kind=kLoop, calls=%fused_computation.93 | loop fusion | flops 163840 | bytes 393216 | tf_op jit(solution)/shard_map/stack | solution.py:25
  1.4 1.0 %pad_maximum_fusion.3 = f32[14,64,128]{2,1,0:T(8,128)S(1)} fusion(f32[8,64,128]{2,1,0:T(8,128)S(1)} %bitcast.243, f32[6,64,128]{2,1,0:T(8,128)} %bitcast.251), kind=kLoop, calls=%fused_computation.68 | loop fusion | flops 114688 | bytes 917504 | tf_op jit(solution)/shard_map/concatenate | solution.py:71
  2.4 2.1 %collective-permute-start.1 = (f32[14,64,128]{2,1,0:T(8,128)S(1)}, f32[14,64,128]{2,1,0:T(8,128)S(1)}, u32[]{:S(2)}, u32[]{:S(2)}) collective-permute-start(f32[14,64,128]{2,1,0:T(8,128)S(1)} %pad_maximum_fusion.3), channel_id=1, source_target_pairs={{4,0},{8,4},{12,8},{5,1},{9,5},{13,9},{6,2},{10,6},{14,10},{7,3},{... | collective-permute-start | bytes 1376264 | tf_op jit(solution)/shard_map/ppermute | solution.py:45
  4.5 3.2 %collective-permute-start = (f32[14,64,128]{2,1,0:T(8,128)S(1)}, f32[14,64,128]{2,1,0:T(8,128)S(1)}, u32[]{:S(2)}, u32[]{:S(2)}) collective-permute-start(f32[14,64,128]{2,1,0:T(8,128)S(1)} %pad_maximum_fusion.3), channel_id=1, source_target_pairs={{0,4},{4,8},{8,12},{1,5},{5,9},{9,13},{2,6},{6,10},{10,14},{3,7},{... | collective-permute-start | bytes 1376264 | tf_op jit(solution)/shard_map/ppermute | solution.py:44
  7.7 8.0 %collective-permute-done.1 = f32[14,64,128]{2,1,0:T(8,128)S(1)} collective-permute-done((f32[14,64,128]{2,1,0:T(8,128)S(1)}, f32[14,64,128]{2,1,0:T(8,128)S(1)}, u32[]{:S(2)}, u32[]{:S(2)}) %collective-permute-start.1) | collective-permute-done | bytes 458784 | tf_op jit(solution)/shard_map/ppermute | solution.py:45
  15.7 1.8 %collective-permute-done = f32[14,64,128]{2,1,0:T(8,128)S(1)} collective-permute-done((f32[14,64,128]{2,1,0:T(8,128)S(1)}, f32[14,64,128]{2,1,0:T(8,128)S(1)}, u32[]{:S(2)}, u32[]{:S(2)}) %collective-permute-start) | collective-permute-done | bytes 458784 | tf_op jit(solution)/shard_map/ppermute | solution.py:44
  17.6 1.9 %collective-permute-start.2 = (f32[14,192,128]{2,1,0:T(8,128)S(1)}, f32[14,192,128]{2,1,0:T(8,128)S(1)}, u32[]{:S(2)}, u32[]{:S(2)}) collective-permute-start(f32[14,192,128]{2,1,0:T(8,128)S(1)} %pad_maximum_fusion.1), channel_id=1, source_target_pairs={{0,1},{1,0},{2,3},{3,2},{4,5},{5,4},{6,7},{7,6},{8,9},{9,8},{10,11... | collective-permute-start | bytes 4128776 | tf_op jit(solution)/shard_map/ppermute | solution.py:47
  19.5 0.6 multiply_reduce_fusion
  21.6 1.7 %reshape.56 = f32[2,192,383]{2,1,0:T(8,128)} reshape(f32[2,73536]{1,0:T(2,128)S(1)} %slice.231) | data formatting | bytes 1176576 | tf_op jit(solution)/shard_map/reshape | solution.py:15
  23.3 1.1 %fusion.57 = (f32[1,192,192]{2,1,0:T(8,128)S(1)}, f32[1,192,192]{2,1,0:T(8,128)S(1)}, f32[1,192,192]{2,1,0:T(8,128)S(1)}) fusion(f32[2,192,383]{2,1,0:T(8,128)} %reshape.56), kind=kLoop, calls=%fused_computation.118 | loop fusion | flops 36864 | bytes 737280 | tf_op jit(solution)/shard_map/slice | solution.py:16
  26.6 1.0 %convolution_bitcast_fusion.3 = f32[3,2,160,192,1]{3,2,1,4,0:T(8,128)S(1)} fusion(f32[3,1,192,192]{3,2,1,0:T(8,128)S(1)} %get-tuple-element.14, f32[3,1,192,192]{3,2,1,0:T(8,128)S(1)} %get-tuple-element.13, f32[1,2,192,192]{3,2,1,0:T(8,128)S(1)} %get-tuple-element.39, f32[1,2,192,192]{3,2,1,0:T(8,128)S(1)} %get-tuple-element.38), kind=kOutput, calls=%fused_computation.15 | convolution fusion | flops 425017344 | bytes 2211840 | tf_op jit(solution)/shard_map/dcab,icbj->idaj/dot_general | solution.py:91
  27.6 1.0 %convolution_bitcast_fusion.2 = f32[3,2,160,192]{3,2,1,0:T(8,128)S(1)} fusion(f32[3,2,160,192,1]{3,2,1,4,0:T(8,128)S(1)} %convolution_bitcast_fusion.3, f32[1,2,192,192]{3,2,1,0:T(8,128)S(1)} %get-tuple-element.38, f32[1,2,192,192]{3,2,1,0:T(8,128)S(1)} %get-tuple-element.39), kind=kOutput, calls=%fused_computation.14 | convolution fusion | flops 424820736 | bytes 2064384 | tf_op jit(solution)/shard_map/dcyj,icxj->idxy/dot_general | solution.py:94
  28.7 1.4 %convolution_bitcast_fusion.11 = f32[3,2,128,192,1]{2,3,1,4,0:T(8,128)S(1)} fusion(f32[3,1,160,192]{3,2,1,0:T(8,128)S(1)} %get-tuple-element.24, f32[3,1,160,192]{3,2,1,0:T(8,128)S(1)} %get-tuple-element.23, f32[1,2,192,192]{3,2,1,0:T(8,128)S(1)} %get-tuple-element.39, f32[1,2,192,192]{3,2,1,0:T(8,128)S(1)} %get-tuple-element.38), kind=kOutput, calls=%fused_computation.23 | convolution fusion | flops 283381760 | bytes 1916928 | tf_op jit(solution)/shard_map/dcab,icbj->idaj/dot_general | solution.py:91
  30.1 0.8 %convolution_bitcast_fusion.10 = f32[3,2,128,192]{2,3,1,0:T(8,128)S(1)} fusion(f32[3,2,128,192,1]{2,3,1,4,0:T(8,128)S(1)} %convolution_bitcast_fusion.11, f32[1,2,192,192]{3,2,1,0:T(8,128)S(1)} %get-tuple-element.38, f32[1,2,192,192]{3,2,1,0:T(8,128)S(1)} %get-tuple-element.39), kind=kOutput, calls=%fused_computation.22 | convolution fusion | flops 339886080 | bytes 1769472 | tf_op jit(solution)/shard_map/dcyj,icxj->idxy/dot_general | solution.py:94
  31.6 0.6 %convolution_bitcast_fusion.8 = f32[3,2,96,192]{3,2,1,0:T(8,128)S(1)} fusion(f32[3,2,96,192,1]{3,2,1,4,0:T(8,128)S(1)} %convolution_bitcast_fusion.9, f32[1,2,192,192]{3,2,1,0:T(8,128)S(1)} %get-tuple-element.38, f32[1,2,192,192]{3,2,1,0:T(8,128)S(1)} %get-tuple-element.39), kind=kOutput, calls=%fused_computation.20 | convolution fusion | flops 254951424 | bytes 1474560 | tf_op jit(solution)/shard_map/dcyj,icxj->idxy/dot_general | solution.py:94
  32.8 0.5 convolution_bitcast_fusion.14
  33.4 1.3 %collective-permute-start.3 = (f32[3,2,64,128]{3,2,1,0:T(8,128)S(1)}, f32[3,2,64,128]{3,2,1,0:T(8,128)S(1)}, u32[]{:S(2)}, u32[]{:S(2)}) collective-permute-start(f32[3,2,64,128]{3,2,1,0:T(8,128)S(1)} %dynamic-slice_bitcast_fusion), channel_id=1, source_target_pairs={{0,2},{1,3},{4,6},{5,7},{8,10},{9,11},{12,14},{13,15},{16,18},{17,... | collective-permute-start | bytes 589832 | tf_op jit(solution)/shard_map/ppermute | solution.py:111
  34.7 7.1 %collective-permute-done.3 = f32[3,2,64,128]{3,2,1,0:T(8,128)S(1)} collective-permute-done((f32[3,2,64,128]{3,2,1,0:T(8,128)S(1)}, f32[3,2,64,128]{3,2,1,0:T(8,128)S(1)}, u32[]{:S(2)}, u32[]{:S(2)}) %collective-permute-start.3) | collective-permute-done | bytes 196640 | tf_op jit(solution)/shard_map/ppermute | solution.py:111
  41.8 1.9 %collective-permute-start.5 = (f32[6,64,128]{2,1,0:T(8,128)S(1)}, f32[6,64,128]{2,1,0:T(8,128)S(1)}, u32[]{:S(2)}, u32[]{:S(2)}) collective-permute-start(f32[6,64,128]{2,1,0:T(8,128)S(1)} %bitcast.246), channel_id=1, source_target_pairs={{4,0},{8,4},{12,8},{5,1},{9,5},{13,9},{6,2},{10,6},{14,10},{7,3},{... | collective-permute-start | bytes 589832 | tf_op jit(solution)/shard_map/ppermute | solution.py:45
  43.7 3.5 %collective-permute-start.4 = (f32[6,64,128]{2,1,0:T(8,128)S(1)}, f32[6,64,128]{2,1,0:T(8,128)S(1)}, u32[]{:S(2)}, u32[]{:S(2)}) collective-permute-start(f32[6,64,128]{2,1,0:T(8,128)S(1)} %bitcast.247), channel_id=1, source_target_pairs={{0,4},{4,8},{8,12},{1,5},{5,9},{9,13},{2,6},{6,10},{10,14},{3,7},{... | collective-permute-start | bytes 589832 | tf_op jit(solution)/shard_map/ppermute | solution.py:44
  47.3 2.0 %collective-permute-done.5 = f32[6,64,128]{2,1,0:T(8,128)S(1)} collective-permute-done((f32[6,64,128]{2,1,0:T(8,128)S(1)}, f32[6,64,128]{2,1,0:T(8,128)S(1)}, u32[]{:S(2)}, u32[]{:S(2)}) %collective-permute-start.5) | collective-permute-done | bytes 196640 | tf_op jit(solution)/shard_map/ppermute | solution.py:45
  49.3 1.9 %collective-permute-done.4 = f32[6,64,128]{2,1,0:T(8,128)S(1)} collective-permute-done((f32[6,64,128]{2,1,0:T(8,128)S(1)}, f32[6,64,128]{2,1,0:T(8,128)S(1)}, u32[]{:S(2)}, u32[]{:S(2)}) %collective-permute-start.4) | collective-permute-done | bytes 196640 | tf_op jit(solution)/shard_map/ppermute | solution.py:44
  51.2 0.9 %pad_maximum_fusion.2 = f32[6,192,128]{2,1,0:T(8,128)} fusion(f32[6,64,128]{2,1,0:T(8,128)S(1)} %collective-permute-done.5, f32[6,64,128]{2,1,0:T(8,128)S(1)} %bitcast.248, f32[6,64,128]{2,1,0:T(8,128)S(1)} %collective-permute-done.4), kind=kLoop, calls=%fused_computation.51 | loop fusion | flops 294912 | bytes 1179648 | tf_op jit(solution)/shard_map/concatenate | solution.py:46
  52.1 1.7 %collective-permute-start.6 = (f32[6,192,128]{2,1,0:T(8,128)}, f32[6,192,128]{2,1,0:T(8,128)S(1)}, u32[]{:S(2)}, u32[]{:S(2)}) collective-permute-start(f32[6,192,128]{2,1,0:T(8,128)} %pad_maximum_fusion.2), channel_id=1, source_target_pairs={{0,1},{1,0},{2,3},{3,2},{4,5},{5,4},{6,7},{7,6},{8,9},{9,8},{10,11... | collective-permute-start | bytes 1769480 | tf_op jit(solution)/shard_map/ppermute | solution.py:47
  53.8 1.8 %collective-permute-done.6 = f32[6,192,128]{2,1,0:T(8,128)S(1)} collective-permute-done((f32[6,192,128]{2,1,0:T(8,128)}, f32[6,192,128]{2,1,0:T(8,128)S(1)}, u32[]{:S(2)}, u32[]{:S(2)}) %collective-permute-start.6) | collective-permute-done | bytes 589856 | tf_op jit(solution)/shard_map/ppermute | solution.py:47
  56.4 1.0 %convolution_bitcast_fusion.1 = f32[3,2,160,192,1]{3,2,1,4,0:T(8,128)S(1)} fusion(f32[3,1,192,192]{3,2,1,0:T(8,128)S(1)} %get-tuple-element.6, f32[3,1,192,192]{3,2,1,0:T(8,128)S(1)} %get-tuple-element.5, f32[1,2,192,192]{3,2,1,0:T(8,128)S(1)} %get-tuple-element.39, f32[1,2,192,192]{3,2,1,0:T(8,128)S(1)} %get-tuple-element.38), kind=kOutput, calls=%fused_computation.13 | convolution fusion | flops 425017344 | bytes 2211840 | tf_op jit(solution)/shard_map/dcab,icbj->idaj/dot_general | solution.py:91
  57.4 0.9 %convolution_bitcast_fusion = f32[3,2,160,192]{3,2,1,0:T(8,128)S(1)} fusion(f32[3,2,160,192,1]{3,2,1,4,0:T(8,128)S(1)} %convolution_bitcast_fusion.1, f32[1,2,192,192]{3,2,1,0:T(8,128)S(1)} %get-tuple-element.38, f32[1,2,192,192]{3,2,1,0:T(8,128)S(1)} %get-tuple-element.39), kind=kOutput, calls=%fused_computation.12 | convolution fusion | flops 424820736 | bytes 2064384 | tf_op jit(solution)/shard_map/dcyj,icxj->idxy/dot_general | solution.py:94
  58.5 1.4 %convolution_bitcast_fusion.7 = f32[3,2,128,192,1]{2,3,1,4,0:T(8,128)S(1)} fusion(f32[3,1,160,192]{3,2,1,0:T(8,128)S(1)} %get-tuple-element.22, f32[3,1,160,192]{3,2,1,0:T(8,128)S(1)} %get-tuple-element.21, f32[1,2,192,192]{3,2,1,0:T(8,128)S(1)} %get-tuple-element.39, f32[1,2,192,192]{3,2,1,0:T(8,128)S(1)} %get-tuple-element.38), kind=kOutput, calls=%fused_computation.19 | convolution fusion | flops 283381760 | bytes 1916928 | tf_op jit(solution)/shard_map/dcab,icbj->idaj/dot_general | solution.py:91
  59.9 0.8 %convolution_bitcast_fusion.6 = f32[3,2,128,192]{2,3,1,0:T(8,128)S(1)} fusion(f32[3,2,128,192,1]{2,3,1,4,0:T(8,128)S(1)} %convolution_bitcast_fusion.7, f32[1,2,192,192]{3,2,1,0:T(8,128)S(1)} %get-tuple-element.38, f32[1,2,192,192]{3,2,1,0:T(8,128)S(1)} %get-tuple-element.39), kind=kOutput, calls=%fused_computation.18 | convolution fusion | flops 339886080 | bytes 1769472 | tf_op jit(solution)/shard_map/dcyj,icxj->idxy/dot_general | solution.py:94
  61.2 0.6 %convolution_bitcast_fusion.4 = f32[3,2,96,192]{3,2,1,0:T(8,128)S(1)} fusion(f32[3,2,96,192,1]{3,2,1,4,0:T(8,128)S(1)} %convolution_bitcast_fusion.5, f32[1,2,192,192]{3,2,1,0:T(8,128)S(1)} %get-tuple-element.38, f32[1,2,192,192]{3,2,1,0:T(8,128)S(1)} %get-tuple-element.39), kind=kOutput, calls=%fused_computation.16 | convolution fusion | flops 254951424 | bytes 1474560 | tf_op jit(solution)/shard_map/dcyj,icxj->idxy/dot_general | solution.py:94
  62.4 0.5 convolution_bitcast_fusion.12
  62.9 0.9 %fusion.25 = f32[1,3,2,64,128]{4,3,2,1,0:T(8,128)} fusion(f32[3,64,2,192]{3,1,2,0:T(8,128)S(1)} %convolution_bitcast_fusion.12, s32[]{:T(128)S(6)} %select_n.52, pred[]{:T(512)S(6)} %eq.13, pred[]{:T(512)S(6)} %eq.11, f32[3,64,2,192]{3,1,2,0:T(8,128)S(1)} %convolution_bitcast_fusion.14), kind=kLoop, calls=%fused_computation.86 | loop fusion | flops 98304 | bytes 589830 | tf_op jit(solution)/shard_map/broadcast_in_dim | solution.py:114
  (44 shorter events, 6.4 us)
Async XLA Ops:
  0.0 17.5 %copy-start = (f32[3,2,64,128]{3,2,1,0:T(8,128)S(1)}, f32[3,2,64,128]{3,2,1,0:T(8,128)}, u32[]{:S(2)}) copy-start(f32[3,2,64,128]{3,2,1,0:T(8,128)} %param.4) | copy-start | bytes 589828
  2.4 17.1 %copy-start.1 = (f32[2,33]{1,0:T(2,128)S(1)}, f32[2,33]{1,0:T(2,128)}, u32[]{:S(2)}) copy-start(f32[2,33]{1,0:T(2,128)} %param.7) | copy-start | bytes 796
  2.4 13.3 %collective-permute-start.1 = (f32[14,64,128]{2,1,0:T(8,128)S(1)}, f32[14,64,128]{2,1,0:T(8,128)S(1)}, u32[]{:S(2)}, u32[]{:S(2)}) collective-permute-start(f32[14,64,128]{2,1,0:T(8,128)S(1)} %pad_maximum_fusion.3), channel_id=1, source_target_pairs={{4,0},{8,4},{12,8},{5,1},{9,5},{13,9},{6,2},{10,6},{14,10},{7,3},{... | collective-permute-start | bytes 1376264 | tf_op jit(solution)/shard_map/ppermute | solution.py:45
  4.5 13.0 %collective-permute-start = (f32[14,64,128]{2,1,0:T(8,128)S(1)}, f32[14,64,128]{2,1,0:T(8,128)S(1)}, u32[]{:S(2)}, u32[]{:S(2)}) collective-permute-start(f32[14,64,128]{2,1,0:T(8,128)S(1)} %pad_maximum_fusion.3), channel_id=1, source_target_pairs={{0,4},{4,8},{8,12},{1,5},{5,9},{9,13},{2,6},{6,10},{10,14},{3,7},{... | collective-permute-start | bytes 1376264 | tf_op jit(solution)/shard_map/ppermute | solution.py:44
  17.6 6.9 %collective-permute-start.2 = (f32[14,192,128]{2,1,0:T(8,128)S(1)}, f32[14,192,128]{2,1,0:T(8,128)S(1)}, u32[]{:S(2)}, u32[]{:S(2)}) collective-permute-start(f32[14,192,128]{2,1,0:T(8,128)S(1)} %pad_maximum_fusion.1), channel_id=1, source_target_pairs={{0,1},{1,0},{2,3},{3,2},{4,5},{5,4},{6,7},{7,6},{8,9},{9,8},{10,11... | collective-permute-start | bytes 4128776 | tf_op jit(solution)/shard_map/ppermute | solution.py:47
  33.4 8.4 %collective-permute-start.3 = (f32[3,2,64,128]{3,2,1,0:T(8,128)S(1)}, f32[3,2,64,128]{3,2,1,0:T(8,128)S(1)}, u32[]{:S(2)}, u32[]{:S(2)}) collective-permute-start(f32[3,2,64,128]{3,2,1,0:T(8,128)S(1)} %dynamic-slice_bitcast_fusion), channel_id=1, source_target_pairs={{0,2},{1,3},{4,6},{5,7},{8,10},{9,11},{12,14},{13,15},{16,18},{17,... | collective-permute-start | bytes 589832 | tf_op jit(solution)/shard_map/ppermute | solution.py:111
  41.8 7.5 %collective-permute-start.5 = (f32[6,64,128]{2,1,0:T(8,128)S(1)}, f32[6,64,128]{2,1,0:T(8,128)S(1)}, u32[]{:S(2)}, u32[]{:S(2)}) collective-permute-start(f32[6,64,128]{2,1,0:T(8,128)S(1)} %bitcast.246), channel_id=1, source_target_pairs={{4,0},{8,4},{12,8},{5,1},{9,5},{13,9},{6,2},{10,6},{14,10},{7,3},{... | collective-permute-start | bytes 589832 | tf_op jit(solution)/shard_map/ppermute | solution.py:45
  43.7 7.5 %collective-permute-start.4 = (f32[6,64,128]{2,1,0:T(8,128)S(1)}, f32[6,64,128]{2,1,0:T(8,128)S(1)}, u32[]{:S(2)}, u32[]{:S(2)}) collective-permute-start(f32[6,64,128]{2,1,0:T(8,128)S(1)} %bitcast.247), channel_id=1, source_target_pairs={{0,4},{4,8},{8,12},{1,5},{5,9},{9,13},{2,6},{6,10},{10,14},{3,7},{... | collective-permute-start | bytes 589832 | tf_op jit(solution)/shard_map/ppermute | solution.py:44
  52.1 3.6 %collective-permute-start.6 = (f32[6,192,128]{2,1,0:T(8,128)}, f32[6,192,128]{2,1,0:T(8,128)S(1)}, u32[]{:S(2)}, u32[]{:S(2)}) collective-permute-start(f32[6,192,128]{2,1,0:T(8,128)} %pad_maximum_fusion.2), channel_id=1, source_target_pairs={{0,1},{1,0},{2,3},{3,2},{4,5},{5,4},{6,7},{7,6},{8,9},{9,8},{10,11... | collective-permute-start | bytes 1769480 | tf_op jit(solution)/shard_map/ppermute | solution.py:47

commit v4 on v2

--- a/solution.py
+++ b/solution.py
@@ -37,18 +37,33 @@
     )
 
 
-def grow(stack, halo):
+def send_rows(pieces, axis, pairs):
+    flat = jnp.concatenate([p.reshape(-1, p.shape[-1]) for p in pieces], axis=0)
+    moved = lax.ppermute(flat, axis, pairs)
+    out, start = [], 0
+    for p in pieces:
+        count = p.shape[0] * p.shape[1]
+        out.append(moved[start:start + count].reshape(p.shape))
+        start += count
+    return out
+
+
+def grow(pieces, row_halos, col_halo):
     tiles = lax.axis_size("tile")
     wave = lax.axis_index("wave")
-    rows = stack.shape[-2]
-    from_prev = lax.ppermute(stack[:, rows - halo:], "tile", [(i, i + 1) for i in range(tiles - 1)])
-    from_next = lax.ppermute(stack[:, :halo], "tile", [(i + 1, i) for i in range(tiles - 1)])
-    tall = jnp.concatenate([from_prev, stack, from_next], axis=-2)
-    width = tall.shape[-1]
-    edge = jnp.where(wave == 0, tall[..., width - halo:], tall[..., :halo])
-    got = lax.ppermute(edge, "wave", [(0, 1), (1, 0)])
-    joined = jnp.concatenate([got, tall, got], axis=-1)
-    return lax.dynamic_slice_in_dim(joined, halo * (1 - wave), width + halo, axis=-1)
+    cols = pieces[0].shape[-1]
+    tails = [p[:, p.shape[1] - r:] for p, r in zip(pieces, row_halos)]
+    heads = [p[:, :r] for p, r in zip(pieces, row_halos)]
+    from_prev = send_rows(tails, "tile", [(i, i + 1) for i in range(tiles - 1)])
+    from_next = send_rows(heads, "tile", [(i + 1, i) for i in range(tiles - 1)])
+    talls = [jnp.concatenate(trio, axis=1) for trio in zip(from_prev, pieces, from_next)]
+    others = send_rows(talls, "wave", [(0, 1), (1, 0)])
+    out = []
+    for own, other in zip(talls, others):
+        left = jnp.concatenate([own, other[..., :col_halo]], axis=-1)
+        right = jnp.concatenate([other[..., cols - col_halo:], own], axis=-1)
+        out.append(jnp.where(wave == 0, left, right))
+    return out
 
 
 def per_device(incident, phase_shift, absorption, fir_taps):
@@ -64,11 +79,12 @@
     trans_own = transmission(phase_shift, absorption)
     illum = incident.shape[0]
     grown = grow(
-        jnp.concatenate([incident.reshape(2 * illum, rows, cols), trans_own.reshape(2 * slices, rows, cols)]),
+        [incident.reshape(2 * illum, rows, cols)] + [trans_own[s] for s in range(slices)],
+        [reach] + [reach - HALF * s for s in range(slices)],
         reach,
     )
-    first_field = grown[: 2 * illum].reshape(illum, 2, rows + 2 * reach, cols + reach)
-    trans_reg = grown[2 * illum:].reshape(slices, 2, rows + 2 * reach, cols + reach)
+    first_field = grown[0].reshape(illum, 2, rows + 2 * reach, cols + reach)
+    trans_reg = grown[1:]
     width = cols + reach
     tall = rows + 2 * reach
 
@@ -82,7 +98,7 @@
     def depth_section(field):
         current = field
         for s in range(slices):
-            moved = modulate(current, trans_reg[s, :, HALF * s: tall - HALF * s])
+            moved = modulate(current, trans_reg[s])
             rows_done = jnp.einsum(
                 "dcab,icbj->idaj", row_bands[s], moved, precision=lax.Precision.HIGH
             )
@@ -97,7 +113,7 @@
         if step == 0:
             field = first_field
         else:
-            field = grow(carried.reshape(2 * illum, rows, cols), reach).reshape(
+            field = grow([carried.reshape(2 * illum, rows, cols)], [reach], reach)[0].reshape(
                 illum, 2, tall, width
             )
         result = depth_section(field)

time: 77.5 us -> 68 us (0.88)
  waiting for transfers between devices: 27.3 us -> 22.6 us
  other arithmetic: 9.41 us -> 7.13 us
  matrix products: 13.8 us -> 12.3 us
    ppermute x6, waiting for transfers between devices: 20.6 us -> 15.5 us  [send_rows(): moved = lax.ppermute(flat, axis, pairs)]
    concatenate x5 -> x6, other arithmetic: 5.08 us -> 0.96 us  [grow(): jnp.concatenate(trio, axis=1)]
    unnamed x36 -> x45, local copies, waits for them, and re-layouts: 2.27 us -> 4.38 us
    select_n x2 -> x6, other arithmetic: 0.47 us -> 2.34 us  [grow(): out.append(jnp.where(wave == 0, left, right))]
    ppermute x1 -> x0, local copies, waits for them, and re-layouts: 1.59 us -> none  [grow(): got = lax.ppermute(edge, 'wave', [(0, 1), (1, 0)])]
    select_n x1 -> x0, local copies, waits for them, and re-layouts: 1.45 us -> none  [grow(): edge = jnp.where(wave == 0, tall[..., width - halo:], tall[..., :halo])]
    dot_general x8, matrix products: 7.15 us -> 5.72 us  [depth_section(): jnp.einsum('dcyj,icxj->idxy', col_band, rows_done, precision=lax.Precisio...]
  transfers between devices with their start and end apart: 7 -> 7, of which waited for: 7 -> 6; matrix products, arithmetic and copies ran while one was open for 3% -> 3% of each run, Pallas kernels for 0% -> 0%
where the time goes in v4:
time: 68 us; the launch traced here: 67.5 us
  waiting for transfers between devices  22.6 us (33%)
  starting transfers between devices  15.9 us (23%)
  matrix products  12.3 us (18%)
  local copies, waits for them, and re-layouts  8.08 us (12%)
  other arithmetic  7.13 us (10%)
  between operations  1.45 us (2%)
    ppermute x6, waiting for transfers between devices, send_rows(): moved = lax.ppermute(flat, axis, pairs)  15.5 us
    ppermute x6, starting transfers between devices, send_rows(): moved = lax.ppermute(flat, axis, pairs)  14.6 us
    ppermute x1, waiting for transfers between devices, per_device(): lax.ppermute(result, 'depth', [(i, i + 1) for i in range(depth_count - 1)])  7.12 us
    dot_general x8, matrix products, depth_section(): jnp.einsum('dcab,icbj->idaj', row_bands[s], moved, precision=lax.Precisio...  6.55 us
    dot_general x8, matrix products, depth_section(): jnp.einsum('dcyj,icxj->idxy', col_band, rows_done, precision=lax.Precisio...  5.72 us
    unnamed x45, local copies, waits for them, and re-layouts  4.38 us
    select_n x6, other arithmetic, grow(): out.append(jnp.where(wave == 0, left, right))  2.34 us
    another operation x1, other arithmetic, transmission(): jnp.stack([amplitude * jnp.cos(angle_part), amplitude * jnp.sin(angle_par...  1.4 us
  transfers between devices with their start and end apart: 7, of which 6 were waited for; matrix products, arithmetic and copies ran while one was open for 3% of the time, Pallas kernels for 0%

profile of v4, /device:TPU:15, one launch (start us, length us, event | category | flops | bytes accessed | tf_op | source)
XLA Modules:
  0.0 67.5 jit_solution(685177215618954443)
XLA Ops:
  0.0 1.4 %fusion.31 = (f32[4,1,64,128]{3,2,0,1:T(8,128)S(1)}, f32[4,1,64,128]{3,2,0,1:T(8,128)S(1)}) fusion(bf16[4,64,128]{2,1,0:T(8,128)(2,1)} %param.5, bf16[4,64,128]{2,1,0:T(8,128)(2,1)} %param.6), kind=kLoop, calls=%fused_computation.103 | loop fusion | flops 163840 | bytes 393216 | tf_op jit(solution)/shard_map/stack | solution.py:25
  1.6 3.2 %collective-permute-start = (f32[704,128]{1,0:T(8,128)S(1)}, f32[704,128]{1,0:T(8,128)S(1)}, u32[]{:S(2)}, u32[]{:S(2)}) collective-permute-start(f32[704,128]{1,0:T(8,128)S(1)} %constant_dynamic-update-slice_fusion), channel_id=1, source_target_pairs={{0,4},{4,8},{8,12},{1,5},{5,9},{9,13},{2,6},{6,10},{10,14},{3,7},{... | collective-permute-start | bytes 1081352 | tf_op jit(solution)/shard_map/ppermute | solution.py:42
  4.8 2.1 %collective-permute-start.1 = (f32[704,128]{1,0:T(8,128)S(1)}, f32[704,128]{1,0:T(8,128)S(1)}, u32[]{:S(2)}, u32[]{:S(2)}) collective-permute-start(f32[704,128]{1,0:T(8,128)S(1)} %constant_dynamic-update-slice_fusion.5), channel_id=1, source_target_pairs={{4,0},{8,4},{12,8},{5,1},{9,5},{13,9},{6,2},{10,6},{14,10},{7,3},{... | collective-permute-start | bytes 1081352 | tf_op jit(solution)/shard_map/ppermute | solution.py:42
  7.0 5.8 %collective-permute-done = f32[704,128]{1,0:T(8,128)S(1)} collective-permute-done((f32[704,128]{1,0:T(8,128)S(1)}, f32[704,128]{1,0:T(8,128)S(1)}, u32[]{:S(2)}, u32[]{:S(2)}) %collective-permute-start) | collective-permute-done | bytes 360480 | tf_op jit(solution)/shard_map/ppermute | solution.py:42
  12.8 2.9 %collective-permute-done.1 = f32[704,128]{1,0:T(8,128)S(1)} collective-permute-done((f32[704,128]{1,0:T(8,128)S(1)}, f32[704,128]{1,0:T(8,128)S(1)}, u32[]{:S(2)}, u32[]{:S(2)}) %collective-permute-start.1) | collective-permute-done | bytes 360480 | tf_op jit(solution)/shard_map/ppermute | solution.py:42
  15.8 0.9 %constant_dynamic-update-slice_fusion.14 = f32[2304,128]{1,0:T(8,128)} fusion(f32[1152,128]{1,0:T(8,128)S(1)} %bitcast.272), kind=kLoop, calls=%fused_computation.134 | loop fusion | bytes 1179648
  16.7 0.7 %constant_dynamic-update-slice_fusion.13 = f32[2304,128]{1,0:T(8,128)} fusion(f32[2304,128]{1,0:T(8,128)} %constant_dynamic-update-slice_fusion.14, f32[384,128]{1,0:T(8,128)S(1)} %bitcast.298), kind=kLoop, calls=%fused_computation.133 | loop fusion | bytes 393216
  17.4 0.7 constant_dynamic-update-slice_fusion.12
  18.2 0.7 constant_dynamic-update-slice_fusion.11
  19.5 1.9 %collective-permute-start.2 = (f32[2304,128]{1,0:T(8,128)}, f32[2304,128]{1,0:T(8,128)S(1)}, u32[]{:S(2)}, u32[]{:S(2)}) collective-permute-start(f32[2304,128]{1,0:T(8,128)} %constant_dynamic-update-slice_fusion.10), channel_id=1, source_target_pairs={{0,1},{1,0},{2,3},{3,2},{4,5},{5,4},{6,7},{7,6},{8,9},{9,8},{10,11... | collective-permute-start | bytes 3538952 | tf_op jit(solution)/shard_map/ppermute | solution.py:42
  23.5 0.8 %reshape.161 = f32[2,192,383]{2,1,0:T(8,128)S(1)} reshape(f32[2,73536]{1,0:T(2,128)S(1)} %slice.339) | data formatting | bytes 1176576 | tf_op jit(solution)/shard_map/reshape | solution.py:15
  25.2 0.7 %slice_bitcast_fusion.7 = (f32[96,192]{1,0:T(8,128)}, f32[96,192]{1,0:T(8,128)}) fusion(f32[2,96,192]{2,1,0:T(8,128)S(1)} %maximum_select_fusion.5), kind=kLoop, calls=%fused_computation.111 | loop fusion | bytes 294912 | tf_op jit(solution)/shard_map/mul | solution.py:33
  26.5 1.1 %maximum_select_fusion.3 = f32[2,160,192]{2,1,0:T(8,128)S(1)} fusion(f32[2,160,64]{2,1,0:T(8,128)S(1)} %get-tuple-element.45, f32[2,48,128]{2,1,0:T(8,128)} %bitcast.308, f32[2,64,128]{2,1,0:T(8,128)S(1)} %get-tuple-element.36, f32[2,48,128]{2,1,0:T(8,128)} %bitcast.306, f32[2,160,64]{2,1,0:T(8,128)S(1)} %get-tuple-element.44, pred[]{:T(512)S(6)} %eq.7), kind=kLoop, calls=%fused_computation.75 | loop fusion | flops 430080 | bytes 573441 | tf_op jit(solution)/shard_map/jit(_where)/select_n | solution.py:65
  29.0 1.0 %convolution_bitcast_fusion.3 = f32[3,2,160,192,1]{3,2,1,4,0:T(8,128)S(1)} fusion(f32[3,1,192,192]{3,2,1,0:T(8,128)S(1)} %get-tuple-element.8, f32[3,1,192,192]{3,2,1,0:T(8,128)S(1)} %get-tuple-element.7, f32[1,2,192,192]{3,2,1,0:T(8,128)S(1)} %get-tuple-element.41, f32[1,2,192,192]{3,2,1,0:T(8,128)S(1)} %get-tuple-element.40), kind=kOutput, calls=%fused_computation.12 | convolution fusion | flops 425017344 | bytes 2211840 | tf_op jit(solution)/shard_map/dcab,icbj->idaj/dot_general | solution.py:102
  29.9 0.9 %convolution_bitcast_fusion.2 = f32[3,2,160,192]{3,2,1,0:T(8,128)S(1)} fusion(f32[3,2,160,192,1]{3,2,1,4,0:T(8,128)S(1)} %convolution_bitcast_fusion.3, f32[1,2,192,192]{3,2,1,0:T(8,128)S(1)} %get-tuple-element.40, f32[1,2,192,192]{3,2,1,0:T(8,128)S(1)} %get-tuple-element.41), kind=kOutput, calls=%fused_computation.11 | convolution fusion | flops 424820736 | bytes 2064384 | tf_op jit(solution)/shard_map/dcyj,icxj->idxy/dot_general | solution.py:105
  31.0 1.4 %convolution_bitcast_fusion.11 = f32[3,2,128,192,1]{2,3,1,4,0:T(8,128)S(1)} fusion(f32[3,1,160,192]{3,2,1,0:T(8,128)S(1)} %get-tuple-element.12, f32[3,1,160,192]{3,2,1,0:T(8,128)S(1)} %get-tuple-element.11, f32[1,2,192,192]{3,2,1,0:T(8,128)S(1)} %get-tuple-element.41, f32[1,2,192,192]{3,2,1,0:T(8,128)S(1)} %get-tuple-element.40), kind=kOutput, calls=%fused_computation.20 | convolution fusion | flops 283381760 | bytes 1916928 | tf_op jit(solution)/shard_map/dcab,icbj->idaj/dot_general | solution.py:102
  32.5 0.8 %convolution_bitcast_fusion.10 = f32[3,2,128,192]{2,3,1,0:T(8,128)S(1)} fusion(f32[3,2,128,192,1]{2,3,1,4,0:T(8,128)S(1)} %convolution_bitcast_fusion.11, f32[1,2,192,192]{3,2,1,0:T(8,128)S(1)} %get-tuple-element.40, f32[1,2,192,192]{3,2,1,0:T(8,128)S(1)} %get-tuple-element.41), kind=kOutput, calls=%fused_computation.19 | convolution fusion | flops 339886080 | bytes 1769472 | tf_op jit(solution)/shard_map/dcyj,icxj->idxy/dot_general | solution.py:105
  33.8 0.7 convolution_bitcast_fusion.8
  35.8 1.3 %collective-permute-start.3 = (f32[3,2,64,128]{3,2,1,0:T(8,128)S(1)}, f32[3,2,64,128]{3,2,1,0:T(8,128)S(1)}, u32[]{:S(2)}, u32[]{:S(2)}) collective-permute-start(f32[3,2,64,128]{3,2,1,0:T(8,128)S(1)} %dynamic-slice_bitcast_fusion), channel_id=1, source_target_pairs={{0,2},{1,3},{4,6},{5,7},{8,10},{9,11},{12,14},{13,15},{16,18},{17,... | collective-permute-start | bytes 589832 | tf_op jit(solution)/shard_map/ppermute | solution.py:122
  37.1 7.1 %collective-permute-done.3 = f32[3,2,64,128]{3,2,1,0:T(8,128)S(1)} collective-permute-done((f32[3,2,64,128]{3,2,1,0:T(8,128)S(1)}, f32[3,2,64,128]{3,2,1,0:T(8,128)S(1)}, u32[]{:S(2)}, u32[]{:S(2)}) %collective-permute-start.3) | collective-permute-done | bytes 196640 | tf_op jit(solution)/shard_map/ppermute | solution.py:122
  44.3 3.2 %collective-permute-start.4 = (f32[384,128]{1,0:T(8,128)S(1)}, f32[384,128]{1,0:T(8,128)S(1)}, u32[]{:S(2)}, u32[]{:S(2)}) collective-permute-start(f32[384,128]{1,0:T(8,128)S(1)} %bitcast.291), channel_id=1, source_target_pairs={{0,4},{4,8},{8,12},{1,5},{5,9},{9,13},{2,6},{6,10},{10,14},{3,7},{... | collective-permute-start | bytes 589832 | tf_op jit(solution)/shard_map/ppermute | solution.py:42
  47.5 2.3 %collective-permute-start.5 = (f32[384,128]{1,0:T(8,128)S(1)}, f32[384,128]{1,0:T(8,128)S(1)}, u32[]{:S(2)}, u32[]{:S(2)}) collective-permute-start(f32[384,128]{1,0:T(8,128)S(1)} %bitcast.292), channel_id=1, source_target_pairs={{4,0},{8,4},{12,8},{5,1},{9,5},{13,9},{6,2},{10,6},{14,10},{7,3},{... | collective-permute-start | bytes 589832 | tf_op jit(solution)/shard_map/ppermute | solution.py:42
  49.7 2.0 %collective-permute-done.4 = f32[384,128]{1,0:T(8,128)S(1)} collective-permute-done((f32[384,128]{1,0:T(8,128)S(1)}, f32[384,128]{1,0:T(8,128)S(1)}, u32[]{:S(2)}, u32[]{:S(2)}) %collective-permute-start.4) | collective-permute-done | bytes 196640 | tf_op jit(solution)/shard_map/ppermute | solution.py:42
  51.8 2.9 %collective-permute-done.5 = f32[384,128]{1,0:T(8,128)S(1)} collective-permute-done((f32[384,128]{1,0:T(8,128)S(1)}, f32[384,128]{1,0:T(8,128)S(1)}, u32[]{:S(2)}, u32[]{:S(2)}) %collective-permute-start.5) | collective-permute-done | bytes 196640 | tf_op jit(solution)/shard_map/ppermute | solution.py:42
  54.7 0.9 %pad_maximum_fusion.2 = f32[6,192,128]{2,1,0:T(8,128)} fusion(f32[6,64,128]{2,1,0:T(8,128)S(1)} %bitcast.296, f32[6,64,128]{2,1,0:T(8,128)S(1)} %bitcast.293, f32[6,64,128]{2,1,0:T(8,128)S(1)} %bitcast.294), kind=kLoop, calls=%fused_computation.49 | loop fusion | flops 294912 | bytes 1179648 | tf_op jit(solution)/shard_map/concatenate | solution.py:59
  55.5 2.0 %collective-permute-start.6 = (f32[1152,128]{1,0:T(8,128)}, f32[1152,128]{1,0:T(8,128)S(1)}, u32[]{:S(2)}, u32[]{:S(2)}) collective-permute-start(f32[1152,128]{1,0:T(8,128)} %bitcast.103), channel_id=1, source_target_pairs={{0,1},{1,0},{2,3},{3,2},{4,5},{5,4},{6,7},{7,6},{8,9},{9,8},{10,11... | collective-permute-start | bytes 1769480 | tf_op jit(solution)/shard_map/ppermute | solution.py:42
  57.5 1.8 %collective-permute-done.6 = f32[1152,128]{1,0:T(8,128)S(1)} collective-permute-done((f32[1152,128]{1,0:T(8,128)}, f32[1152,128]{1,0:T(8,128)S(1)}, u32[]{:S(2)}, u32[]{:S(2)}) %collective-permute-start.6) | collective-permute-done | bytes 589856 | tf_op jit(solution)/shard_map/ppermute | solution.py:42
  60.1 1.0 %convolution_bitcast_fusion.1 = f32[3,2,160,192,1]{3,2,1,4,0:T(8,128)S(1)} fusion(f32[3,1,192,192]{3,2,1,0:T(8,128)S(1)} %get-tuple-element.6, f32[3,1,192,192]{3,2,1,0:T(8,128)S(1)} %get-tuple-element.5, f32[1,2,192,192]{3,2,1,0:T(8,128)S(1)} %get-tuple-element.41, f32[1,2,192,192]{3,2,1,0:T(8,128)S(1)} %get-tuple-element.40), kind=kOutput, calls=%fused_computation.10 | convolution fusion | flops 425017344 | bytes 2211840 | tf_op jit(solution)/shard_map/dcab,icbj->idaj/dot_general | solution.py:102
  61.1 0.9 %convolution_bitcast_fusion = f32[3,2,160,192]{3,2,1,0:T(8,128)S(1)} fusion(f32[3,2,160,192,1]{3,2,1,4,0:T(8,128)S(1)} %convolution_bitcast_fusion.1, f32[1,2,192,192]{3,2,1,0:T(8,128)S(1)} %get-tuple-element.40, f32[1,2,192,192]{3,2,1,0:T(8,128)S(1)} %get-tuple-element.41), kind=kOutput, calls=%fused_computation.9 | convolution fusion | flops 424820736 | bytes 2064384 | tf_op jit(solution)/shard_map/dcyj,icxj->idxy/dot_general | solution.py:105
  62.2 1.4 %convolution_bitcast_fusion.7 = f32[3,2,128,192,1]{2,3,1,4,0:T(8,128)S(1)} fusion(f32[3,1,160,192]{3,2,1,0:T(8,128)S(1)} %get-tuple-element.10, f32[3,1,160,192]{3,2,1,0:T(8,128)S(1)} %get-tuple-element.9, f32[1,2,192,192]{3,2,1,0:T(8,128)S(1)} %get-tuple-element.41, f32[1,2,192,192]{3,2,1,0:T(8,128)S(1)} %get-tuple-element.40), kind=kOutput, calls=%fused_computation.16 | convolution fusion | flops 283381760 | bytes 1916928 | tf_op jit(solution)/shard_map/dcab,icbj->idaj/dot_general | solution.py:102
  63.6 0.8 %convolution_bitcast_fusion.6 = f32[3,2,128,192]{2,3,1,0:T(8,128)S(1)} fusion(f32[3,2,128,192,1]{2,3,1,4,0:T(8,128)S(1)} %convolution_bitcast_fusion.7, f32[1,2,192,192]{3,2,1,0:T(8,128)S(1)} %get-tuple-element.40, f32[1,2,192,192]{3,2,1,0:T(8,128)S(1)} %get-tuple-element.41), kind=kOutput, calls=%fused_computation.15 | convolution fusion | flops 339886080 | bytes 1769472 | tf_op jit(solution)/shard_map/dcyj,icxj->idxy/dot_general | solution.py:105
  66.6 0.9 %fusion.25 = f32[1,3,2,64,128]{4,3,2,1,0:T(8,128)} fusion(f32[3,64,2,192]{3,1,2,0:T(8,128)S(1)} %convolution_bitcast_fusion.12, s32[]{:T(128)S(6)} %select_n.75, pred[]{:T(512)S(6)} %eq.16, pred[]{:T(512)S(6)} %eq.6, f32[3,64,2,192]{3,1,2,0:T(8,128)S(1)} %convolution_bitcast_fusion.14), kind=kLoop, calls=%fused_computation.93 | loop fusion | flops 98304 | bytes 589830 | tf_op jit(solution)/shard_map/broadcast_in_dim | solution.py:125
  (110 shorter events, 10.0 us)
Async XLA Ops:
  0.0 1.5 %copy-start = (f32[3,2,64,128]{3,2,1,0:T(8,128)S(1)}, f32[3,2,64,128]{3,2,1,0:T(8,128)}, u32[]{:S(2)}) copy-start(f32[3,2,64,128]{3,2,1,0:T(8,128)} %param.4) | copy-start | bytes 589828
  1.6 11.2 %collective-permute-start = (f32[704,128]{1,0:T(8,128)S(1)}, f32[704,128]{1,0:T(8,128)S(1)}, u32[]{:S(2)}, u32[]{:S(2)}) collective-permute-start(f32[704,128]{1,0:T(8,128)S(1)} %constant_dynamic-update-slice_fusion), channel_id=1, source_target_pairs={{0,4},{4,8},{8,12},{1,5},{5,9},{9,13},{2,6},{6,10},{10,14},{3,7},{... | collective-permute-start | bytes 1081352 | tf_op jit(solution)/shard_map/ppermute | solution.py:42
  4.8 10.9 %collective-permute-start.1 = (f32[704,128]{1,0:T(8,128)S(1)}, f32[704,128]{1,0:T(8,128)S(1)}, u32[]{:S(2)}, u32[]{:S(2)}) collective-permute-start(f32[704,128]{1,0:T(8,128)S(1)} %constant_dynamic-update-slice_fusion.5), channel_id=1, source_target_pairs={{4,0},{8,4},{12,8},{5,1},{9,5},{13,9},{6,2},{10,6},{14,10},{7,3},{... | collective-permute-start | bytes 1081352 | tf_op jit(solution)/shard_map/ppermute | solution.py:42
  16.7 2.2 %copy-start.5 = (f32[128,128]{1,0:T(8,128)}, f32[128,128]{1,0:T(8,128)S(1)}, u32[]{:S(2)}) copy-start(f32[128,128]{1,0:T(8,128)S(1)} %slice.322) | copy-start | bytes 196612
  16.7 4.7 %copy-start.15 = (f32[2,33]{1,0:T(2,128)S(1)}, f32[2,33]{1,0:T(2,128)}, u32[]{:S(2)}) copy-start(f32[2,33]{1,0:T(2,128)} %param.7) | copy-start | bytes 796
  17.4 6.0 %copy-start.7 = (f32[96,128]{1,0:T(8,128)}, f32[96,128]{1,0:T(8,128)S(1)}, u32[]{:S(2)}) copy-start(f32[96,128]{1,0:T(8,128)S(1)} %slice.323) | copy-start | bytes 147460
  17.4 6.0 %copy-start.8 = (f32[96,128]{1,0:T(8,128)}, f32[96,128]{1,0:T(8,128)S(1)}, u32[]{:S(2)}) copy-start(f32[96,128]{1,0:T(8,128)S(1)} %slice.324) | copy-start | bytes 147460
  18.1 5.3 %copy-start.9 = (f32[64,128]{1,0:T(8,128)}, f32[64,128]{1,0:T(8,128)S(1)}, u32[]{:S(2)}) copy-start(f32[64,128]{1,0:T(8,128)S(1)} %slice.325) | copy-start | bytes 98308
  18.1 5.3 %copy-start.11 = (f32[64,128]{1,0:T(8,128)}, f32[64,128]{1,0:T(8,128)S(1)}, u32[]{:S(2)}) copy-start(f32[64,128]{1,0:T(8,128)S(1)} %slice.326) | copy-start | bytes 98308
  18.8 4.6 %copy-start.13 = (f32[32,128]{1,0:T(8,128)}, f32[32,128]{1,0:T(8,128)S(1)}, u32[]{:S(2)}) copy-start(f32[32,128]{1,0:T(8,128)S(1)} %slice.328) | copy-start | bytes 49156
  19.5 5.0 %collective-permute-start.2 = (f32[2304,128]{1,0:T(8,128)}, f32[2304,128]{1,0:T(8,128)S(1)}, u32[]{:S(2)}, u32[]{:S(2)}) collective-permute-start(f32[2304,128]{1,0:T(8,128)} %constant_dynamic-update-slice_fusion.10), channel_id=1, source_target_pairs={{0,1},{1,0},{2,3},{3,2},{4,5},{5,4},{6,7},{7,6},{8,9},{9,8},{10,11... | collective-permute-start | bytes 3538952 | tf_op jit(solution)/shard_map/ppermute | solution.py:42
  24.4 0.7 %copy-start.14 = (f32[32,128]{1,0:T(8,128)S(1)}, f32[32,128]{1,0:T(8,128)}, u32[]{:S(2)}) copy-start(f32[32,128]{1,0:T(8,128)} %copy-done.13) | copy-start | bytes 49156
  24.4 1.6 %copy-start.10 = (f32[64,128]{1,0:T(8,128)S(1)}, f32[64,128]{1,0:T(8,128)}, u32[]{:S(2)}) copy-start(f32[64,128]{1,0:T(8,128)} %copy-done.9) | copy-start | bytes 98308
  24.4 1.6 %copy-start.12 = (f32[64,128]{1,0:T(8,128)S(1)}, f32[64,128]{1,0:T(8,128)}, u32[]{:S(2)}) copy-start(f32[64,128]{1,0:T(8,128)} %copy-done.11) | copy-start | bytes 98308
  24.5 1.9 %copy-start.1 = (f32[2304,128]{1,0:T(8,128)}, f32[2304,128]{1,0:T(8,128)S(1)}, u32[]{:S(2)}) copy-start(f32[2304,128]{1,0:T(8,128)S(1)} %collective-permute-done.2) | copy-start | bytes 3538948
  26.4 1.4 %copy-start.2 = (f32[2304,128]{1,0:T(8,128)S(1)}, f32[2304,128]{1,0:T(8,128)}, u32[]{:S(2)}) copy-start(f32[2304,128]{1,0:T(8,128)} %copy-done.1) | copy-start | bytes 3538948
  26.5 1.4 %copy-start.6 = (f32[128,128]{1,0:T(8,128)S(1)}, f32[128,128]{1,0:T(8,128)}, u32[]{:S(2)}) copy-start(f32[128,128]{1,0:T(8,128)} %copy-done.5) | copy-start | bytes 196612
  33.7 0.9 %copy-start.3 = (f32[96,192]{1,0:T(8,128)S(1)}, f32[96,192]{1,0:T(8,128)}, u32[]{:S(2)}) copy-start(f32[96,192]{1,0:T(8,128)} %get-tuple-element.38) | copy-start | bytes 221188
  33.8 0.9 %copy-start.4 = (f32[96,192]{1,0:T(8,128)S(1)}, f32[96,192]{1,0:T(8,128)}, u32[]{:S(2)}) copy-start(f32[96,192]{1,0:T(8,128)} %get-tuple-element.39) | copy-start | bytes 221188
  35.8 8.4 %collective-permute-start.3 = (f32[3,2,64,128]{3,2,1,0:T(8,128)S(1)}, f32[3,2,64,128]{3,2,1,0:T(8,128)S(1)}, u32[]{:S(2)}, u32[]{:S(2)}) collective-permute-start(f32[3,2,64,128]{3,2,1,0:T(8,128)S(1)} %dynamic-slice_bitcast_fusion), channel_id=1, source_target_pairs={{0,2},{1,3},{4,6},{5,7},{8,10},{9,11},{12,14},{13,15},{16,18},{17,... | collective-permute-start | bytes 589832 | tf_op jit(solution)/shard_map/ppermute | solution.py:122
  44.3 7.5 %collective-permute-start.4 = (f32[384,128]{1,0:T(8,128)S(1)}, f32[384,128]{1,0:T(8,128)S(1)}, u32[]{:S(2)}, u32[]{:S(2)}) collective-permute-start(f32[384,128]{1,0:T(8,128)S(1)} %bitcast.291), channel_id=1, source_target_pairs={{0,4},{4,8},{8,12},{1,5},{5,9},{9,13},{2,6},{6,10},{10,14},{3,7},{... | collective-permute-start | bytes 589832 | tf_op jit(solution)/shard_map/ppermute | solution.py:42
  47.5 7.2 %collective-permute-start.5 = (f32[384,128]{1,0:T(8,128)S(1)}, f32[384,128]{1,0:T(8,128)S(1)}, u32[]{:S(2)}, u32[]{:S(2)}) collective-permute-start(f32[384,128]{1,0:T(8,128)S(1)} %bitcast.292), channel_id=1, source_target_pairs={{4,0},{8,4},{12,8},{5,1},{9,5},{13,9},{6,2},{10,6},{14,10},{7,3},{... | collective-permute-start | bytes 589832 | tf_op jit(solution)/shard_map/ppermute | solution.py:42
  55.5 3.8 %collective-permute-start.6 = (f32[1152,128]{1,0:T(8,128)}, f32[1152,128]{1,0:T(8,128)S(1)}, u32[]{:S(2)}, u32[]{:S(2)}) collective-permute-start(f32[1152,128]{1,0:T(8,128)} %bitcast.103), channel_id=1, source_target_pairs={{0,1},{1,0},{2,3},{3,2},{4,5},{5,4},{6,7},{7,6},{8,9},{9,8},{10,11... | collective-permute-start | bytes 1769480 | tf_op jit(solution)/shard_map/ppermute | solution.py:42

commit v5 on v3

--- a/solution.py
+++ b/solution.py
@@ -44,6 +44,12 @@
     from_prev = lax.ppermute(stack[:, rows - halo:], "tile", [(i, i + 1) for i in range(tiles - 1)])
     from_next = lax.ppermute(stack[:, :halo], "tile", [(i + 1, i) for i in range(tiles - 1)])
     tall = jnp.concatenate([from_prev, stack, from_next], axis=-2)
+    return widen(tall, halo, splits)
+
+
+def widen(tall, halo, splits):
+    wave = lax.axis_index("wave")
+    cols = tall.shape[-1]
     got = lax.ppermute(tall, "wave", [(0, 1), (1, 0)])
     out, start = [], 0
     for size in splits:
@@ -97,19 +103,24 @@
         return lax.dynamic_slice_in_dim(current, reach * wave, cols, axis=-1)
 
     exits = jnp.zeros(incident.shape, jnp.float32)
-    carried = None
+    tiles = lax.axis_size("tile")
+    spot = lambda t, d: t * depth_count + d
+    ahead = range(depth_count - 1)
+    own_pairs = [(spot(t, d), spot(t, d + 1)) for t in range(tiles) for d in ahead]
+    prev_pairs = [(spot(t - 1, d), spot(t, d + 1)) for t in range(1, tiles) for d in ahead]
+    next_pairs = [(spot(t + 1, d), spot(t, d + 1)) for t in range(tiles - 1) for d in ahead]
+    field = first_field
     for step in range(depth_count):
-        if step == 0:
-            field = first_field
-        else:
-            field = grow(carried.reshape(2 * illum, rows, cols), reach, (2 * illum,))[0].reshape(
-                illum, 2, tall, width
-            )
         result = depth_section(field)
         exits = jnp.where(depth_index == step, result, exits)
         if step + 1 < depth_count:
-            carried = lax.ppermute(
-                result, "depth", [(i, i + 1) for i in range(depth_count - 1)]
+            flat = result.reshape(2 * illum, rows, cols)
+            grid = ("tile", "depth")
+            from_prev = lax.ppermute(flat[:, rows - reach:], grid, prev_pairs)
+            mine = lax.ppermute(flat, grid, own_pairs)
+            from_next = lax.ppermute(flat[:, :reach], grid, next_pairs)
+            field = widen(jnp.concatenate([from_prev, mine, from_next], axis=1), reach, (2 * illum,))[0].reshape(
+                illum, 2, tall, width
             )
     return exits[None]
 

time: 64.2 us -> 62.5 us (0.974)
  starting transfers between devices: 15.7 us -> 11.8 us
  waiting for transfers between devices: 22.6 us -> 25.4 us
  other arithmetic: 8.52 us -> 7.65 us
    ppermute x3 -> x5, waiting for transfers between devices: 8.93 us -> 15.6 us  [the longest x1 8.73 us: per_device(): mine = lax.ppermute(flat, grid, own_pairs)]
    ppermute x2 -> x1, starting transfers between devices: 6.75 us -> 3.2 us  [grow(): lax.ppermute(stack[:, rows - halo:], 'tile', [(i, i + 1) for i in range(t...]
    ppermute x2 -> x1, waiting for transfers between devices: 9.99 us -> 7.98 us  [grow(): lax.ppermute(stack[:, :halo], 'tile', [(i + 1, i) for i in range(tiles -...]
    ppermute x2 -> x1, waiting for transfers between devices: 3.7 us -> 1.77 us  [grow(): lax.ppermute(stack[:, rows - halo:], 'tile', [(i, i + 1) for i in range(t...]
    ppermute x2 -> x1, starting transfers between devices: 3.99 us -> 2.08 us  [grow(): lax.ppermute(stack[:, :halo], 'tile', [(i + 1, i) for i in range(tiles -...]
    ppermute x3 -> x5, starting transfers between devices: 4.94 us -> 6.49 us  [the longest x2 2.43 us: widen(): got = lax.ppermute(tall, 'wave', [(0, 1), (1, 0)])]
    concatenate x2 -> x1, other arithmetic: 0.98 us -> 0.12 us  [grow(): tall = jnp.concatenate([from_prev, stack, from_next], axis=-2)]
  transfers between devices with their start and end apart: 7 -> 7, of which waited for: 6 -> 5; matrix products, arithmetic and copies ran while one was open for 7% -> 7% of each run, Pallas kernels for 0% -> 0%
where the time goes in v5:
time: 62.5 us; the launch traced here: 62.1 us
  waiting for transfers between devices  25.4 us (41%)
  matrix products  12.3 us (20%)
  starting transfers between devices  11.8 us (19%)
  other arithmetic  7.65 us (12%)
  local copies, waits for them, and re-layouts  3.9 us (6%)
  between operations  1.17 us (2%)
    ppermute x1, waiting for transfers between devices, per_device(): mine = lax.ppermute(flat, grid, own_pairs)  8.73 us
    ppermute x1, waiting for transfers between devices, grow(): lax.ppermute(stack[:, :halo], 'tile', [(i + 1, i) for i in range(tiles -...  7.98 us
    dot_general x8, matrix products, depth_section(): jnp.einsum('dcab,icbj->idaj', row_bands[s], moved, precision=lax.Precisio...  6.55 us
    dot_general x8, matrix products, depth_section(): jnp.einsum('dcyj,icxj->idxy', col_band, rows_done, precision=lax.Precisio...  5.71 us
    ppermute x1, waiting for transfers between devices, per_device(): from_prev = lax.ppermute(flat[:, rows - reach:], grid, prev_pairs)  5.27 us
    ppermute x1, starting transfers between devices, grow(): lax.ppermute(stack[:, rows - halo:], 'tile', [(i, i + 1) for i in range(t...  3.2 us
    ppermute x2, starting transfers between devices, widen(): got = lax.ppermute(tall, 'wave', [(0, 1), (1, 0)])  2.43 us
    ppermute x1, starting transfers between devices, grow(): lax.ppermute(stack[:, :halo], 'tile', [(i + 1, i) for i in range(tiles -...  2.08 us
  transfers between devices with their start and end apart: 7, of which 5 were waited for; matrix products, arithmetic and copies ran while one was open for 7% of the time, Pallas kernels for 0%

profile of v5, /device:TPU:15, one launch (start us, length us, event | category | flops | bytes accessed | tf_op | source)
XLA Modules:
  0.0 62.1 jit_solution(17247842522644732355)
XLA Ops:
  0.0 1.4 %fusion.29 = (f32[4,1,64,128]{3,2,1,0:T(8,128)S(1)}, f32[4,1,64,128]{3,2,1,0:T(8,128)S(1)}) fusion(bf16[4,64,128]{2,1,0:T(8,128)(2,1)} %param.5, bf16[4,64,128]{2,1,0:T(8,128)(2,1)} %param.6), kind=kLoop, calls=%fused_computation.92 | loop fusion | flops 163840 | bytes 393216 | tf_op jit(solution)/shard_map/stack | solution.py:25
  1.4 1.0 %pad_maximum_fusion.2 = f32[14,64,128]{2,1,0:T(8,128)S(1)} fusion(f32[8,64,128]{2,1,0:T(8,128)S(1)} %bitcast.243, f32[6,64,128]{2,1,0:T(8,128)} %bitcast.247), kind=kLoop, calls=%fused_computation.67 | loop fusion | flops 114688 | bytes 917504 | tf_op jit(solution)/shard_map/concatenate | solution.py:77
  2.4 2.1 %collective-permute-start.1 = (f32[14,64,128]{2,1,0:T(8,128)S(1)}, f32[14,64,128]{2,1,0:T(8,128)S(1)}, u32[]{:S(2)}, u32[]{:S(2)}) collective-permute-start(f32[14,64,128]{2,1,0:T(8,128)S(1)} %pad_maximum_fusion.2), channel_id=1, source_target_pairs={{4,0},{8,4},{12,8},{5,1},{9,5},{13,9},{6,2},{10,6},{14,10},{7,3},{... | collective-permute-start | bytes 1376264 | tf_op jit(solution)/shard_map/ppermute | solution.py:45
  4.5 3.2 %collective-permute-start = (f32[14,64,128]{2,1,0:T(8,128)S(1)}, f32[14,64,128]{2,1,0:T(8,128)S(1)}, u32[]{:S(2)}, u32[]{:S(2)}) collective-permute-start(f32[14,64,128]{2,1,0:T(8,128)S(1)} %pad_maximum_fusion.2), channel_id=1, source_target_pairs={{0,4},{4,8},{8,12},{1,5},{5,9},{9,13},{2,6},{6,10},{10,14},{3,7},{... | collective-permute-start | bytes 1376264 | tf_op jit(solution)/shard_map/ppermute | solution.py:44
  7.7 8.0 %collective-permute-done.1 = f32[14,64,128]{2,1,0:T(8,128)S(1)} collective-permute-done((f32[14,64,128]{2,1,0:T(8,128)S(1)}, f32[14,64,128]{2,1,0:T(8,128)S(1)}, u32[]{:S(2)}, u32[]{:S(2)}) %collective-permute-start.1) | collective-permute-done | bytes 458784 | tf_op jit(solution)/shard_map/ppermute | solution.py:45
  15.7 1.8 %collective-permute-done = f32[14,64,128]{2,1,0:T(8,128)S(1)} collective-permute-done((f32[14,64,128]{2,1,0:T(8,128)S(1)}, f32[14,64,128]{2,1,0:T(8,128)S(1)}, u32[]{:S(2)}, u32[]{:S(2)}) %collective-permute-start) | collective-permute-done | bytes 458784 | tf_op jit(solution)/shard_map/ppermute | solution.py:44
  17.6 1.9 %collective-permute-start.2 = (f32[14,192,128]{2,1,0:T(8,128)S(1)}, f32[14,192,128]{2,1,0:T(8,128)S(1)}, u32[]{:S(2)}, u32[]{:S(2)}) collective-permute-start(f32[14,192,128]{2,1,0:T(8,128)S(1)} %pad_maximum_fusion.1), channel_id=1, source_target_pairs={{0,1},{1,0},{2,3},{3,2},{4,5},{5,4},{6,7},{7,6},{8,9},{9,8},{10,11... | collective-permute-start | bytes 4128776 | tf_op jit(solution)/shard_map/ppermute | solution.py:53
  19.5 0.6 multiply_reduce_fusion
  21.6 1.7 %reshape.48 = f32[2,192,383]{2,1,0:T(8,128)} reshape(f32[2,73536]{1,0:T(2,128)S(1)} %slice.231) | data formatting | bytes 1176576 | tf_op jit(solution)/shard_map/reshape | solution.py:15
  23.3 1.1 %fusion.57 = (f32[1,192,192]{2,1,0:T(8,128)S(1)}, f32[1,192,192]{2,1,0:T(8,128)S(1)}, f32[1,192,192]{2,1,0:T(8,128)S(1)}) fusion(f32[2,192,383]{2,1,0:T(8,128)} %reshape.48), kind=kLoop, calls=%fused_computation.121 | loop fusion | flops 36864 | bytes 737280 | tf_op jit(solution)/shard_map/slice | solution.py:16
  24.8 0.5 maximum_select_fusion
  25.3 0.5 maximum_select_fusion.1
  26.7 1.0 %convolution_bitcast_fusion.3 = f32[3,2,160,192,1]{3,2,1,4,0:T(8,128)S(1)} fusion(f32[3,1,192,192]{3,2,1,0:T(8,128)S(1)} %get-tuple-element.14, f32[3,1,192,192]{3,2,1,0:T(8,128)S(1)} %get-tuple-element.13, f32[1,2,192,192]{3,2,1,0:T(8,128)S(1)} %get-tuple-element.39, f32[1,2,192,192]{3,2,1,0:T(8,128)S(1)} %get-tuple-element.38), kind=kOutput, calls=%fused_computation.15 | convolution fusion | flops 425017344 | bytes 2211840 | tf_op jit(solution)/shard_map/dcab,icbj->idaj/dot_general | solution.py:97
  27.6 1.0 %convolution_bitcast_fusion.2 = f32[3,2,160,192]{3,2,1,0:T(8,128)S(1)} fusion(f32[3,2,160,192,1]{3,2,1,4,0:T(8,128)S(1)} %convolution_bitcast_fusion.3, f32[1,2,192,192]{3,2,1,0:T(8,128)S(1)} %get-tuple-element.38, f32[1,2,192,192]{3,2,1,0:T(8,128)S(1)} %get-tuple-element.39), kind=kOutput, calls=%fused_computation.14 | convolution fusion | flops 424820736 | bytes 2064384 | tf_op jit(solution)/shard_map/dcyj,icxj->idxy/dot_general | solution.py:100
  28.7 1.4 %convolution_bitcast_fusion.11 = f32[3,2,128,192,1]{2,3,1,4,0:T(8,128)S(1)} fusion(f32[3,1,160,192]{3,2,1,0:T(8,128)S(1)} %get-tuple-element.24, f32[3,1,160,192]{3,2,1,0:T(8,128)S(1)} %get-tuple-element.23, f32[1,2,192,192]{3,2,1,0:T(8,128)S(1)} %get-tuple-element.39, f32[1,2,192,192]{3,2,1,0:T(8,128)S(1)} %get-tuple-element.38), kind=kOutput, calls=%fused_computation.23 | convolution fusion | flops 283381760 | bytes 1916928 | tf_op jit(solution)/shard_map/dcab,icbj->idaj/dot_general | solution.py:97
  30.2 0.8 %convolution_bitcast_fusion.10 = f32[3,2,128,192]{2,3,1,0:T(8,128)S(1)} fusion(f32[3,2,128,192,1]{2,3,1,4,0:T(8,128)S(1)} %convolution_bitcast_fusion.11, f32[1,2,192,192]{3,2,1,0:T(8,128)S(1)} %get-tuple-element.38, f32[1,2,192,192]{3,2,1,0:T(8,128)S(1)} %get-tuple-element.39), kind=kOutput, calls=%fused_computation.22 | convolution fusion | flops 339886080 | bytes 1769472 | tf_op jit(solution)/shard_map/dcyj,icxj->idxy/dot_general | solution.py:100
  31.6 0.6 %convolution_bitcast_fusion.8 = f32[3,2,96,192]{3,2,1,0:T(8,128)S(1)} fusion(f32[3,2,96,192,1]{3,2,1,4,0:T(8,128)S(1)} %convolution_bitcast_fusion.9, f32[1,2,192,192]{3,2,1,0:T(8,128)S(1)} %get-tuple-element.38, f32[1,2,192,192]{3,2,1,0:T(8,128)S(1)} %get-tuple-element.39), kind=kOutput, calls=%fused_computation.20 | convolution fusion | flops 254951424 | bytes 1474560 | tf_op jit(solution)/shard_map/dcyj,icxj->idxy/dot_general | solution.py:100
  32.8 0.5 convolution_bitcast_fusion.14
  33.5 1.3 %collective-permute-start.3 = (f32[6,64,128]{2,1,0:T(8,128)S(1)}, f32[6,64,128]{2,1,0:T(8,128)S(1)}, u32[]{:S(2)}, u32[]{:S(2)}) collective-permute-start(f32[6,64,128]{2,1,0:T(8,128)S(1)} %bitcast.249), channel_id=1, source_target_pairs={{0,6},{4,10},{8,14},{1,7},{5,11},{9,15},{16,22},{20,26},{24,30},{1... | collective-permute-start | bytes 589832 | tf_op jit(solution)/shard_map/ppermute | solution.py:119
  34.8 1.3 %collective-permute-start.4 = (f32[6,64,128]{2,1,0:T(8,128)S(1)}, f32[6,64,128]{2,1,0:T(8,128)S(1)}, u32[]{:S(2)}, u32[]{:S(2)}) collective-permute-start(f32[6,64,128]{2,1,0:T(8,128)S(1)} %bitcast.250), channel_id=1, source_target_pairs={{0,2},{4,6},{8,10},{12,14},{1,3},{5,7},{9,11},{13,15},{16,18},{20,... | collective-permute-start | bytes 589832 | tf_op jit(solution)/shard_map/ppermute | solution.py:120
  36.1 1.5 %collective-permute-start.5 = (f32[6,64,128]{2,1,0:T(8,128)S(1)}, f32[6,64,128]{2,1,0:T(8,128)S(1)}, u32[]{:S(2)}, u32[]{:S(2)}) collective-permute-start(f32[6,64,128]{2,1,0:T(8,128)S(1)} %bitcast.251), channel_id=1, source_target_pairs={{4,2},{8,6},{12,10},{5,3},{9,7},{13,11},{20,18},{24,22},{28,26},{2... | collective-permute-start | bytes 589832 | tf_op jit(solution)/shard_map/ppermute | solution.py:121
  37.5 5.3 %collective-permute-done.3 = f32[6,64,128]{2,1,0:T(8,128)S(1)} collective-permute-done((f32[6,64,128]{2,1,0:T(8,128)S(1)}, f32[6,64,128]{2,1,0:T(8,128)S(1)}, u32[]{:S(2)}, u32[]{:S(2)}) %collective-permute-start.3) | collective-permute-done | bytes 196640 | tf_op jit(solution)/shard_map/ppermute | solution.py:119
  42.8 8.7 %collective-permute-done.4 = f32[6,64,128]{2,1,0:T(8,128)S(1)} collective-permute-done((f32[6,64,128]{2,1,0:T(8,128)S(1)}, f32[6,64,128]{2,1,0:T(8,128)S(1)}, u32[]{:S(2)}, u32[]{:S(2)}) %collective-permute-start.4) | collective-permute-done | bytes 196640 | tf_op jit(solution)/shard_map/ppermute | solution.py:120
  51.6 0.5 collective-permute-start.6
  52.1 1.6 %collective-permute-done.6 = f32[6,192,128]{2,1,0:T(8,128)S(1)} collective-permute-done((f32[6,192,128]{2,1,0:T(8,128)S(1)}, f32[6,192,128]{2,1,0:T(8,128)S(1)}, u32[]{:S(2)}, u32[]{:S(2)}) %collective-permute-start.6) | collective-permute-done | bytes 589856 | tf_op jit(solution)/shard_map/ppermute | solution.py:53
  54.5 1.0 %convolution_bitcast_fusion.1 = f32[3,2,160,192,1]{3,2,1,4,0:T(8,128)S(1)} fusion(f32[3,1,192,192]{3,2,1,0:T(8,128)S(1)} %get-tuple-element.6, f32[3,1,192,192]{3,2,1,0:T(8,128)S(1)} %get-tuple-element.5, f32[1,2,192,192]{3,2,1,0:T(8,128)S(1)} %get-tuple-element.39, f32[1,2,192,192]{3,2,1,0:T(8,128)S(1)} %get-tuple-element.38), kind=kOutput, calls=%fused_computation.13 | convolution fusion | flops 425017344 | bytes 2211840 | tf_op jit(solution)/shard_map/dcab,icbj->idaj/dot_general | solution.py:97
  55.5 0.9 %convolution_bitcast_fusion = f32[3,2,160,192]{3,2,1,0:T(8,128)S(1)} fusion(f32[3,2,160,192,1]{3,2,1,4,0:T(8,128)S(1)} %convolution_bitcast_fusion.1, f32[1,2,192,192]{3,2,1,0:T(8,128)S(1)} %get-tuple-element.38, f32[1,2,192,192]{3,2,1,0:T(8,128)S(1)} %get-tuple-element.39), kind=kOutput, calls=%fused_computation.12 | convolution fusion | flops 424820736 | bytes 2064384 | tf_op jit(solution)/shard_map/dcyj,icxj->idxy/dot_general | solution.py:100
  56.6 1.4 %convolution_bitcast_fusion.7 = f32[3,2,128,192,1]{2,3,1,4,0:T(8,128)S(1)} fusion(f32[3,1,160,192]{3,2,1,0:T(8,128)S(1)} %get-tuple-element.22, f32[3,1,160,192]{3,2,1,0:T(8,128)S(1)} %get-tuple-element.21, f32[1,2,192,192]{3,2,1,0:T(8,128)S(1)} %get-tuple-element.39, f32[1,2,192,192]{3,2,1,0:T(8,128)S(1)} %get-tuple-element.38), kind=kOutput, calls=%fused_computation.19 | convolution fusion | flops 283381760 | bytes 1916928 | tf_op jit(solution)/shard_map/dcab,icbj->idaj/dot_general | solution.py:97
  58.0 0.8 %convolution_bitcast_fusion.6 = f32[3,2,128,192]{2,3,1,0:T(8,128)S(1)} fusion(f32[3,2,128,192,1]{2,3,1,4,0:T(8,128)S(1)} %convolution_bitcast_fusion.7, f32[1,2,192,192]{3,2,1,0:T(8,128)S(1)} %get-tuple-element.38, f32[1,2,192,192]{3,2,1,0:T(8,128)S(1)} %get-tuple-element.39), kind=kOutput, calls=%fused_computation.18 | convolution fusion | flops 339886080 | bytes 1769472 | tf_op jit(solution)/shard_map/dcyj,icxj->idxy/dot_general | solution.py:100
  59.3 0.6 %convolution_bitcast_fusion.4 = f32[3,2,96,192]{3,2,1,0:T(8,128)S(1)} fusion(f32[3,2,96,192,1]{3,2,1,4,0:T(8,128)S(1)} %convolution_bitcast_fusion.5, f32[1,2,192,192]{3,2,1,0:T(8,128)S(1)} %get-tuple-element.38, f32[1,2,192,192]{3,2,1,0:T(8,128)S(1)} %get-tuple-element.39), kind=kOutput, calls=%fused_computation.16 | convolution fusion | flops 254951424 | bytes 1474560 | tf_op jit(solution)/shard_map/dcyj,icxj->idxy/dot_general | solution.py:100
  60.8 0.5 convolution_bitcast_fusion.12
  61.3 0.9 %fusion.25 = f32[1,3,2,64,128]{4,3,2,1,0:T(8,128)} fusion(f32[3,64,2,192]{3,1,2,0:T(8,128)S(1)} %convolution_bitcast_fusion.12, s32[]{:T(128)S(6)} %select_n.52, pred[]{:T(512)S(6)} %eq.13, pred[]{:T(512)S(6)} %eq.11, f32[3,64,2,192]{3,1,2,0:T(8,128)S(1)} %convolution_bitcast_fusion.14), kind=kLoop, calls=%fused_computation.85 | loop fusion | flops 98304 | bytes 589830 | tf_op jit(solution)/shard_map/broadcast_in_dim | solution.py:125
  (54 shorter events, 5.8 us)
Async XLA Ops:
  0.0 17.5 %copy-start.4 = (f32[3,2,64,128]{3,2,1,0:T(8,128)S(1)}, f32[3,2,64,128]{3,2,1,0:T(8,128)}, u32[]{:S(2)}) copy-start(f32[3,2,64,128]{3,2,1,0:T(8,128)} %param.4) | copy-start | bytes 589828
  2.4 17.1 %copy-start.5 = (f32[2,33]{1,0:T(2,128)S(1)}, f32[2,33]{1,0:T(2,128)}, u32[]{:S(2)}) copy-start(f32[2,33]{1,0:T(2,128)} %param.7) | copy-start | bytes 796
  2.4 13.3 %collective-permute-start.1 = (f32[14,64,128]{2,1,0:T(8,128)S(1)}, f32[14,64,128]{2,1,0:T(8,128)S(1)}, u32[]{:S(2)}, u32[]{:S(2)}) collective-permute-start(f32[14,64,128]{2,1,0:T(8,128)S(1)} %pad_maximum_fusion.2), channel_id=1, source_target_pairs={{4,0},{8,4},{12,8},{5,1},{9,5},{13,9},{6,2},{10,6},{14,10},{7,3},{... | collective-permute-start | bytes 1376264 | tf_op jit(solution)/shard_map/ppermute | solution.py:45
  4.5 13.0 %collective-permute-start = (f32[14,64,128]{2,1,0:T(8,128)S(1)}, f32[14,64,128]{2,1,0:T(8,128)S(1)}, u32[]{:S(2)}, u32[]{:S(2)}) collective-permute-start(f32[14,64,128]{2,1,0:T(8,128)S(1)} %pad_maximum_fusion.2), channel_id=1, source_target_pairs={{0,4},{4,8},{8,12},{1,5},{5,9},{9,13},{2,6},{6,10},{10,14},{3,7},{... | collective-permute-start | bytes 1376264 | tf_op jit(solution)/shard_map/ppermute | solution.py:44
  17.6 7.0 %collective-permute-start.2 = (f32[14,192,128]{2,1,0:T(8,128)S(1)}, f32[14,192,128]{2,1,0:T(8,128)S(1)}, u32[]{:S(2)}, u32[]{:S(2)}) collective-permute-start(f32[14,192,128]{2,1,0:T(8,128)S(1)} %pad_maximum_fusion.1), channel_id=1, source_target_pairs={{0,1},{1,0},{2,3},{3,2},{4,5},{5,4},{6,7},{7,6},{8,9},{9,8},{10,11... | collective-permute-start | bytes 4128776 | tf_op jit(solution)/shard_map/ppermute | solution.py:53
  25.9 6.4 %copy-start = (f32[96,192]{1,0:T(8,128)}, f32[96,192]{1,0:T(8,128)S(1)}, u32[]{:S(2)}) copy-start(f32[96,192]{1,0:T(8,128)S(1)} %get-tuple-element.7) | copy-start | bytes 221188
  25.9 6.4 %copy-start.2 = (f32[96,192]{1,0:T(8,128)}, f32[96,192]{1,0:T(8,128)S(1)}, u32[]{:S(2)}) copy-start(f32[96,192]{1,0:T(8,128)S(1)} %get-tuple-element.8) | copy-start | bytes 221188
  33.5 9.3 %collective-permute-start.3 = (f32[6,64,128]{2,1,0:T(8,128)S(1)}, f32[6,64,128]{2,1,0:T(8,128)S(1)}, u32[]{:S(2)}, u32[]{:S(2)}) collective-permute-start(f32[6,64,128]{2,1,0:T(8,128)S(1)} %bitcast.249), channel_id=1, source_target_pairs={{0,6},{4,10},{8,14},{1,7},{5,11},{9,15},{16,22},{20,26},{24,30},{1... | collective-permute-start | bytes 589832 | tf_op jit(solution)/shard_map/ppermute | solution.py:119
  34.8 16.8 %collective-permute-start.4 = (f32[6,64,128]{2,1,0:T(8,128)S(1)}, f32[6,64,128]{2,1,0:T(8,128)S(1)}, u32[]{:S(2)}, u32[]{:S(2)}) collective-permute-start(f32[6,64,128]{2,1,0:T(8,128)S(1)} %bitcast.250), channel_id=1, source_target_pairs={{0,2},{4,6},{8,10},{12,14},{1,3},{5,7},{9,11},{13,15},{16,18},{20,... | collective-permute-start | bytes 589832 | tf_op jit(solution)/shard_map/ppermute | solution.py:120
  36.1 15.5 %collective-permute-start.5 = (f32[6,64,128]{2,1,0:T(8,128)S(1)}, f32[6,64,128]{2,1,0:T(8,128)S(1)}, u32[]{:S(2)}, u32[]{:S(2)}) collective-permute-start(f32[6,64,128]{2,1,0:T(8,128)S(1)} %bitcast.251), channel_id=1, source_target_pairs={{4,2},{8,6},{12,10},{5,3},{9,7},{13,11},{20,18},{24,22},{28,26},{2... | collective-permute-start | bytes 589832 | tf_op jit(solution)/shard_map/ppermute | solution.py:121
  51.6 2.1 %collective-permute-start.6 = (f32[6,192,128]{2,1,0:T(8,128)S(1)}, f32[6,192,128]{2,1,0:T(8,128)S(1)}, u32[]{:S(2)}, u32[]{:S(2)}) collective-permute-start(f32[6,192,128]{2,1,0:T(8,128)S(1)} %constant_dynamic-update-slice_fusion), channel_id=1, source_target_pairs={{0,1},{1,0},{2,3},{3,2},{4,5},{5,4},{6,7},{7,6},{8,9},{9,8},{10,11... | collective-permute-start | bytes 1769480 | tf_op jit(solution)/shard_map/ppermute | solution.py:53
  59.3 0.9 %copy-start.1 = (f32[96,192]{1,0:T(8,128)S(1)}, f32[96,192]{1,0:T(8,128)}, u32[]{:S(2)}) copy-start(f32[96,192]{1,0:T(8,128)} %copy-done) | copy-start | bytes 221188
  59.3 0.9 %copy-start.3 = (f32[96,192]{1,0:T(8,128)S(1)}, f32[96,192]{1,0:T(8,128)}, u32[]{:S(2)}) copy-start(f32[96,192]{1,0:T(8,128)} %copy-done.2) | copy-start | bytes 221188

commit v6 on v5

--- a/solution.py
+++ b/solution.py
@@ -73,13 +73,14 @@
 
     trans_own = transmission(phase_shift, absorption)
     illum = incident.shape[0]
-    field_grown, trans_grown = grow(
-        jnp.concatenate([incident.reshape(2 * illum, rows, cols), trans_own.reshape(2 * slices, rows, cols)]),
+    first_field, trans_head = grow(
+        jnp.concatenate([incident.reshape(2 * illum, rows, cols), trans_own[0]]),
         reach,
-        (2 * illum, 2 * slices),
+        (2 * illum, 2),
     )
-    first_field = field_grown.reshape(illum, 2, rows + 2 * reach, cols + reach)
-    trans_reg = trans_grown.reshape(slices, 2, rows + 2 * reach, cols + reach)
+    (trans_rest,) = grow(trans_own[1:].reshape(2 * slices - 2, rows, cols), reach, (2 * slices - 2,))
+    first_field = first_field.reshape(illum, 2, rows + 2 * reach, cols + reach)
+    trans_reg = jnp.concatenate([trans_head[None], trans_rest.reshape(slices - 1, 2, rows + 2 * reach, cols + reach)])
     width = cols + reach
     tall = rows + 2 * reach
 

time: 62.5 us -> 71.3 us (1.14)
  local copies, waits for them, and re-layouts: 3.9 us -> 11.9 us
  waiting for transfers between devices: 25.4 us -> 19.5 us
  starting transfers between devices: 11.8 us -> 17.5 us
    ppermute x1 -> x2, waiting for transfers between devices: 7.98 us -> 3.1 us  [grow(): lax.ppermute(stack[:, :halo], 'tile', [(i + 1, i) for i in range(tiles -...]
    unnamed x16 -> x44, local copies, waits for them, and re-layouts: 0.82 us -> 4.36 us
    ppermute x1 -> x2, starting transfers between devices: 3.2 us -> 6.4 us  [grow(): lax.ppermute(stack[:, rows - halo:], 'tile', [(i, i + 1) for i in range(t...]
    mul x5, local copies, waits for them, and re-layouts: 0.18 us -> 2.46 us  [modulate(): field_real * trans[0] - field_imag * trans[1]]
    ppermute x1 -> x2, starting transfers between devices: 2.08 us -> 4.19 us  [grow(): lax.ppermute(stack[:, :halo], 'tile', [(i + 1, i) for i in range(tiles -...]
    concatenate x1 -> x2, other arithmetic: 0.12 us -> 1.93 us  [grow(): tall = jnp.concatenate([from_prev, stack, from_next], axis=-2)]
    mul x1, local copies, waits for them, and re-layouts: 0.09 us -> 1.66 us  [modulate(): field_imag * trans[1]]
    slice x2, local copies, waits for them, and re-layouts: 0.09 us -> 1.55 us  [widen(): own, other = (tall[start:start + size], got[start:start + size])]
  transfers between devices with their start and end apart: 7 -> 10, of which waited for: 5 -> 5; matrix products, arithmetic and copies ran while one was open for 7% -> 15% of each run, Pallas kernels for 0% -> 0%
where the time goes in v6:
time: 71.3 us; the launch traced here: 70.5 us
  waiting for transfers between devices  19.5 us (27%)
  starting transfers between devices  17.5 us (25%)
  matrix products  12.3 us (17%)
  local copies, waits for them, and re-layouts  11.9 us (17%)
  other arithmetic  7.99 us (11%)
  between operations  1.3 us (2%)
    ppermute x1, waiting for transfers between devices, per_device(): mine = lax.ppermute(flat, grid, own_pairs)  9.07 us
    dot_general x8, matrix products, depth_section(): jnp.einsum('dcab,icbj->idaj', row_bands[s], moved, precision=lax.Precisio...  6.55 us
    ppermute x2, starting transfers between devices, grow(): lax.ppermute(stack[:, rows - halo:], 'tile', [(i, i + 1) for i in range(t...  6.4 us
    dot_general x8, matrix products, depth_section(): jnp.einsum('dcyj,icxj->idxy', col_band, rows_done, precision=lax.Precisio...  5.72 us
    ppermute x1, waiting for transfers between devices, per_device(): from_prev = lax.ppermute(flat[:, rows - reach:], grid, prev_pairs)  4.88 us
    unnamed x44, local copies, waits for them, and re-layouts  4.36 us
    ppermute x2, starting transfers between devices, grow(): lax.ppermute(stack[:, :halo], 'tile', [(i + 1, i) for i in range(tiles -...  4.19 us
    ppermute x2, waiting for transfers between devices, grow(): lax.ppermute(stack[:, :halo], 'tile', [(i + 1, i) for i in range(tiles -...  3.1 us
  transfers between devices with their start and end apart: 10, of which 5 were waited for; matrix products, arithmetic and copies ran while one was open for 15% of the time, Pallas kernels for 0%

profile of v6, /device:TPU:15, one launch (start us, length us, event | category | flops | bytes accessed | tf_op | source)
XLA Modules:
  0.0 70.5 jit_solution(336383978309794821)
XLA Ops:
  0.0 1.4 %fusion.29 = (f32[4,1,64,128]{3,2,1,0:T(8,128)S(1)}, f32[4,1,64,128]{3,2,1,0:T(8,128)S(1)}) fusion(bf16[4,64,128]{2,1,0:T(8,128)(2,1)} %param.5, bf16[4,64,128]{2,1,0:T(8,128)(2,1)} %param.6), kind=kLoop, calls=%fused_computation.93 | loop fusion | flops 163840 | bytes 393216 | tf_op jit(solution)/shard_map/stack | solution.py:25
  1.4 0.9 %pad_maximum_fusion.3 = f32[8,64,128]{2,1,0:T(8,128)S(1)} fusion(f32[2,64,128]{2,1,0:T(8,128)S(1)} %maximum_bitcast_fusion.18, f32[6,64,128]{2,1,0:T(8,128)} %bitcast.252), kind=kLoop, calls=%fused_computation.79 | loop fusion | flops 65536 | bytes 524288 | tf_op jit(solution)/shard_map/concatenate | solution.py:77
  2.3 3.2 %collective-permute-start = (f32[8,64,128]{2,1,0:T(8,128)S(1)}, f32[8,64,128]{2,1,0:T(8,128)S(1)}, u32[]{:S(2)}, u32[]{:S(2)}) collective-permute-start(f32[8,64,128]{2,1,0:T(8,128)S(1)} %pad_maximum_fusion.3), channel_id=1, source_target_pairs={{0,4},{4,8},{8,12},{1,5},{5,9},{9,13},{2,6},{6,10},{10,14},{3,7},{... | collective-permute-start | bytes 786440 | tf_op jit(solution)/shard_map/ppermute | solution.py:44
  5.6 2.1 %collective-permute-start.1 = (f32[8,64,128]{2,1,0:T(8,128)S(1)}, f32[8,64,128]{2,1,0:T(8,128)}, u32[]{:S(2)}, u32[]{:S(2)}) collective-permute-start(f32[8,64,128]{2,1,0:T(8,128)S(1)} %pad_maximum_fusion.3), channel_id=1, source_target_pairs={{4,0},{8,4},{12,8},{5,1},{9,5},{13,9},{6,2},{10,6},{14,10},{7,3},{... | collective-permute-start | bytes 786440 | tf_op jit(solution)/shard_map/ppermute | solution.py:45
  7.7 3.2 %collective-permute-start.3 = (f32[6,64,128]{2,1,0:T(8,128)S(1)}, f32[6,64,128]{2,1,0:T(8,128)S(1)}, u32[]{:S(2)}, u32[]{:S(2)}) collective-permute-start(f32[6,64,128]{2,1,0:T(8,128)S(1)} %bitcast.246), channel_id=1, source_target_pairs={{0,4},{4,8},{8,12},{1,5},{5,9},{9,13},{2,6},{6,10},{10,14},{3,7},{... | collective-permute-start | bytes 589832 | tf_op jit(solution)/shard_map/ppermute | solution.py:44
  10.9 2.1 %collective-permute-start.4 = (f32[6,64,128]{2,1,0:T(8,128)S(1)}, f32[6,64,128]{2,1,0:T(8,128)S(1)}, u32[]{:S(2)}, u32[]{:S(2)}) collective-permute-start(f32[6,64,128]{2,1,0:T(8,128)S(1)} %bitcast.247), channel_id=1, source_target_pairs={{4,0},{8,4},{12,8},{5,1},{9,5},{13,9},{6,2},{10,6},{14,10},{7,3},{... | collective-permute-start | bytes 589832 | tf_op jit(solution)/shard_map/ppermute | solution.py:45
  14.5 0.8 %collective-permute-done.3 = f32[6,64,128]{2,1,0:T(8,128)S(1)} collective-permute-done((f32[6,64,128]{2,1,0:T(8,128)S(1)}, f32[6,64,128]{2,1,0:T(8,128)S(1)}, u32[]{:S(2)}, u32[]{:S(2)}) %collective-permute-start.3) | collective-permute-done | bytes 196640 | tf_op jit(solution)/shard_map/ppermute | solution.py:44
  15.4 3.1 %collective-permute-done.4 = f32[6,64,128]{2,1,0:T(8,128)S(1)} collective-permute-done((f32[6,64,128]{2,1,0:T(8,128)S(1)}, f32[6,64,128]{2,1,0:T(8,128)S(1)}, u32[]{:S(2)}, u32[]{:S(2)}) %collective-permute-start.4) | collective-permute-done | bytes 196640 | tf_op jit(solution)/shard_map/ppermute | solution.py:45
  18.5 0.9 %pad_maximum_fusion.2 = f32[6,192,128]{2,1,0:T(8,128)} fusion(f32[6,64,128]{2,1,0:T(8,128)S(1)} %collective-permute-done.4, f32[6,64,128]{2,1,0:T(8,128)S(1)} %bitcast.248, f32[6,64,128]{2,1,0:T(8,128)S(1)} %collective-permute-done.3), kind=kLoop, calls=%fused_computation.44 | loop fusion | flops 294912 | bytes 1179648 | tf_op jit(solution)/shard_map/concatenate | solution.py:46
  19.4 2.2 %collective-permute-start.5 = (f32[6,192,128]{2,1,0:T(8,128)}, f32[6,192,128]{2,1,0:T(8,128)S(1)}, u32[]{:S(2)}, u32[]{:S(2)}) collective-permute-start(f32[6,192,128]{2,1,0:T(8,128)} %pad_maximum_fusion.2), channel_id=1, source_target_pairs={{0,1},{1,0},{2,3},{3,2},{4,5},{5,4},{6,7},{7,6},{8,9},{9,8},{10,11... | collective-permute-start | bytes 1769480 | tf_op jit(solution)/shard_map/ppermute | solution.py:53
  22.2 0.8 %reshape.52 = f32[2,192,383]{2,1,0:T(8,128)S(1)} reshape(f32[2,73536]{1,0:T(2,128)S(1)} %slice.241) | data formatting | bytes 1176576 | tf_op jit(solution)/shard_map/reshape | solution.py:15
  23.2 0.8 %copy-done.18 = f32[3,2,64,128]{3,2,1,0:T(8,128)S(1)} copy-done((f32[3,2,64,128]{3,2,1,0:T(8,128)S(1)}, f32[3,2,64,128]{3,2,1,0:T(8,128)}, u32[]{:S(2)}) %copy-start.18) | copy-done | bytes 196632
  24.0 1.0 %pad_maximum_fusion.1 = f32[8,192,128]{2,1,0:T(8,128)S(1)} fusion(f32[8,64,128]{2,1,0:T(8,128)} %collective-permute-done.1, f32[2,64,128]{2,1,0:T(8,128)S(1)} %maximum_bitcast_fusion.18, f32[6,64,128]{2,1,0:T(8,128)S(1)} %bitcast.253, f32[8,64,128]{2,1,0:T(8,128)S(1)} %collective-permute-done), kind=kLoop, calls=%fused_computation.41 | loop fusion | flops 589824 | bytes 1572864 | tf_op jit(solution)/shard_map/concatenate | solution.py:46
  25.8 0.9 %slice.231 = f32[6,192,128]{2,1,0:T(8,128)} slice(f32[8,192,128]{2,1,0:T(8,128)S(1)} %pad_maximum_fusion.1), slice={[0:6], [0:192], [0:128]} | slice | bytes 1179648 | tf_op jit(solution)/shard_map/slice | solution.py:56
  28.9 1.6 %copy.16 = f32[128,192]{0,1:T(8,128)} copy(f32[128,192]{1,0:T(8,128)} %get-tuple-element.15) | data formatting | bytes 196608 | tf_op jit(solution)/shard_map/mul | solution.py:33
  30.5 1.7 %copy.17 = f32[128,192]{0,1:T(8,128)} copy(f32[128,192]{1,0:T(8,128)} %get-tuple-element.16) | data formatting | bytes 196608 | tf_op jit(solution)/shard_map/mul | solution.py:33
  32.4 0.9 %copy-done.17 = f32[2,192,128]{2,1,0:T(8,128)S(1)} copy-done((f32[2,192,128]{2,1,0:T(8,128)S(1)}, f32[2,192,128]{2,1,0:T(8,128)}, u32[]{:S(2)}) %copy-start.17) | copy-done | bytes 196632
  33.7 0.8 %copy-done = f32[6,192,128]{2,1,0:T(8,128)S(1)} copy-done((f32[6,192,128]{2,1,0:T(8,128)S(1)}, f32[6,192,128]{2,1,0:T(8,128)}, u32[]{:S(2)}) %copy-start) | copy-done | bytes 589848
  35.0 1.0 %convolution_bitcast_fusion.3 = f32[3,2,160,192,1]{3,2,1,4,0:T(8,128)S(1)} fusion(f32[3,1,192,192]{3,2,1,0:T(8,128)S(1)} %get-tuple-element.8, f32[3,1,192,192]{3,2,1,0:T(8,128)S(1)} %get-tuple-element.7, f32[1,2,192,192]{3,2,1,0:T(8,128)S(1)} %get-tuple-element.41, f32[1,2,192,192]{3,2,1,0:T(8,128)S(1)} %get-tuple-element.40), kind=kOutput, calls=%fused_computation.12 | convolution fusion | flops 425017344 | bytes 2211840 | tf_op jit(solution)/shard_map/dcab,icbj->idaj/dot_general | solution.py:98
  36.0 1.0 %convolution_bitcast_fusion.2 = f32[3,2,160,192]{3,2,1,0:T(8,128)S(1)} fusion(f32[3,2,160,192,1]{3,2,1,4,0:T(8,128)S(1)} %convolution_bitcast_fusion.3, f32[1,2,192,192]{3,2,1,0:T(8,128)S(1)} %get-tuple-element.40, f32[1,2,192,192]{3,2,1,0:T(8,128)S(1)} %get-tuple-element.41), kind=kOutput, calls=%fused_computation.11 | convolution fusion | flops 424820736 | bytes 2064384 | tf_op jit(solution)/shard_map/dcyj,icxj->idxy/dot_general | solution.py:101
  37.1 1.4 %convolution_bitcast_fusion.11 = f32[3,2,128,192,1]{2,3,1,4,0:T(8,128)S(1)} fusion(f32[3,1,160,192]{3,2,1,0:T(8,128)S(1)} %get-tuple-element.12, f32[3,1,160,192]{3,2,1,0:T(8,128)S(1)} %get-tuple-element.11, f32[1,2,192,192]{3,2,1,0:T(8,128)S(1)} %get-tuple-element.41, f32[1,2,192,192]{3,2,1,0:T(8,128)S(1)} %get-tuple-element.40), kind=kOutput, calls=%fused_computation.20 | convolution fusion | flops 283381760 | bytes 1916928 | tf_op jit(solution)/shard_map/dcab,icbj->idaj/dot_general | solution.py:98
  41.8 1.3 %collective-permute-start.6 = (f32[6,64,128]{2,1,0:T(8,128)S(1)}, f32[6,64,128]{2,1,0:T(8,128)S(1)}, u32[]{:S(2)}, u32[]{:S(2)}) collective-permute-start(f32[6,64,128]{2,1,0:T(8,128)S(1)} %bitcast.254), channel_id=1, source_target_pairs={{0,6},{4,10},{8,14},{1,7},{5,11},{9,15},{16,22},{20,26},{24,30},{1... | collective-permute-start | bytes 589832 | tf_op jit(solution)/shard_map/ppermute | solution.py:120
  43.1 1.3 %collective-permute-start.7 = (f32[6,64,128]{2,1,0:T(8,128)S(1)}, f32[6,64,128]{2,1,0:T(8,128)S(1)}, u32[]{:S(2)}, u32[]{:S(2)}) collective-permute-start(f32[6,64,128]{2,1,0:T(8,128)S(1)} %bitcast.255), channel_id=1, source_target_pairs={{0,2},{4,6},{8,10},{12,14},{1,3},{5,7},{9,11},{13,15},{16,18},{20,... | collective-permute-start | bytes 589832 | tf_op jit(solution)/shard_map/ppermute | solution.py:121
  44.4 1.5 %collective-permute-start.8 = (f32[6,64,128]{2,1,0:T(8,128)S(1)}, f32[6,64,128]{2,1,0:T(8,128)S(1)}, u32[]{:S(2)}, u32[]{:S(2)}) collective-permute-start(f32[6,64,128]{2,1,0:T(8,128)S(1)} %bitcast.256), channel_id=1, source_target_pairs={{4,2},{8,6},{12,10},{5,3},{9,7},{13,11},{20,18},{24,22},{28,26},{2... | collective-permute-start | bytes 589832 | tf_op jit(solution)/shard_map/ppermute | solution.py:122
  45.9 4.9 %collective-permute-done.6 = f32[6,64,128]{2,1,0:T(8,128)S(1)} collective-permute-done((f32[6,64,128]{2,1,0:T(8,128)S(1)}, f32[6,64,128]{2,1,0:T(8,128)S(1)}, u32[]{:S(2)}, u32[]{:S(2)}) %collective-permute-start.6) | collective-permute-done | bytes 196640 | tf_op jit(solution)/shard_map/ppermute | solution.py:120
  50.8 9.1 %collective-permute-done.7 = f32[6,64,128]{2,1,0:T(8,128)S(1)} collective-permute-done((f32[6,64,128]{2,1,0:T(8,128)S(1)}, f32[6,64,128]{2,1,0:T(8,128)S(1)}, u32[]{:S(2)}, u32[]{:S(2)}) %collective-permute-start.7) | collective-permute-done | bytes 196640 | tf_op jit(solution)/shard_map/ppermute | solution.py:121
  60.5 1.6 %collective-permute-done.9 = f32[6,192,128]{2,1,0:T(8,128)S(1)} collective-permute-done((f32[6,192,128]{2,1,0:T(8,128)S(1)}, f32[6,192,128]{2,1,0:T(8,128)S(1)}, u32[]{:S(2)}, u32[]{:S(2)}) %collective-permute-start.9) | collective-permute-done | bytes 589856 | tf_op jit(solution)/shard_map/ppermute | solution.py:53
  62.9 1.0 %convolution_bitcast_fusion.1 = f32[3,2,160,192,1]{3,2,1,4,0:T(8,128)S(1)} fusion(f32[3,1,192,192]{3,2,1,0:T(8,128)S(1)} %get-tuple-element.6, f32[3,1,192,192]{3,2,1,0:T(8,128)S(1)} %get-tuple-element.5, f32[1,2,192,192]{3,2,1,0:T(8,128)S(1)} %get-tuple-element.41, f32[1,2,192,192]{3,2,1,0:T(8,128)S(1)} %get-tuple-element.40), kind=kOutput, calls=%fused_computation.10 | convolution fusion | flops 425017344 | bytes 2211840 | tf_op jit(solution)/shard_map/dcab,icbj->idaj/dot_general | solution.py:98
  63.9 0.9 %convolution_bitcast_fusion = f32[3,2,160,192]{3,2,1,0:T(8,128)S(1)} fusion(f32[3,2,160,192,1]{3,2,1,4,0:T(8,128)S(1)} %convolution_bitcast_fusion.1, f32[1,2,192,192]{3,2,1,0:T(8,128)S(1)} %get-tuple-element.40, f32[1,2,192,192]{3,2,1,0:T(8,128)S(1)} %get-tuple-element.41), kind=kOutput, calls=%fused_computation.9 | convolution fusion | flops 424820736 | bytes 2064384 | tf_op jit(solution)/shard_map/dcyj,icxj->idxy/dot_general | solution.py:101
  65.0 1.4 %convolution_bitcast_fusion.7 = f32[3,2,128,192,1]{2,3,1,4,0:T(8,128)S(1)} fusion(f32[3,1,160,192]{3,2,1,0:T(8,128)S(1)} %get-tuple-element.10, f32[3,1,160,192]{3,2,1,0:T(8,128)S(1)} %get-tuple-element.9, f32[1,2,192,192]{3,2,1,0:T(8,128)S(1)} %get-tuple-element.41, f32[1,2,192,192]{3,2,1,0:T(8,128)S(1)} %get-tuple-element.40), kind=kOutput, calls=%fused_computation.16 | convolution fusion | flops 283381760 | bytes 1916928 | tf_op jit(solution)/shard_map/dcab,icbj->idaj/dot_general | solution.py:98
  66.4 0.8 %convolution_bitcast_fusion.6 = f32[3,2,128,192]{2,3,1,0:T(8,128)S(1)} fusion(f32[3,2,128,192,1]{2,3,1,4,0:T(8,128)S(1)} %convolution_bitcast_fusion.7, f32[1,2,192,192]{3,2,1,0:T(8,128)S(1)} %get-tuple-element.40, f32[1,2,192,192]{3,2,1,0:T(8,128)S(1)} %get-tuple-element.41), kind=kOutput, calls=%fused_computation.15 | convolution fusion | flops 339886080 | bytes 1769472 | tf_op jit(solution)/shard_map/dcyj,icxj->idxy/dot_general | solution.py:101
  69.7 0.9 %fusion.25 = f32[1,3,2,64,128]{4,3,2,1,0:T(8,128)} fusion(f32[3,64,2,192]{3,1,2,0:T(8,128)S(1)} %convolution_bitcast_fusion.12, s32[]{:T(128)S(6)} %select_n.51, pred[]{:T(512)S(6)} %eq.14, pred[]{:T(512)S(6)} %eq.12, f32[3,64,2,192]{3,1,2,0:T(8,128)S(1)} %convolution_bitcast_fusion.14), kind=kLoop, calls=%fused_computation.86 | loop fusion | flops 98304 | bytes 589830 | tf_op jit(solution)/shard_map/broadcast_in_dim | solution.py:126
  (91 shorter events, 12.8 us)
Async XLA Ops:
  0.0 13.0 %copy-start.19 = (f32[2,33]{1,0:T(2,128)S(1)}, f32[2,33]{1,0:T(2,128)}, u32[]{:S(2)}) copy-start(f32[2,33]{1,0:T(2,128)} %param.7) | copy-start | bytes 796
  2.3 20.8 %collective-permute-start = (f32[8,64,128]{2,1,0:T(8,128)S(1)}, f32[8,64,128]{2,1,0:T(8,128)S(1)}, u32[]{:S(2)}, u32[]{:S(2)}) collective-permute-start(f32[8,64,128]{2,1,0:T(8,128)S(1)} %pad_maximum_fusion.3), channel_id=1, source_target_pairs={{0,4},{4,8},{8,12},{1,5},{5,9},{9,13},{2,6},{6,10},{10,14},{3,7},{... | collective-permute-start | bytes 786440 | tf_op jit(solution)/shard_map/ppermute | solution.py:44
  5.6 17.6 %collective-permute-start.1 = (f32[8,64,128]{2,1,0:T(8,128)S(1)}, f32[8,64,128]{2,1,0:T(8,128)}, u32[]{:S(2)}, u32[]{:S(2)}) collective-permute-start(f32[8,64,128]{2,1,0:T(8,128)S(1)} %pad_maximum_fusion.3), channel_id=1, source_target_pairs={{4,0},{8,4},{12,8},{5,1},{9,5},{13,9},{6,2},{10,6},{14,10},{7,3},{... | collective-permute-start | bytes 786440 | tf_op jit(solution)/shard_map/ppermute | solution.py:45
  7.7 11.7 %copy-start.1 = (f32[3,2,64,128]{3,2,1,0:T(8,128)}, f32[3,2,64,128]{3,2,1,0:T(8,128)S(1)}, u32[]{:S(2)}) copy-start(f32[3,2,64,128]{3,2,1,0:T(8,128)S(1)} %pad_maximum_fusion.4) | copy-start | bytes 589828
  7.7 7.7 %collective-permute-start.3 = (f32[6,64,128]{2,1,0:T(8,128)S(1)}, f32[6,64,128]{2,1,0:T(8,128)S(1)}, u32[]{:S(2)}, u32[]{:S(2)}) collective-permute-start(f32[6,64,128]{2,1,0:T(8,128)S(1)} %bitcast.246), channel_id=1, source_target_pairs={{0,4},{4,8},{8,12},{1,5},{5,9},{9,13},{2,6},{6,10},{10,14},{3,7},{... | collective-permute-start | bytes 589832 | tf_op jit(solution)/shard_map/ppermute | solution.py:44
  10.9 7.6 %collective-permute-start.4 = (f32[6,64,128]{2,1,0:T(8,128)S(1)}, f32[6,64,128]{2,1,0:T(8,128)S(1)}, u32[]{:S(2)}, u32[]{:S(2)}) collective-permute-start(f32[6,64,128]{2,1,0:T(8,128)S(1)} %bitcast.247), channel_id=1, source_target_pairs={{4,0},{8,4},{12,8},{5,1},{9,5},{13,9},{6,2},{10,6},{14,10},{7,3},{... | collective-permute-start | bytes 589832 | tf_op jit(solution)/shard_map/ppermute | solution.py:45
  15.4 4.0 %copy-start.13 = (f32[6,64,128]{2,1,0:T(8,128)}, f32[6,64,128]{2,1,0:T(8,128)S(1)}, u32[]{:S(2)}) copy-start(f32[6,64,128]{2,1,0:T(8,128)S(1)} %collective-permute-done.3) | copy-start | bytes 589828
  18.5 0.9 %copy-start.15 = (f32[6,64,128]{2,1,0:T(8,128)}, f32[6,64,128]{2,1,0:T(8,128)S(1)}, u32[]{:S(2)}) copy-start(f32[6,64,128]{2,1,0:T(8,128)S(1)} %collective-permute-done.4) | copy-start | bytes 589828
  19.4 7.2 %collective-permute-start.5 = (f32[6,192,128]{2,1,0:T(8,128)}, f32[6,192,128]{2,1,0:T(8,128)S(1)}, u32[]{:S(2)}, u32[]{:S(2)}) collective-permute-start(f32[6,192,128]{2,1,0:T(8,128)} %pad_maximum_fusion.2), channel_id=1, source_target_pairs={{0,1},{1,0},{2,3},{3,2},{4,5},{5,4},{6,7},{7,6},{8,9},{9,8},{10,11... | collective-permute-start | bytes 1769480 | tf_op jit(solution)/shard_map/ppermute | solution.py:53
  23.0 0.9 %copy-start.18 = (f32[3,2,64,128]{3,2,1,0:T(8,128)S(1)}, f32[3,2,64,128]{3,2,1,0:T(8,128)}, u32[]{:S(2)}) copy-start(f32[3,2,64,128]{3,2,1,0:T(8,128)} %param.4) | copy-start | bytes 589828
  25.0 7.3 %collective-permute-start.2 = (f32[8,192,128]{2,1,0:T(8,128)S(1)}, f32[8,192,128]{2,1,0:T(8,128)S(1)}, u32[]{:S(2)}, u32[]{:S(2)}) collective-permute-start(f32[8,192,128]{2,1,0:T(8,128)S(1)} %pad_maximum_fusion.1), channel_id=1, source_target_pairs={{0,1},{1,0},{2,3},{3,2},{4,5},{5,4},{6,7},{7,6},{8,9},{9,8},{10,11... | collective-permute-start | bytes 2359304 | tf_op jit(solution)/shard_map/ppermute | solution.py:53
  26.6 0.9 %copy-start.2 = (f32[3,2,64,128]{3,2,1,0:T(8,128)S(1)}, f32[3,2,64,128]{3,2,1,0:T(8,128)}, u32[]{:S(2)}) copy-start(f32[3,2,64,128]{3,2,1,0:T(8,128)} %copy-done.1) | copy-start | bytes 589828
  26.6 1.0 %copy-start.14 = (f32[6,64,128]{2,1,0:T(8,128)S(1)}, f32[6,64,128]{2,1,0:T(8,128)}, u32[]{:S(2)}) copy-start(f32[6,64,128]{2,1,0:T(8,128)} %copy-done.13) | copy-start | bytes 589828
  26.6 1.1 %copy-start.16 = (f32[6,64,128]{2,1,0:T(8,128)S(1)}, f32[6,64,128]{2,1,0:T(8,128)}, u32[]{:S(2)}) copy-start(f32[6,64,128]{2,1,0:T(8,128)} %copy-done.15) | copy-start | bytes 589828
  32.2 1.1 %copy-start.17 = (f32[2,192,128]{2,1,0:T(8,128)S(1)}, f32[2,192,128]{2,1,0:T(8,128)}, u32[]{:S(2)}) copy-start(f32[2,192,128]{2,1,0:T(8,128)} %slice.235) | copy-start | bytes 589828
  32.2 8.5 %copy-start.9 = (f32[96,192]{1,0:T(8,128)}, f32[96,192]{1,0:T(8,128)S(1)}, u32[]{:S(2)}) copy-start(f32[96,192]{1,0:T(8,128)S(1)} %get-tuple-element.13) | copy-start | bytes 221188
  32.2 8.5 %copy-start.11 = (f32[96,192]{1,0:T(8,128)}, f32[96,192]{1,0:T(8,128)S(1)}, u32[]{:S(2)}) copy-start(f32[96,192]{1,0:T(8,128)S(1)} %get-tuple-element.14) | copy-start | bytes 221188
  32.2 4.7 %copy-start.3 = (f32[160,192]{1,0:T(8,128)}, f32[160,192]{1,0:T(8,128)S(1)}, u32[]{:S(2)}) copy-start(f32[160,192]{1,0:T(8,128)S(1)} %get-tuple-element.17) | copy-start | bytes 368644
  32.2 4.7 %copy-start.5 = (f32[160,192]{1,0:T(8,128)}, f32[160,192]{1,0:T(8,128)S(1)}, u32[]{:S(2)}) copy-start(f32[160,192]{1,0:T(8,128)S(1)} %get-tuple-element.18) | copy-start | bytes 368644
  33.4 1.1 %copy-start = (f32[6,192,128]{2,1,0:T(8,128)S(1)}, f32[6,192,128]{2,1,0:T(8,128)}, u32[]{:S(2)}) copy-start(f32[6,192,128]{2,1,0:T(8,128)} %slice.231) | copy-start | bytes 1769476
  38.5 0.9 %copy-start.7 = (f32[128,192]{0,1:T(8,128)S(1)}, f32[128,192]{0,1:T(8,128)}, u32[]{:S(2)}) copy-start(f32[128,192]{0,1:T(8,128)} %copy.16) | copy-start | bytes 294916
  38.6 0.9 %copy-start.8 = (f32[128,192]{0,1:T(8,128)S(1)}, f32[128,192]{0,1:T(8,128)}, u32[]{:S(2)}) copy-start(f32[128,192]{0,1:T(8,128)} %copy.17) | copy-start | bytes 294916
  41.8 9.0 %collective-permute-start.6 = (f32[6,64,128]{2,1,0:T(8,128)S(1)}, f32[6,64,128]{2,1,0:T(8,128)S(1)}, u32[]{:S(2)}, u32[]{:S(2)}) collective-permute-start(f32[6,64,128]{2,1,0:T(8,128)S(1)} %bitcast.254), channel_id=1, source_target_pairs={{0,6},{4,10},{8,14},{1,7},{5,11},{9,15},{16,22},{20,26},{24,30},{1... | collective-permute-start | bytes 589832 | tf_op jit(solution)/shard_map/ppermute | solution.py:120
  43.1 16.7 %collective-permute-start.7 = (f32[6,64,128]{2,1,0:T(8,128)S(1)}, f32[6,64,128]{2,1,0:T(8,128)S(1)}, u32[]{:S(2)}, u32[]{:S(2)}) collective-permute-start(f32[6,64,128]{2,1,0:T(8,128)S(1)} %bitcast.255), channel_id=1, source_target_pairs={{0,2},{4,6},{8,10},{12,14},{1,3},{5,7},{9,11},{13,15},{16,18},{20,... | collective-permute-start | bytes 589832 | tf_op jit(solution)/shard_map/ppermute | solution.py:121
  44.4 15.5 %collective-permute-start.8 = (f32[6,64,128]{2,1,0:T(8,128)S(1)}, f32[6,64,128]{2,1,0:T(8,128)S(1)}, u32[]{:S(2)}, u32[]{:S(2)}) collective-permute-start(f32[6,64,128]{2,1,0:T(8,128)S(1)} %bitcast.256), channel_id=1, source_target_pairs={{4,2},{8,6},{12,10},{5,3},{9,7},{13,11},{20,18},{24,22},{28,26},{2... | collective-permute-start | bytes 589832 | tf_op jit(solution)/shard_map/ppermute | solution.py:122
  59.9 2.2 %collective-permute-start.9 = (f32[6,192,128]{2,1,0:T(8,128)S(1)}, f32[6,192,128]{2,1,0:T(8,128)S(1)}, u32[]{:S(2)}, u32[]{:S(2)}) collective-permute-start(f32[6,192,128]{2,1,0:T(8,128)S(1)} %constant_dynamic-update-slice_fusion), channel_id=1, source_target_pairs={{0,1},{1,0},{2,3},{3,2},{4,5},{5,4},{6,7},{7,6},{8,9},{9,8},{10,11... | collective-permute-start | bytes 1769480 | tf_op jit(solution)/shard_map/ppermute | solution.py:53
  63.9 1.0 %copy-start.4 = (f32[160,192]{1,0:T(8,128)S(1)}, f32[160,192]{1,0:T(8,128)}, u32[]{:S(2)}) copy-start(f32[160,192]{1,0:T(8,128)} %copy-done.3) | copy-start | bytes 368644
  63.9 1.0 %copy-start.6 = (f32[160,192]{1,0:T(8,128)S(1)}, f32[160,192]{1,0:T(8,128)}, u32[]{:S(2)}) copy-start(f32[160,192]{1,0:T(8,128)} %copy-done.5) | copy-start | bytes 368644
  67.7 0.9 %copy-start.10 = (f32[96,192]{1,0:T(8,128)S(1)}, f32[96,192]{1,0:T(8,128)}, u32[]{:S(2)}) copy-start(f32[96,192]{1,0:T(8,128)} %copy-done.9) | copy-start | bytes 221188
  67.7 0.9 %copy-start.12 = (f32[96,192]{1,0:T(8,128)S(1)}, f32[96,192]{1,0:T(8,128)}, u32[]{:S(2)}) copy-start(f32[96,192]{1,0:T(8,128)} %copy-done.11) | copy-start | bytes 221188

commit v7 on v5

--- a/solution.py
+++ b/solution.py
@@ -37,14 +37,15 @@
     )
 
 
-def grow(stack, halo, splits):
+def grow(stack, halo, splits, rider):
     tiles = lax.axis_size("tile")
     wave = lax.axis_index("wave")
     rows, cols = stack.shape[-2], stack.shape[-1]
     from_prev = lax.ppermute(stack[:, rows - halo:], "tile", [(i, i + 1) for i in range(tiles - 1)])
     from_next = lax.ppermute(stack[:, :halo], "tile", [(i + 1, i) for i in range(tiles - 1)])
     tall = jnp.concatenate([from_prev, stack, from_next], axis=-2)
-    return widen(tall, halo, splits)
+    rider, tall = lax.optimization_barrier((rider, tall))
+    return widen(tall, halo, splits), rider
 
 
 def widen(tall, halo, splits):
@@ -73,17 +74,17 @@
 
     trans_own = transmission(phase_shift, absorption)
     illum = incident.shape[0]
-    field_grown, trans_grown = grow(
+    width = cols + reach
+    tall = rows + 2 * reach
+    band = toeplitz(kernel, max(tall, width), HALF)
+    (field_grown, trans_grown), band = grow(
         jnp.concatenate([incident.reshape(2 * illum, rows, cols), trans_own.reshape(2 * slices, rows, cols)]),
         reach,
         (2 * illum, 2 * slices),
+        band,
     )
     first_field = field_grown.reshape(illum, 2, rows + 2 * reach, cols + reach)
     trans_reg = trans_grown.reshape(slices, 2, rows + 2 * reach, cols + reach)
-    width = cols + reach
-    tall = rows + 2 * reach
-
-    band = toeplitz(kernel, max(tall, width), HALF)
     col_band = band[:, :, :width, :width]
     row_bands = [
         band[:, :, HALF * (s + 1): tall - HALF * (s + 1), HALF * s: tall - HALF * s]

time: 62.5 us -> 61.1 us (0.978)
  local copies, waits for them, and re-layouts: 3.9 us -> 2.79 us
    ppermute x1, waiting for transfers between devices: 7.98 us -> 4.95 us  [grow(): lax.ppermute(stack[:, :halo], 'tile', [(i + 1, i) for i in range(tiles -...]
    ppermute x2, waiting for transfers between devices: 1.63 us -> 4.28 us  [widen(): got = lax.ppermute(tall, 'wave', [(0, 1), (1, 0)])]
    concatenate x1, other arithmetic: 0.12 us -> 1.26 us  [grow(): tall = jnp.concatenate([from_prev, stack, from_next], axis=-2)]
    slice x1 -> x0, other arithmetic: 1.06 us -> none  [toeplitz(): band_real, band_imag = (bands[0], bands[1])]
    reshape x1, local copies, waits for them, and re-layouts: 1.68 us -> 0.83 us  [toeplitz(): bands = rolled.reshape(2, size, period - 1)[:, :, :size]]
  transfers between devices with their start and end apart: 7 -> 7, of which waited for: 5 -> 6; matrix products, arithmetic and copies ran while one was open for 7% -> 4% of each run, Pallas kernels for 0% -> 0%
where the time goes in v7:
time: 61.1 us; the launch traced here: 60.8 us
  waiting for transfers between devices  25 us (41%)
  matrix products  12.3 us (20%)
  starting transfers between devices  11.8 us (19%)
  other arithmetic  7.8 us (13%)
  local copies, waits for them, and re-layouts  2.79 us (5%)
  between operations  1.2 us (2%)
    ppermute x1, waiting for transfers between devices, per_device(): mine = lax.ppermute(flat, grid, own_pairs)  9.09 us
    dot_general x8, matrix products, depth_section(): jnp.einsum('dcab,icbj->idaj', row_bands[s], moved, precision=lax.Precisio...  6.53 us
    dot_general x8, matrix products, depth_section(): jnp.einsum('dcyj,icxj->idxy', col_band, rows_done, precision=lax.Precisio...  5.72 us
    ppermute x1, waiting for transfers between devices, grow(): lax.ppermute(stack[:, :halo], 'tile', [(i + 1, i) for i in range(tiles -...  4.95 us
    ppermute x1, waiting for transfers between devices, per_device(): from_prev = lax.ppermute(flat[:, rows - reach:], grid, prev_pairs)  4.87 us
    ppermute x2, waiting for transfers between devices, widen(): got = lax.ppermute(tall, 'wave', [(0, 1), (1, 0)])  4.28 us
    ppermute x1, starting transfers between devices, grow(): lax.ppermute(stack[:, rows - halo:], 'tile', [(i, i + 1) for i in range(t...  3.21 us
    ppermute x2, starting transfers between devices, widen(): got = lax.ppermute(tall, 'wave', [(0, 1), (1, 0)])  2.47 us
  transfers between devices with their start and end apart: 7, of which 6 were waited for; matrix products, arithmetic and copies ran while one was open for 4% of the time, Pallas kernels for 0%

profile of v7, /device:TPU:15, one launch (start us, length us, event | category | flops | bytes accessed | tf_op | source)
XLA Modules:
  0.0 60.8 jit_solution(13167299191500990239)
XLA Ops:
  0.0 1.4 %fusion.38 = (f32[4,1,64,128]{3,2,1,0:T(8,128)S(1)}, f32[4,1,64,128]{3,2,1,0:T(8,128)S(1)}) fusion(bf16[4,64,128]{2,1,0:T(8,128)(2,1)} %param.5, bf16[4,64,128]{2,1,0:T(8,128)(2,1)} %param.6), kind=kLoop, calls=%fused_computation.97 | loop fusion | flops 163840 | bytes 393216 | tf_op jit(solution)/shard_map/stack | solution.py:25
  1.4 1.0 %pad_maximum_fusion.2 = f32[14,64,128]{2,1,0:T(8,128)S(1)} fusion(f32[8,64,128]{2,1,0:T(8,128)S(1)} %bitcast.254, f32[6,64,128]{2,1,0:T(8,128)} %bitcast.258), kind=kLoop, calls=%fused_computation.70 | loop fusion | flops 114688 | bytes 917504 | tf_op jit(solution)/shard_map/concatenate | solution.py:81
  2.4 2.1 %collective-permute-start.1 = (f32[14,64,128]{2,1,0:T(8,128)S(1)}, f32[14,64,128]{2,1,0:T(8,128)}, u32[]{:S(2)}, u32[]{:S(2)}) collective-permute-start(f32[14,64,128]{2,1,0:T(8,128)S(1)} %pad_maximum_fusion.2), channel_id=1, source_target_pairs={{4,0},{8,4},{12,8},{5,1},{9,5},{13,9},{6,2},{10,6},{14,10},{7,3},{... | collective-permute-start | bytes 1376264 | tf_op jit(solution)/shard_map/ppermute | solution.py:45
  4.5 3.2 %collective-permute-start = (f32[14,64,128]{2,1,0:T(8,128)S(1)}, f32[14,64,128]{2,1,0:T(8,128)}, u32[]{:S(2)}, u32[]{:S(2)}) collective-permute-start(f32[14,64,128]{2,1,0:T(8,128)S(1)} %pad_maximum_fusion.2), channel_id=1, source_target_pairs={{0,4},{4,8},{8,12},{1,5},{5,9},{9,13},{2,6},{6,10},{10,14},{3,7},{... | collective-permute-start | bytes 1376264 | tf_op jit(solution)/shard_map/ppermute | solution.py:44
  7.7 0.6 multiply_reduce_fusion
  9.8 0.8 %reshape.46 = f32[2,192,383]{2,1,0:T(8,128)S(1)} reshape(f32[2,73536]{1,0:T(2,128)S(1)} %slice.221) | data formatting | bytes 1176576 | tf_op jit(solution)/shard_map/reshape | solution.py:15
  10.8 4.9 %collective-permute-done.1 = f32[14,64,128]{2,1,0:T(8,128)} collective-permute-done((f32[14,64,128]{2,1,0:T(8,128)S(1)}, f32[14,64,128]{2,1,0:T(8,128)}, u32[]{:S(2)}, u32[]{:S(2)}) %collective-permute-start.1) | collective-permute-done | bytes 458784 | tf_op jit(solution)/shard_map/ppermute | solution.py:45
  15.8 1.8 %collective-permute-done = f32[14,64,128]{2,1,0:T(8,128)} collective-permute-done((f32[14,64,128]{2,1,0:T(8,128)S(1)}, f32[14,64,128]{2,1,0:T(8,128)}, u32[]{:S(2)}, u32[]{:S(2)}) %collective-permute-start) | collective-permute-done | bytes 458784 | tf_op jit(solution)/shard_map/ppermute | solution.py:44
  17.5 1.3 %pad_maximum_fusion = f32[14,192,128]{2,1,0:T(8,128)S(1)} fusion(f32[14,64,128]{2,1,0:T(8,128)} %collective-permute-done.1, f32[8,64,128]{2,1,0:T(8,128)S(1)} %bitcast.255, f32[6,64,128]{2,1,0:T(8,128)S(1)} %bitcast.259, f32[14,64,128]{2,1,0:T(8,128)} %collective-permute-done), kind=kLoop, calls=%fused_computation.2 | loop fusion | flops 1032192 | bytes 2752512 | tf_op jit(solution)/shard_map/concatenate | solution.py:46
  18.8 1.9 %collective-permute-start.2 = (f32[14,192,128]{2,1,0:T(8,128)S(1)}, f32[14,192,128]{2,1,0:T(8,128)S(1)}, u32[]{:S(2)}, u32[]{:S(2)}) collective-permute-start(f32[14,192,128]{2,1,0:T(8,128)S(1)} %pad_maximum_fusion), channel_id=1, source_target_pairs={{0,1},{1,0},{2,3},{3,2},{4,5},{5,4},{6,7},{7,6},{8,9},{9,8},{10,11... | collective-permute-start | bytes 4128776 | tf_op jit(solution)/shard_map/ppermute | solution.py:54
  20.8 2.7 %collective-permute-done.2 = f32[14,192,128]{2,1,0:T(8,128)S(1)} collective-permute-done((f32[14,192,128]{2,1,0:T(8,128)S(1)}, f32[14,192,128]{2,1,0:T(8,128)S(1)}, u32[]{:S(2)}, u32[]{:S(2)}) %collective-permute-start.2) | collective-permute-done | bytes 1376288 | tf_op jit(solution)/shard_map/ppermute | solution.py:54
  23.8 0.5 maximum_select_fusion
  25.6 1.0 %convolution_bitcast_fusion.3 = f32[3,2,160,192,1]{3,2,1,4,0:T(8,128)S(1)} fusion(f32[3,1,192,192]{3,2,1,0:T(8,128)S(1)} %get-tuple-element.18, f32[3,1,192,192]{3,2,1,0:T(8,128)S(1)} %get-tuple-element.17, f32[2,2,192,192]{3,2,1,0:T(8,128)S(1)} %pad_maximum_fusion.1), kind=kOutput, calls=%fused_computation.6 | convolution fusion | flops 424894464 | bytes 2572288 | tf_op jit(solution)/shard_map/dcab,icbj->idaj/dot_general | solution.py:98
  26.6 1.0 %convolution_bitcast_fusion.2 = f32[3,2,160,192]{3,2,1,0:T(8,128)S(1)} fusion(f32[3,2,160,192,1]{3,2,1,4,0:T(8,128)S(1)} %convolution_bitcast_fusion.3, f32[2,2,192,192]{3,2,1,0:T(8,128)S(1)} %pad_maximum_fusion.1), kind=kOutput, calls=%fused_computation.5 | convolution fusion | flops 424673280 | bytes 2064384 | tf_op jit(solution)/shard_map/dcyj,icxj->idxy/dot_general | solution.py:101
  27.7 1.4 %convolution_bitcast_fusion.11 = f32[3,2,128,192,1]{2,3,1,4,0:T(8,128)S(1)} fusion(f32[3,1,160,192]{3,2,1,0:T(8,128)S(1)} %get-tuple-element.28, f32[3,1,160,192]{3,2,1,0:T(8,128)S(1)} %get-tuple-element.27, f32[2,2,192,192]{3,2,1,0:T(8,128)S(1)} %pad_maximum_fusion.1), kind=kOutput, calls=%fused_computation.14 | convolution fusion | flops 283299840 | bytes 2097152 | tf_op jit(solution)/shard_map/dcab,icbj->idaj/dot_general | solution.py:98
  29.1 0.8 %convolution_bitcast_fusion.10 = f32[3,2,128,192]{2,3,1,0:T(8,128)S(1)} fusion(f32[3,2,128,192,1]{2,3,1,4,0:T(8,128)S(1)} %convolution_bitcast_fusion.11, f32[2,2,192,192]{3,2,1,0:T(8,128)S(1)} %pad_maximum_fusion.1), kind=kOutput, calls=%fused_computation.13 | convolution fusion | flops 339738624 | bytes 1769472 | tf_op jit(solution)/shard_map/dcyj,icxj->idxy/dot_general | solution.py:101
  30.6 0.7 %convolution_bitcast_fusion.8 = f32[3,2,96,192]{3,2,1,0:T(8,128)S(1)} fusion(f32[3,2,96,192,1]{3,2,1,4,0:T(8,128)S(1)} %convolution_bitcast_fusion.9, f32[2,2,192,192]{3,2,1,0:T(8,128)S(1)} %pad_maximum_fusion.1), kind=kOutput, calls=%fused_computation.11 | convolution fusion | flops 254803968 | bytes 1474560 | tf_op jit(solution)/shard_map/dcyj,icxj->idxy/dot_general | solution.py:101
  31.8 0.5 convolution_bitcast_fusion.14
  32.4 1.3 %collective-permute-start.3 = (f32[6,64,128]{2,1,0:T(8,128)S(1)}, f32[6,64,128]{2,1,0:T(8,128)S(1)}, u32[]{:S(2)}, u32[]{:S(2)}) collective-permute-start(f32[6,64,128]{2,1,0:T(8,128)S(1)} %bitcast.260), channel_id=1, source_target_pairs={{0,6},{4,10},{8,14},{1,7},{5,11},{9,15},{16,22},{20,26},{24,30},{1... | collective-permute-start | bytes 589832 | tf_op jit(solution)/shard_map/ppermute | solution.py:120
  33.7 1.3 %collective-permute-start.4 = (f32[6,64,128]{2,1,0:T(8,128)S(1)}, f32[6,64,128]{2,1,0:T(8,128)S(1)}, u32[]{:S(2)}, u32[]{:S(2)}) collective-permute-start(f32[6,64,128]{2,1,0:T(8,128)S(1)} %bitcast.261), channel_id=1, source_target_pairs={{0,2},{4,6},{8,10},{12,14},{1,3},{5,7},{9,11},{13,15},{16,18},{20,... | collective-permute-start | bytes 589832 | tf_op jit(solution)/shard_map/ppermute | solution.py:121
  35.0 1.5 %collective-permute-start.5 = (f32[6,64,128]{2,1,0:T(8,128)S(1)}, f32[6,64,128]{2,1,0:T(8,128)S(1)}, u32[]{:S(2)}, u32[]{:S(2)}) collective-permute-start(f32[6,64,128]{2,1,0:T(8,128)S(1)} %bitcast.262), channel_id=1, source_target_pairs={{4,2},{8,6},{12,10},{5,3},{9,7},{13,11},{20,18},{24,22},{28,26},{2... | collective-permute-start | bytes 589832 | tf_op jit(solution)/shard_map/ppermute | solution.py:122
  36.5 4.9 %collective-permute-done.3 = f32[6,64,128]{2,1,0:T(8,128)S(1)} collective-permute-done((f32[6,64,128]{2,1,0:T(8,128)S(1)}, f32[6,64,128]{2,1,0:T(8,128)S(1)}, u32[]{:S(2)}, u32[]{:S(2)}) %collective-permute-start.3) | collective-permute-done | bytes 196640 | tf_op jit(solution)/shard_map/ppermute | solution.py:120
  41.4 9.1 %collective-permute-done.4 = f32[6,64,128]{2,1,0:T(8,128)S(1)} collective-permute-done((f32[6,64,128]{2,1,0:T(8,128)S(1)}, f32[6,64,128]{2,1,0:T(8,128)S(1)}, u32[]{:S(2)}, u32[]{:S(2)}) %collective-permute-start.4) | collective-permute-done | bytes 196640 | tf_op jit(solution)/shard_map/ppermute | solution.py:121
  50.5 0.5 collective-permute-start.6
  51.1 1.6 %collective-permute-done.6 = f32[6,192,128]{2,1,0:T(8,128)S(1)} collective-permute-done((f32[6,192,128]{2,1,0:T(8,128)S(1)}, f32[6,192,128]{2,1,0:T(8,128)S(1)}, u32[]{:S(2)}, u32[]{:S(2)}) %collective-permute-start.6) | collective-permute-done | bytes 589856 | tf_op jit(solution)/shard_map/ppermute | solution.py:54
  53.5 1.0 %convolution_bitcast_fusion.1 = f32[3,2,160,192,1]{3,2,1,4,0:T(8,128)S(1)} fusion(f32[3,1,192,192]{3,2,1,0:T(8,128)S(1)} %get-tuple-element.10, f32[3,1,192,192]{3,2,1,0:T(8,128)S(1)} %get-tuple-element.9, f32[2,2,192,192]{3,2,1,0:T(8,128)S(1)} %pad_maximum_fusion.1), kind=kOutput, calls=%fused_computation.4 | convolution fusion | flops 424894464 | bytes 2572288 | tf_op jit(solution)/shard_map/dcab,icbj->idaj/dot_general | solution.py:98
  54.4 1.0 %convolution_bitcast_fusion = f32[3,2,160,192]{3,2,1,0:T(8,128)S(1)} fusion(f32[3,2,160,192,1]{3,2,1,4,0:T(8,128)S(1)} %convolution_bitcast_fusion.1, f32[2,2,192,192]{3,2,1,0:T(8,128)S(1)} %pad_maximum_fusion.1), kind=kOutput, calls=%fused_computation.3 | convolution fusion | flops 424673280 | bytes 2064384 | tf_op jit(solution)/shard_map/dcyj,icxj->idxy/dot_general | solution.py:101
  55.5 1.4 %convolution_bitcast_fusion.7 = f32[3,2,128,192,1]{2,3,1,4,0:T(8,128)S(1)} fusion(f32[3,1,160,192]{3,2,1,0:T(8,128)S(1)} %get-tuple-element.26, f32[3,1,160,192]{3,2,1,0:T(8,128)S(1)} %get-tuple-element.25, f32[2,2,192,192]{3,2,1,0:T(8,128)S(1)} %pad_maximum_fusion.1), kind=kOutput, calls=%fused_computation.10 | convolution fusion | flops 283299840 | bytes 2097152 | tf_op jit(solution)/shard_map/dcab,icbj->idaj/dot_general | solution.py:98
  57.0 0.8 %convolution_bitcast_fusion.6 = f32[3,2,128,192]{2,3,1,0:T(8,128)S(1)} fusion(f32[3,2,128,192,1]{2,3,1,4,0:T(8,128)S(1)} %convolution_bitcast_fusion.7, f32[2,2,192,192]{3,2,1,0:T(8,128)S(1)} %pad_maximum_fusion.1), kind=kOutput, calls=%fused_computation.9 | convolution fusion | flops 339738624 | bytes 1769472 | tf_op jit(solution)/shard_map/dcyj,icxj->idxy/dot_general | solution.py:101
  58.3 0.7 %convolution_bitcast_fusion.4 = f32[3,2,96,192]{3,2,1,0:T(8,128)S(1)} fusion(f32[3,2,96,192,1]{3,2,1,4,0:T(8,128)S(1)} %convolution_bitcast_fusion.5, f32[2,2,192,192]{3,2,1,0:T(8,128)S(1)} %pad_maximum_fusion.1), kind=kOutput, calls=%fused_computation.7 | convolution fusion | flops 254803968 | bytes 1474560 | tf_op jit(solution)/shard_map/dcyj,icxj->idxy/dot_general | solution.py:101
  59.5 0.5 convolution_bitcast_fusion.12
  60.0 0.9 %fusion.32 = f32[1,3,2,64,128]{4,3,2,1,0:T(8,128)} fusion(f32[3,64,2,192]{3,1,2,0:T(8,128)S(1)} %convolution_bitcast_fusion.12, s32[]{:T(128)S(6)} %select_n.52, pred[]{:T(512)S(6)} %eq.13, pred[]{:T(512)S(6)} %eq.11, f32[3,64,2,192]{3,1,2,0:T(8,128)S(1)} %convolution_bitcast_fusion.14), kind=kLoop, calls=%fused_computation.86 | loop fusion | flops 98304 | bytes 589830 | tf_op jit(solution)/shard_map/broadcast_in_dim | solution.py:126
  (55 shorter events, 6.0 us)
Async XLA Ops:
  0.0 7.7 %copy-start.5 = (f32[2,33]{1,0:T(2,128)S(1)}, f32[2,33]{1,0:T(2,128)}, u32[]{:S(2)}) copy-start(f32[2,33]{1,0:T(2,128)} %param.7) | copy-start | bytes 796
  2.4 13.4 %collective-permute-start.1 = (f32[14,64,128]{2,1,0:T(8,128)S(1)}, f32[14,64,128]{2,1,0:T(8,128)}, u32[]{:S(2)}, u32[]{:S(2)}) collective-permute-start(f32[14,64,128]{2,1,0:T(8,128)S(1)} %pad_maximum_fusion.2), channel_id=1, source_target_pairs={{4,0},{8,4},{12,8},{5,1},{9,5},{13,9},{6,2},{10,6},{14,10},{7,3},{... | collective-permute-start | bytes 1376264 | tf_op jit(solution)/shard_map/ppermute | solution.py:45
  4.5 13.1 %collective-permute-start = (f32[14,64,128]{2,1,0:T(8,128)S(1)}, f32[14,64,128]{2,1,0:T(8,128)}, u32[]{:S(2)}, u32[]{:S(2)}) collective-permute-start(f32[14,64,128]{2,1,0:T(8,128)S(1)} %pad_maximum_fusion.2), channel_id=1, source_target_pairs={{0,4},{4,8},{8,12},{1,5},{5,9},{9,13},{2,6},{6,10},{10,14},{3,7},{... | collective-permute-start | bytes 1376264 | tf_op jit(solution)/shard_map/ppermute | solution.py:44
  10.7 6.9 %copy-start.4 = (f32[3,2,64,128]{3,2,1,0:T(8,128)S(1)}, f32[3,2,64,128]{3,2,1,0:T(8,128)}, u32[]{:S(2)}) copy-start(f32[3,2,64,128]{3,2,1,0:T(8,128)} %param.4) | copy-start | bytes 589828
  18.8 4.7 %collective-permute-start.2 = (f32[14,192,128]{2,1,0:T(8,128)S(1)}, f32[14,192,128]{2,1,0:T(8,128)S(1)}, u32[]{:S(2)}, u32[]{:S(2)}) collective-permute-start(f32[14,192,128]{2,1,0:T(8,128)S(1)} %pad_maximum_fusion), channel_id=1, source_target_pairs={{0,1},{1,0},{2,3},{3,2},{4,5},{5,4},{6,7},{7,6},{8,9},{9,8},{10,11... | collective-permute-start | bytes 4128776 | tf_op jit(solution)/shard_map/ppermute | solution.py:54
  24.8 6.4 %copy-start = (f32[96,192]{1,0:T(8,128)}, f32[96,192]{1,0:T(8,128)S(1)}, u32[]{:S(2)}) copy-start(f32[96,192]{1,0:T(8,128)S(1)} %get-tuple-element.11) | copy-start | bytes 221188
  24.8 6.4 %copy-start.2 = (f32[96,192]{1,0:T(8,128)}, f32[96,192]{1,0:T(8,128)S(1)}, u32[]{:S(2)}) copy-start(f32[96,192]{1,0:T(8,128)S(1)} %get-tuple-element.12) | copy-start | bytes 221188
  32.4 9.0 %collective-permute-start.3 = (f32[6,64,128]{2,1,0:T(8,128)S(1)}, f32[6,64,128]{2,1,0:T(8,128)S(1)}, u32[]{:S(2)}, u32[]{:S(2)}) collective-permute-start(f32[6,64,128]{2,1,0:T(8,128)S(1)} %bitcast.260), channel_id=1, source_target_pairs={{0,6},{4,10},{8,14},{1,7},{5,11},{9,15},{16,22},{20,26},{24,30},{1... | collective-permute-start | bytes 589832 | tf_op jit(solution)/shard_map/ppermute | solution.py:120
  33.7 16.8 %collective-permute-start.4 = (f32[6,64,128]{2,1,0:T(8,128)S(1)}, f32[6,64,128]{2,1,0:T(8,128)S(1)}, u32[]{:S(2)}, u32[]{:S(2)}) collective-permute-start(f32[6,64,128]{2,1,0:T(8,128)S(1)} %bitcast.261), channel_id=1, source_target_pairs={{0,2},{4,6},{8,10},{12,14},{1,3},{5,7},{9,11},{13,15},{16,18},{20,... | collective-permute-start | bytes 589832 | tf_op jit(solution)/shard_map/ppermute | solution.py:121
  35.0 15.5 %collective-permute-start.5 = (f32[6,64,128]{2,1,0:T(8,128)S(1)}, f32[6,64,128]{2,1,0:T(8,128)S(1)}, u32[]{:S(2)}, u32[]{:S(2)}) collective-permute-start(f32[6,64,128]{2,1,0:T(8,128)S(1)} %bitcast.262), channel_id=1, source_target_pairs={{4,2},{8,6},{12,10},{5,3},{9,7},{13,11},{20,18},{24,22},{28,26},{2... | collective-permute-start | bytes 589832 | tf_op jit(solution)/shard_map/ppermute | solution.py:122
  50.5 2.2 %collective-permute-start.6 = (f32[6,192,128]{2,1,0:T(8,128)S(1)}, f32[6,192,128]{2,1,0:T(8,128)S(1)}, u32[]{:S(2)}, u32[]{:S(2)}) collective-permute-start(f32[6,192,128]{2,1,0:T(8,128)S(1)} %constant_dynamic-update-slice_fusion), channel_id=1, source_target_pairs={{0,1},{1,0},{2,3},{3,2},{4,5},{5,4},{6,7},{7,6},{8,9},{9,8},{10,11... | collective-permute-start | bytes 1769480 | tf_op jit(solution)/shard_map/ppermute | solution.py:54
  57.8 1.1 %copy-start.1 = (f32[96,192]{1,0:T(8,128)S(1)}, f32[96,192]{1,0:T(8,128)}, u32[]{:S(2)}) copy-start(f32[96,192]{1,0:T(8,128)} %copy-done) | copy-start | bytes 221188
  57.8 1.1 %copy-start.3 = (f32[96,192]{1,0:T(8,128)S(1)}, f32[96,192]{1,0:T(8,128)}, u32[]{:S(2)}) copy-start(f32[96,192]{1,0:T(8,128)} %copy-done.2) | copy-start | bytes 221188

commit v8 on v7

--- a/solution.py
+++ b/solution.py
@@ -91,6 +91,8 @@
         for s in range(slices)
     ]
 
+    last_band = jnp.where(wave == 0, col_band[:, :, :cols], col_band[:, :, reach:reach + cols])
+
     def depth_section(field):
         current = field
         for s in range(slices):
@@ -99,9 +101,12 @@
                 "dcab,icbj->idaj", row_bands[s], moved, precision=lax.Precision.HIGH
             )
             current = jnp.einsum(
-                "dcyj,icxj->idxy", col_band, rows_done, precision=lax.Precision.HIGH
+                "dcyj,icxj->idxy",
+                last_band if s == slices - 1 else col_band,
+                rows_done,
+                precision=lax.Precision.HIGH,
             )
-        return lax.dynamic_slice_in_dim(current, reach * wave, cols, axis=-1)
+        return current
 
     exits = jnp.zeros(incident.shape, jnp.float32)
     tiles = lax.axis_size("tile")

time: 61.1 us -> 60.6 us (level)
  other arithmetic: 7.8 us -> 6.94 us
    broadcast_in_dim x1 -> x0, other arithmetic: 0.86 us -> none  [per_device(): return exits[None]]
where the time goes in v8:
time: 60.6 us; the launch traced here: 60.3 us
  waiting for transfers between devices  25 us (41%)
  matrix products  12.8 us (21%)
  starting transfers between devices  11.8 us (19%)
  other arithmetic  6.94 us (11%)
  local copies, waits for them, and re-layouts  2.65 us (4%)
  between operations  1.12 us (2%)
    ppermute x1, waiting for transfers between devices, per_device(): mine = lax.ppermute(flat, grid, own_pairs)  9.09 us
    dot_general x8, matrix products, depth_section(): jnp.einsum('dcab,icbj->idaj', row_bands[s], moved, precision=lax.Precisio...  6.54 us
    dot_general x8, matrix products, depth_section(): jnp.einsum('dcyj,icxj->idxy', last_band if s == slices - 1 else col_band,...  6.26 us
    ppermute x1, waiting for transfers between devices, grow(): lax.ppermute(stack[:, :halo], 'tile', [(i + 1, i) for i in range(tiles -...  4.95 us
    ppermute x1, waiting for transfers between devices, per_device(): from_prev = lax.ppermute(flat[:, rows - reach:], grid, prev_pairs)  4.87 us
    ppermute x2, waiting for transfers between devices, widen(): got = lax.ppermute(tall, 'wave', [(0, 1), (1, 0)])  4.28 us
    ppermute x1, starting transfers between devices, grow(): lax.ppermute(stack[:, rows - halo:], 'tile', [(i, i + 1) for i in range(t...  3.21 us
    ppermute x2, starting transfers between devices, widen(): got = lax.ppermute(tall, 'wave', [(0, 1), (1, 0)])  2.47 us
  transfers between devices with their start and end apart: 7, of which 6 were waited for; matrix products, arithmetic and copies ran while one was open for 4% of the time, Pallas kernels for 0%

profile of v8, /device:TPU:15, one launch (start us, length us, event | category | flops | bytes accessed | tf_op | source)
XLA Modules:
  0.0 60.3 jit_solution(4799701817751506004)
XLA Ops:
  0.0 1.4 %fusion.40 = (f32[4,1,64,128]{3,2,1,0:T(8,128)S(1)}, f32[4,1,64,128]{3,2,1,0:T(8,128)S(1)}) fusion(bf16[4,64,128]{2,1,0:T(8,128)(2,1)} %param.5, bf16[4,64,128]{2,1,0:T(8,128)(2,1)} %param.6), kind=kLoop, calls=%fused_computation.98 | loop fusion | flops 163840 | bytes 393216 | tf_op jit(solution)/shard_map/stack | solution.py:25
  1.4 1.0 %pad_maximum_fusion.2 = f32[14,64,128]{2,1,0:T(8,128)S(1)} fusion(f32[8,64,128]{2,1,0:T(8,128)S(1)} %bitcast.258, f32[6,64,128]{2,1,0:T(8,128)} %bitcast.262), kind=kLoop, calls=%fused_computation.73 | loop fusion | flops 114688 | bytes 917504 | tf_op jit(solution)/shard_map/concatenate | solution.py:81
  2.4 2.1 %collective-permute-start.1 = (f32[14,64,128]{2,1,0:T(8,128)S(1)}, f32[14,64,128]{2,1,0:T(8,128)}, u32[]{:S(2)}, u32[]{:S(2)}) collective-permute-start(f32[14,64,128]{2,1,0:T(8,128)S(1)} %pad_maximum_fusion.2), channel_id=1, source_target_pairs={{4,0},{8,4},{12,8},{5,1},{9,5},{13,9},{6,2},{10,6},{14,10},{7,3},{... | collective-permute-start | bytes 1376264 | tf_op jit(solution)/shard_map/ppermute | solution.py:45
  4.5 3.2 %collective-permute-start = (f32[14,64,128]{2,1,0:T(8,128)S(1)}, f32[14,64,128]{2,1,0:T(8,128)}, u32[]{:S(2)}, u32[]{:S(2)}) collective-permute-start(f32[14,64,128]{2,1,0:T(8,128)S(1)} %pad_maximum_fusion.2), channel_id=1, source_target_pairs={{0,4},{4,8},{8,12},{1,5},{5,9},{9,13},{2,6},{6,10},{10,14},{3,7},{... | collective-permute-start | bytes 1376264 | tf_op jit(solution)/shard_map/ppermute | solution.py:44
  7.7 0.6 multiply_reduce_fusion
  9.3 0.5 copy.54
  9.8 0.8 %reshape.46 = f32[2,192,383]{2,1,0:T(8,128)S(1)} reshape(f32[2,73536]{1,0:T(2,128)S(1)} %slice.229) | data formatting | bytes 1176576 | tf_op jit(solution)/shard_map/reshape | solution.py:15
  10.8 4.9 %collective-permute-done.1 = f32[14,64,128]{2,1,0:T(8,128)} collective-permute-done((f32[14,64,128]{2,1,0:T(8,128)S(1)}, f32[14,64,128]{2,1,0:T(8,128)}, u32[]{:S(2)}, u32[]{:S(2)}) %collective-permute-start.1) | collective-permute-done | bytes 458784 | tf_op jit(solution)/shard_map/ppermute | solution.py:45
  15.8 1.8 %collective-permute-done = f32[14,64,128]{2,1,0:T(8,128)} collective-permute-done((f32[14,64,128]{2,1,0:T(8,128)S(1)}, f32[14,64,128]{2,1,0:T(8,128)}, u32[]{:S(2)}, u32[]{:S(2)}) %collective-permute-start) | collective-permute-done | bytes 458784 | tf_op jit(solution)/shard_map/ppermute | solution.py:44
  17.5 1.3 %pad_maximum_fusion = f32[14,192,128]{2,1,0:T(8,128)S(1)} fusion(f32[14,64,128]{2,1,0:T(8,128)} %collective-permute-done.1, f32[8,64,128]{2,1,0:T(8,128)S(1)} %bitcast.259, f32[6,64,128]{2,1,0:T(8,128)S(1)} %bitcast.263, f32[14,64,128]{2,1,0:T(8,128)} %collective-permute-done), kind=kLoop, calls=%fused_computation.2 | loop fusion | flops 1032192 | bytes 2752512 | tf_op jit(solution)/shard_map/concatenate | solution.py:46
  18.8 1.9 %collective-permute-start.2 = (f32[14,192,128]{2,1,0:T(8,128)S(1)}, f32[14,192,128]{2,1,0:T(8,128)S(1)}, u32[]{:S(2)}, u32[]{:S(2)}) collective-permute-start(f32[14,192,128]{2,1,0:T(8,128)S(1)} %pad_maximum_fusion), channel_id=1, source_target_pairs={{0,1},{1,0},{2,3},{3,2},{4,5},{5,4},{6,7},{7,6},{8,9},{9,8},{10,11... | collective-permute-start | bytes 4128776 | tf_op jit(solution)/shard_map/ppermute | solution.py:54
  20.8 2.7 %collective-permute-done.2 = f32[14,192,128]{2,1,0:T(8,128)S(1)} collective-permute-done((f32[14,192,128]{2,1,0:T(8,128)S(1)}, f32[14,192,128]{2,1,0:T(8,128)S(1)}, u32[]{:S(2)}, u32[]{:S(2)}) %collective-permute-start.2) | collective-permute-done | bytes 1376288 | tf_op jit(solution)/shard_map/ppermute | solution.py:54
  23.8 0.5 maximum_select_fusion
  24.2 0.5 maximum_select_fusion.1
  25.6 1.0 %convolution_bitcast_fusion.3 = f32[3,2,160,192,1]{3,2,1,4,0:T(8,128)S(1)} fusion(f32[3,1,192,192]{3,2,1,0:T(8,128)S(1)} %get-tuple-element.18, f32[3,1,192,192]{3,2,1,0:T(8,128)S(1)} %get-tuple-element.17, f32[2,2,192,192]{3,2,1,0:T(8,128)S(1)} %pad_maximum_fusion.1), kind=kOutput, calls=%fused_computation.6 | convolution fusion | flops 424894464 | bytes 2572288 | tf_op jit(solution)/shard_map/dcab,icbj->idaj/dot_general | solution.py:100
  26.5 1.0 %convolution_bitcast_fusion.2 = f32[3,2,160,192]{3,2,1,0:T(8,128)S(1)} fusion(f32[3,2,160,192,1]{3,2,1,4,0:T(8,128)S(1)} %convolution_bitcast_fusion.3, f32[2,2,192,192]{3,2,1,0:T(8,128)S(1)} %pad_maximum_fusion.1), kind=kOutput, calls=%fused_computation.5 | convolution fusion | flops 424673280 | bytes 2064384 | tf_op jit(solution)/shard_map/dcyj,icxj->idxy/dot_general | solution.py:103
  27.6 1.4 %convolution_bitcast_fusion.11 = f32[3,2,128,192,1]{2,3,1,4,0:T(8,128)S(1)} fusion(f32[3,1,160,192]{3,2,1,0:T(8,128)S(1)} %get-tuple-element.28, f32[3,1,160,192]{3,2,1,0:T(8,128)S(1)} %get-tuple-element.27, f32[2,2,192,192]{3,2,1,0:T(8,128)S(1)} %pad_maximum_fusion.1), kind=kOutput, calls=%fused_computation.14 | convolution fusion | flops 283299840 | bytes 2097152 | tf_op jit(solution)/shard_map/dcab,icbj->idaj/dot_general | solution.py:100
  29.1 0.8 %convolution_bitcast_fusion.10 = f32[3,2,128,192]{2,3,1,0:T(8,128)S(1)} fusion(f32[3,2,128,192,1]{2,3,1,4,0:T(8,128)S(1)} %convolution_bitcast_fusion.11, f32[2,2,192,192]{3,2,1,0:T(8,128)S(1)} %pad_maximum_fusion.1), kind=kOutput, calls=%fused_computation.13 | convolution fusion | flops 339738624 | bytes 1769472 | tf_op jit(solution)/shard_map/dcyj,icxj->idxy/dot_general | solution.py:103
  30.5 0.7 %convolution_bitcast_fusion.8 = f32[3,2,96,192]{3,2,1,0:T(8,128)S(1)} fusion(f32[3,2,96,192,1]{3,2,1,4,0:T(8,128)S(1)} %convolution_bitcast_fusion.9, f32[2,2,192,192]{3,2,1,0:T(8,128)S(1)} %pad_maximum_fusion.1), kind=kOutput, calls=%fused_computation.11 | convolution fusion | flops 254803968 | bytes 1474560 | tf_op jit(solution)/shard_map/dcyj,icxj->idxy/dot_general | solution.py:103
  32.2 1.3 %collective-permute-start.3 = (f32[6,64,128]{2,1,0:T(8,128)S(1)}, f32[6,64,128]{2,1,0:T(8,128)S(1)}, u32[]{:S(2)}, u32[]{:S(2)}) collective-permute-start(f32[6,64,128]{2,1,0:T(8,128)S(1)} %bitcast.264), channel_id=1, source_target_pairs={{0,6},{4,10},{8,14},{1,7},{5,11},{9,15},{16,22},{20,26},{24,30},{1... | collective-permute-start | bytes 589832 | tf_op jit(solution)/shard_map/ppermute | solution.py:125
  33.5 1.3 %collective-permute-start.4 = (f32[6,64,128]{2,1,0:T(8,128)S(1)}, f32[6,64,128]{2,1,0:T(8,128)S(1)}, u32[]{:S(2)}, u32[]{:S(2)}) collective-permute-start(f32[6,64,128]{2,1,0:T(8,128)S(1)} %bitcast.265), channel_id=1, source_target_pairs={{0,2},{4,6},{8,10},{12,14},{1,3},{5,7},{9,11},{13,15},{16,18},{20,... | collective-permute-start | bytes 589832 | tf_op jit(solution)/shard_map/ppermute | solution.py:126
  34.8 1.5 %collective-permute-start.5 = (f32[6,64,128]{2,1,0:T(8,128)S(1)}, f32[6,64,128]{2,1,0:T(8,128)S(1)}, u32[]{:S(2)}, u32[]{:S(2)}) collective-permute-start(f32[6,64,128]{2,1,0:T(8,128)S(1)} %bitcast.266), channel_id=1, source_target_pairs={{4,2},{8,6},{12,10},{5,3},{9,7},{13,11},{20,18},{24,22},{28,26},{2... | collective-permute-start | bytes 589832 | tf_op jit(solution)/shard_map/ppermute | solution.py:127
  36.2 4.9 %collective-permute-done.3 = f32[6,64,128]{2,1,0:T(8,128)S(1)} collective-permute-done((f32[6,64,128]{2,1,0:T(8,128)S(1)}, f32[6,64,128]{2,1,0:T(8,128)S(1)}, u32[]{:S(2)}, u32[]{:S(2)}) %collective-permute-start.3) | collective-permute-done | bytes 196640 | tf_op jit(solution)/shard_map/ppermute | solution.py:125
  41.1 9.1 %collective-permute-done.4 = f32[6,64,128]{2,1,0:T(8,128)S(1)} collective-permute-done((f32[6,64,128]{2,1,0:T(8,128)S(1)}, f32[6,64,128]{2,1,0:T(8,128)S(1)}, u32[]{:S(2)}, u32[]{:S(2)}) %collective-permute-start.4) | collective-permute-done | bytes 196640 | tf_op jit(solution)/shard_map/ppermute | solution.py:126
  50.3 0.5 collective-permute-start.6
  50.8 1.6 %collective-permute-done.6 = f32[6,192,128]{2,1,0:T(8,128)S(1)} collective-permute-done((f32[6,192,128]{2,1,0:T(8,128)S(1)}, f32[6,192,128]{2,1,0:T(8,128)S(1)}, u32[]{:S(2)}, u32[]{:S(2)}) %collective-permute-start.6) | collective-permute-done | bytes 589856 | tf_op jit(solution)/shard_map/ppermute | solution.py:54
  53.2 1.0 %convolution_bitcast_fusion.1 = f32[3,2,160,192,1]{3,2,1,4,0:T(8,128)S(1)} fusion(f32[3,1,192,192]{3,2,1,0:T(8,128)S(1)} %get-tuple-element.10, f32[3,1,192,192]{3,2,1,0:T(8,128)S(1)} %get-tuple-element.9, f32[2,2,192,192]{3,2,1,0:T(8,128)S(1)} %pad_maximum_fusion.1), kind=kOutput, calls=%fused_computation.4 | convolution fusion | flops 424894464 | bytes 2572288 | tf_op jit(solution)/shard_map/dcab,icbj->idaj/dot_general | solution.py:100
  54.2 1.0 %convolution_bitcast_fusion = f32[3,2,160,192]{3,2,1,0:T(8,128)S(1)} fusion(f32[3,2,160,192,1]{3,2,1,4,0:T(8,128)S(1)} %convolution_bitcast_fusion.1, f32[2,2,192,192]{3,2,1,0:T(8,128)S(1)} %pad_maximum_fusion.1), kind=kOutput, calls=%fused_computation.3 | convolution fusion | flops 424673280 | bytes 2064384 | tf_op jit(solution)/shard_map/dcyj,icxj->idxy/dot_general | solution.py:103
  55.3 1.4 %convolution_bitcast_fusion.7 = f32[3,2,128,192,1]{2,3,1,4,0:T(8,128)S(1)} fusion(f32[3,1,160,192]{3,2,1,0:T(8,128)S(1)} %get-tuple-element.26, f32[3,1,160,192]{3,2,1,0:T(8,128)S(1)} %get-tuple-element.25, f32[2,2,192,192]{3,2,1,0:T(8,128)S(1)} %pad_maximum_fusion.1), kind=kOutput, calls=%fused_computation.10 | convolution fusion | flops 283299840 | bytes 2097152 | tf_op jit(solution)/shard_map/dcab,icbj->idaj/dot_general | solution.py:100
  56.7 0.8 %convolution_bitcast_fusion.6 = f32[3,2,128,192]{2,3,1,0:T(8,128)S(1)} fusion(f32[3,2,128,192,1]{2,3,1,4,0:T(8,128)S(1)} %convolution_bitcast_fusion.7, f32[2,2,192,192]{3,2,1,0:T(8,128)S(1)} %pad_maximum_fusion.1), kind=kOutput, calls=%fused_computation.9 | convolution fusion | flops 339738624 | bytes 1769472 | tf_op jit(solution)/shard_map/dcyj,icxj->idxy/dot_general | solution.py:103
  58.0 0.7 %convolution_bitcast_fusion.4 = f32[3,2,96,192]{3,2,1,0:T(8,128)S(1)} fusion(f32[3,2,96,192,1]{3,2,1,4,0:T(8,128)S(1)} %convolution_bitcast_fusion.5, f32[2,2,192,192]{3,2,1,0:T(8,128)S(1)} %pad_maximum_fusion.1), kind=kOutput, calls=%fused_computation.7 | convolution fusion | flops 254803968 | bytes 1474560 | tf_op jit(solution)/shard_map/dcyj,icxj->idxy/dot_general | solution.py:103
  59.2 1.1 %fusion.5 = f32[1,3,2,64,128]{4,3,2,1,0:T(8,128)} fusion(f32[3,2,64,192,1]{3,2,1,4,0:T(8,128)S(1)} %convolution_bitcast_fusion.12, f32[3,64,2,128,1]{3,1,4,2,0:T(8,128)S(1)} %fusion.29, f32[2,2,192,192]{3,2,1,0:T(8,128)S(1)} %pad_maximum_fusion.1, pred[]{:T(512)S(6)} %eq.13, pred[]{:T(512)S(6)} %eq.14, pred[]{:T(512)S(6)} %eq.12), kind=kOutput, calls=%fused_computation.27 | convolution fusion | flops 113442816 | bytes 1835011 | tf_op jit(solution)/shard_map/dcyj,icxj->idxy/dot_general | solution.py:103
  (45 shorter events, 5.3 us)
Async XLA Ops:
  0.0 7.7 %copy-start.1 = (f32[2,33]{1,0:T(2,128)S(1)}, f32[2,33]{1,0:T(2,128)}, u32[]{:S(2)}) copy-start(f32[2,33]{1,0:T(2,128)} %param.7) | copy-start | bytes 796
  2.4 13.4 %collective-permute-start.1 = (f32[14,64,128]{2,1,0:T(8,128)S(1)}, f32[14,64,128]{2,1,0:T(8,128)}, u32[]{:S(2)}, u32[]{:S(2)}) collective-permute-start(f32[14,64,128]{2,1,0:T(8,128)S(1)} %pad_maximum_fusion.2), channel_id=1, source_target_pairs={{4,0},{8,4},{12,8},{5,1},{9,5},{13,9},{6,2},{10,6},{14,10},{7,3},{... | collective-permute-start | bytes 1376264 | tf_op jit(solution)/shard_map/ppermute | solution.py:45
  4.5 13.1 %collective-permute-start = (f32[14,64,128]{2,1,0:T(8,128)S(1)}, f32[14,64,128]{2,1,0:T(8,128)}, u32[]{:S(2)}, u32[]{:S(2)}) collective-permute-start(f32[14,64,128]{2,1,0:T(8,128)S(1)} %pad_maximum_fusion.2), channel_id=1, source_target_pairs={{0,4},{4,8},{8,12},{1,5},{5,9},{9,13},{2,6},{6,10},{10,14},{3,7},{... | collective-permute-start | bytes 1376264 | tf_op jit(solution)/shard_map/ppermute | solution.py:44
  10.7 6.9 %copy-start = (f32[3,2,64,128]{3,2,1,0:T(8,128)S(1)}, f32[3,2,64,128]{3,2,1,0:T(8,128)}, u32[]{:S(2)}) copy-start(f32[3,2,64,128]{3,2,1,0:T(8,128)} %param.4) | copy-start | bytes 589828
  18.8 4.7 %collective-permute-start.2 = (f32[14,192,128]{2,1,0:T(8,128)S(1)}, f32[14,192,128]{2,1,0:T(8,128)S(1)}, u32[]{:S(2)}, u32[]{:S(2)}) collective-permute-start(f32[14,192,128]{2,1,0:T(8,128)S(1)} %pad_maximum_fusion), channel_id=1, source_target_pairs={{0,1},{1,0},{2,3},{3,2},{4,5},{5,4},{6,7},{7,6},{8,9},{9,8},{10,11... | collective-permute-start | bytes 4128776 | tf_op jit(solution)/shard_map/ppermute | solution.py:54
  32.2 9.0 %collective-permute-start.3 = (f32[6,64,128]{2,1,0:T(8,128)S(1)}, f32[6,64,128]{2,1,0:T(8,128)S(1)}, u32[]{:S(2)}, u32[]{:S(2)}) collective-permute-start(f32[6,64,128]{2,1,0:T(8,128)S(1)} %bitcast.264), channel_id=1, source_target_pairs={{0,6},{4,10},{8,14},{1,7},{5,11},{9,15},{16,22},{20,26},{24,30},{1... | collective-permute-start | bytes 589832 | tf_op jit(solution)/shard_map/ppermute | solution.py:125
  33.5 16.8 %collective-permute-start.4 = (f32[6,64,128]{2,1,0:T(8,128)S(1)}, f32[6,64,128]{2,1,0:T(8,128)S(1)}, u32[]{:S(2)}, u32[]{:S(2)}) collective-permute-start(f32[6,64,128]{2,1,0:T(8,128)S(1)} %bitcast.265), channel_id=1, source_target_pairs={{0,2},{4,6},{8,10},{12,14},{1,3},{5,7},{9,11},{13,15},{16,18},{20,... | collective-permute-start | bytes 589832 | tf_op jit(solution)/shard_map/ppermute | solution.py:126
  34.8 15.5 %collective-permute-start.5 = (f32[6,64,128]{2,1,0:T(8,128)S(1)}, f32[6,64,128]{2,1,0:T(8,128)S(1)}, u32[]{:S(2)}, u32[]{:S(2)}) collective-permute-start(f32[6,64,128]{2,1,0:T(8,128)S(1)} %bitcast.266), channel_id=1, source_target_pairs={{4,2},{8,6},{12,10},{5,3},{9,7},{13,11},{20,18},{24,22},{28,26},{2... | collective-permute-start | bytes 589832 | tf_op jit(solution)/shard_map/ppermute | solution.py:127
  50.3 2.2 %collective-permute-start.6 = (f32[6,192,128]{2,1,0:T(8,128)S(1)}, f32[6,192,128]{2,1,0:T(8,128)S(1)}, u32[]{:S(2)}, u32[]{:S(2)}) collective-permute-start(f32[6,192,128]{2,1,0:T(8,128)S(1)} %constant_dynamic-update-slice_fusion), channel_id=1, source_target_pairs={{0,1},{1,0},{2,3},{3,2},{4,5},{5,4},{6,7},{7,6},{8,9},{9,8},{10,11... | collective-permute-start | bytes 1769480 | tf_op jit(solution)/shard_map/ppermute | solution.py:54

commit v9 on v8

--- a/solution.py
+++ b/solution.py
@@ -56,9 +56,8 @@
     for size in splits:
         own, other = tall[start:start + size], got[start:start + size]
         start += size
-        left = jnp.concatenate([own, other[..., :halo]], axis=-1)
-        right = jnp.concatenate([other[..., cols - halo:], own], axis=-1)
-        out.append(jnp.where(wave == 0, left, right))
+        part = jnp.where(wave == 0, other[..., :halo], jnp.flip(other[..., cols - halo:], axis=-1))
+        out.append(jnp.concatenate([own, part], axis=-1))
     return out
 
 
@@ -85,24 +84,26 @@
     )
     first_field = field_grown.reshape(illum, 2, rows + 2 * reach, cols + reach)
     trans_reg = trans_grown.reshape(slices, 2, rows + 2 * reach, cols + reach)
-    col_band = band[:, :, :width, :width]
+    natural = band[:, :, :width, :width]
+    turned = jnp.concatenate([natural[:, :, reach:], jnp.flip(natural[:, :, :reach], axis=2)], axis=2)
+    turned = jnp.concatenate([turned[..., reach:], jnp.flip(turned[..., :reach], axis=3)], axis=3)
+    col_band = jnp.where(wave == 0, natural, turned)
     row_bands = [
         band[:, :, HALF * (s + 1): tall - HALF * (s + 1), HALF * s: tall - HALF * s]
         for s in range(slices)
     ]
 
-    last_band = jnp.where(wave == 0, col_band[:, :, :cols], col_band[:, :, reach:reach + cols])
-
     def depth_section(field):
         current = field
         for s in range(slices):
-            moved = modulate(current, trans_reg[s, :, HALF * s: tall - HALF * s])
+            keep = width - HALF * s
+            moved = modulate(current, trans_reg[s, :, HALF * s: tall - HALF * s, :keep])
             rows_done = jnp.einsum(
                 "dcab,icbj->idaj", row_bands[s], moved, precision=lax.Precision.HIGH
             )
             current = jnp.einsum(
                 "dcyj,icxj->idxy",
-                last_band if s == slices - 1 else col_band,
+                col_band[:, :, : keep - HALF, :keep],
                 rows_done,
                 precision=lax.Precision.HIGH,
             )

time: 60.6 us -> 84.8 us (1.40)
  local copies, waits for them, and re-layouts: 2.65 us -> 27.3 us
  waiting for transfers between devices: 25 us -> 21.9 us
  other arithmetic: 6.94 us -> 8.79 us
    rev x0 -> x5, local copies, waits for them, and re-layouts: none -> 12.6 us  [the longest x3 11.2 us: widen(): jnp.flip(other[..., cols - halo:], axis=-1)]
    unnamed x8 -> x54, local copies, waits for them, and re-layouts: 0.54 us -> 4.17 us
    slice x3 -> x5, local copies, waits for them, and re-layouts: 0.71 us -> 3.88 us  [the longest x3 3.83 us: widen(): other[..., cols - halo:]]
    slice x2, local copies, waits for them, and re-layouts: 0.09 us -> 3.11 us  [widen(): own, other = (tall[start:start + size], got[start:start + size])]
    ppermute x2, waiting for transfers between devices: 4.28 us -> 1.33 us  [widen(): got = lax.ppermute(tall, 'wave', [(0, 1), (1, 0)])]
    mul x5, local copies, waits for them, and re-layouts: 0.18 us -> 2.37 us  [modulate(): field_real * trans[0] - field_imag * trans[1]]
  transfers between devices with their start and end apart: 7 -> 7, of which waited for: 6 -> 5; matrix products, arithmetic and copies ran while one was open for 4% -> 9% of each run, Pallas kernels for 0% -> 0%
where the time goes in v9:
time: 84.8 us; the launch traced here: 83.7 us
  local copies, waits for them, and re-layouts  27.3 us (32%)
  waiting for transfers between devices  21.9 us (26%)
  matrix products  12.4 us (15%)
  starting transfers between devices  11.7 us (14%)
  other arithmetic  8.79 us (10%)
  between operations  1.49 us (2%)
    rev x3, local copies, waits for them, and re-layouts, widen(): jnp.flip(other[..., cols - halo:], axis=-1)  11.2 us
    ppermute x1, waiting for transfers between devices, per_device(): mine = lax.ppermute(flat, grid, own_pairs)  8.71 us
    dot_general x8, matrix products, depth_section(): jnp.einsum('dcab,icbj->idaj', row_bands[s], moved, precision=lax.Precisio...  6.41 us
    dot_general x8, matrix products, depth_section(): jnp.einsum('dcyj,icxj->idxy', col_band[:, :, :keep - HALF, :keep], rows_d...  6.02 us
    ppermute x1, waiting for transfers between devices, per_device(): from_prev = lax.ppermute(flat[:, rows - reach:], grid, prev_pairs)  5.29 us
    ppermute x1, waiting for transfers between devices, grow(): lax.ppermute(stack[:, :halo], 'tile', [(i + 1, i) for i in range(tiles -...  4.85 us
    unnamed x54, local copies, waits for them, and re-layouts  4.17 us
    slice x3, local copies, waits for them, and re-layouts, widen(): other[..., cols - halo:]  3.83 us
  transfers between devices with their start and end apart: 7, of which 5 were waited for; matrix products, arithmetic and copies ran while one was open for 9% of the time, Pallas kernels for 0%

profile of v9, /device:TPU:15, one launch (start us, length us, event | category | flops | bytes accessed | tf_op | source)
XLA Modules:
  0.0 83.7 jit_solution(8654541977095913002)
XLA Ops:
  0.0 1.4 %fusion.37 = (f32[4,1,64,128]{3,2,1,0:T(8,128)S(1)}, f32[4,1,64,128]{3,2,1,0:T(8,128)S(1)}) fusion(bf16[4,64,128]{2,1,0:T(8,128)(2,1)} %param.5, bf16[4,64,128]{2,1,0:T(8,128)(2,1)} %param.6), kind=kLoop, calls=%fused_computation.106 | loop fusion | flops 163840 | bytes 393216 | tf_op jit(solution)/shard_map/stack | solution.py:25
  1.4 1.0 %pad_maximum_fusion.5 = f32[14,64,128]{2,1,0:T(8,128)S(1)} fusion(f32[8,64,128]{2,1,0:T(8,128)S(1)} %bitcast.247, f32[6,64,128]{2,1,0:T(8,128)} %bitcast.250), kind=kLoop, calls=%fused_computation.71 | loop fusion | flops 114688 | bytes 917504 | tf_op jit(solution)/shard_map/concatenate | solution.py:80
  2.4 2.1 %collective-permute-start.1 = (f32[14,64,128]{2,1,0:T(8,128)S(1)}, f32[14,64,128]{2,1,0:T(8,128)S(1)}, u32[]{:S(2)}, u32[]{:S(2)}) collective-permute-start(f32[14,64,128]{2,1,0:T(8,128)S(1)} %pad_maximum_fusion.5), channel_id=1, source_target_pairs={{4,0},{8,4},{12,8},{5,1},{9,5},{13,9},{6,2},{10,6},{14,10},{7,3},{... | collective-permute-start | bytes 1376264 | tf_op jit(solution)/shard_map/ppermute | solution.py:45
  4.5 3.2 %collective-permute-start = (f32[14,64,128]{2,1,0:T(8,128)S(1)}, f32[14,64,128]{2,1,0:T(8,128)S(1)}, u32[]{:S(2)}, u32[]{:S(2)}) collective-permute-start(f32[14,64,128]{2,1,0:T(8,128)S(1)} %pad_maximum_fusion.5), channel_id=1, source_target_pairs={{0,4},{4,8},{8,12},{1,5},{5,9},{9,13},{2,6},{6,10},{10,14},{3,7},{... | collective-permute-start | bytes 1376264 | tf_op jit(solution)/shard_map/ppermute | solution.py:44
  10.8 4.8 %collective-permute-done.1 = f32[14,64,128]{2,1,0:T(8,128)S(1)} collective-permute-done((f32[14,64,128]{2,1,0:T(8,128)S(1)}, f32[14,64,128]{2,1,0:T(8,128)S(1)}, u32[]{:S(2)}, u32[]{:S(2)}) %collective-permute-start.1) | collective-permute-done | bytes 458784 | tf_op jit(solution)/shard_map/ppermute | solution.py:45
  15.6 1.8 %collective-permute-done = f32[14,64,128]{2,1,0:T(8,128)S(1)} collective-permute-done((f32[14,64,128]{2,1,0:T(8,128)S(1)}, f32[14,64,128]{2,1,0:T(8,128)S(1)}, u32[]{:S(2)}, u32[]{:S(2)}) %collective-permute-start) | collective-permute-done | bytes 458784 | tf_op jit(solution)/shard_map/ppermute | solution.py:44
  17.4 1.2 %pad_maximum_fusion.1 = f32[14,192,128]{2,1,0:T(8,128)} fusion(f32[14,64,128]{2,1,0:T(8,128)S(1)} %collective-permute-done.1, f32[8,64,128]{2,1,0:T(8,128)S(1)} %bitcast.248, f32[6,64,128]{2,1,0:T(8,128)S(1)} %bitcast.251, f32[14,64,128]{2,1,0:T(8,128)S(1)} %collective-permute-done), kind=kLoop, calls=%fused_computation.5 | loop fusion | flops 1032192 | bytes 2752512 | tf_op jit(solution)/shard_map/concatenate | solution.py:46
  18.6 1.9 %collective-permute-start.2 = (f32[14,192,128]{2,1,0:T(8,128)}, f32[14,192,128]{2,1,0:T(8,128)}, u32[]{:S(2)}, u32[]{:S(2)}) collective-permute-start(f32[14,192,128]{2,1,0:T(8,128)} %pad_maximum_fusion.1), channel_id=1, source_target_pairs={{0,1},{1,0},{2,3},{3,2},{4,5},{5,4},{6,7},{7,6},{8,9},{9,8},{10,11... | collective-permute-start | bytes 4128776 | tf_op jit(solution)/shard_map/ppermute | solution.py:54
  20.5 1.9 %slice.213 = f32[6,192,128]{2,1,0:T(8,128)} slice(f32[14,192,128]{2,1,0:T(8,128)} %pad_maximum_fusion.1), slice={[0:6], [0:192], [0:128]} | slice | bytes 1179648 | tf_op jit(solution)/shard_map/slice | solution.py:57
  22.4 1.2 %slice.217 = f32[8,192,128]{2,1,0:T(8,128)S(1)} slice(f32[14,192,128]{2,1,0:T(8,128)} %pad_maximum_fusion.1), slice={[6:14], [0:192], [0:128]} | slice | bytes 1572864 | tf_op jit(solution)/shard_map/slice | solution.py:57
  23.8 1.2 %rev.22 = f32[2,2,192,64]{3,2,1,0:T(8,128)S(1)} reverse(f32[2,2,192,64]{3,2,1,0:T(8,128)S(1)} %pad_maximum_fusion.6), dimensions={3} | reverse | bytes 393216 | tf_op jit(solution)/shard_map/jit(_flip)/rev | solution.py:89
  25.3 2.3 %slice.264 = f32[8,192,64]{2,1,0:T(8,128)} slice(f32[14,192,128]{2,1,0:T(8,128)} %collective-permute-done.2), slice={[6:14], [0:192], [64:128]} | slice | bytes 786432 | tf_op jit(solution)/shard_map/slice | solution.py:59
  27.6 7.6 %rev.20 = f32[8,192,64]{2,1,0:T(8,128)S(1)} reverse(f32[8,192,64]{2,1,0:T(8,128)} %slice.264), dimensions={2} | reverse | bytes 786432 | tf_op jit(solution)/shard_map/jit(_flip)/rev | solution.py:59
  35.3 1.2 %slice_select_fusion = f32[8,192,64]{2,1,0:T(8,128)S(1)} fusion(f32[8,192,64]{2,1,0:T(8,128)S(1)} %rev.20, f32[14,192,128]{2,1,0:T(8,128)} %collective-permute-done.2, pred[]{:T(512)S(6)} %eq.13), kind=kLoop, calls=%fused_computation.37 | loop fusion | flops 98304 | bytes 1179649 | tf_op jit(solution)/shard_map/jit(_where)/select_n | solution.py:59
  39.5 1.3 %slice.261 = f32[6,192,64]{2,1,0:T(8,128)S(1)} slice(f32[14,192,128]{2,1,0:T(8,128)} %collective-permute-done.2), slice={[0:6], [0:192], [64:128]} | slice | bytes 589824 | tf_op jit(solution)/shard_map/slice | solution.py:59
  40.8 1.8 %rev.19 = f32[6,192,64]{2,1,0:T(8,128)S(1)} reverse(f32[6,192,64]{2,1,0:T(8,128)S(1)} %slice.261), dimensions={2} | reverse | bytes 589824 | tf_op jit(solution)/shard_map/jit(_flip)/rev | solution.py:59
  42.6 1.1 %slice_select_fusion.2 = f32[6,192,64]{2,1,0:T(8,128)S(1)} fusion(f32[6,192,64]{2,1,0:T(8,128)S(1)} %rev.19, f32[14,192,128]{2,1,0:T(8,128)} %collective-permute-done.2, pred[]{:T(512)S(6)} %eq.13), kind=kLoop, calls=%fused_computation.50 | loop fusion | flops 73728 | bytes 884737 | tf_op jit(solution)/shard_map/jit(_where)/select_n | solution.py:59
  44.8 1.0 %convolution_bitcast_fusion.3 = f32[3,2,160,192,1]{3,2,1,4,0:T(8,128)S(1)} fusion(f32[3,1,192,192]{3,2,1,0:T(8,128)S(1)} %get-tuple-element.18, f32[3,1,192,192]{3,2,1,0:T(8,128)S(1)} %get-tuple-element.17, f32[2,2,192,192]{3,2,1,0:T(8,128)S(1)} %pad_maximum_fusion.4), kind=kOutput, calls=%fused_computation.9 | convolution fusion | flops 424894464 | bytes 2572288 | tf_op jit(solution)/shard_map/dcab,icbj->idaj/dot_general | solution.py:101
  45.9 1.0 %convolution_bitcast_fusion.2 = f32[3,2,160,176]{3,2,1,0:T(8,128)S(1)} fusion(f32[3,2,160,192,1]{3,2,1,4,0:T(8,128)S(1)} %convolution_bitcast_fusion.3, f32[2,2,192,192]{3,2,1,0:T(8,128)S(1)} %maximum_select_fusion), kind=kOutput, calls=%fused_computation.8 | convolution fusion | flops 389283840 | bytes 2379776 | tf_op jit(solution)/shard_map/dcyj,icxj->idxy/dot_general | solution.py:104
  47.0 1.4 %convolution_bitcast_fusion.5 = f32[3,2,128,176,1]{2,3,1,4,0:T(8,128)S(1)} fusion(f32[3,1,160,176]{3,2,1,0:T(8,128)S(1)} %get-tuple-element.24, f32[3,1,160,176]{3,2,1,0:T(8,128)S(1)} %get-tuple-element.23, f32[2,2,192,192]{3,2,1,0:T(8,128)S(1)} %pad_maximum_fusion.4), kind=kOutput, calls=%fused_computation.11 | convolution fusion | flops 259691520 | bytes 2048000 | tf_op jit(solution)/shard_map/dcab,icbj->idaj/dot_general | solution.py:101
  51.7 1.3 %collective-permute-start.3 = (f32[6,64,128]{2,1,0:T(8,128)S(1)}, f32[6,64,128]{2,1,0:T(8,128)S(1)}, u32[]{:S(2)}, u32[]{:S(2)}) collective-permute-start(f32[6,64,128]{2,1,0:T(8,128)S(1)} %bitcast.252), channel_id=1, source_target_pairs={{0,6},{4,10},{8,14},{1,7},{5,11},{9,15},{16,22},{20,26},{24,30},{1... | collective-permute-start | bytes 589832 | tf_op jit(solution)/shard_map/ppermute | solution.py:126
  53.0 1.3 %collective-permute-start.4 = (f32[6,64,128]{2,1,0:T(8,128)S(1)}, f32[6,64,128]{2,1,0:T(8,128)S(1)}, u32[]{:S(2)}, u32[]{:S(2)}) collective-permute-start(f32[6,64,128]{2,1,0:T(8,128)S(1)} %bitcast.253), channel_id=1, source_target_pairs={{0,2},{4,6},{8,10},{12,14},{1,3},{5,7},{9,11},{13,15},{16,18},{20,... | collective-permute-start | bytes 589832 | tf_op jit(solution)/shard_map/ppermute | solution.py:127
  54.3 1.5 %collective-permute-start.5 = (f32[6,64,128]{2,1,0:T(8,128)S(1)}, f32[6,64,128]{2,1,0:T(8,128)S(1)}, u32[]{:S(2)}, u32[]{:S(2)}) collective-permute-start(f32[6,64,128]{2,1,0:T(8,128)S(1)} %bitcast.254), channel_id=1, source_target_pairs={{4,2},{8,6},{12,10},{5,3},{9,7},{13,11},{20,18},{24,22},{28,26},{2... | collective-permute-start | bytes 589832 | tf_op jit(solution)/shard_map/ppermute | solution.py:128
  55.8 5.3 %collective-permute-done.3 = f32[6,64,128]{2,1,0:T(8,128)S(1)} collective-permute-done((f32[6,64,128]{2,1,0:T(8,128)S(1)}, f32[6,64,128]{2,1,0:T(8,128)S(1)}, u32[]{:S(2)}, u32[]{:S(2)}) %collective-permute-start.3) | collective-permute-done | bytes 196640 | tf_op jit(solution)/shard_map/ppermute | solution.py:126
  61.1 8.7 %collective-permute-done.4 = f32[6,64,128]{2,1,0:T(8,128)S(1)} collective-permute-done((f32[6,64,128]{2,1,0:T(8,128)S(1)}, f32[6,64,128]{2,1,0:T(8,128)S(1)}, u32[]{:S(2)}, u32[]{:S(2)}) %collective-permute-start.4) | collective-permute-done | bytes 196640 | tf_op jit(solution)/shard_map/ppermute | solution.py:127
  70.7 1.3 %collective-permute-done.6 = f32[6,192,128]{2,1,0:T(8,128)S(1)} collective-permute-done((f32[6,192,128]{2,1,0:T(8,128)S(1)}, f32[6,192,128]{2,1,0:T(8,128)S(1)}, u32[]{:S(2)}, u32[]{:S(2)}) %collective-permute-start.6) | collective-permute-done | bytes 589856 | tf_op jit(solution)/shard_map/ppermute | solution.py:54
  72.2 1.8 %rev.23 = f32[6,192,64]{2,1,0:T(8,128)S(1)} reverse(f32[6,192,64]{2,1,0:T(8,128)S(1)} %slice.289), dimensions={2} | reverse | bytes 589824 | tf_op jit(solution)/shard_map/jit(_flip)/rev | solution.py:59
  74.1 1.0 %copy-done.8 = f32[6,192,128]{2,1,0:T(8,128)S(1)} copy-done((f32[6,192,128]{2,1,0:T(8,128)S(1)}, f32[6,192,128]{2,1,0:T(8,128)}, u32[]{:S(2)}) %copy-start.8) | copy-done | bytes 589848
  76.2 1.0 %convolution_bitcast_fusion.1 = f32[3,2,160,192,1]{3,2,1,4,0:T(8,128)S(1)} fusion(f32[3,1,192,192]{3,2,1,0:T(8,128)S(1)} %get-tuple-element.10, f32[3,1,192,192]{3,2,1,0:T(8,128)S(1)} %get-tuple-element.9, f32[2,2,192,192]{3,2,1,0:T(8,128)S(1)} %pad_maximum_fusion.4), kind=kOutput, calls=%fused_computation.7 | convolution fusion | flops 424894464 | bytes 2572288 | tf_op jit(solution)/shard_map/dcab,icbj->idaj/dot_general | solution.py:101
  77.2 1.0 %convolution_bitcast_fusion = f32[3,2,160,176]{3,2,1,0:T(8,128)S(1)} fusion(f32[3,2,160,192,1]{3,2,1,4,0:T(8,128)S(1)} %convolution_bitcast_fusion.1, f32[2,2,192,192]{3,2,1,0:T(8,128)S(1)} %maximum_select_fusion), kind=kOutput, calls=%fused_computation.6 | convolution fusion | flops 389283840 | bytes 2379776 | tf_op jit(solution)/shard_map/dcyj,icxj->idxy/dot_general | solution.py:104
  78.3 1.4 %convolution_bitcast_fusion.4 = f32[3,2,128,176,1]{2,3,1,4,0:T(8,128)S(1)} fusion(f32[3,1,160,176]{3,2,1,0:T(8,128)S(1)} %get-tuple-element.22, f32[3,1,160,176]{3,2,1,0:T(8,128)S(1)} %get-tuple-element.21, f32[2,2,192,192]{3,2,1,0:T(8,128)S(1)} %pad_maximum_fusion.4), kind=kOutput, calls=%fused_computation.10 | convolution fusion | flops 259691520 | bytes 2048000 | tf_op jit(solution)/shard_map/dcab,icbj->idaj/dot_general | solution.py:101
  82.5 1.1 %fusion.5 = f32[1,3,2,64,128]{4,3,2,1,0:T(8,128)} fusion(f32[3,2,64,144,1]{3,2,1,4,0:T(8,128)S(1)} %convolution_bitcast_fusion.12, f32[2,2,192,192]{3,2,1,0:T(8,128)S(1)} %maximum_select_fusion, f32[3,64,2,128,1]{3,1,4,2,0:T(8,128)S(1)} %copy-done.11, pred[]{:T(512)S(6)} %eq.14, pred[]{:T(512)S(6)} %eq.12), kind=kOutput, calls=%fused_computation.30 | convolution fusion | flops 85032960 | bytes 1310722 | tf_op jit(solution)/shard_map/dcyj,icxj->idxy/dot_general | solution.py:104
  (105 shorter events, 15.3 us)
Async XLA Ops:
  0.0 7.7 %copy-start.24 = (f32[2,33]{1,0:T(2,128)S(1)}, f32[2,33]{1,0:T(2,128)}, u32[]{:S(2)}) copy-start(f32[2,33]{1,0:T(2,128)} %param.7) | copy-start | bytes 796
  2.4 13.3 %collective-permute-start.1 = (f32[14,64,128]{2,1,0:T(8,128)S(1)}, f32[14,64,128]{2,1,0:T(8,128)S(1)}, u32[]{:S(2)}, u32[]{:S(2)}) collective-permute-start(f32[14,64,128]{2,1,0:T(8,128)S(1)} %pad_maximum_fusion.5), channel_id=1, source_target_pairs={{4,0},{8,4},{12,8},{5,1},{9,5},{13,9},{6,2},{10,6},{14,10},{7,3},{... | collective-permute-start | bytes 1376264 | tf_op jit(solution)/shard_map/ppermute | solution.py:45
  4.5 13.0 %collective-permute-start = (f32[14,64,128]{2,1,0:T(8,128)S(1)}, f32[14,64,128]{2,1,0:T(8,128)S(1)}, u32[]{:S(2)}, u32[]{:S(2)}) collective-permute-start(f32[14,64,128]{2,1,0:T(8,128)S(1)} %pad_maximum_fusion.5), channel_id=1, source_target_pairs={{0,4},{4,8},{8,12},{1,5},{5,9},{9,13},{2,6},{6,10},{10,14},{3,7},{... | collective-permute-start | bytes 1376264 | tf_op jit(solution)/shard_map/ppermute | solution.py:44
  10.7 6.8 %copy-start.9 = (f32[3,2,64,128]{3,2,1,0:T(8,128)S(1)}, f32[3,2,64,128]{3,2,1,0:T(8,128)}, u32[]{:S(2)}) copy-start(f32[3,2,64,128]{3,2,1,0:T(8,128)} %param.4) | copy-start | bytes 589828
  18.6 6.7 %collective-permute-start.2 = (f32[14,192,128]{2,1,0:T(8,128)}, f32[14,192,128]{2,1,0:T(8,128)}, u32[]{:S(2)}, u32[]{:S(2)}) collective-permute-start(f32[14,192,128]{2,1,0:T(8,128)} %pad_maximum_fusion.1), channel_id=1, source_target_pairs={{0,1},{1,0},{2,3},{3,2},{4,5},{5,4},{6,7},{7,6},{8,9},{9,8},{10,11... | collective-permute-start | bytes 4128776 | tf_op jit(solution)/shard_map/ppermute | solution.py:54
  40.8 3.0 %copy-start = (f32[6,192,128]{2,1,0:T(8,128)S(1)}, f32[6,192,128]{2,1,0:T(8,128)}, u32[]{:S(2)}) copy-start(f32[6,192,128]{2,1,0:T(8,128)} %slice.213) | copy-start | bytes 1769476
  43.8 0.9 %copy-start.1 = (f32[192,192]{1,0:T(8,128)S(1)}, f32[192,192]{1,0:T(8,128)}, u32[]{:S(2)}) copy-start(f32[192,192]{1,0:T(8,128)} %get-tuple-element.20) | copy-start | bytes 442372
  45.8 1.0 %copy-start.3 = (f32[160,176]{1,0:T(8,128)S(1)}, f32[160,176]{1,0:T(8,128)}, u32[]{:S(2)}) copy-start(f32[160,176]{1,0:T(8,128)} %get-tuple-element.15) | copy-start | bytes 337924
  45.8 1.0 %copy-start.5 = (f32[160,176]{1,0:T(8,128)S(1)}, f32[160,176]{1,0:T(8,128)}, u32[]{:S(2)}) copy-start(f32[160,176]{1,0:T(8,128)} %get-tuple-element.16) | copy-start | bytes 337924
  47.0 2.1 %copy-start.21 = (f32[128,160]{1,0:T(8,128)S(1)}, f32[128,160]{1,0:T(8,128)}, u32[]{:S(2)}) copy-start(f32[128,160]{1,0:T(8,128)} %get-tuple-element.14) | copy-start | bytes 245764
  48.4 0.9 %copy-start.20 = (f32[128,160]{1,0:T(8,128)S(1)}, f32[128,160]{1,0:T(8,128)}, u32[]{:S(2)}) copy-start(f32[128,160]{1,0:T(8,128)} %get-tuple-element.13) | copy-start | bytes 245764
  49.1 1.4 %copy-start.12 = (f32[128,160]{0,1:T(8,128)}, f32[128,160]{0,1:T(8,128)S(1)}, u32[]{:S(2)}) copy-start(f32[128,160]{0,1:T(8,128)S(1)} %copy.13) | copy-start | bytes 245764
  49.4 1.2 %copy-start.14 = (f32[128,160]{0,1:T(8,128)}, f32[128,160]{0,1:T(8,128)S(1)}, u32[]{:S(2)}) copy-start(f32[128,160]{0,1:T(8,128)S(1)} %copy.12) | copy-start | bytes 245764
  49.4 1.1 %copy-start.23 = (f32[96,144]{1,0:T(8,128)S(1)}, f32[96,144]{1,0:T(8,128)}, u32[]{:S(2)}) copy-start(f32[96,144]{1,0:T(8,128)} %get-tuple-element.12) | copy-start | bytes 165892
  49.4 1.2 %copy-start.22 = (f32[96,144]{1,0:T(8,128)S(1)}, f32[96,144]{1,0:T(8,128)}, u32[]{:S(2)}) copy-start(f32[96,144]{1,0:T(8,128)} %get-tuple-element.11) | copy-start | bytes 165892
  50.7 1.0 %copy-start.16 = (f32[96,144]{0,1:T(8,128)}, f32[96,144]{0,1:T(8,128)S(1)}, u32[]{:S(2)}) copy-start(f32[96,144]{0,1:T(8,128)S(1)} %copy.15) | copy-start | bytes 165892
  50.8 0.9 %copy-start.18 = (f32[96,144]{0,1:T(8,128)}, f32[96,144]{0,1:T(8,128)S(1)}, u32[]{:S(2)}) copy-start(f32[96,144]{0,1:T(8,128)S(1)} %copy.14) | copy-start | bytes 165892
  51.7 18.1 %copy-start.10 = (f32[3,64,2,128,1]{3,1,4,2,0:T(8,128)}, f32[3,64,2,128,1]{3,1,4,2,0:T(8,128)S(1)}, u32[]{:S(2)}) copy-start(f32[3,64,2,128,1]{3,1,4,2,0:T(8,128)S(1)} %fusion.22) | copy-start | bytes 589828
  51.7 9.4 %collective-permute-start.3 = (f32[6,64,128]{2,1,0:T(8,128)S(1)}, f32[6,64,128]{2,1,0:T(8,128)S(1)}, u32[]{:S(2)}, u32[]{:S(2)}) collective-permute-start(f32[6,64,128]{2,1,0:T(8,128)S(1)} %bitcast.252), channel_id=1, source_target_pairs={{0,6},{4,10},{8,14},{1,7},{5,11},{9,15},{16,22},{20,26},{24,30},{1... | collective-permute-start | bytes 589832 | tf_op jit(solution)/shard_map/ppermute | solution.py:126
  53.0 16.8 %collective-permute-start.4 = (f32[6,64,128]{2,1,0:T(8,128)S(1)}, f32[6,64,128]{2,1,0:T(8,128)S(1)}, u32[]{:S(2)}, u32[]{:S(2)}) collective-permute-start(f32[6,64,128]{2,1,0:T(8,128)S(1)} %bitcast.253), channel_id=1, source_target_pairs={{0,2},{4,6},{8,10},{12,14},{1,3},{5,7},{9,11},{13,15},{16,18},{20,... | collective-permute-start | bytes 589832 | tf_op jit(solution)/shard_map/ppermute | solution.py:127
  54.3 15.5 %collective-permute-start.5 = (f32[6,64,128]{2,1,0:T(8,128)S(1)}, f32[6,64,128]{2,1,0:T(8,128)S(1)}, u32[]{:S(2)}, u32[]{:S(2)}) collective-permute-start(f32[6,64,128]{2,1,0:T(8,128)S(1)} %bitcast.254), channel_id=1, source_target_pairs={{4,2},{8,6},{12,10},{5,3},{9,7},{13,11},{20,18},{24,22},{28,26},{2... | collective-permute-start | bytes 589832 | tf_op jit(solution)/shard_map/ppermute | solution.py:128
  69.9 0.8 copy-start.7
  69.9 2.1 %collective-permute-start.6 = (f32[6,192,128]{2,1,0:T(8,128)S(1)}, f32[6,192,128]{2,1,0:T(8,128)S(1)}, u32[]{:S(2)}, u32[]{:S(2)}) collective-permute-start(f32[6,192,128]{2,1,0:T(8,128)S(1)} %constant_dynamic-update-slice_fusion), channel_id=1, source_target_pairs={{0,1},{1,0},{2,3},{3,2},{4,5},{5,4},{6,7},{7,6},{8,9},{9,8},{10,11... | collective-permute-start | bytes 1769480 | tf_op jit(solution)/shard_map/ppermute | solution.py:54
  74.0 1.1 %copy-start.8 = (f32[6,192,128]{2,1,0:T(8,128)S(1)}, f32[6,192,128]{2,1,0:T(8,128)}, u32[]{:S(2)}) copy-start(f32[6,192,128]{2,1,0:T(8,128)} %copy-done.7) | copy-start | bytes 1769476
  75.1 0.9 %copy-start.2 = (f32[192,192]{1,0:T(8,128)S(1)}, f32[192,192]{1,0:T(8,128)}, u32[]{:S(2)}) copy-start(f32[192,192]{1,0:T(8,128)} %get-tuple-element.20) | copy-start | bytes 442372
  77.2 1.0 %copy-start.4 = (f32[160,176]{1,0:T(8,128)S(1)}, f32[160,176]{1,0:T(8,128)}, u32[]{:S(2)}) copy-start(f32[160,176]{1,0:T(8,128)} %get-tuple-element.15) | copy-start | bytes 337924
  77.2 1.0 %copy-start.6 = (f32[160,176]{1,0:T(8,128)S(1)}, f32[160,176]{1,0:T(8,128)}, u32[]{:S(2)}) copy-start(f32[160,176]{1,0:T(8,128)} %get-tuple-element.16) | copy-start | bytes 337924
  78.3 2.1 %copy-start.13 = (f32[128,160]{0,1:T(8,128)S(1)}, f32[128,160]{0,1:T(8,128)}, u32[]{:S(2)}) copy-start(f32[128,160]{0,1:T(8,128)} %copy-done.12) | copy-start | bytes 245764
  78.3 2.1 %copy-start.15 = (f32[128,160]{0,1:T(8,128)S(1)}, f32[128,160]{0,1:T(8,128)}, u32[]{:S(2)}) copy-start(f32[128,160]{0,1:T(8,128)} %copy-done.14) | copy-start | bytes 245764
  80.5 1.1 %copy-start.17 = (f32[96,144]{0,1:T(8,128)S(1)}, f32[96,144]{0,1:T(8,128)}, u32[]{:S(2)}) copy-start(f32[96,144]{0,1:T(8,128)} %copy-done.16) | copy-start | bytes 165892
  80.5 1.1 %copy-start.19 = (f32[96,144]{0,1:T(8,128)S(1)}, f32[96,144]{0,1:T(8,128)}, u32[]{:S(2)}) copy-start(f32[96,144]{0,1:T(8,128)} %copy-done.18) | copy-start | bytes 165892
  81.6 0.9 %copy-start.11 = (f32[3,64,2,128,1]{3,1,4,2,0:T(8,128)S(1)}, f32[3,64,2,128,1]{3,1,4,2,0:T(8,128)}, u32[]{:S(2)}) copy-start(f32[3,64,2,128,1]{3,1,4,2,0:T(8,128)} %copy-done.10) | copy-start | bytes 589828

commit v10 on v8

--- a/solution.py
+++ b/solution.py
@@ -37,13 +37,42 @@
     )
 
 
-def grow(stack, halo, splits, rider):
+def grow(stack, halo, splits, rider, needs=None):
     tiles = lax.axis_size("tile")
-    wave = lax.axis_index("wave")
     rows, cols = stack.shape[-2], stack.shape[-1]
-    from_prev = lax.ppermute(stack[:, rows - halo:], "tile", [(i, i + 1) for i in range(tiles - 1)])
-    from_next = lax.ppermute(stack[:, :halo], "tile", [(i + 1, i) for i in range(tiles - 1)])
-    tall = jnp.concatenate([from_prev, stack, from_next], axis=-2)
+    needs = [halo] * stack.shape[0] if needs is None else needs
+    slabs, places = [], []
+    for c in sorted(range(len(needs)), key=lambda c: -needs[c]):
+        for n, used in enumerate(slabs):
+            if used + needs[c] <= halo:
+                places.append((c, n, used))
+                slabs[n] += needs[c]
+                break
+        else:
+            places.append((c, len(slabs), 0))
+            slabs.append(needs[c])
+
+    def pack(take):
+        bins = [[] for _ in slabs]
+        for c, n, _ in places:
+            bins[n].append(take(c))
+        return jnp.stack([
+            jnp.concatenate(b + [jnp.zeros((halo - used, cols), stack.dtype)] * (used < halo), axis=0)
+            for b, used in zip(bins, slabs)
+        ])
+
+    sent_prev = pack(lambda c: stack[c, rows - needs[c]:])
+    sent_next = pack(lambda c: stack[c, :needs[c]])
+    from_prev = lax.ppermute(sent_prev, "tile", [(i, i + 1) for i in range(tiles - 1)])
+    from_next = lax.ppermute(sent_next, "tile", [(i + 1, i) for i in range(tiles - 1)])
+    columns = [None] * len(needs)
+    for c, n, at in places:
+        gap = [jnp.zeros((halo - needs[c], cols), stack.dtype)] * (needs[c] < halo)
+        columns[c] = jnp.concatenate(
+            gap + [from_prev[n, at:at + needs[c]], stack[c], from_next[n, at:at + needs[c]]] + gap,
+            axis=0,
+        )
+    tall = jnp.stack(columns)
     rider, tall = lax.optimization_barrier((rider, tall))
     return widen(tall, halo, splits), rider
 
@@ -82,6 +111,7 @@
         reach,
         (2 * illum, 2 * slices),
         band,
+        [reach] * (2 * illum) + [reach - HALF * s for s in range(slices) for _ in range(2)],
     )
     first_field = field_grown.reshape(illum, 2, rows + 2 * reach, cols + reach)
     trans_reg = trans_grown.reshape(slices, 2, rows + 2 * reach, cols + reach)

time: 60.6 us -> 58.2 us (0.960)
  waiting for transfers between devices: 25 us -> 20.9 us
  local copies, waits for them, and re-layouts: 2.65 us -> 6.04 us
  other arithmetic: 6.94 us -> 4.9 us
    ppermute x2, waiting for transfers between devices: 6.72 us -> 2.63 us  [the longest x1 2.63 us: grow(): lax.ppermute(sent_prev, 'tile', [(i, i + 1) for i in range(tiles - 1)])]
    unnamed x8 -> x45, local copies, waits for them, and re-layouts: 0.54 us -> 3.2 us
    concatenate x2 -> x0, other arithmetic: 2.22 us -> none  [the longest x1 1.26 us: grow(): tall = jnp.concatenate([from_prev, stack, from_next], axis=-2)]
    squeeze x0 -> x7, local copies, waits for them, and re-layouts: none -> 0.71 us  [the longest x2 0.64 us: grow(): stack[c]]
  transfers between devices with their start and end apart: 7 -> 7, of which waited for: 6 -> 5; matrix products, arithmetic and copies ran while one was open for 4% -> 8% of each run, Pallas kernels for 0% -> 0%
where the time goes in v10:
time: 58.2 us; the launch traced here: 57.9 us
  waiting for transfers between devices  20.9 us (36%)
  matrix products  12.8 us (22%)
  starting transfers between devices  11.8 us (20%)
  local copies, waits for them, and re-layouts  6.04 us (10%)
  other arithmetic  4.9 us (8%)
  between operations  1.49 us (3%)
    ppermute x1, waiting for transfers between devices, per_device(): mine = lax.ppermute(flat, grid, own_pairs)  9.1 us
    dot_general x8, matrix products, depth_section(): jnp.einsum('dcab,icbj->idaj', row_bands[s], moved, precision=lax.Precisio...  6.53 us
    dot_general x8, matrix products, depth_section(): jnp.einsum('dcyj,icxj->idxy', last_band if s == slices - 1 else col_band,...  6.26 us
    ppermute x1, waiting for transfers between devices, per_device(): from_prev = lax.ppermute(flat[:, rows - reach:], grid, prev_pairs)  4.87 us
    ppermute x2, waiting for transfers between devices, widen(): got = lax.ppermute(tall, 'wave', [(0, 1), (1, 0)])  4.28 us
    ppermute x1, starting transfers between devices, grow(): lax.ppermute(sent_prev, 'tile', [(i, i + 1) for i in range(tiles - 1)])  3.2 us
    unnamed x45, local copies, waits for them, and re-layouts  3.2 us
    ppermute x1, waiting for transfers between devices, grow(): lax.ppermute(sent_prev, 'tile', [(i, i + 1) for i in range(tiles - 1)])  2.63 us
  transfers between devices with their start and end apart: 7, of which 5 were waited for; matrix products, arithmetic and copies ran while one was open for 8% of the time, Pallas kernels for 0%

profile of v10, /device:TPU:15, one launch (start us, length us, event | category | flops | bytes accessed | tf_op | source)
XLA Modules:
  0.0 57.9 jit_solution(11481994619728276019)
XLA Ops:
  0.0 1.4 %fusion.40 = (f32[4,1,64,128]{3,2,1,0:T(8,128)S(1)}, f32[4,1,64,128]{3,2,1,0:T(8,128)S(1)}) fusion(bf16[4,64,128]{2,1,0:T(8,128)(2,1)} %param.5, bf16[4,64,128]{2,1,0:T(8,128)(2,1)} %param.6), kind=kLoop, calls=%fused_computation.98 | loop fusion | flops 163840 | bytes 393216 | tf_op jit(solution)/shard_map/stack | solution.py:25
  1.6 2.1 %collective-permute-start.1 = (f32[11,64,128]{2,1,0:T(8,128)S(1)}, f32[11,64,128]{2,1,0:T(8,128)S(1)}, u32[]{:S(2)}, u32[]{:S(2)}) collective-permute-start(f32[11,64,128]{2,1,0:T(8,128)S(1)} %constant_dynamic-update-slice_fusion.5), channel_id=1, source_target_pairs={{4,0},{8,4},{12,8},{5,1},{9,5},{13,9},{6,2},{10,6},{14,10},{7,3},{... | collective-permute-start | bytes 1081352 | tf_op jit(solution)/shard_map/ppermute | solution.py:67
  3.7 3.2 %collective-permute-start = (f32[11,64,128]{2,1,0:T(8,128)S(1)}, f32[11,64,128]{2,1,0:T(8,128)S(1)}, u32[]{:S(2)}, u32[]{:S(2)}) collective-permute-start(f32[11,64,128]{2,1,0:T(8,128)S(1)} %constant_dynamic-update-slice_fusion), channel_id=1, source_target_pairs={{0,4},{4,8},{8,12},{1,5},{5,9},{9,13},{2,6},{6,10},{10,14},{3,7},{... | collective-permute-start | bytes 1081352 | tf_op jit(solution)/shard_map/ppermute | solution.py:66
  6.9 0.6 %slice_bitcast_fusion.15 = (f32[64,128]{1,0:T(8,128)}, f32[64,128]{1,0:T(8,128)}) fusion(f32[8,64,128]{2,1,0:T(8,128)S(1)} %bitcast.480), kind=kLoop, calls=%fused_computation.184 | loop fusion | bytes 131072 | tf_op jit(solution)/shard_map/squeeze | solution.py:72
  7.6 0.6 %constant_dynamic-update-slice_fusion.24 = (f32[192,128]{1,0:T(8,128)}, f32[192,128]{1,0:T(8,128)}) fusion(), kind=kLoop, calls=%fused_computation.132 | loop fusion | bytes 32768
  8.2 0.6 %constant_dynamic-update-slice_fusion.14 = (f32[192,128]{1,0:T(8,128)}, f32[192,128]{1,0:T(8,128)}) fusion(), kind=kLoop, calls=%fused_computation.122 | loop fusion | bytes 16384
  8.8 0.6 %multiply_reduce_fusion = f32[]{:T(128)} fusion(f32[2,33]{1,0:T(2,128)S(1)} %copy-done.11), kind=kLoop, calls=%fused_computation.238 | loop fusion | flops 131 | bytes 268 | tf_op jit(solution)/shard_map/reduce_sum | solution.py:95
  10.9 0.8 %reshape.48 = f32[2,192,383]{2,1,0:T(8,128)S(1)} reshape(f32[2,73536]{1,0:T(2,128)S(1)} %slice.473) | data formatting | bytes 1176576 | tf_op jit(solution)/shard_map/reshape | solution.py:15
  12.0 2.6 %collective-permute-done = f32[11,64,128]{2,1,0:T(8,128)S(1)} collective-permute-done((f32[11,64,128]{2,1,0:T(8,128)S(1)}, f32[11,64,128]{2,1,0:T(8,128)S(1)}, u32[]{:S(2)}, u32[]{:S(2)}) %collective-permute-start) | collective-permute-done | bytes 360480 | tf_op jit(solution)/shard_map/ppermute | solution.py:66
  14.9 0.6 copy-done.1
  15.7 0.7 %copy-done.2 = f32[192,128]{1,0:T(8,128)S(1)} copy-done((f32[192,128]{1,0:T(8,128)S(1)}, f32[192,128]{1,0:T(8,128)}, u32[]{:S(2)}) %copy-start.2) | copy-done | bytes 98328
  16.4 1.9 %collective-permute-start.2 = (f32[14,192,128]{2,1,0:T(8,128)S(1)}, f32[14,192,128]{2,1,0:T(8,128)S(1)}, u32[]{:S(2)}, u32[]{:S(2)}) collective-permute-start(f32[14,192,128]{2,1,0:T(8,128)S(1)} %constant_dynamic-update-slice_fusion.40), channel_id=1, source_target_pairs={{0,1},{1,0},{2,3},{3,2},{4,5},{5,4},{6,7},{7,6},{8,9},{9,8},{10,11... | collective-permute-start | bytes 4128776 | tf_op jit(solution)/shard_map/ppermute | solution.py:83
  18.5 2.7 %collective-permute-done.2 = f32[14,192,128]{2,1,0:T(8,128)S(1)} collective-permute-done((f32[14,192,128]{2,1,0:T(8,128)S(1)}, f32[14,192,128]{2,1,0:T(8,128)S(1)}, u32[]{:S(2)}, u32[]{:S(2)}) %collective-permute-start.2) | collective-permute-done | bytes 1376288 | tf_op jit(solution)/shard_map/ppermute | solution.py:83
  21.4 0.5 maximum_select_fusion
  23.2 1.0 %convolution_bitcast_fusion.3 = f32[3,2,160,192,1]{3,2,1,4,0:T(8,128)S(1)} fusion(f32[3,1,192,192]{3,2,1,0:T(8,128)S(1)} %get-tuple-element.18, f32[3,1,192,192]{3,2,1,0:T(8,128)S(1)} %get-tuple-element.17, f32[2,2,192,192]{3,2,1,0:T(8,128)S(1)} %pad_maximum_fusion), kind=kOutput, calls=%fused_computation.5 | convolution fusion | flops 424894464 | bytes 2572288 | tf_op jit(solution)/shard_map/dcab,icbj->idaj/dot_general | solution.py:130
  24.2 1.0 %convolution_bitcast_fusion.2 = f32[3,2,160,192]{3,2,1,0:T(8,128)S(1)} fusion(f32[3,2,160,192,1]{3,2,1,4,0:T(8,128)S(1)} %convolution_bitcast_fusion.3, f32[2,2,192,192]{3,2,1,0:T(8,128)S(1)} %pad_maximum_fusion), kind=kOutput, calls=%fused_computation.4 | convolution fusion | flops 424673280 | bytes 2064384 | tf_op jit(solution)/shard_map/dcyj,icxj->idxy/dot_general | solution.py:133
  25.3 1.4 %convolution_bitcast_fusion.11 = f32[3,2,128,192,1]{2,3,1,4,0:T(8,128)S(1)} fusion(f32[3,1,160,192]{3,2,1,0:T(8,128)S(1)} %get-tuple-element.28, f32[3,1,160,192]{3,2,1,0:T(8,128)S(1)} %get-tuple-element.27, f32[2,2,192,192]{3,2,1,0:T(8,128)S(1)} %pad_maximum_fusion), kind=kOutput, calls=%fused_computation.13 | convolution fusion | flops 283299840 | bytes 2097152 | tf_op jit(solution)/shard_map/dcab,icbj->idaj/dot_general | solution.py:130
  26.7 0.8 %convolution_bitcast_fusion.10 = f32[3,2,128,192]{2,3,1,0:T(8,128)S(1)} fusion(f32[3,2,128,192,1]{2,3,1,4,0:T(8,128)S(1)} %convolution_bitcast_fusion.11, f32[2,2,192,192]{3,2,1,0:T(8,128)S(1)} %pad_maximum_fusion), kind=kOutput, calls=%fused_computation.12 | convolution fusion | flops 339738624 | bytes 1769472 | tf_op jit(solution)/shard_map/dcyj,icxj->idxy/dot_general | solution.py:133
  28.2 0.7 %convolution_bitcast_fusion.8 = f32[3,2,96,192]{3,2,1,0:T(8,128)S(1)} fusion(f32[3,2,96,192,1]{3,2,1,4,0:T(8,128)S(1)} %convolution_bitcast_fusion.9, f32[2,2,192,192]{3,2,1,0:T(8,128)S(1)} %pad_maximum_fusion), kind=kOutput, calls=%fused_computation.10 | convolution fusion | flops 254803968 | bytes 1474560 | tf_op jit(solution)/shard_map/dcyj,icxj->idxy/dot_general | solution.py:133
  29.8 1.3 %collective-permute-start.3 = (f32[6,64,128]{2,1,0:T(8,128)S(1)}, f32[6,64,128]{2,1,0:T(8,128)S(1)}, u32[]{:S(2)}, u32[]{:S(2)}) collective-permute-start(f32[6,64,128]{2,1,0:T(8,128)S(1)} %bitcast.485), channel_id=1, source_target_pairs={{0,6},{4,10},{8,14},{1,7},{5,11},{9,15},{16,22},{20,26},{24,30},{1... | collective-permute-start | bytes 589832 | tf_op jit(solution)/shard_map/ppermute | solution.py:155
  31.1 1.3 %collective-permute-start.4 = (f32[6,64,128]{2,1,0:T(8,128)S(1)}, f32[6,64,128]{2,1,0:T(8,128)S(1)}, u32[]{:S(2)}, u32[]{:S(2)}) collective-permute-start(f32[6,64,128]{2,1,0:T(8,128)S(1)} %bitcast.486), channel_id=1, source_target_pairs={{0,2},{4,6},{8,10},{12,14},{1,3},{5,7},{9,11},{13,15},{16,18},{20,... | collective-permute-start | bytes 589832 | tf_op jit(solution)/shard_map/ppermute | solution.py:156
  32.4 1.5 %collective-permute-start.5 = (f32[6,64,128]{2,1,0:T(8,128)S(1)}, f32[6,64,128]{2,1,0:T(8,128)S(1)}, u32[]{:S(2)}, u32[]{:S(2)}) collective-permute-start(f32[6,64,128]{2,1,0:T(8,128)S(1)} %bitcast.487), channel_id=1, source_target_pairs={{4,2},{8,6},{12,10},{5,3},{9,7},{13,11},{20,18},{24,22},{28,26},{2... | collective-permute-start | bytes 589832 | tf_op jit(solution)/shard_map/ppermute | solution.py:157
  33.9 4.9 %collective-permute-done.3 = f32[6,64,128]{2,1,0:T(8,128)S(1)} collective-permute-done((f32[6,64,128]{2,1,0:T(8,128)S(1)}, f32[6,64,128]{2,1,0:T(8,128)S(1)}, u32[]{:S(2)}, u32[]{:S(2)}) %collective-permute-start.3) | collective-permute-done | bytes 196640 | tf_op jit(solution)/shard_map/ppermute | solution.py:155
  38.7 9.1 %collective-permute-done.4 = f32[6,64,128]{2,1,0:T(8,128)S(1)} collective-permute-done((f32[6,64,128]{2,1,0:T(8,128)S(1)}, f32[6,64,128]{2,1,0:T(8,128)S(1)}, u32[]{:S(2)}, u32[]{:S(2)}) %collective-permute-start.4) | collective-permute-done | bytes 196640 | tf_op jit(solution)/shard_map/ppermute | solution.py:156
  47.9 0.5 collective-permute-start.6
  48.4 1.6 %collective-permute-done.6 = f32[6,192,128]{2,1,0:T(8,128)S(1)} collective-permute-done((f32[6,192,128]{2,1,0:T(8,128)S(1)}, f32[6,192,128]{2,1,0:T(8,128)S(1)}, u32[]{:S(2)}, u32[]{:S(2)}) %collective-permute-start.6) | collective-permute-done | bytes 589856 | tf_op jit(solution)/shard_map/ppermute | solution.py:83
  50.8 1.0 %convolution_bitcast_fusion.1 = f32[3,2,160,192,1]{3,2,1,4,0:T(8,128)S(1)} fusion(f32[3,1,192,192]{3,2,1,0:T(8,128)S(1)} %get-tuple-element.10, f32[3,1,192,192]{3,2,1,0:T(8,128)S(1)} %get-tuple-element.9, f32[2,2,192,192]{3,2,1,0:T(8,128)S(1)} %pad_maximum_fusion), kind=kOutput, calls=%fused_computation.3 | convolution fusion | flops 424894464 | bytes 2572288 | tf_op jit(solution)/shard_map/dcab,icbj->idaj/dot_general | solution.py:130
  51.8 1.0 %convolution_bitcast_fusion = f32[3,2,160,192]{3,2,1,0:T(8,128)S(1)} fusion(f32[3,2,160,192,1]{3,2,1,4,0:T(8,128)S(1)} %convolution_bitcast_fusion.1, f32[2,2,192,192]{3,2,1,0:T(8,128)S(1)} %pad_maximum_fusion), kind=kOutput, calls=%fused_computation.2 | convolution fusion | flops 424673280 | bytes 2064384 | tf_op jit(solution)/shard_map/dcyj,icxj->idxy/dot_general | solution.py:133
  52.9 1.4 %convolution_bitcast_fusion.7 = f32[3,2,128,192,1]{2,3,1,4,0:T(8,128)S(1)} fusion(f32[3,1,160,192]{3,2,1,0:T(8,128)S(1)} %get-tuple-element.26, f32[3,1,160,192]{3,2,1,0:T(8,128)S(1)} %get-tuple-element.25, f32[2,2,192,192]{3,2,1,0:T(8,128)S(1)} %pad_maximum_fusion), kind=kOutput, calls=%fused_computation.9 | convolution fusion | flops 283299840 | bytes 2097152 | tf_op jit(solution)/shard_map/dcab,icbj->idaj/dot_general | solution.py:130
  54.3 0.8 %convolution_bitcast_fusion.6 = f32[3,2,128,192]{2,3,1,0:T(8,128)S(1)} fusion(f32[3,2,128,192,1]{2,3,1,4,0:T(8,128)S(1)} %convolution_bitcast_fusion.7, f32[2,2,192,192]{3,2,1,0:T(8,128)S(1)} %pad_maximum_fusion), kind=kOutput, calls=%fused_computation.8 | convolution fusion | flops 339738624 | bytes 1769472 | tf_op jit(solution)/shard_map/dcyj,icxj->idxy/dot_general | solution.py:133
  55.6 0.7 %convolution_bitcast_fusion.4 = f32[3,2,96,192]{3,2,1,0:T(8,128)S(1)} fusion(f32[3,2,96,192,1]{3,2,1,4,0:T(8,128)S(1)} %convolution_bitcast_fusion.5, f32[2,2,192,192]{3,2,1,0:T(8,128)S(1)} %pad_maximum_fusion), kind=kOutput, calls=%fused_computation.6 | convolution fusion | flops 254803968 | bytes 1474560 | tf_op jit(solution)/shard_map/dcyj,icxj->idxy/dot_general | solution.py:133
  56.8 1.1 %fusion.5 = f32[1,3,2,64,128]{4,3,2,1,0:T(8,128)} fusion(f32[3,2,64,192,1]{3,2,1,4,0:T(8,128)S(1)} %convolution_bitcast_fusion.12, f32[3,64,2,128,1]{3,1,4,2,0:T(8,128)S(1)} %fusion.29, f32[2,2,192,192]{3,2,1,0:T(8,128)S(1)} %pad_maximum_fusion, pred[]{:T(512)S(6)} %eq.13, pred[]{:T(512)S(6)} %eq.14, pred[]{:T(512)S(6)} %eq.12), kind=kOutput, calls=%fused_computation.26 | convolution fusion | flops 113442816 | bytes 1835011 | tf_op jit(solution)/shard_map/dcyj,icxj->idxy/dot_general | solution.py:133
  (109 shorter events, 6.7 us)
Async XLA Ops:
  0.0 1.5 %copy-start = (f32[3,2,64,128]{3,2,1,0:T(8,128)S(1)}, f32[3,2,64,128]{3,2,1,0:T(8,128)}, u32[]{:S(2)}) copy-start(f32[3,2,64,128]{3,2,1,0:T(8,128)} %param.4) | copy-start | bytes 589828
  1.4 7.4 %copy-start.11 = (f32[2,33]{1,0:T(2,128)S(1)}, f32[2,33]{1,0:T(2,128)}, u32[]{:S(2)}) copy-start(f32[2,33]{1,0:T(2,128)} %param.7) | copy-start | bytes 796
  1.6 13.1 %collective-permute-start.1 = (f32[11,64,128]{2,1,0:T(8,128)S(1)}, f32[11,64,128]{2,1,0:T(8,128)S(1)}, u32[]{:S(2)}, u32[]{:S(2)}) collective-permute-start(f32[11,64,128]{2,1,0:T(8,128)S(1)} %constant_dynamic-update-slice_fusion.5), channel_id=1, source_target_pairs={{4,0},{8,4},{12,8},{5,1},{9,5},{13,9},{6,2},{10,6},{14,10},{7,3},{... | collective-permute-start | bytes 1081352 | tf_op jit(solution)/shard_map/ppermute | solution.py:67
  3.7 10.9 %collective-permute-start = (f32[11,64,128]{2,1,0:T(8,128)S(1)}, f32[11,64,128]{2,1,0:T(8,128)S(1)}, u32[]{:S(2)}, u32[]{:S(2)}) collective-permute-start(f32[11,64,128]{2,1,0:T(8,128)S(1)} %constant_dynamic-update-slice_fusion), channel_id=1, source_target_pairs={{0,4},{4,8},{8,12},{1,5},{5,9},{9,13},{2,6},{6,10},{10,14},{3,7},{... | collective-permute-start | bytes 1081352 | tf_op jit(solution)/shard_map/ppermute | solution.py:66
  11.8 2.8 %copy-start.5 = (f32[192,128]{1,0:T(8,128)S(1)}, f32[192,128]{1,0:T(8,128)}, u32[]{:S(2)}) copy-start(f32[192,128]{1,0:T(8,128)} %get-tuple-element.102) | copy-start | bytes 294916
  11.8 2.8 %copy-start.6 = (f32[192,128]{1,0:T(8,128)S(1)}, f32[192,128]{1,0:T(8,128)}, u32[]{:S(2)}) copy-start(f32[192,128]{1,0:T(8,128)} %get-tuple-element.103) | copy-start | bytes 294916
  11.8 2.8 %copy-start.9 = (f32[192,128]{1,0:T(8,128)S(1)}, f32[192,128]{1,0:T(8,128)}, u32[]{:S(2)}) copy-start(f32[192,128]{1,0:T(8,128)} %get-tuple-element.104) | copy-start | bytes 294916
  11.8 2.8 %copy-start.10 = (f32[192,128]{1,0:T(8,128)S(1)}, f32[192,128]{1,0:T(8,128)}, u32[]{:S(2)}) copy-start(f32[192,128]{1,0:T(8,128)} %get-tuple-element.105) | copy-start | bytes 294916
  14.7 0.9 %copy-start.8 = (f32[64,128]{1,0:T(8,128)S(1)}, f32[64,128]{1,0:T(8,128)}, u32[]{:S(2)}) copy-start(f32[64,128]{1,0:T(8,128)} %get-tuple-element.77) | copy-start | bytes 98308
  14.7 0.9 %copy-start.7 = (f32[64,128]{1,0:T(8,128)S(1)}, f32[64,128]{1,0:T(8,128)}, u32[]{:S(2)}) copy-start(f32[64,128]{1,0:T(8,128)} %get-tuple-element.76) | copy-start | bytes 98308
  14.8 0.6 %copy-start.1 = (f32[192,128]{1,0:T(8,128)}, f32[192,128]{1,0:T(8,128)S(1)}, u32[]{:S(2)}) copy-start(f32[192,128]{1,0:T(8,128)S(1)} %constant_dynamic-update-slice_fusion.30) | copy-start | bytes 294916
  14.8 0.6 %copy-start.3 = (f32[192,128]{1,0:T(8,128)}, f32[192,128]{1,0:T(8,128)S(1)}, u32[]{:S(2)}) copy-start(f32[192,128]{1,0:T(8,128)S(1)} %constant_dynamic-update-slice_fusion.35) | copy-start | bytes 294916
  15.5 0.9 %copy-start.2 = (f32[192,128]{1,0:T(8,128)S(1)}, f32[192,128]{1,0:T(8,128)}, u32[]{:S(2)}) copy-start(f32[192,128]{1,0:T(8,128)} %copy-done.1) | copy-start | bytes 294916
  15.5 0.9 %copy-start.4 = (f32[192,128]{1,0:T(8,128)S(1)}, f32[192,128]{1,0:T(8,128)}, u32[]{:S(2)}) copy-start(f32[192,128]{1,0:T(8,128)} %copy-done.3) | copy-start | bytes 294916
  16.4 4.7 %collective-permute-start.2 = (f32[14,192,128]{2,1,0:T(8,128)S(1)}, f32[14,192,128]{2,1,0:T(8,128)S(1)}, u32[]{:S(2)}, u32[]{:S(2)}) collective-permute-start(f32[14,192,128]{2,1,0:T(8,128)S(1)} %constant_dynamic-update-slice_fusion.40), channel_id=1, source_target_pairs={{0,1},{1,0},{2,3},{3,2},{4,5},{5,4},{6,7},{7,6},{8,9},{9,8},{10,11... | collective-permute-start | bytes 4128776 | tf_op jit(solution)/shard_map/ppermute | solution.py:83
  29.8 8.9 %collective-permute-start.3 = (f32[6,64,128]{2,1,0:T(8,128)S(1)}, f32[6,64,128]{2,1,0:T(8,128)S(1)}, u32[]{:S(2)}, u32[]{:S(2)}) collective-permute-start(f32[6,64,128]{2,1,0:T(8,128)S(1)} %bitcast.485), channel_id=1, source_target_pairs={{0,6},{4,10},{8,14},{1,7},{5,11},{9,15},{16,22},{20,26},{24,30},{1... | collective-permute-start | bytes 589832 | tf_op jit(solution)/shard_map/ppermute | solution.py:155
  31.1 16.8 %collective-permute-start.4 = (f32[6,64,128]{2,1,0:T(8,128)S(1)}, f32[6,64,128]{2,1,0:T(8,128)S(1)}, u32[]{:S(2)}, u32[]{:S(2)}) collective-permute-start(f32[6,64,128]{2,1,0:T(8,128)S(1)} %bitcast.486), channel_id=1, source_target_pairs={{0,2},{4,6},{8,10},{12,14},{1,3},{5,7},{9,11},{13,15},{16,18},{20,... | collective-permute-start | bytes 589832 | tf_op jit(solution)/shard_map/ppermute | solution.py:156
  32.4 15.5 %collective-permute-start.5 = (f32[6,64,128]{2,1,0:T(8,128)S(1)}, f32[6,64,128]{2,1,0:T(8,128)S(1)}, u32[]{:S(2)}, u32[]{:S(2)}) collective-permute-start(f32[6,64,128]{2,1,0:T(8,128)S(1)} %bitcast.487), channel_id=1, source_target_pairs={{4,2},{8,6},{12,10},{5,3},{9,7},{13,11},{20,18},{24,22},{28,26},{2... | collective-permute-start | bytes 589832 | tf_op jit(solution)/shard_map/ppermute | solution.py:157
  47.9 2.2 %collective-permute-start.6 = (f32[6,192,128]{2,1,0:T(8,128)S(1)}, f32[6,192,128]{2,1,0:T(8,128)S(1)}, u32[]{:S(2)}, u32[]{:S(2)}) collective-permute-start(f32[6,192,128]{2,1,0:T(8,128)S(1)} %constant_dynamic-update-slice_fusion.54), channel_id=1, source_target_pairs={{0,1},{1,0},{2,3},{3,2},{4,5},{5,4},{6,7},{7,6},{8,9},{9,8},{10,11... | collective-permute-start | bytes 1769480 | tf_op jit(solution)/shard_map/ppermute | solution.py:83

commit v11 on v10

--- a/solution.py
+++ b/solution.py
@@ -79,14 +79,27 @@
 
 def widen(tall, halo, splits):
     wave = lax.axis_index("wave")
-    cols = tall.shape[-1]
-    got = lax.ppermute(tall, "wave", [(0, 1), (1, 0)])
+    count, cols = tall.shape[0], tall.shape[-1]
+    if 2 * halo == cols:
+        if count % 2:
+            tall = jnp.concatenate([tall, jnp.zeros_like(tall[:1])])
+        half = tall.shape[0] // 2
+        slabs = jnp.where(
+            wave == 0,
+            jnp.concatenate([tall[:half, :, halo:], tall[half:, :, halo:]], axis=-1),
+            jnp.concatenate([tall[:half, :, :halo], tall[half:, :, :halo]], axis=-1),
+        )
+        got = lax.ppermute(slabs, "wave", [(0, 1), (1, 0)])
+        parts = jnp.concatenate([got[..., :halo], got[..., halo:]], axis=0)
+    else:
+        got = lax.ppermute(tall, "wave", [(0, 1), (1, 0)])
+        parts = jnp.where(wave == 0, got[..., :halo], got[..., cols - halo:])
     out, start = [], 0
     for size in splits:
-        own, other = tall[start:start + size], got[start:start + size]
+        own, part = tall[start:start + size], parts[start:start + size]
         start += size
-        left = jnp.concatenate([own, other[..., :halo]], axis=-1)
-        right = jnp.concatenate([other[..., cols - halo:], own], axis=-1)
+        left = jnp.concatenate([own, part], axis=-1)
+        right = jnp.concatenate([part, own], axis=-1)
         out.append(jnp.where(wave == 0, left, right))
     return out
 

time: 58.2 us -> 56.6 us (0.973)
  local copies, waits for them, and re-layouts: 6.04 us -> 4.54 us
  waiting for transfers between devices: 20.9 us -> 20.1 us
  other arithmetic: 4.9 us -> 5.61 us
    ppermute x2, waiting for transfers between devices: 4.28 us -> 2.88 us  [widen(): got = lax.ppermute(slabs, 'wave', [(0, 1), (1, 0)])]
    unnamed x45 -> x33, local copies, waits for them, and re-layouts: 3.2 us -> 1.91 us
    ppermute x1, waiting for transfers between devices: 2.63 us -> 3.3 us  [grow(): lax.ppermute(sent_prev, 'tile', [(i, i + 1) for i in range(tiles - 1)])]
    select_n x0 -> x2, other arithmetic: none -> 0.65 us  [widen(): jnp.where(wave == 0, jnp.concatenate([tall[:half, :, halo:], tall[half:,...]
    squeeze x2, local copies, waits for them, and re-layouts: 0.64 us -> 0.02 us  [grow(): stack[c]]
    slice x5 -> x7, local copies, waits for them, and re-layouts: 0.8 us -> 1.21 us  [the longest x2 0.69 us: widen(): tall[:half, :, :halo]]
  transfers between devices with their start and end apart: 7 -> 7, of which waited for: 5 -> 5; matrix products, arithmetic and copies ran while one was open for 8% -> 7% of each run, Pallas kernels for 0% -> 0%
where the time goes in v11:
time: 56.6 us; the launch traced here: 56.4 us
  waiting for transfers between devices  20.1 us (36%)
  matrix products  12.8 us (23%)
  starting transfers between devices  11.8 us (21%)
  other arithmetic  5.61 us (10%)
  local copies, waits for them, and re-layouts  4.54 us (8%)
  between operations  1.47 us (3%)
    ppermute x1, waiting for transfers between devices, per_device(): mine = lax.ppermute(flat, grid, own_pairs)  9.09 us
    dot_general x8, matrix products, depth_section(): jnp.einsum('dcab,icbj->idaj', row_bands[s], moved, precision=lax.Precisio...  6.54 us
    dot_general x8, matrix products, depth_section(): jnp.einsum('dcyj,icxj->idxy', last_band if s == slices - 1 else col_band,...  6.26 us
    ppermute x1, waiting for transfers between devices, per_device(): from_prev = lax.ppermute(flat[:, rows - reach:], grid, prev_pairs)  4.87 us
    ppermute x1, waiting for transfers between devices, grow(): lax.ppermute(sent_prev, 'tile', [(i, i + 1) for i in range(tiles - 1)])  3.3 us
    ppermute x1, starting transfers between devices, grow(): lax.ppermute(sent_prev, 'tile', [(i, i + 1) for i in range(tiles - 1)])  3.2 us
    ppermute x2, waiting for transfers between devices, widen(): got = lax.ppermute(slabs, 'wave', [(0, 1), (1, 0)])  2.88 us
    ppermute x2, starting transfers between devices, widen(): got = lax.ppermute(slabs, 'wave', [(0, 1), (1, 0)])  2.47 us
  transfers between devices with their start and end apart: 7, of which 5 were waited for; matrix products, arithmetic and copies ran while one was open for 7% of the time, Pallas kernels for 0%

profile of v11, /device:TPU:15, one launch (start us, length us, event | category | flops | bytes accessed | tf_op | source)
XLA Modules:
  0.0 56.4 jit_solution(15814159256794902987)
XLA Ops:
  0.0 1.4 %fusion.40 = (f32[4,1,64,128]{3,2,1,0:T(8,128)S(1)}, f32[4,1,64,128]{3,2,1,0:T(8,128)S(1)}) fusion(bf16[4,64,128]{2,1,0:T(8,128)(2,1)} %param.5, bf16[4,64,128]{2,1,0:T(8,128)(2,1)} %param.6), kind=kLoop, calls=%fused_computation.102 | loop fusion | flops 163840 | bytes 393216 | tf_op jit(solution)/shard_map/stack | solution.py:25
  1.6 2.1 %collective-permute-start.1 = (f32[11,64,128]{2,1,0:T(8,128)S(1)}, f32[11,64,128]{2,1,0:T(8,128)S(1)}, u32[]{:S(2)}, u32[]{:S(2)}) collective-permute-start(f32[11,64,128]{2,1,0:T(8,128)S(1)} %constant_dynamic-update-slice_fusion.5), channel_id=1, source_target_pairs={{4,0},{8,4},{12,8},{5,1},{9,5},{13,9},{6,2},{10,6},{14,10},{7,3},{... | collective-permute-start | bytes 1081352 | tf_op jit(solution)/shard_map/ppermute | solution.py:67
  3.7 3.2 %collective-permute-start = (f32[11,64,128]{2,1,0:T(8,128)S(1)}, f32[11,64,128]{2,1,0:T(8,128)S(1)}, u32[]{:S(2)}, u32[]{:S(2)}) collective-permute-start(f32[11,64,128]{2,1,0:T(8,128)S(1)} %constant_dynamic-update-slice_fusion), channel_id=1, source_target_pairs={{0,4},{4,8},{8,12},{1,5},{5,9},{9,13},{2,6},{6,10},{10,14},{3,7},{... | collective-permute-start | bytes 1081352 | tf_op jit(solution)/shard_map/ppermute | solution.py:66
  7.0 0.6 %constant_dynamic-update-slice_fusion.24 = (f32[192,128]{1,0:T(8,128)}, f32[192,128]{1,0:T(8,128)}) fusion(), kind=kLoop, calls=%fused_computation.136 | loop fusion | bytes 32768
  7.6 0.6 %constant_dynamic-update-slice_fusion.14 = (f32[192,128]{1,0:T(8,128)}, f32[192,128]{1,0:T(8,128)}) fusion(), kind=kLoop, calls=%fused_computation.126 | loop fusion | bytes 16384
  8.2 0.6 %multiply_reduce_fusion = f32[]{:T(128)} fusion(f32[2,33]{1,0:T(2,128)S(1)} %copy-done.5), kind=kLoop, calls=%fused_computation.242 | loop fusion | flops 131 | bytes 268 | tf_op jit(solution)/shard_map/reduce_sum | solution.py:108
  9.7 0.5 copy.54
  10.2 0.8 %reshape.48 = f32[2,192,383]{2,1,0:T(8,128)S(1)} reshape(f32[2,73536]{1,0:T(2,128)S(1)} %slice.500) | data formatting | bytes 1176576 | tf_op jit(solution)/shard_map/reshape | solution.py:15
  11.3 3.3 %collective-permute-done = f32[11,64,128]{2,1,0:T(8,128)S(1)} collective-permute-done((f32[11,64,128]{2,1,0:T(8,128)S(1)}, f32[11,64,128]{2,1,0:T(8,128)S(1)}, u32[]{:S(2)}, u32[]{:S(2)}) %collective-permute-start) | collective-permute-done | bytes 360480 | tf_op jit(solution)/shard_map/ppermute | solution.py:66
  15.1 0.5 fusion.57
  16.0 1.9 %collective-permute-start.2 = (f32[7,192,128]{2,1,0:T(8,128)S(1)}, f32[7,192,128]{2,1,0:T(8,128)S(1)}, u32[]{:S(2)}, u32[]{:S(2)}) collective-permute-start(f32[7,192,128]{2,1,0:T(8,128)S(1)} %maximum_select_fusion.4), channel_id=1, source_target_pairs={{0,1},{1,0},{2,3},{3,2},{4,5},{5,4},{6,7},{7,6},{8,9},{9,8},{10,11... | collective-permute-start | bytes 2064392 | tf_op jit(solution)/shard_map/ppermute | solution.py:92
  18.0 1.7 %collective-permute-done.2 = f32[7,192,128]{2,1,0:T(8,128)S(1)} collective-permute-done((f32[7,192,128]{2,1,0:T(8,128)S(1)}, f32[7,192,128]{2,1,0:T(8,128)S(1)}, u32[]{:S(2)}, u32[]{:S(2)}) %collective-permute-start.2) | collective-permute-done | bytes 688160 | tf_op jit(solution)/shard_map/ppermute | solution.py:92
  20.0 0.5 maximum_select_fusion
  20.5 0.5 maximum_select_fusion.1
  21.6 1.0 %convolution_bitcast_fusion.3 = f32[3,2,160,192,1]{3,2,1,4,0:T(8,128)S(1)} fusion(f32[3,1,192,192]{3,2,1,0:T(8,128)S(1)} %get-tuple-element.18, f32[3,1,192,192]{3,2,1,0:T(8,128)S(1)} %get-tuple-element.17, f32[2,2,192,192]{3,2,1,0:T(8,128)S(1)} %pad_maximum_fusion.1), kind=kOutput, calls=%fused_computation.5 | convolution fusion | flops 424894464 | bytes 2572288 | tf_op jit(solution)/shard_map/dcab,icbj->idaj/dot_general | solution.py:143
  22.6 1.0 %convolution_bitcast_fusion.2 = f32[3,2,160,192]{3,2,1,0:T(8,128)S(1)} fusion(f32[3,2,160,192,1]{3,2,1,4,0:T(8,128)S(1)} %convolution_bitcast_fusion.3, f32[2,2,192,192]{3,2,1,0:T(8,128)S(1)} %pad_maximum_fusion.1), kind=kOutput, calls=%fused_computation.4 | convolution fusion | flops 424673280 | bytes 2064384 | tf_op jit(solution)/shard_map/dcyj,icxj->idxy/dot_general | solution.py:146
  23.7 1.4 %convolution_bitcast_fusion.11 = f32[3,2,128,192,1]{2,3,1,4,0:T(8,128)S(1)} fusion(f32[3,1,160,192]{3,2,1,0:T(8,128)S(1)} %get-tuple-element.28, f32[3,1,160,192]{3,2,1,0:T(8,128)S(1)} %get-tuple-element.27, f32[2,2,192,192]{3,2,1,0:T(8,128)S(1)} %pad_maximum_fusion.1), kind=kOutput, calls=%fused_computation.13 | convolution fusion | flops 283299840 | bytes 2097152 | tf_op jit(solution)/shard_map/dcab,icbj->idaj/dot_general | solution.py:143
  25.2 0.8 %convolution_bitcast_fusion.10 = f32[3,2,128,192]{2,3,1,0:T(8,128)S(1)} fusion(f32[3,2,128,192,1]{2,3,1,4,0:T(8,128)S(1)} %convolution_bitcast_fusion.11, f32[2,2,192,192]{3,2,1,0:T(8,128)S(1)} %pad_maximum_fusion.1), kind=kOutput, calls=%fused_computation.12 | convolution fusion | flops 339738624 | bytes 1769472 | tf_op jit(solution)/shard_map/dcyj,icxj->idxy/dot_general | solution.py:146
  26.6 0.7 %convolution_bitcast_fusion.8 = f32[3,2,96,192]{3,2,1,0:T(8,128)S(1)} fusion(f32[3,2,96,192,1]{3,2,1,4,0:T(8,128)S(1)} %convolution_bitcast_fusion.9, f32[2,2,192,192]{3,2,1,0:T(8,128)S(1)} %pad_maximum_fusion.1), kind=kOutput, calls=%fused_computation.10 | convolution fusion | flops 254803968 | bytes 1474560 | tf_op jit(solution)/shard_map/dcyj,icxj->idxy/dot_general | solution.py:146
  28.2 1.3 %collective-permute-start.3 = (f32[6,64,128]{2,1,0:T(8,128)S(1)}, f32[6,64,128]{2,1,0:T(8,128)S(1)}, u32[]{:S(2)}, u32[]{:S(2)}) collective-permute-start(f32[6,64,128]{2,1,0:T(8,128)S(1)} %bitcast.479), channel_id=1, source_target_pairs={{0,6},{4,10},{8,14},{1,7},{5,11},{9,15},{16,22},{20,26},{24,30},{1... | collective-permute-start | bytes 589832 | tf_op jit(solution)/shard_map/ppermute | solution.py:168
  29.5 1.5 %collective-permute-start.4 = (f32[6,64,128]{2,1,0:T(8,128)S(1)}, f32[6,64,128]{2,1,0:T(8,128)S(1)}, u32[]{:S(2)}, u32[]{:S(2)}) collective-permute-start(f32[6,64,128]{2,1,0:T(8,128)S(1)} %bitcast.480), channel_id=1, source_target_pairs={{0,2},{4,6},{8,10},{12,14},{1,3},{5,7},{9,11},{13,15},{16,18},{20,... | collective-permute-start | bytes 589832 | tf_op jit(solution)/shard_map/ppermute | solution.py:169
  31.0 1.3 %collective-permute-start.5 = (f32[6,64,128]{2,1,0:T(8,128)S(1)}, f32[6,64,128]{2,1,0:T(8,128)S(1)}, u32[]{:S(2)}, u32[]{:S(2)}) collective-permute-start(f32[6,64,128]{2,1,0:T(8,128)S(1)} %bitcast.481), channel_id=1, source_target_pairs={{4,2},{8,6},{12,10},{5,3},{9,7},{13,11},{20,18},{24,22},{28,26},{2... | collective-permute-start | bytes 589832 | tf_op jit(solution)/shard_map/ppermute | solution.py:170
  32.3 4.9 %collective-permute-done.3 = f32[6,64,128]{2,1,0:T(8,128)S(1)} collective-permute-done((f32[6,64,128]{2,1,0:T(8,128)S(1)}, f32[6,64,128]{2,1,0:T(8,128)S(1)}, u32[]{:S(2)}, u32[]{:S(2)}) %collective-permute-start.3) | collective-permute-done | bytes 196640 | tf_op jit(solution)/shard_map/ppermute | solution.py:168
  37.2 9.1 %collective-permute-done.4 = f32[6,64,128]{2,1,0:T(8,128)S(1)} collective-permute-done((f32[6,64,128]{2,1,0:T(8,128)S(1)}, f32[6,64,128]{2,1,0:T(8,128)S(1)}, u32[]{:S(2)}, u32[]{:S(2)}) %collective-permute-start.4) | collective-permute-done | bytes 196640 | tf_op jit(solution)/shard_map/ppermute | solution.py:169
  46.8 0.5 collective-permute-start.6
  47.3 1.2 %collective-permute-done.6 = f32[3,192,128]{2,1,0:T(8,128)S(1)} collective-permute-done((f32[3,192,128]{2,1,0:T(8,128)S(1)}, f32[3,192,128]{2,1,0:T(8,128)S(1)}, u32[]{:S(2)}, u32[]{:S(2)}) %collective-permute-start.6) | collective-permute-done | bytes 294944 | tf_op jit(solution)/shard_map/ppermute | solution.py:92
  49.3 1.0 %convolution_bitcast_fusion.1 = f32[3,2,160,192,1]{3,2,1,4,0:T(8,128)S(1)} fusion(f32[3,1,192,192]{3,2,1,0:T(8,128)S(1)} %get-tuple-element.10, f32[3,1,192,192]{3,2,1,0:T(8,128)S(1)} %get-tuple-element.9, f32[2,2,192,192]{3,2,1,0:T(8,128)S(1)} %pad_maximum_fusion.1), kind=kOutput, calls=%fused_computation.3 | convolution fusion | flops 424894464 | bytes 2572288 | tf_op jit(solution)/shard_map/dcab,icbj->idaj/dot_general | solution.py:143
  50.3 1.0 %convolution_bitcast_fusion = f32[3,2,160,192]{3,2,1,0:T(8,128)S(1)} fusion(f32[3,2,160,192,1]{3,2,1,4,0:T(8,128)S(1)} %convolution_bitcast_fusion.1, f32[2,2,192,192]{3,2,1,0:T(8,128)S(1)} %pad_maximum_fusion.1), kind=kOutput, calls=%fused_computation.2 | convolution fusion | flops 424673280 | bytes 2064384 | tf_op jit(solution)/shard_map/dcyj,icxj->idxy/dot_general | solution.py:146
  51.4 1.4 %convolution_bitcast_fusion.7 = f32[3,2,128,192,1]{2,3,1,4,0:T(8,128)S(1)} fusion(f32[3,1,160,192]{3,2,1,0:T(8,128)S(1)} %get-tuple-element.26, f32[3,1,160,192]{3,2,1,0:T(8,128)S(1)} %get-tuple-element.25, f32[2,2,192,192]{3,2,1,0:T(8,128)S(1)} %pad_maximum_fusion.1), kind=kOutput, calls=%fused_computation.9 | convolution fusion | flops 283299840 | bytes 2097152 | tf_op jit(solution)/shard_map/dcab,icbj->idaj/dot_general | solution.py:143
  52.8 0.7 %convolution_bitcast_fusion.6 = f32[3,2,128,192]{2,3,1,0:T(8,128)S(1)} fusion(f32[3,2,128,192,1]{2,3,1,4,0:T(8,128)S(1)} %convolution_bitcast_fusion.7, f32[2,2,192,192]{3,2,1,0:T(8,128)S(1)} %pad_maximum_fusion.1), kind=kOutput, calls=%fused_computation.8 | convolution fusion | flops 339738624 | bytes 1769472 | tf_op jit(solution)/shard_map/dcyj,icxj->idxy/dot_general | solution.py:146
  54.1 0.7 %convolution_bitcast_fusion.4 = f32[3,2,96,192]{3,2,1,0:T(8,128)S(1)} fusion(f32[3,2,96,192,1]{3,2,1,4,0:T(8,128)S(1)} %convolution_bitcast_fusion.5, f32[2,2,192,192]{3,2,1,0:T(8,128)S(1)} %pad_maximum_fusion.1), kind=kOutput, calls=%fused_computation.6 | convolution fusion | flops 254803968 | bytes 1474560 | tf_op jit(solution)/shard_map/dcyj,icxj->idxy/dot_general | solution.py:146
  55.3 1.1 %fusion.5 = f32[1,3,2,64,128]{4,3,2,1,0:T(8,128)} fusion(f32[3,2,64,192,1]{3,2,1,4,0:T(8,128)S(1)} %convolution_bitcast_fusion.12, f32[3,64,2,128,1]{3,1,4,2,0:T(8,128)S(1)} %fusion.29, f32[2,2,192,192]{3,2,1,0:T(8,128)S(1)} %pad_maximum_fusion.1, pred[]{:T(512)S(6)} %eq.7, pred[]{:T(512)S(6)} %eq.16, pred[]{:T(512)S(6)} %eq.6), kind=kOutput, calls=%fused_computation.26 | convolution fusion | flops 113442816 | bytes 1835011 | tf_op jit(solution)/shard_map/dcyj,icxj->idxy/dot_general | solution.py:146
  (103 shorter events, 6.4 us)
Async XLA Ops:
  0.0 1.5 %copy-start = (f32[3,2,64,128]{3,2,1,0:T(8,128)S(1)}, f32[3,2,64,128]{3,2,1,0:T(8,128)}, u32[]{:S(2)}) copy-start(f32[3,2,64,128]{3,2,1,0:T(8,128)} %param.4) | copy-start | bytes 589828
  1.4 6.8 %copy-start.5 = (f32[2,33]{1,0:T(2,128)S(1)}, f32[2,33]{1,0:T(2,128)}, u32[]{:S(2)}) copy-start(f32[2,33]{1,0:T(2,128)} %param.7) | copy-start | bytes 796
  1.6 13.1 %collective-permute-start.1 = (f32[11,64,128]{2,1,0:T(8,128)S(1)}, f32[11,64,128]{2,1,0:T(8,128)S(1)}, u32[]{:S(2)}, u32[]{:S(2)}) collective-permute-start(f32[11,64,128]{2,1,0:T(8,128)S(1)} %constant_dynamic-update-slice_fusion.5), channel_id=1, source_target_pairs={{4,0},{8,4},{12,8},{5,1},{9,5},{13,9},{6,2},{10,6},{14,10},{7,3},{... | collective-permute-start | bytes 1081352 | tf_op jit(solution)/shard_map/ppermute | solution.py:67
  3.7 10.9 %collective-permute-start = (f32[11,64,128]{2,1,0:T(8,128)S(1)}, f32[11,64,128]{2,1,0:T(8,128)S(1)}, u32[]{:S(2)}, u32[]{:S(2)}) collective-permute-start(f32[11,64,128]{2,1,0:T(8,128)S(1)} %constant_dynamic-update-slice_fusion), channel_id=1, source_target_pairs={{0,4},{4,8},{8,12},{1,5},{5,9},{9,13},{2,6},{6,10},{10,14},{3,7},{... | collective-permute-start | bytes 1081352 | tf_op jit(solution)/shard_map/ppermute | solution.py:66
  11.1 3.5 %copy-start.1 = (f32[192,128]{1,0:T(8,128)S(1)}, f32[192,128]{1,0:T(8,128)}, u32[]{:S(2)}) copy-start(f32[192,128]{1,0:T(8,128)} %get-tuple-element.108) | copy-start | bytes 294916
  11.1 3.5 %copy-start.2 = (f32[192,128]{1,0:T(8,128)S(1)}, f32[192,128]{1,0:T(8,128)}, u32[]{:S(2)}) copy-start(f32[192,128]{1,0:T(8,128)} %get-tuple-element.109) | copy-start | bytes 294916
  11.1 3.5 %copy-start.3 = (f32[192,128]{1,0:T(8,128)S(1)}, f32[192,128]{1,0:T(8,128)}, u32[]{:S(2)}) copy-start(f32[192,128]{1,0:T(8,128)} %get-tuple-element.110) | copy-start | bytes 294916
  11.1 3.5 %copy-start.4 = (f32[192,128]{1,0:T(8,128)S(1)}, f32[192,128]{1,0:T(8,128)}, u32[]{:S(2)}) copy-start(f32[192,128]{1,0:T(8,128)} %get-tuple-element.111) | copy-start | bytes 294916
  16.0 3.7 %collective-permute-start.2 = (f32[7,192,128]{2,1,0:T(8,128)S(1)}, f32[7,192,128]{2,1,0:T(8,128)S(1)}, u32[]{:S(2)}, u32[]{:S(2)}) collective-permute-start(f32[7,192,128]{2,1,0:T(8,128)S(1)} %maximum_select_fusion.4), channel_id=1, source_target_pairs={{0,1},{1,0},{2,3},{3,2},{4,5},{5,4},{6,7},{7,6},{8,9},{9,8},{10,11... | collective-permute-start | bytes 2064392 | tf_op jit(solution)/shard_map/ppermute | solution.py:92
  28.2 9.0 %collective-permute-start.3 = (f32[6,64,128]{2,1,0:T(8,128)S(1)}, f32[6,64,128]{2,1,0:T(8,128)S(1)}, u32[]{:S(2)}, u32[]{:S(2)}) collective-permute-start(f32[6,64,128]{2,1,0:T(8,128)S(1)} %bitcast.479), channel_id=1, source_target_pairs={{0,6},{4,10},{8,14},{1,7},{5,11},{9,15},{16,22},{20,26},{24,30},{1... | collective-permute-start | bytes 589832 | tf_op jit(solution)/shard_map/ppermute | solution.py:168
  29.5 16.8 %collective-permute-start.4 = (f32[6,64,128]{2,1,0:T(8,128)S(1)}, f32[6,64,128]{2,1,0:T(8,128)S(1)}, u32[]{:S(2)}, u32[]{:S(2)}) collective-permute-start(f32[6,64,128]{2,1,0:T(8,128)S(1)} %bitcast.480), channel_id=1, source_target_pairs={{0,2},{4,6},{8,10},{12,14},{1,3},{5,7},{9,11},{13,15},{16,18},{20,... | collective-permute-start | bytes 589832 | tf_op jit(solution)/shard_map/ppermute | solution.py:169
  31.0 15.3 %collective-permute-start.5 = (f32[6,64,128]{2,1,0:T(8,128)S(1)}, f32[6,64,128]{2,1,0:T(8,128)S(1)}, u32[]{:S(2)}, u32[]{:S(2)}) collective-permute-start(f32[6,64,128]{2,1,0:T(8,128)S(1)} %bitcast.481), channel_id=1, source_target_pairs={{4,2},{8,6},{12,10},{5,3},{9,7},{13,11},{20,18},{24,22},{28,26},{2... | collective-permute-start | bytes 589832 | tf_op jit(solution)/shard_map/ppermute | solution.py:170
  46.8 1.8 %collective-permute-start.6 = (f32[3,192,128]{2,1,0:T(8,128)S(1)}, f32[3,192,128]{2,1,0:T(8,128)S(1)}, u32[]{:S(2)}, u32[]{:S(2)}) collective-permute-start(f32[3,192,128]{2,1,0:T(8,128)S(1)} %maximum_select_fusion.5), channel_id=1, source_target_pairs={{0,1},{1,0},{2,3},{3,2},{4,5},{5,4},{6,7},{7,6},{8,9},{9,8},{10,11... | collective-permute-start | bytes 884744 | tf_op jit(solution)/shard_map/ppermute | solution.py:92

commit v12 on v11

--- a/solution.py
+++ b/solution.py
@@ -129,17 +129,20 @@
     first_field = field_grown.reshape(illum, 2, rows + 2 * reach, cols + reach)
     trans_reg = trans_grown.reshape(slices, 2, rows + 2 * reach, cols + reach)
     col_band = band[:, :, :width, :width]
-    row_bands = [
-        band[:, :, HALF * (s + 1): tall - HALF * (s + 1), HALF * s: tall - HALF * s]
-        for s in range(slices)
-    ]
+    spans, start, length = [], 0, tall
+    for s in range(slices):
+        exact = tall - 2 * HALF * (s + 1)
+        margin = 8 if exact % 128 == 0 and s + 1 < slices else 0
+        spans.append((start, length, HALF * (s + 1) - margin, exact + 2 * margin))
+        start, length = spans[-1][2], spans[-1][3]
+    row_bands = [band[:, :, o: o + n, i: i + m] for i, m, o, n in spans]
 
     last_band = jnp.where(wave == 0, col_band[:, :, :cols], col_band[:, :, reach:reach + cols])
 
     def depth_section(field):
         current = field
         for s in range(slices):
-            moved = modulate(current, trans_reg[s, :, HALF * s: tall - HALF * s])
+            moved = modulate(current, trans_reg[s, :, spans[s][0]: spans[s][0] + spans[s][1]])
             rows_done = jnp.einsum(
                 "dcab,icbj->idaj", row_bands[s], moved, precision=lax.Precision.HIGH
             )

time: 56.6 us -> 56.7 us (level)
  no operation moved by 1% of the time
where the time goes in v12:
time: 56.7 us; the launch traced here: 56.4 us
  waiting for transfers between devices  20.1 us (35%)
  matrix products  13 us (23%)
  starting transfers between devices  11.8 us (21%)
  other arithmetic  5.68 us (10%)
  local copies, waits for them, and re-layouts  4.36 us (8%)
  between operations  1.45 us (3%)
    ppermute x1, waiting for transfers between devices, per_device(): mine = lax.ppermute(flat, grid, own_pairs)  9.08 us
    dot_general x8, matrix products, depth_section(): jnp.einsum('dcyj,icxj->idxy', last_band if s == slices - 1 else col_band,...  6.53 us
    dot_general x8, matrix products, depth_section(): jnp.einsum('dcab,icbj->idaj', row_bands[s], moved, precision=lax.Precisio...  6.45 us
    ppermute x1, waiting for transfers between devices, per_device(): from_prev = lax.ppermute(flat[:, rows - reach:], grid, prev_pairs)  4.88 us
    ppermute x1, waiting for transfers between devices, grow(): lax.ppermute(sent_prev, 'tile', [(i, i + 1) for i in range(tiles - 1)])  3.3 us
    ppermute x1, starting transfers between devices, grow(): lax.ppermute(sent_prev, 'tile', [(i, i + 1) for i in range(tiles - 1)])  3.2 us
    ppermute x2, waiting for transfers between devices, widen(): got = lax.ppermute(slabs, 'wave', [(0, 1), (1, 0)])  2.88 us
    ppermute x2, starting transfers between devices, widen(): got = lax.ppermute(slabs, 'wave', [(0, 1), (1, 0)])  2.47 us
  transfers between devices with their start and end apart: 7, of which 5 were waited for; matrix products, arithmetic and copies ran while one was open for 7% of the time, Pallas kernels for 0%

profile of v12, /device:TPU:15, one launch (start us, length us, event | category | flops | bytes accessed | tf_op | source)
XLA Modules:
  0.0 56.4 jit_solution(15248594939727177982)
XLA Ops:
  0.0 1.4 %fusion.40 = (f32[4,1,64,128]{3,2,1,0:T(8,128)S(1)}, f32[4,1,64,128]{3,2,1,0:T(8,128)S(1)}) fusion(bf16[4,64,128]{2,1,0:T(8,128)(2,1)} %param.5, bf16[4,64,128]{2,1,0:T(8,128)(2,1)} %param.6), kind=kLoop, calls=%fused_computation.104 | loop fusion | flops 163840 | bytes 393216 | tf_op jit(solution)/shard_map/stack | solution.py:25
  1.6 2.1 %collective-permute-start.1 = (f32[11,64,128]{2,1,0:T(8,128)S(1)}, f32[11,64,128]{2,1,0:T(8,128)S(1)}, u32[]{:S(2)}, u32[]{:S(2)}) collective-permute-start(f32[11,64,128]{2,1,0:T(8,128)S(1)} %constant_dynamic-update-slice_fusion.5), channel_id=1, source_target_pairs={{4,0},{8,4},{12,8},{5,1},{9,5},{13,9},{6,2},{10,6},{14,10},{7,3},{... | collective-permute-start | bytes 1081352 | tf_op jit(solution)/shard_map/ppermute | solution.py:67
  3.7 3.2 %collective-permute-start = (f32[11,64,128]{2,1,0:T(8,128)S(1)}, f32[11,64,128]{2,1,0:T(8,128)S(1)}, u32[]{:S(2)}, u32[]{:S(2)}) collective-permute-start(f32[11,64,128]{2,1,0:T(8,128)S(1)} %constant_dynamic-update-slice_fusion), channel_id=1, source_target_pairs={{0,4},{4,8},{8,12},{1,5},{5,9},{9,13},{2,6},{6,10},{10,14},{3,7},{... | collective-permute-start | bytes 1081352 | tf_op jit(solution)/shard_map/ppermute | solution.py:66
  7.0 0.6 %constant_dynamic-update-slice_fusion.24 = (f32[192,128]{1,0:T(8,128)}, f32[192,128]{1,0:T(8,128)}) fusion(), kind=kLoop, calls=%fused_computation.136 | loop fusion | bytes 32768
  7.6 0.6 %constant_dynamic-update-slice_fusion.14 = (f32[192,128]{1,0:T(8,128)}, f32[192,128]{1,0:T(8,128)}) fusion(), kind=kLoop, calls=%fused_computation.126 | loop fusion | bytes 16384
  8.2 0.6 %multiply_reduce_fusion = f32[]{:T(128)} fusion(f32[2,33]{1,0:T(2,128)S(1)} %copy-done.5), kind=kLoop, calls=%fused_computation.242 | loop fusion | flops 131 | bytes 268 | tf_op jit(solution)/shard_map/reduce_sum | solution.py:108
  10.2 0.8 %reshape.48 = f32[2,192,383]{2,1,0:T(8,128)S(1)} reshape(f32[2,73536]{1,0:T(2,128)S(1)} %slice.500) | data formatting | bytes 1176576 | tf_op jit(solution)/shard_map/reshape | solution.py:15
  11.3 3.3 %collective-permute-done = f32[11,64,128]{2,1,0:T(8,128)S(1)} collective-permute-done((f32[11,64,128]{2,1,0:T(8,128)S(1)}, f32[11,64,128]{2,1,0:T(8,128)S(1)}, u32[]{:S(2)}, u32[]{:S(2)}) %collective-permute-start) | collective-permute-done | bytes 360480 | tf_op jit(solution)/shard_map/ppermute | solution.py:66
  16.0 1.9 %collective-permute-start.2 = (f32[7,192,128]{2,1,0:T(8,128)S(1)}, f32[7,192,128]{2,1,0:T(8,128)S(1)}, u32[]{:S(2)}, u32[]{:S(2)}) collective-permute-start(f32[7,192,128]{2,1,0:T(8,128)S(1)} %maximum_select_fusion.4), channel_id=1, source_target_pairs={{0,1},{1,0},{2,3},{3,2},{4,5},{5,4},{6,7},{7,6},{8,9},{9,8},{10,11... | collective-permute-start | bytes 2064392 | tf_op jit(solution)/shard_map/ppermute | solution.py:92
  18.0 1.7 %collective-permute-done.2 = f32[7,192,128]{2,1,0:T(8,128)S(1)} collective-permute-done((f32[7,192,128]{2,1,0:T(8,128)S(1)}, f32[7,192,128]{2,1,0:T(8,128)S(1)}, u32[]{:S(2)}, u32[]{:S(2)}) %collective-permute-start.2) | collective-permute-done | bytes 688160 | tf_op jit(solution)/shard_map/ppermute | solution.py:92
  20.0 0.5 maximum_select_fusion
  20.5 0.5 maximum_select_fusion.1
  21.7 1.0 %convolution_bitcast_fusion.3 = f32[3,2,160,192,1]{3,2,1,4,0:T(8,128)S(1)} fusion(f32[3,1,192,192]{3,2,1,0:T(8,128)S(1)} %get-tuple-element.18, f32[3,1,192,192]{3,2,1,0:T(8,128)S(1)} %get-tuple-element.17, f32[2,2,192,192]{3,2,1,0:T(8,128)S(1)} %pad_maximum_fusion.1), kind=kOutput, calls=%fused_computation.5 | convolution fusion | flops 424894464 | bytes 2572288 | tf_op jit(solution)/shard_map/dcab,icbj->idaj/dot_general | solution.py:146
  22.6 1.0 %convolution_bitcast_fusion.2 = f32[3,2,160,192]{3,2,1,0:T(8,128)S(1)} fusion(f32[3,2,160,192,1]{3,2,1,4,0:T(8,128)S(1)} %convolution_bitcast_fusion.3, f32[2,2,192,192]{3,2,1,0:T(8,128)S(1)} %pad_maximum_fusion.1), kind=kOutput, calls=%fused_computation.4 | convolution fusion | flops 424673280 | bytes 2064384 | tf_op jit(solution)/shard_map/dcyj,icxj->idxy/dot_general | solution.py:149
  23.7 1.0 %convolution_bitcast_fusion.7 = f32[3,2,144,192,1]{3,2,1,4,0:T(8,128)S(1)} fusion(f32[3,1,160,192]{3,2,1,0:T(8,128)S(1)} %get-tuple-element.28, f32[3,1,160,192]{3,2,1,0:T(8,128)S(1)} %get-tuple-element.27, f32[2,2,192,192]{3,2,1,0:T(8,128)S(1)} %pad_maximum_fusion.1), kind=kOutput, calls=%fused_computation.9 | convolution fusion | flops 318689280 | bytes 2236416 | tf_op jit(solution)/shard_map/dcab,icbj->idaj/dot_general | solution.py:146
  24.8 0.9 %convolution_bitcast_fusion.5 = f32[3,2,144,192]{3,2,1,0:T(8,128)S(1)} fusion(f32[3,2,144,192,1]{3,2,1,4,0:T(8,128)S(1)} %convolution_bitcast_fusion.7, f32[2,2,192,192]{3,2,1,0:T(8,128)S(1)} %pad_maximum_fusion.1), kind=kOutput, calls=%fused_computation.7 | convolution fusion | flops 382205952 | bytes 1916928 | tf_op jit(solution)/shard_map/dcyj,icxj->idxy/dot_general | solution.py:149
  25.8 0.8 %convolution_bitcast_fusion.11 = f32[3,2,96,192,1]{3,2,1,4,0:T(8,128)S(1)} fusion(f32[3,1,144,192]{3,2,1,0:T(8,128)S(1)} %get-tuple-element.32, f32[3,1,144,192]{3,2,1,0:T(8,128)S(1)} %get-tuple-element.31, f32[2,2,192,192]{3,2,1,0:T(8,128)S(1)} %pad_maximum_fusion.1), kind=kOutput, calls=%fused_computation.13 | convolution fusion | flops 191268864 | bytes 1720320 | tf_op jit(solution)/shard_map/dcab,icbj->idaj/dot_general | solution.py:146
  26.6 0.7 %convolution_bitcast_fusion.10 = f32[3,2,96,192]{3,2,1,0:T(8,128)S(1)} fusion(f32[3,2,96,192,1]{3,2,1,4,0:T(8,128)S(1)} %convolution_bitcast_fusion.11, f32[2,2,192,192]{3,2,1,0:T(8,128)S(1)} %pad_maximum_fusion.1), kind=kOutput, calls=%fused_computation.12 | convolution fusion | flops 254803968 | bytes 1474560 | tf_op jit(solution)/shard_map/dcyj,icxj->idxy/dot_general | solution.py:149
  28.2 1.3 %collective-permute-start.3 = (f32[6,64,128]{2,1,0:T(8,128)S(1)}, f32[6,64,128]{2,1,0:T(8,128)S(1)}, u32[]{:S(2)}, u32[]{:S(2)}) collective-permute-start(f32[6,64,128]{2,1,0:T(8,128)S(1)} %bitcast.479), channel_id=1, source_target_pairs={{0,6},{4,10},{8,14},{1,7},{5,11},{9,15},{16,22},{20,26},{24,30},{1... | collective-permute-start | bytes 589832 | tf_op jit(solution)/shard_map/ppermute | solution.py:171
  29.5 1.5 %collective-permute-start.4 = (f32[6,64,128]{2,1,0:T(8,128)S(1)}, f32[6,64,128]{2,1,0:T(8,128)S(1)}, u32[]{:S(2)}, u32[]{:S(2)}) collective-permute-start(f32[6,64,128]{2,1,0:T(8,128)S(1)} %bitcast.480), channel_id=1, source_target_pairs={{0,2},{4,6},{8,10},{12,14},{1,3},{5,7},{9,11},{13,15},{16,18},{20,... | collective-permute-start | bytes 589832 | tf_op jit(solution)/shard_map/ppermute | solution.py:172
  31.0 1.3 %collective-permute-start.5 = (f32[6,64,128]{2,1,0:T(8,128)S(1)}, f32[6,64,128]{2,1,0:T(8,128)S(1)}, u32[]{:S(2)}, u32[]{:S(2)}) collective-permute-start(f32[6,64,128]{2,1,0:T(8,128)S(1)} %bitcast.481), channel_id=1, source_target_pairs={{4,2},{8,6},{12,10},{5,3},{9,7},{13,11},{20,18},{24,22},{28,26},{2... | collective-permute-start | bytes 589832 | tf_op jit(solution)/shard_map/ppermute | solution.py:173
  32.3 4.9 %collective-permute-done.3 = f32[6,64,128]{2,1,0:T(8,128)S(1)} collective-permute-done((f32[6,64,128]{2,1,0:T(8,128)S(1)}, f32[6,64,128]{2,1,0:T(8,128)S(1)}, u32[]{:S(2)}, u32[]{:S(2)}) %collective-permute-start.3) | collective-permute-done | bytes 196640 | tf_op jit(solution)/shard_map/ppermute | solution.py:171
  37.2 9.1 %collective-permute-done.4 = f32[6,64,128]{2,1,0:T(8,128)S(1)} collective-permute-done((f32[6,64,128]{2,1,0:T(8,128)S(1)}, f32[6,64,128]{2,1,0:T(8,128)S(1)}, u32[]{:S(2)}, u32[]{:S(2)}) %collective-permute-start.4) | collective-permute-done | bytes 196640 | tf_op jit(solution)/shard_map/ppermute | solution.py:172
  46.7 0.5 collective-permute-start.6
  47.3 1.2 %collective-permute-done.6 = f32[3,192,128]{2,1,0:T(8,128)S(1)} collective-permute-done((f32[3,192,128]{2,1,0:T(8,128)S(1)}, f32[3,192,128]{2,1,0:T(8,128)S(1)}, u32[]{:S(2)}, u32[]{:S(2)}) %collective-permute-start.6) | collective-permute-done | bytes 294944 | tf_op jit(solution)/shard_map/ppermute | solution.py:92
  49.2 1.0 %convolution_bitcast_fusion.1 = f32[3,2,160,192,1]{3,2,1,4,0:T(8,128)S(1)} fusion(f32[3,1,192,192]{3,2,1,0:T(8,128)S(1)} %get-tuple-element.10, f32[3,1,192,192]{3,2,1,0:T(8,128)S(1)} %get-tuple-element.9, f32[2,2,192,192]{3,2,1,0:T(8,128)S(1)} %pad_maximum_fusion.1), kind=kOutput, calls=%fused_computation.3 | convolution fusion | flops 424894464 | bytes 2572288 | tf_op jit(solution)/shard_map/dcab,icbj->idaj/dot_general | solution.py:146
  50.2 1.0 %convolution_bitcast_fusion = f32[3,2,160,192]{3,2,1,0:T(8,128)S(1)} fusion(f32[3,2,160,192,1]{3,2,1,4,0:T(8,128)S(1)} %convolution_bitcast_fusion.1, f32[2,2,192,192]{3,2,1,0:T(8,128)S(1)} %pad_maximum_fusion.1), kind=kOutput, calls=%fused_computation.2 | convolution fusion | flops 424673280 | bytes 2064384 | tf_op jit(solution)/shard_map/dcyj,icxj->idxy/dot_general | solution.py:149
  51.3 1.0 %convolution_bitcast_fusion.6 = f32[3,2,144,192,1]{3,2,1,4,0:T(8,128)S(1)} fusion(f32[3,1,160,192]{3,2,1,0:T(8,128)S(1)} %get-tuple-element.26, f32[3,1,160,192]{3,2,1,0:T(8,128)S(1)} %get-tuple-element.25, f32[2,2,192,192]{3,2,1,0:T(8,128)S(1)} %pad_maximum_fusion.1), kind=kOutput, calls=%fused_computation.8 | convolution fusion | flops 318689280 | bytes 2236416 | tf_op jit(solution)/shard_map/dcab,icbj->idaj/dot_general | solution.py:146
  52.4 0.9 %convolution_bitcast_fusion.4 = f32[3,2,144,192]{3,2,1,0:T(8,128)S(1)} fusion(f32[3,2,144,192,1]{3,2,1,4,0:T(8,128)S(1)} %convolution_bitcast_fusion.6, f32[2,2,192,192]{3,2,1,0:T(8,128)S(1)} %pad_maximum_fusion.1), kind=kOutput, calls=%fused_computation.6 | convolution fusion | flops 382205952 | bytes 1916928 | tf_op jit(solution)/shard_map/dcyj,icxj->idxy/dot_general | solution.py:149
  53.4 0.8 %convolution_bitcast_fusion.9 = f32[3,2,96,192,1]{3,2,1,4,0:T(8,128)S(1)} fusion(f32[3,1,144,192]{3,2,1,0:T(8,128)S(1)} %get-tuple-element.30, f32[3,1,144,192]{3,2,1,0:T(8,128)S(1)} %get-tuple-element.29, f32[2,2,192,192]{3,2,1,0:T(8,128)S(1)} %pad_maximum_fusion.1), kind=kOutput, calls=%fused_computation.11 | convolution fusion | flops 191268864 | bytes 1720320 | tf_op jit(solution)/shard_map/dcab,icbj->idaj/dot_general | solution.py:146
  54.1 0.7 %convolution_bitcast_fusion.8 = f32[3,2,96,192]{3,2,1,0:T(8,128)S(1)} fusion(f32[3,2,96,192,1]{3,2,1,4,0:T(8,128)S(1)} %convolution_bitcast_fusion.9, f32[2,2,192,192]{3,2,1,0:T(8,128)S(1)} %pad_maximum_fusion.1), kind=kOutput, calls=%fused_computation.10 | convolution fusion | flops 254803968 | bytes 1474560 | tf_op jit(solution)/shard_map/dcyj,icxj->idxy/dot_general | solution.py:149
  55.3 1.1 %fusion.5 = f32[1,3,2,64,128]{4,3,2,1,0:T(8,128)} fusion(f32[3,2,64,192,1]{3,2,1,4,0:T(8,128)S(1)} %convolution_bitcast_fusion.12, f32[3,64,2,128,1]{3,1,4,2,0:T(8,128)S(1)} %fusion.33, f32[2,2,192,192]{3,2,1,0:T(8,128)S(1)} %pad_maximum_fusion.1, pred[]{:T(512)S(6)} %eq.7, pred[]{:T(512)S(6)} %eq.16, pred[]{:T(512)S(6)} %eq.6), kind=kOutput, calls=%fused_computation.26 | convolution fusion | flops 113442816 | bytes 1835011 | tf_op jit(solution)/shard_map/dcyj,icxj->idxy/dot_general | solution.py:149
  (101 shorter events, 6.3 us)
Async XLA Ops:
  0.0 1.5 %copy-start = (f32[3,2,64,128]{3,2,1,0:T(8,128)S(1)}, f32[3,2,64,128]{3,2,1,0:T(8,128)}, u32[]{:S(2)}) copy-start(f32[3,2,64,128]{3,2,1,0:T(8,128)} %param.4) | copy-start | bytes 589828
  1.4 6.8 %copy-start.5 = (f32[2,33]{1,0:T(2,128)S(1)}, f32[2,33]{1,0:T(2,128)}, u32[]{:S(2)}) copy-start(f32[2,33]{1,0:T(2,128)} %param.7) | copy-start | bytes 796
  1.6 13.1 %collective-permute-start.1 = (f32[11,64,128]{2,1,0:T(8,128)S(1)}, f32[11,64,128]{2,1,0:T(8,128)S(1)}, u32[]{:S(2)}, u32[]{:S(2)}) collective-permute-start(f32[11,64,128]{2,1,0:T(8,128)S(1)} %constant_dynamic-update-slice_fusion.5), channel_id=1, source_target_pairs={{4,0},{8,4},{12,8},{5,1},{9,5},{13,9},{6,2},{10,6},{14,10},{7,3},{... | collective-permute-start | bytes 1081352 | tf_op jit(solution)/shard_map/ppermute | solution.py:67
  3.7 10.9 %collective-permute-start = (f32[11,64,128]{2,1,0:T(8,128)S(1)}, f32[11,64,128]{2,1,0:T(8,128)S(1)}, u32[]{:S(2)}, u32[]{:S(2)}) collective-permute-start(f32[11,64,128]{2,1,0:T(8,128)S(1)} %constant_dynamic-update-slice_fusion), channel_id=1, source_target_pairs={{0,4},{4,8},{8,12},{1,5},{5,9},{9,13},{2,6},{6,10},{10,14},{3,7},{... | collective-permute-start | bytes 1081352 | tf_op jit(solution)/shard_map/ppermute | solution.py:66
  11.1 3.5 %copy-start.1 = (f32[192,128]{1,0:T(8,128)S(1)}, f32[192,128]{1,0:T(8,128)}, u32[]{:S(2)}) copy-start(f32[192,128]{1,0:T(8,128)} %get-tuple-element.108) | copy-start | bytes 294916
  11.1 3.5 %copy-start.2 = (f32[192,128]{1,0:T(8,128)S(1)}, f32[192,128]{1,0:T(8,128)}, u32[]{:S(2)}) copy-start(f32[192,128]{1,0:T(8,128)} %get-tuple-element.109) | copy-start | bytes 294916
  11.1 3.5 %copy-start.3 = (f32[192,128]{1,0:T(8,128)S(1)}, f32[192,128]{1,0:T(8,128)}, u32[]{:S(2)}) copy-start(f32[192,128]{1,0:T(8,128)} %get-tuple-element.110) | copy-start | bytes 294916
  11.1 3.5 %copy-start.4 = (f32[192,128]{1,0:T(8,128)S(1)}, f32[192,128]{1,0:T(8,128)}, u32[]{:S(2)}) copy-start(f32[192,128]{1,0:T(8,128)} %get-tuple-element.111) | copy-start | bytes 294916
  16.0 3.7 %collective-permute-start.2 = (f32[7,192,128]{2,1,0:T(8,128)S(1)}, f32[7,192,128]{2,1,0:T(8,128)S(1)}, u32[]{:S(2)}, u32[]{:S(2)}) collective-permute-start(f32[7,192,128]{2,1,0:T(8,128)S(1)} %maximum_select_fusion.4), channel_id=1, source_target_pairs={{0,1},{1,0},{2,3},{3,2},{4,5},{5,4},{6,7},{7,6},{8,9},{9,8},{10,11... | collective-permute-start | bytes 2064392 | tf_op jit(solution)/shard_map/ppermute | solution.py:92
  28.2 9.0 %collective-permute-start.3 = (f32[6,64,128]{2,1,0:T(8,128)S(1)}, f32[6,64,128]{2,1,0:T(8,128)S(1)}, u32[]{:S(2)}, u32[]{:S(2)}) collective-permute-start(f32[6,64,128]{2,1,0:T(8,128)S(1)} %bitcast.479), channel_id=1, source_target_pairs={{0,6},{4,10},{8,14},{1,7},{5,11},{9,15},{16,22},{20,26},{24,30},{1... | collective-permute-start | bytes 589832 | tf_op jit(solution)/shard_map/ppermute | solution.py:171
  29.5 16.8 %collective-permute-start.4 = (f32[6,64,128]{2,1,0:T(8,128)S(1)}, f32[6,64,128]{2,1,0:T(8,128)S(1)}, u32[]{:S(2)}, u32[]{:S(2)}) collective-permute-start(f32[6,64,128]{2,1,0:T(8,128)S(1)} %bitcast.480), channel_id=1, source_target_pairs={{0,2},{4,6},{8,10},{12,14},{1,3},{5,7},{9,11},{13,15},{16,18},{20,... | collective-permute-start | bytes 589832 | tf_op jit(solution)/shard_map/ppermute | solution.py:172
  31.0 15.3 %collective-permute-start.5 = (f32[6,64,128]{2,1,0:T(8,128)S(1)}, f32[6,64,128]{2,1,0:T(8,128)S(1)}, u32[]{:S(2)}, u32[]{:S(2)}) collective-permute-start(f32[6,64,128]{2,1,0:T(8,128)S(1)} %bitcast.481), channel_id=1, source_target_pairs={{4,2},{8,6},{12,10},{5,3},{9,7},{13,11},{20,18},{24,22},{28,26},{2... | collective-permute-start | bytes 589832 | tf_op jit(solution)/shard_map/ppermute | solution.py:173
  46.7 1.8 %collective-permute-start.6 = (f32[3,192,128]{2,1,0:T(8,128)S(1)}, f32[3,192,128]{2,1,0:T(8,128)S(1)}, u32[]{:S(2)}, u32[]{:S(2)}) collective-permute-start(f32[3,192,128]{2,1,0:T(8,128)S(1)} %maximum_select_fusion.5), channel_id=1, source_target_pairs={{0,1},{1,0},{2,3},{3,2},{4,5},{5,4},{6,7},{7,6},{8,9},{9,8},{10,11... | collective-permute-start | bytes 884744 | tf_op jit(solution)/shard_map/ppermute | solution.py:92

commit v13 on v11

--- a/solution.py
+++ b/solution.py
@@ -160,7 +160,7 @@
     next_pairs = [(spot(t + 1, d), spot(t, d + 1)) for t in range(tiles - 1) for d in ahead]
     field = first_field
     for step in range(depth_count):
-        result = depth_section(field)
+        result = lax.optimization_barrier(depth_section(field))
         exits = jnp.where(depth_index == step, result, exits)
         if step + 1 < depth_count:
             flat = result.reshape(2 * illum, rows, cols)

time: 56.6 us -> 56.6 us (level)
  matrix products: 12.8 us -> 12.1 us
  other arithmetic: 5.61 us -> 6.31 us
    broadcast_in_dim x0 -> x1, other arithmetic: none -> 0.7 us  [per_device(): return exits[None]]
    dot_general x8, matrix products: 6.26 us -> 5.58 us  [depth_section(): jnp.einsum('dcyj,icxj->idxy', last_band if s == slices - 1 else col_band,...]
where the time goes in v13:
time: 56.6 us; the launch traced here: 56.4 us
  waiting for transfers between devices  20.1 us (36%)
  matrix products  12.1 us (21%)
  starting transfers between devices  11.8 us (21%)
  other arithmetic  6.31 us (11%)
  local copies, waits for them, and re-layouts  4.54 us (8%)
  between operations  1.48 us (3%)
    ppermute x1, waiting for transfers between devices, per_device(): mine = lax.ppermute(flat, grid, own_pairs)  9.09 us
    dot_general x8, matrix products, depth_section(): jnp.einsum('dcab,icbj->idaj', row_bands[s], moved, precision=lax.Precisio...  6.54 us
    dot_general x8, matrix products, depth_section(): jnp.einsum('dcyj,icxj->idxy', last_band if s == slices - 1 else col_band,...  5.58 us
    ppermute x1, waiting for transfers between devices, per_device(): from_prev = lax.ppermute(flat[:, rows - reach:], grid, prev_pairs)  4.87 us
    ppermute x1, waiting for transfers between devices, grow(): lax.ppermute(sent_prev, 'tile', [(i, i + 1) for i in range(tiles - 1)])  3.3 us
    ppermute x1, starting transfers between devices, grow(): lax.ppermute(sent_prev, 'tile', [(i, i + 1) for i in range(tiles - 1)])  3.2 us
    ppermute x2, waiting for transfers between devices, widen(): got = lax.ppermute(slabs, 'wave', [(0, 1), (1, 0)])  2.88 us
    ppermute x2, starting transfers between devices, widen(): got = lax.ppermute(slabs, 'wave', [(0, 1), (1, 0)])  2.47 us
  transfers between devices with their start and end apart: 7, of which 5 were waited for; matrix products, arithmetic and copies ran while one was open for 7% of the time, Pallas kernels for 0%

profile of v13, /device:TPU:15, one launch (start us, length us, event | category | flops | bytes accessed | tf_op | source)
XLA Modules:
  0.0 56.4 jit_solution(7513223172360838887)
XLA Ops:
  0.0 1.4 %fusion.37 = (f32[4,1,64,128]{3,2,1,0:T(8,128)S(1)}, f32[4,1,64,128]{3,2,1,0:T(8,128)S(1)}) fusion(bf16[4,64,128]{2,1,0:T(8,128)(2,1)} %param.5, bf16[4,64,128]{2,1,0:T(8,128)(2,1)} %param.6), kind=kLoop, calls=%fused_computation.100 | loop fusion | flops 163840 | bytes 393216 | tf_op jit(solution)/shard_map/stack | solution.py:25
  1.6 2.1 %collective-permute-start.1 = (f32[11,64,128]{2,1,0:T(8,128)S(1)}, f32[11,64,128]{2,1,0:T(8,128)S(1)}, u32[]{:S(2)}, u32[]{:S(2)}) collective-permute-start(f32[11,64,128]{2,1,0:T(8,128)S(1)} %constant_dynamic-update-slice_fusion.5), channel_id=1, source_target_pairs={{4,0},{8,4},{12,8},{5,1},{9,5},{13,9},{6,2},{10,6},{14,10},{7,3},{... | collective-permute-start | bytes 1081352 | tf_op jit(solution)/shard_map/ppermute | solution.py:67
  3.7 3.2 %collective-permute-start = (f32[11,64,128]{2,1,0:T(8,128)S(1)}, f32[11,64,128]{2,1,0:T(8,128)S(1)}, u32[]{:S(2)}, u32[]{:S(2)}) collective-permute-start(f32[11,64,128]{2,1,0:T(8,128)S(1)} %constant_dynamic-update-slice_fusion), channel_id=1, source_target_pairs={{0,4},{4,8},{8,12},{1,5},{5,9},{9,13},{2,6},{6,10},{10,14},{3,7},{... | collective-permute-start | bytes 1081352 | tf_op jit(solution)/shard_map/ppermute | solution.py:66
  7.0 0.6 %constant_dynamic-update-slice_fusion.24 = (f32[192,128]{1,0:T(8,128)}, f32[192,128]{1,0:T(8,128)}) fusion(), kind=kLoop, calls=%fused_computation.134 | loop fusion | bytes 32768
  7.6 0.6 %constant_dynamic-update-slice_fusion.14 = (f32[192,128]{1,0:T(8,128)}, f32[192,128]{1,0:T(8,128)}) fusion(), kind=kLoop, calls=%fused_computation.124 | loop fusion | bytes 16384
  8.2 0.6 %multiply_reduce_fusion = f32[]{:T(128)} fusion(f32[2,33]{1,0:T(2,128)S(1)} %copy-done.5), kind=kLoop, calls=%fused_computation.240 | loop fusion | flops 131 | bytes 268 | tf_op jit(solution)/shard_map/reduce_sum | solution.py:108
  9.7 0.5 copy.54
  10.2 0.8 %reshape.48 = f32[2,192,383]{2,1,0:T(8,128)S(1)} reshape(f32[2,73536]{1,0:T(2,128)S(1)} %slice.500) | data formatting | bytes 1176576 | tf_op jit(solution)/shard_map/reshape | solution.py:15
  11.3 3.3 %collective-permute-done = f32[11,64,128]{2,1,0:T(8,128)S(1)} collective-permute-done((f32[11,64,128]{2,1,0:T(8,128)S(1)}, f32[11,64,128]{2,1,0:T(8,128)S(1)}, u32[]{:S(2)}, u32[]{:S(2)}) %collective-permute-start) | collective-permute-done | bytes 360480 | tf_op jit(solution)/shard_map/ppermute | solution.py:66
  15.1 0.5 fusion.54
  16.0 1.9 %collective-permute-start.2 = (f32[7,192,128]{2,1,0:T(8,128)S(1)}, f32[7,192,128]{2,1,0:T(8,128)S(1)}, u32[]{:S(2)}, u32[]{:S(2)}) collective-permute-start(f32[7,192,128]{2,1,0:T(8,128)S(1)} %maximum_select_fusion.4), channel_id=1, source_target_pairs={{0,1},{1,0},{2,3},{3,2},{4,5},{5,4},{6,7},{7,6},{8,9},{9,8},{10,11... | collective-permute-start | bytes 2064392 | tf_op jit(solution)/shard_map/ppermute | solution.py:92
  18.0 1.7 %collective-permute-done.2 = f32[7,192,128]{2,1,0:T(8,128)S(1)} collective-permute-done((f32[7,192,128]{2,1,0:T(8,128)S(1)}, f32[7,192,128]{2,1,0:T(8,128)S(1)}, u32[]{:S(2)}, u32[]{:S(2)}) %collective-permute-start.2) | collective-permute-done | bytes 688160 | tf_op jit(solution)/shard_map/ppermute | solution.py:92
  20.0 0.5 maximum_select_fusion
  20.5 0.5 maximum_select_fusion.1
  21.6 1.0 %convolution_bitcast_fusion.3 = f32[3,2,160,192,1]{3,2,1,4,0:T(8,128)S(1)} fusion(f32[3,1,192,192]{3,2,1,0:T(8,128)S(1)} %get-tuple-element.18, f32[3,1,192,192]{3,2,1,0:T(8,128)S(1)} %get-tuple-element.17, f32[2,2,192,192]{3,2,1,0:T(8,128)S(1)} %pad_maximum_fusion.1), kind=kOutput, calls=%fused_computation.5 | convolution fusion | flops 424894464 | bytes 2572288 | tf_op jit(solution)/shard_map/dcab,icbj->idaj/dot_general | solution.py:143
  22.6 1.0 %convolution_bitcast_fusion.2 = f32[3,2,160,192]{3,2,1,0:T(8,128)S(1)} fusion(f32[3,2,160,192,1]{3,2,1,4,0:T(8,128)S(1)} %convolution_bitcast_fusion.3, f32[2,2,192,192]{3,2,1,0:T(8,128)S(1)} %pad_maximum_fusion.1), kind=kOutput, calls=%fused_computation.4 | convolution fusion | flops 424673280 | bytes 2064384 | tf_op jit(solution)/shard_map/dcyj,icxj->idxy/dot_general | solution.py:146
  23.7 1.4 %convolution_bitcast_fusion.11 = f32[3,2,128,192,1]{2,3,1,4,0:T(8,128)S(1)} fusion(f32[3,1,160,192]{3,2,1,0:T(8,128)S(1)} %get-tuple-element.28, f32[3,1,160,192]{3,2,1,0:T(8,128)S(1)} %get-tuple-element.27, f32[2,2,192,192]{3,2,1,0:T(8,128)S(1)} %pad_maximum_fusion.1), kind=kOutput, calls=%fused_computation.13 | convolution fusion | flops 283299840 | bytes 2097152 | tf_op jit(solution)/shard_map/dcab,icbj->idaj/dot_general | solution.py:143
  25.2 0.8 %convolution_bitcast_fusion.10 = f32[3,2,128,192]{2,3,1,0:T(8,128)S(1)} fusion(f32[3,2,128,192,1]{2,3,1,4,0:T(8,128)S(1)} %convolution_bitcast_fusion.11, f32[2,2,192,192]{3,2,1,0:T(8,128)S(1)} %pad_maximum_fusion.1), kind=kOutput, calls=%fused_computation.12 | convolution fusion | flops 339738624 | bytes 1769472 | tf_op jit(solution)/shard_map/dcyj,icxj->idxy/dot_general | solution.py:146
  26.6 0.7 %convolution_bitcast_fusion.8 = f32[3,2,96,192]{3,2,1,0:T(8,128)S(1)} fusion(f32[3,2,96,192,1]{3,2,1,4,0:T(8,128)S(1)} %convolution_bitcast_fusion.9, f32[2,2,192,192]{3,2,1,0:T(8,128)S(1)} %pad_maximum_fusion.1), kind=kOutput, calls=%fused_computation.10 | convolution fusion | flops 254803968 | bytes 1474560 | tf_op jit(solution)/shard_map/dcyj,icxj->idxy/dot_general | solution.py:146
  28.2 1.3 %collective-permute-start.3 = (f32[6,64,128]{2,1,0:T(8,128)S(1)}, f32[6,64,128]{2,1,0:T(8,128)S(1)}, u32[]{:S(2)}, u32[]{:S(2)}) collective-permute-start(f32[6,64,128]{2,1,0:T(8,128)S(1)} %bitcast.472), channel_id=1, source_target_pairs={{0,6},{4,10},{8,14},{1,7},{5,11},{9,15},{16,22},{20,26},{24,30},{1... | collective-permute-start | bytes 589832 | tf_op jit(solution)/shard_map/ppermute | solution.py:168
  29.5 1.5 %collective-permute-start.4 = (f32[6,64,128]{2,1,0:T(8,128)S(1)}, f32[6,64,128]{2,1,0:T(8,128)S(1)}, u32[]{:S(2)}, u32[]{:S(2)}) collective-permute-start(f32[6,64,128]{2,1,0:T(8,128)S(1)} %bitcast.473), channel_id=1, source_target_pairs={{0,2},{4,6},{8,10},{12,14},{1,3},{5,7},{9,11},{13,15},{16,18},{20,... | collective-permute-start | bytes 589832 | tf_op jit(solution)/shard_map/ppermute | solution.py:169
  31.0 1.3 %collective-permute-start.5 = (f32[6,64,128]{2,1,0:T(8,128)S(1)}, f32[6,64,128]{2,1,0:T(8,128)S(1)}, u32[]{:S(2)}, u32[]{:S(2)}) collective-permute-start(f32[6,64,128]{2,1,0:T(8,128)S(1)} %bitcast.474), channel_id=1, source_target_pairs={{4,2},{8,6},{12,10},{5,3},{9,7},{13,11},{20,18},{24,22},{28,26},{2... | collective-permute-start | bytes 589832 | tf_op jit(solution)/shard_map/ppermute | solution.py:170
  32.3 4.9 %collective-permute-done.3 = f32[6,64,128]{2,1,0:T(8,128)S(1)} collective-permute-done((f32[6,64,128]{2,1,0:T(8,128)S(1)}, f32[6,64,128]{2,1,0:T(8,128)S(1)}, u32[]{:S(2)}, u32[]{:S(2)}) %collective-permute-start.3) | collective-permute-done | bytes 196640 | tf_op jit(solution)/shard_map/ppermute | solution.py:168
  37.2 9.1 %collective-permute-done.4 = f32[6,64,128]{2,1,0:T(8,128)S(1)} collective-permute-done((f32[6,64,128]{2,1,0:T(8,128)S(1)}, f32[6,64,128]{2,1,0:T(8,128)S(1)}, u32[]{:S(2)}, u32[]{:S(2)}) %collective-permute-start.4) | collective-permute-done | bytes 196640 | tf_op jit(solution)/shard_map/ppermute | solution.py:169
  46.8 0.5 collective-permute-start.6
  47.3 1.2 %collective-permute-done.6 = f32[3,192,128]{2,1,0:T(8,128)S(1)} collective-permute-done((f32[3,192,128]{2,1,0:T(8,128)S(1)}, f32[3,192,128]{2,1,0:T(8,128)S(1)}, u32[]{:S(2)}, u32[]{:S(2)}) %collective-permute-start.6) | collective-permute-done | bytes 294944 | tf_op jit(solution)/shard_map/ppermute | solution.py:92
  49.3 1.0 %convolution_bitcast_fusion.1 = f32[3,2,160,192,1]{3,2,1,4,0:T(8,128)S(1)} fusion(f32[3,1,192,192]{3,2,1,0:T(8,128)S(1)} %get-tuple-element.10, f32[3,1,192,192]{3,2,1,0:T(8,128)S(1)} %get-tuple-element.9, f32[2,2,192,192]{3,2,1,0:T(8,128)S(1)} %pad_maximum_fusion.1), kind=kOutput, calls=%fused_computation.3 | convolution fusion | flops 424894464 | bytes 2572288 | tf_op jit(solution)/shard_map/dcab,icbj->idaj/dot_general | solution.py:143
  50.3 1.0 %convolution_bitcast_fusion = f32[3,2,160,192]{3,2,1,0:T(8,128)S(1)} fusion(f32[3,2,160,192,1]{3,2,1,4,0:T(8,128)S(1)} %convolution_bitcast_fusion.1, f32[2,2,192,192]{3,2,1,0:T(8,128)S(1)} %pad_maximum_fusion.1), kind=kOutput, calls=%fused_computation.2 | convolution fusion | flops 424673280 | bytes 2064384 | tf_op jit(solution)/shard_map/dcyj,icxj->idxy/dot_general | solution.py:146
  51.4 1.4 %convolution_bitcast_fusion.7 = f32[3,2,128,192,1]{2,3,1,4,0:T(8,128)S(1)} fusion(f32[3,1,160,192]{3,2,1,0:T(8,128)S(1)} %get-tuple-element.26, f32[3,1,160,192]{3,2,1,0:T(8,128)S(1)} %get-tuple-element.25, f32[2,2,192,192]{3,2,1,0:T(8,128)S(1)} %pad_maximum_fusion.1), kind=kOutput, calls=%fused_computation.9 | convolution fusion | flops 283299840 | bytes 2097152 | tf_op jit(solution)/shard_map/dcab,icbj->idaj/dot_general | solution.py:143
  52.8 0.7 %convolution_bitcast_fusion.6 = f32[3,2,128,192]{2,3,1,0:T(8,128)S(1)} fusion(f32[3,2,128,192,1]{2,3,1,4,0:T(8,128)S(1)} %convolution_bitcast_fusion.7, f32[2,2,192,192]{3,2,1,0:T(8,128)S(1)} %pad_maximum_fusion.1), kind=kOutput, calls=%fused_computation.8 | convolution fusion | flops 339738624 | bytes 1769472 | tf_op jit(solution)/shard_map/dcyj,icxj->idxy/dot_general | solution.py:146
  54.1 0.7 %convolution_bitcast_fusion.4 = f32[3,2,96,192]{3,2,1,0:T(8,128)S(1)} fusion(f32[3,2,96,192,1]{3,2,1,4,0:T(8,128)S(1)} %convolution_bitcast_fusion.5, f32[2,2,192,192]{3,2,1,0:T(8,128)S(1)} %pad_maximum_fusion.1), kind=kOutput, calls=%fused_computation.6 | convolution fusion | flops 254803968 | bytes 1474560 | tf_op jit(solution)/shard_map/dcyj,icxj->idxy/dot_general | solution.py:146
  55.7 0.7 %select_bitcast_fusion = f32[1,3,2,64,128]{4,3,2,1,0:T(8,128)} fusion(f32[3,2,64,128]{3,2,1,0:T(8,128)S(1)} %convolution_bitcast_fusion.14, f32[3,2,64,128]{3,2,1,0:T(8,128)S(1)} %convolution_bitcast_fusion.15, pred[]{:T(512)S(6)} %eq.16, pred[]{:T(512)S(6)} %eq.6), kind=kLoop, calls=%fused_computation.92 | loop fusion | flops 98304 | bytes 589826 | tf_op jit(solution)/shard_map/broadcast_in_dim | solution.py:174
  (104 shorter events, 6.8 us)
Async XLA Ops:
  0.0 1.5 %copy-start = (f32[3,2,64,128]{3,2,1,0:T(8,128)S(1)}, f32[3,2,64,128]{3,2,1,0:T(8,128)}, u32[]{:S(2)}) copy-start(f32[3,2,64,128]{3,2,1,0:T(8,128)} %param.4) | copy-start | bytes 589828
  1.4 6.8 %copy-start.5 = (f32[2,33]{1,0:T(2,128)S(1)}, f32[2,33]{1,0:T(2,128)}, u32[]{:S(2)}) copy-start(f32[2,33]{1,0:T(2,128)} %param.7) | copy-start | bytes 796
  1.6 13.1 %collective-permute-start.1 = (f32[11,64,128]{2,1,0:T(8,128)S(1)}, f32[11,64,128]{2,1,0:T(8,128)S(1)}, u32[]{:S(2)}, u32[]{:S(2)}) collective-permute-start(f32[11,64,128]{2,1,0:T(8,128)S(1)} %constant_dynamic-update-slice_fusion.5), channel_id=1, source_target_pairs={{4,0},{8,4},{12,8},{5,1},{9,5},{13,9},{6,2},{10,6},{14,10},{7,3},{... | collective-permute-start | bytes 1081352 | tf_op jit(solution)/shard_map/ppermute | solution.py:67
  3.7 10.9 %collective-permute-start = (f32[11,64,128]{2,1,0:T(8,128)S(1)}, f32[11,64,128]{2,1,0:T(8,128)S(1)}, u32[]{:S(2)}, u32[]{:S(2)}) collective-permute-start(f32[11,64,128]{2,1,0:T(8,128)S(1)} %constant_dynamic-update-slice_fusion), channel_id=1, source_target_pairs={{0,4},{4,8},{8,12},{1,5},{5,9},{9,13},{2,6},{6,10},{10,14},{3,7},{... | collective-permute-start | bytes 1081352 | tf_op jit(solution)/shard_map/ppermute | solution.py:66
  11.1 3.5 %copy-start.1 = (f32[192,128]{1,0:T(8,128)S(1)}, f32[192,128]{1,0:T(8,128)}, u32[]{:S(2)}) copy-start(f32[192,128]{1,0:T(8,128)} %get-tuple-element.108) | copy-start | bytes 294916
  11.1 3.5 %copy-start.2 = (f32[192,128]{1,0:T(8,128)S(1)}, f32[192,128]{1,0:T(8,128)}, u32[]{:S(2)}) copy-start(f32[192,128]{1,0:T(8,128)} %get-tuple-element.109) | copy-start | bytes 294916
  11.1 3.5 %copy-start.3 = (f32[192,128]{1,0:T(8,128)S(1)}, f32[192,128]{1,0:T(8,128)}, u32[]{:S(2)}) copy-start(f32[192,128]{1,0:T(8,128)} %get-tuple-element.110) | copy-start | bytes 294916
  11.1 3.5 %copy-start.4 = (f32[192,128]{1,0:T(8,128)S(1)}, f32[192,128]{1,0:T(8,128)}, u32[]{:S(2)}) copy-start(f32[192,128]{1,0:T(8,128)} %get-tuple-element.111) | copy-start | bytes 294916
  16.0 3.7 %collective-permute-start.2 = (f32[7,192,128]{2,1,0:T(8,128)S(1)}, f32[7,192,128]{2,1,0:T(8,128)S(1)}, u32[]{:S(2)}, u32[]{:S(2)}) collective-permute-start(f32[7,192,128]{2,1,0:T(8,128)S(1)} %maximum_select_fusion.4), channel_id=1, source_target_pairs={{0,1},{1,0},{2,3},{3,2},{4,5},{5,4},{6,7},{7,6},{8,9},{9,8},{10,11... | collective-permute-start | bytes 2064392 | tf_op jit(solution)/shard_map/ppermute | solution.py:92
  28.2 9.0 %collective-permute-start.3 = (f32[6,64,128]{2,1,0:T(8,128)S(1)}, f32[6,64,128]{2,1,0:T(8,128)S(1)}, u32[]{:S(2)}, u32[]{:S(2)}) collective-permute-start(f32[6,64,128]{2,1,0:T(8,128)S(1)} %bitcast.472), channel_id=1, source_target_pairs={{0,6},{4,10},{8,14},{1,7},{5,11},{9,15},{16,22},{20,26},{24,30},{1... | collective-permute-start | bytes 589832 | tf_op jit(solution)/shard_map/ppermute | solution.py:168
  29.5 16.8 %collective-permute-start.4 = (f32[6,64,128]{2,1,0:T(8,128)S(1)}, f32[6,64,128]{2,1,0:T(8,128)S(1)}, u32[]{:S(2)}, u32[]{:S(2)}) collective-permute-start(f32[6,64,128]{2,1,0:T(8,128)S(1)} %bitcast.473), channel_id=1, source_target_pairs={{0,2},{4,6},{8,10},{12,14},{1,3},{5,7},{9,11},{13,15},{16,18},{20,... | collective-permute-start | bytes 589832 | tf_op jit(solution)/shard_map/ppermute | solution.py:169
  31.0 15.3 %collective-permute-start.5 = (f32[6,64,128]{2,1,0:T(8,128)S(1)}, f32[6,64,128]{2,1,0:T(8,128)S(1)}, u32[]{:S(2)}, u32[]{:S(2)}) collective-permute-start(f32[6,64,128]{2,1,0:T(8,128)S(1)} %bitcast.474), channel_id=1, source_target_pairs={{4,2},{8,6},{12,10},{5,3},{9,7},{13,11},{20,18},{24,22},{28,26},{2... | collective-permute-start | bytes 589832 | tf_op jit(solution)/shard_map/ppermute | solution.py:170
  46.8 1.8 %collective-permute-start.6 = (f32[3,192,128]{2,1,0:T(8,128)S(1)}, f32[3,192,128]{2,1,0:T(8,128)S(1)}, u32[]{:S(2)}, u32[]{:S(2)}) collective-permute-start(f32[3,192,128]{2,1,0:T(8,128)S(1)} %maximum_select_fusion.5), channel_id=1, source_target_pairs={{0,1},{1,0},{2,3},{3,2},{4,5},{5,4},{6,7},{7,6},{8,9},{9,8},{10,11... | collective-permute-start | bytes 884744 | tf_op jit(solution)/shard_map/ppermute | solution.py:92

commit v14 on v11

--- a/solution.py
+++ b/solution.py
@@ -129,8 +129,9 @@
     first_field = field_grown.reshape(illum, 2, rows + 2 * reach, cols + reach)
     trans_reg = trans_grown.reshape(slices, 2, rows + 2 * reach, cols + reach)
     col_band = band[:, :, :width, :width]
+    margins = [8 if (tall - 2 * HALF * (s + 1)) % 128 == 0 and s + 1 < slices else 0 for s in range(slices)]
     row_bands = [
-        band[:, :, HALF * (s + 1): tall - HALF * (s + 1), HALF * s: tall - HALF * s]
+        band[:, :, HALF * (s + 1) - margins[s]: tall - HALF * (s + 1) + margins[s], HALF * s: tall - HALF * s]
         for s in range(slices)
     ]
 
@@ -139,6 +140,8 @@
     def depth_section(field):
         current = field
         for s in range(slices):
+            if s and margins[s - 1]:
+                current = current[:, :, margins[s - 1]: current.shape[2] - margins[s - 1]]
             moved = modulate(current, trans_reg[s, :, HALF * s: tall - HALF * s])
             rows_done = jnp.einsum(
                 "dcab,icbj->idaj", row_bands[s], moved, precision=lax.Precision.HIGH

time: 56.6 us -> 56 us (0.989)
    dot_general x8, matrix products: 6.54 us -> 5.8 us  [depth_section(): jnp.einsum('dcab,icbj->idaj', row_bands[s], moved, precision=lax.Precisio...]
where the time goes in v14:
time: 56 us; the launch traced here: 55.8 us
  waiting for transfers between devices  20.1 us (36%)
  matrix products  12.3 us (22%)
  starting transfers between devices  11.8 us (21%)
  other arithmetic  5.65 us (10%)
  local copies, waits for them, and re-layouts  4.36 us (8%)
  between operations  1.45 us (3%)
    ppermute x1, waiting for transfers between devices, per_device(): mine = lax.ppermute(flat, grid, own_pairs)  9.07 us
    dot_general x8, matrix products, depth_section(): jnp.einsum('dcyj,icxj->idxy', last_band if s == slices - 1 else col_band,...  6.53 us
    dot_general x8, matrix products, depth_section(): jnp.einsum('dcab,icbj->idaj', row_bands[s], moved, precision=lax.Precisio...  5.8 us
    ppermute x1, waiting for transfers between devices, per_device(): from_prev = lax.ppermute(flat[:, rows - reach:], grid, prev_pairs)  4.89 us
    ppermute x1, waiting for transfers between devices, grow(): lax.ppermute(sent_prev, 'tile', [(i, i + 1) for i in range(tiles - 1)])  3.3 us
    ppermute x1, starting transfers between devices, grow(): lax.ppermute(sent_prev, 'tile', [(i, i + 1) for i in range(tiles - 1)])  3.2 us
    ppermute x2, waiting for transfers between devices, widen(): got = lax.ppermute(slabs, 'wave', [(0, 1), (1, 0)])  2.88 us
    ppermute x2, starting transfers between devices, widen(): got = lax.ppermute(slabs, 'wave', [(0, 1), (1, 0)])  2.47 us
  transfers between devices with their start and end apart: 7, of which 5 were waited for; matrix products, arithmetic and copies ran while one was open for 7% of the time, Pallas kernels for 0%

profile of v14, /device:TPU:15, one launch (start us, length us, event | category | flops | bytes accessed | tf_op | source)
XLA Modules:
  0.0 55.8 jit_solution(2316455187464739282)
XLA Ops:
  0.0 1.4 %fusion.40 = (f32[4,1,64,128]{3,2,1,0:T(8,128)S(1)}, f32[4,1,64,128]{3,2,1,0:T(8,128)S(1)}) fusion(bf16[4,64,128]{2,1,0:T(8,128)(2,1)} %param.5, bf16[4,64,128]{2,1,0:T(8,128)(2,1)} %param.6), kind=kLoop, calls=%fused_computation.102 | loop fusion | flops 163840 | bytes 393216 | tf_op jit(solution)/shard_map/stack | solution.py:25
  1.6 2.1 %collective-permute-start.1 = (f32[11,64,128]{2,1,0:T(8,128)S(1)}, f32[11,64,128]{2,1,0:T(8,128)S(1)}, u32[]{:S(2)}, u32[]{:S(2)}) collective-permute-start(f32[11,64,128]{2,1,0:T(8,128)S(1)} %constant_dynamic-update-slice_fusion.5), channel_id=1, source_target_pairs={{4,0},{8,4},{12,8},{5,1},{9,5},{13,9},{6,2},{10,6},{14,10},{7,3},{... | collective-permute-start | bytes 1081352 | tf_op jit(solution)/shard_map/ppermute | solution.py:67
  3.7 3.2 %collective-permute-start = (f32[11,64,128]{2,1,0:T(8,128)S(1)}, f32[11,64,128]{2,1,0:T(8,128)S(1)}, u32[]{:S(2)}, u32[]{:S(2)}) collective-permute-start(f32[11,64,128]{2,1,0:T(8,128)S(1)} %constant_dynamic-update-slice_fusion), channel_id=1, source_target_pairs={{0,4},{4,8},{8,12},{1,5},{5,9},{9,13},{2,6},{6,10},{10,14},{3,7},{... | collective-permute-start | bytes 1081352 | tf_op jit(solution)/shard_map/ppermute | solution.py:66
  7.0 0.6 %constant_dynamic-update-slice_fusion.24 = (f32[192,128]{1,0:T(8,128)}, f32[192,128]{1,0:T(8,128)}) fusion(), kind=kLoop, calls=%fused_computation.136 | loop fusion | bytes 32768
  7.6 0.6 %constant_dynamic-update-slice_fusion.14 = (f32[192,128]{1,0:T(8,128)}, f32[192,128]{1,0:T(8,128)}) fusion(), kind=kLoop, calls=%fused_computation.126 | loop fusion | bytes 16384
  8.2 0.6 %multiply_reduce_fusion = f32[]{:T(128)} fusion(f32[2,33]{1,0:T(2,128)S(1)} %copy-done.5), kind=kLoop, calls=%fused_computation.242 | loop fusion | flops 131 | bytes 268 | tf_op jit(solution)/shard_map/reduce_sum | solution.py:108
  9.7 0.5 copy.50
  10.2 0.8 %reshape.48 = f32[2,192,383]{2,1,0:T(8,128)S(1)} reshape(f32[2,73536]{1,0:T(2,128)S(1)} %slice.506) | data formatting | bytes 1176576 | tf_op jit(solution)/shard_map/reshape | solution.py:15
  11.3 3.3 %collective-permute-done = f32[11,64,128]{2,1,0:T(8,128)S(1)} collective-permute-done((f32[11,64,128]{2,1,0:T(8,128)S(1)}, f32[11,64,128]{2,1,0:T(8,128)S(1)}, u32[]{:S(2)}, u32[]{:S(2)}) %collective-permute-start) | collective-permute-done | bytes 360480 | tf_op jit(solution)/shard_map/ppermute | solution.py:66
  15.1 0.5 fusion.57
  16.0 1.9 %collective-permute-start.2 = (f32[7,192,128]{2,1,0:T(8,128)S(1)}, f32[7,192,128]{2,1,0:T(8,128)S(1)}, u32[]{:S(2)}, u32[]{:S(2)}) collective-permute-start(f32[7,192,128]{2,1,0:T(8,128)S(1)} %maximum_select_fusion.4), channel_id=1, source_target_pairs={{0,1},{1,0},{2,3},{3,2},{4,5},{5,4},{6,7},{7,6},{8,9},{9,8},{10,11... | collective-permute-start | bytes 2064392 | tf_op jit(solution)/shard_map/ppermute | solution.py:92
  18.0 1.7 %collective-permute-done.2 = f32[7,192,128]{2,1,0:T(8,128)S(1)} collective-permute-done((f32[7,192,128]{2,1,0:T(8,128)S(1)}, f32[7,192,128]{2,1,0:T(8,128)S(1)}, u32[]{:S(2)}, u32[]{:S(2)}) %collective-permute-start.2) | collective-permute-done | bytes 688160 | tf_op jit(solution)/shard_map/ppermute | solution.py:92
  20.0 0.5 maximum_select_fusion
  20.5 0.5 maximum_select_fusion.1
  21.6 1.0 %convolution_bitcast_fusion.3 = f32[3,2,160,192,1]{3,2,1,4,0:T(8,128)S(1)} fusion(f32[3,1,192,192]{3,2,1,0:T(8,128)S(1)} %get-tuple-element.18, f32[3,1,192,192]{3,2,1,0:T(8,128)S(1)} %get-tuple-element.17, f32[2,2,192,192]{3,2,1,0:T(8,128)S(1)} %pad_maximum_fusion.1), kind=kOutput, calls=%fused_computation.5 | convolution fusion | flops 424894464 | bytes 2572288 | tf_op jit(solution)/shard_map/dcab,icbj->idaj/dot_general | solution.py:146
  22.6 1.0 %convolution_bitcast_fusion.2 = f32[3,2,160,192]{3,2,1,0:T(8,128)S(1)} fusion(f32[3,2,160,192,1]{3,2,1,4,0:T(8,128)S(1)} %convolution_bitcast_fusion.3, f32[2,2,192,192]{3,2,1,0:T(8,128)S(1)} %pad_maximum_fusion.1), kind=kOutput, calls=%fused_computation.4 | convolution fusion | flops 424673280 | bytes 2064384 | tf_op jit(solution)/shard_map/dcyj,icxj->idxy/dot_general | solution.py:149
  23.7 1.0 %convolution_bitcast_fusion.7 = f32[3,2,144,192,1]{3,2,1,4,0:T(8,128)S(1)} fusion(f32[3,1,160,192]{3,2,1,0:T(8,128)S(1)} %get-tuple-element.28, f32[3,1,160,192]{3,2,1,0:T(8,128)S(1)} %get-tuple-element.27, f32[2,2,192,192]{3,2,1,0:T(8,128)S(1)} %pad_maximum_fusion.1), kind=kOutput, calls=%fused_computation.9 | convolution fusion | flops 318689280 | bytes 2236416 | tf_op jit(solution)/shard_map/dcab,icbj->idaj/dot_general | solution.py:146
  24.8 0.9 %convolution_bitcast_fusion.5 = f32[3,2,144,192]{3,2,1,0:T(8,128)S(1)} fusion(f32[3,2,144,192,1]{3,2,1,4,0:T(8,128)S(1)} %convolution_bitcast_fusion.7, f32[2,2,192,192]{3,2,1,0:T(8,128)S(1)} %pad_maximum_fusion.1), kind=kOutput, calls=%fused_computation.7 | convolution fusion | flops 382205952 | bytes 1916928 | tf_op jit(solution)/shard_map/dcyj,icxj->idxy/dot_general | solution.py:149
  26.2 0.7 %convolution_bitcast_fusion.9 = f32[3,2,96,192]{3,2,1,0:T(8,128)S(1)} fusion(f32[3,2,96,192,1]{3,2,1,4,0:T(8,128)S(1)} %convolution_bitcast_fusion.11, f32[2,2,192,192]{3,2,1,0:T(8,128)S(1)} %pad_maximum_fusion.1), kind=kOutput, calls=%fused_computation.11 | convolution fusion | flops 254803968 | bytes 1474560 | tf_op jit(solution)/shard_map/dcyj,icxj->idxy/dot_general | solution.py:149
  27.8 1.3 %collective-permute-start.3 = (f32[6,64,128]{2,1,0:T(8,128)S(1)}, f32[6,64,128]{2,1,0:T(8,128)S(1)}, u32[]{:S(2)}, u32[]{:S(2)}) collective-permute-start(f32[6,64,128]{2,1,0:T(8,128)S(1)} %bitcast.479), channel_id=1, source_target_pairs={{0,6},{4,10},{8,14},{1,7},{5,11},{9,15},{16,22},{20,26},{24,30},{1... | collective-permute-start | bytes 589832 | tf_op jit(solution)/shard_map/ppermute | solution.py:171
  29.1 1.3 %collective-permute-start.4 = (f32[6,64,128]{2,1,0:T(8,128)S(1)}, f32[6,64,128]{2,1,0:T(8,128)S(1)}, u32[]{:S(2)}, u32[]{:S(2)}) collective-permute-start(f32[6,64,128]{2,1,0:T(8,128)S(1)} %bitcast.480), channel_id=1, source_target_pairs={{0,2},{4,6},{8,10},{12,14},{1,3},{5,7},{9,11},{13,15},{16,18},{20,... | collective-permute-start | bytes 589832 | tf_op jit(solution)/shard_map/ppermute | solution.py:172
  30.4 1.5 %collective-permute-start.5 = (f32[6,64,128]{2,1,0:T(8,128)S(1)}, f32[6,64,128]{2,1,0:T(8,128)S(1)}, u32[]{:S(2)}, u32[]{:S(2)}) collective-permute-start(f32[6,64,128]{2,1,0:T(8,128)S(1)} %bitcast.481), channel_id=1, source_target_pairs={{4,2},{8,6},{12,10},{5,3},{9,7},{13,11},{20,18},{24,22},{28,26},{2... | collective-permute-start | bytes 589832 | tf_op jit(solution)/shard_map/ppermute | solution.py:173
  31.9 4.9 %collective-permute-done.3 = f32[6,64,128]{2,1,0:T(8,128)S(1)} collective-permute-done((f32[6,64,128]{2,1,0:T(8,128)S(1)}, f32[6,64,128]{2,1,0:T(8,128)S(1)}, u32[]{:S(2)}, u32[]{:S(2)}) %collective-permute-start.3) | collective-permute-done | bytes 196640 | tf_op jit(solution)/shard_map/ppermute | solution.py:171
  36.8 9.1 %collective-permute-done.4 = f32[6,64,128]{2,1,0:T(8,128)S(1)} collective-permute-done((f32[6,64,128]{2,1,0:T(8,128)S(1)}, f32[6,64,128]{2,1,0:T(8,128)S(1)}, u32[]{:S(2)}, u32[]{:S(2)}) %collective-permute-start.4) | collective-permute-done | bytes 196640 | tf_op jit(solution)/shard_map/ppermute | solution.py:172
  46.4 0.5 collective-permute-start.6
  46.9 1.2 %collective-permute-done.6 = f32[3,192,128]{2,1,0:T(8,128)S(1)} collective-permute-done((f32[3,192,128]{2,1,0:T(8,128)S(1)}, f32[3,192,128]{2,1,0:T(8,128)S(1)}, u32[]{:S(2)}, u32[]{:S(2)}) %collective-permute-start.6) | collective-permute-done | bytes 294944 | tf_op jit(solution)/shard_map/ppermute | solution.py:92
  48.9 1.0 %convolution_bitcast_fusion.1 = f32[3,2,160,192,1]{3,2,1,4,0:T(8,128)S(1)} fusion(f32[3,1,192,192]{3,2,1,0:T(8,128)S(1)} %get-tuple-element.10, f32[3,1,192,192]{3,2,1,0:T(8,128)S(1)} %get-tuple-element.9, f32[2,2,192,192]{3,2,1,0:T(8,128)S(1)} %pad_maximum_fusion.1), kind=kOutput, calls=%fused_computation.3 | convolution fusion | flops 424894464 | bytes 2572288 | tf_op jit(solution)/shard_map/dcab,icbj->idaj/dot_general | solution.py:146
  49.9 1.0 %convolution_bitcast_fusion = f32[3,2,160,192]{3,2,1,0:T(8,128)S(1)} fusion(f32[3,2,160,192,1]{3,2,1,4,0:T(8,128)S(1)} %convolution_bitcast_fusion.1, f32[2,2,192,192]{3,2,1,0:T(8,128)S(1)} %pad_maximum_fusion.1), kind=kOutput, calls=%fused_computation.2 | convolution fusion | flops 424673280 | bytes 2064384 | tf_op jit(solution)/shard_map/dcyj,icxj->idxy/dot_general | solution.py:149
  51.0 1.0 %convolution_bitcast_fusion.6 = f32[3,2,144,192,1]{3,2,1,4,0:T(8,128)S(1)} fusion(f32[3,1,160,192]{3,2,1,0:T(8,128)S(1)} %get-tuple-element.26, f32[3,1,160,192]{3,2,1,0:T(8,128)S(1)} %get-tuple-element.25, f32[2,2,192,192]{3,2,1,0:T(8,128)S(1)} %pad_maximum_fusion.1), kind=kOutput, calls=%fused_computation.8 | convolution fusion | flops 318689280 | bytes 2236416 | tf_op jit(solution)/shard_map/dcab,icbj->idaj/dot_general | solution.py:146
  52.0 0.9 %convolution_bitcast_fusion.4 = f32[3,2,144,192]{3,2,1,0:T(8,128)S(1)} fusion(f32[3,2,144,192,1]{3,2,1,4,0:T(8,128)S(1)} %convolution_bitcast_fusion.6, f32[2,2,192,192]{3,2,1,0:T(8,128)S(1)} %pad_maximum_fusion.1), kind=kOutput, calls=%fused_computation.6 | convolution fusion | flops 382205952 | bytes 1916928 | tf_op jit(solution)/shard_map/dcyj,icxj->idxy/dot_general | solution.py:149
  53.5 0.7 %convolution_bitcast_fusion.8 = f32[3,2,96,192]{3,2,1,0:T(8,128)S(1)} fusion(f32[3,2,96,192,1]{3,2,1,4,0:T(8,128)S(1)} %convolution_bitcast_fusion.10, f32[2,2,192,192]{3,2,1,0:T(8,128)S(1)} %pad_maximum_fusion.1), kind=kOutput, calls=%fused_computation.10 | convolution fusion | flops 254803968 | bytes 1474560 | tf_op jit(solution)/shard_map/dcyj,icxj->idxy/dot_general | solution.py:149
  54.6 1.1 %fusion.5 = f32[1,3,2,64,128]{4,3,2,1,0:T(8,128)} fusion(f32[3,2,64,192,1]{3,2,1,4,0:T(8,128)S(1)} %convolution_bitcast_fusion.12, f32[3,64,2,128,1]{3,1,4,2,0:T(8,128)S(1)} %fusion.33, f32[2,2,192,192]{3,2,1,0:T(8,128)S(1)} %pad_maximum_fusion.1, pred[]{:T(512)S(6)} %eq.7, pred[]{:T(512)S(6)} %eq.16, pred[]{:T(512)S(6)} %eq.6), kind=kOutput, calls=%fused_computation.26 | convolution fusion | flops 113442816 | bytes 1835011 | tf_op jit(solution)/shard_map/dcyj,icxj->idxy/dot_general | solution.py:149
  (101 shorter events, 6.3 us)
Async XLA Ops:
  0.0 1.5 %copy-start = (f32[3,2,64,128]{3,2,1,0:T(8,128)S(1)}, f32[3,2,64,128]{3,2,1,0:T(8,128)}, u32[]{:S(2)}) copy-start(f32[3,2,64,128]{3,2,1,0:T(8,128)} %param.4) | copy-start | bytes 589828
  1.4 6.8 %copy-start.5 = (f32[2,33]{1,0:T(2,128)S(1)}, f32[2,33]{1,0:T(2,128)}, u32[]{:S(2)}) copy-start(f32[2,33]{1,0:T(2,128)} %param.7) | copy-start | bytes 796
  1.6 13.1 %collective-permute-start.1 = (f32[11,64,128]{2,1,0:T(8,128)S(1)}, f32[11,64,128]{2,1,0:T(8,128)S(1)}, u32[]{:S(2)}, u32[]{:S(2)}) collective-permute-start(f32[11,64,128]{2,1,0:T(8,128)S(1)} %constant_dynamic-update-slice_fusion.5), channel_id=1, source_target_pairs={{4,0},{8,4},{12,8},{5,1},{9,5},{13,9},{6,2},{10,6},{14,10},{7,3},{... | collective-permute-start | bytes 1081352 | tf_op jit(solution)/shard_map/ppermute | solution.py:67
  3.7 10.9 %collective-permute-start = (f32[11,64,128]{2,1,0:T(8,128)S(1)}, f32[11,64,128]{2,1,0:T(8,128)S(1)}, u32[]{:S(2)}, u32[]{:S(2)}) collective-permute-start(f32[11,64,128]{2,1,0:T(8,128)S(1)} %constant_dynamic-update-slice_fusion), channel_id=1, source_target_pairs={{0,4},{4,8},{8,12},{1,5},{5,9},{9,13},{2,6},{6,10},{10,14},{3,7},{... | collective-permute-start | bytes 1081352 | tf_op jit(solution)/shard_map/ppermute | solution.py:66
  11.1 3.5 %copy-start.1 = (f32[192,128]{1,0:T(8,128)S(1)}, f32[192,128]{1,0:T(8,128)}, u32[]{:S(2)}) copy-start(f32[192,128]{1,0:T(8,128)} %get-tuple-element.108) | copy-start | bytes 294916
  11.1 3.5 %copy-start.2 = (f32[192,128]{1,0:T(8,128)S(1)}, f32[192,128]{1,0:T(8,128)}, u32[]{:S(2)}) copy-start(f32[192,128]{1,0:T(8,128)} %get-tuple-element.109) | copy-start | bytes 294916
  11.1 3.5 %copy-start.3 = (f32[192,128]{1,0:T(8,128)S(1)}, f32[192,128]{1,0:T(8,128)}, u32[]{:S(2)}) copy-start(f32[192,128]{1,0:T(8,128)} %get-tuple-element.110) | copy-start | bytes 294916
  11.1 3.5 %copy-start.4 = (f32[192,128]{1,0:T(8,128)S(1)}, f32[192,128]{1,0:T(8,128)}, u32[]{:S(2)}) copy-start(f32[192,128]{1,0:T(8,128)} %get-tuple-element.111) | copy-start | bytes 294916
  16.0 3.7 %collective-permute-start.2 = (f32[7,192,128]{2,1,0:T(8,128)S(1)}, f32[7,192,128]{2,1,0:T(8,128)S(1)}, u32[]{:S(2)}, u32[]{:S(2)}) collective-permute-start(f32[7,192,128]{2,1,0:T(8,128)S(1)} %maximum_select_fusion.4), channel_id=1, source_target_pairs={{0,1},{1,0},{2,3},{3,2},{4,5},{5,4},{6,7},{7,6},{8,9},{9,8},{10,11... | collective-permute-start | bytes 2064392 | tf_op jit(solution)/shard_map/ppermute | solution.py:92
  27.8 9.0 %collective-permute-start.3 = (f32[6,64,128]{2,1,0:T(8,128)S(1)}, f32[6,64,128]{2,1,0:T(8,128)S(1)}, u32[]{:S(2)}, u32[]{:S(2)}) collective-permute-start(f32[6,64,128]{2,1,0:T(8,128)S(1)} %bitcast.479), channel_id=1, source_target_pairs={{0,6},{4,10},{8,14},{1,7},{5,11},{9,15},{16,22},{20,26},{24,30},{1... | collective-permute-start | bytes 589832 | tf_op jit(solution)/shard_map/ppermute | solution.py:171
  29.1 16.8 %collective-permute-start.4 = (f32[6,64,128]{2,1,0:T(8,128)S(1)}, f32[6,64,128]{2,1,0:T(8,128)S(1)}, u32[]{:S(2)}, u32[]{:S(2)}) collective-permute-start(f32[6,64,128]{2,1,0:T(8,128)S(1)} %bitcast.480), channel_id=1, source_target_pairs={{0,2},{4,6},{8,10},{12,14},{1,3},{5,7},{9,11},{13,15},{16,18},{20,... | collective-permute-start | bytes 589832 | tf_op jit(solution)/shard_map/ppermute | solution.py:172
  30.4 15.5 %collective-permute-start.5 = (f32[6,64,128]{2,1,0:T(8,128)S(1)}, f32[6,64,128]{2,1,0:T(8,128)S(1)}, u32[]{:S(2)}, u32[]{:S(2)}) collective-permute-start(f32[6,64,128]{2,1,0:T(8,128)S(1)} %bitcast.481), channel_id=1, source_target_pairs={{4,2},{8,6},{12,10},{5,3},{9,7},{13,11},{20,18},{24,22},{28,26},{2... | collective-permute-start | bytes 589832 | tf_op jit(solution)/shard_map/ppermute | solution.py:173
  46.4 1.8 %collective-permute-start.6 = (f32[3,192,128]{2,1,0:T(8,128)S(1)}, f32[3,192,128]{2,1,0:T(8,128)S(1)}, u32[]{:S(2)}, u32[]{:S(2)}) collective-permute-start(f32[3,192,128]{2,1,0:T(8,128)S(1)} %maximum_select_fusion.5), channel_id=1, source_target_pairs={{0,1},{1,0},{2,3},{3,2},{4,5},{5,4},{6,7},{7,6},{8,9},{9,8},{10,11... | collective-permute-start | bytes 884744 | tf_op jit(solution)/shard_map/ppermute | solution.py:92

commit v15 on v14

--- a/solution.py
+++ b/solution.py
@@ -119,15 +119,16 @@
     width = cols + reach
     tall = rows + 2 * reach
     band = toeplitz(kernel, max(tall, width), HALF)
-    (field_grown, trans_grown), band = grow(
-        jnp.concatenate([incident.reshape(2 * illum, rows, cols), trans_own.reshape(2 * slices, rows, cols)]),
+    first_moved = modulate(incident, trans_own[0])
+    (moved_grown, trans_grown), band = grow(
+        jnp.concatenate([first_moved.reshape(2 * illum, rows, cols), trans_own[1:].reshape(2 * slices - 2, rows, cols)]),
         reach,
-        (2 * illum, 2 * slices),
+        (2 * illum, 2 * slices - 2),
         band,
-        [reach] * (2 * illum) + [reach - HALF * s for s in range(slices) for _ in range(2)],
+        [reach] * (2 * illum) + [reach - HALF * s for s in range(1, slices) for _ in range(2)],
     )
-    first_field = field_grown.reshape(illum, 2, rows + 2 * reach, cols + reach)
-    trans_reg = trans_grown.reshape(slices, 2, rows + 2 * reach, cols + reach)
+    first_field = moved_grown.reshape(illum, 2, tall, width)
+    trans_rest = trans_grown.reshape(slices - 1, 2, tall, width)
     col_band = band[:, :, :width, :width]
     margins = [8 if (tall - 2 * HALF * (s + 1)) % 128 == 0 and s + 1 < slices else 0 for s in range(slices)]
     row_bands = [
@@ -137,12 +138,17 @@
 
     last_band = jnp.where(wave == 0, col_band[:, :, :cols], col_band[:, :, reach:reach + cols])
 
-    def depth_section(field):
+    def depth_section(field, trans_first, late=None):
         current = field
         for s in range(slices):
             if s and margins[s - 1]:
                 current = current[:, :, margins[s - 1]: current.shape[2] - margins[s - 1]]
-            moved = modulate(current, trans_reg[s, :, HALF * s: tall - HALF * s])
+            if s:
+                moved = modulate(current, trans_rest[s - 1, :, HALF * s: tall - HALF * s])
+            elif trans_first is None:
+                moved = current
+            else:
+                moved = modulate(current, trans_first)
             rows_done = jnp.einsum(
                 "dcab,icbj->idaj", row_bands[s], moved, precision=lax.Precision.HIGH
             )
@@ -152,7 +158,10 @@
                 rows_done,
                 precision=lax.Precision.HIGH,
             )
-        return current
+            if s == 0 and late is not None:
+                current, late = lax.optimization_barrier((current, late))
+                (late,), _ = grow(late, reach, (2,), jnp.zeros((), jnp.float32))
+        return current, late
 
     exits = jnp.zeros(incident.shape, jnp.float32)
     tiles = lax.axis_size("tile")
@@ -161,11 +170,13 @@
     own_pairs = [(spot(t, d), spot(t, d + 1)) for t in range(tiles) for d in ahead]
     prev_pairs = [(spot(t - 1, d), spot(t, d + 1)) for t in range(1, tiles) for d in ahead]
     next_pairs = [(spot(t + 1, d), spot(t, d + 1)) for t in range(tiles - 1) for d in ahead]
-    field = first_field
+    field, trans_first, late = first_field, None, trans_own[0]
     for step in range(depth_count):
-        result = depth_section(field)
+        result, late = depth_section(field, trans_first, late)
         exits = jnp.where(depth_index == step, result, exits)
         if step + 1 < depth_count:
+            if late is not None:
+                trans_first, late = late, None
             flat = result.reshape(2 * illum, rows, cols)
             grid = ("tile", "depth")
             from_prev = lax.ppermute(flat[:, rows - reach:], grid, prev_pairs)

time: 56 us -> 62.3 us (1.11)
  starting transfers between devices: 11.8 us -> 18.1 us
  local copies, waits for them, and re-layouts: 4.36 us -> 5.19 us
  other arithmetic: 5.65 us -> 4.84 us
    ppermute x1 -> x2, starting transfers between devices: 3.2 us -> 6.4 us  [grow(): lax.ppermute(sent_prev, 'tile', [(i, i + 1) for i in range(tiles - 1)])]
    ppermute x1 -> x2, waiting for transfers between devices: 0.01 us -> 2.71 us  [grow(): lax.ppermute(sent_next, 'tile', [(i + 1, i) for i in range(tiles - 1)])]
    ppermute x1 -> x2, waiting for transfers between devices: 3.3 us -> 0.65 us  [grow(): lax.ppermute(sent_prev, 'tile', [(i, i + 1) for i in range(tiles - 1)])]
    ppermute x1 -> x2, starting transfers between devices: 2.08 us -> 4.17 us  [grow(): lax.ppermute(sent_next, 'tile', [(i + 1, i) for i in range(tiles - 1)])]
    ppermute x1, waiting for transfers between devices: 9.07 us -> 7.86 us  [per_device(): mine = lax.ppermute(flat, grid, own_pairs)]
    ppermute x1, waiting for transfers between devices: 4.89 us -> 6.03 us  [per_device(): from_prev = lax.ppermute(flat[:, rows - reach:], grid, prev_pairs)]
    ppermute x2 -> x3, starting transfers between devices: 2.47 us -> 3.43 us  [widen(): got = lax.ppermute(slabs, 'wave', [(0, 1), (1, 0)])]
    select_n x4 -> x3, other arithmetic: 1.72 us -> 0.92 us  [widen(): out.append(jnp.where(wave == 0, left, right))]
  transfers between devices with their start and end apart: 7 -> 10, of which waited for: 5 -> 6; matrix products, arithmetic and copies ran while one was open for 7% -> 13% of each run, Pallas kernels for 0% -> 0%
where the time goes in v15:
time: 62.3 us; the launch traced here: 62 us
  waiting for transfers between devices  19.8 us (32%)
  starting transfers between devices  18.1 us (29%)
  matrix products  12.6 us (20%)
  local copies, waits for them, and re-layouts  5.19 us (8%)
  other arithmetic  4.84 us (8%)
  between operations  1.5 us (2%)
    ppermute x1, waiting for transfers between devices, per_device(): mine = lax.ppermute(flat, grid, own_pairs)  7.86 us
    dot_general x8, matrix products, depth_section(): jnp.einsum('dcyj,icxj->idxy', last_band if s == slices - 1 else col_band,...  6.54 us
    ppermute x2, starting transfers between devices, grow(): lax.ppermute(sent_prev, 'tile', [(i, i + 1) for i in range(tiles - 1)])  6.4 us
    dot_general x8, matrix products, depth_section(): jnp.einsum('dcab,icbj->idaj', row_bands[s], moved, precision=lax.Precisio...  6.04 us
    ppermute x1, waiting for transfers between devices, per_device(): from_prev = lax.ppermute(flat[:, rows - reach:], grid, prev_pairs)  6.03 us
    ppermute x2, starting transfers between devices, grow(): lax.ppermute(sent_next, 'tile', [(i + 1, i) for i in range(tiles - 1)])  4.17 us
    ppermute x3, starting transfers between devices, widen(): got = lax.ppermute(slabs, 'wave', [(0, 1), (1, 0)])  3.43 us
    ppermute x2, waiting for transfers between devices, grow(): lax.ppermute(sent_next, 'tile', [(i + 1, i) for i in range(tiles - 1)])  2.71 us
  transfers between devices with their start and end apart: 10, of which 6 were waited for; matrix products, arithmetic and copies ran while one was open for 13% of the time, Pallas kernels for 0%

profile of v15, /device:TPU:15, one launch (start us, length us, event | category | flops | bytes accessed | tf_op | source)
XLA Modules:
  0.0 62.0 jit_solution(17948507109598407739)
XLA Ops:
  0.0 1.4 %fusion.71 = (f32[4,1,64,128]{3,2,1,0:T(8,128)S(1)}, f32[4,1,64,128]{3,2,1,0:T(8,128)S(1)}, f32[4,64,128]{2,1,0:T(8,128)S(1)}, f32[4,64,128]{2,1,0:T(8,128)S(1)}) fusion(bf16[4,64,128]{2,1,0:T(8,128)(2,1)} %param.5, bf16[4,64,128]{2,1,0:T(8,128)(2,1)} %param.6), kind=kLoop, calls=%fused_computation.253 | loop fusion | flops 163840 | bytes 655360 | tf_op jit(solution)/shard_map/stack | solution.py:25
  1.7 3.2 %collective-permute-start = (f32[9,64,128]{2,1,0:T(8,128)S(1)}, f32[9,64,128]{2,1,0:T(8,128)S(1)}, u32[]{:S(2)}, u32[]{:S(2)}) collective-permute-start(f32[9,64,128]{2,1,0:T(8,128)S(1)} %get-tuple-element.96), channel_id=1, source_target_pairs={{0,4},{4,8},{8,12},{1,5},{5,9},{9,13},{2,6},{6,10},{10,14},{3,7},{... | collective-permute-start | bytes 884744 | tf_op jit(solution)/shard_map/ppermute | solution.py:66
  4.9 2.1 %collective-permute-start.1 = (f32[9,64,128]{2,1,0:T(8,128)S(1)}, f32[9,64,128]{2,1,0:T(8,128)S(1)}, u32[]{:S(2)}, u32[]{:S(2)}) collective-permute-start(f32[9,64,128]{2,1,0:T(8,128)S(1)} %get-tuple-element.97), channel_id=1, source_target_pairs={{4,0},{8,4},{12,8},{5,1},{9,5},{13,9},{6,2},{10,6},{14,10},{7,3},{... | collective-permute-start | bytes 884744 | tf_op jit(solution)/shard_map/ppermute | solution.py:67
  7.0 0.6 constant_dynamic-update-slice_fusion.14
  7.6 0.6 %multiply_reduce_fusion = f32[]{:T(128)} fusion(f32[2,33]{1,0:T(2,128)S(1)} %copy-done.4), kind=kLoop, calls=%fused_computation.242 | loop fusion | flops 131 | bytes 268 | tf_op jit(solution)/shard_map/reduce_sum | solution.py:108
  9.7 0.8 %reshape.103 = f32[2,192,383]{2,1,0:T(8,128)S(1)} reshape(f32[2,73536]{1,0:T(2,128)S(1)} %slice.529) | data formatting | bytes 1176576 | tf_op jit(solution)/shard_map/reshape | solution.py:15
  10.8 0.6 %collective-permute-done = f32[9,64,128]{2,1,0:T(8,128)S(1)} collective-permute-done((f32[9,64,128]{2,1,0:T(8,128)S(1)}, f32[9,64,128]{2,1,0:T(8,128)S(1)}, u32[]{:S(2)}, u32[]{:S(2)}) %collective-permute-start) | collective-permute-done | bytes 294944 | tf_op jit(solution)/shard_map/ppermute | solution.py:66
  11.6 2.7 %collective-permute-done.1 = f32[9,64,128]{2,1,0:T(8,128)S(1)} collective-permute-done((f32[9,64,128]{2,1,0:T(8,128)S(1)}, f32[9,64,128]{2,1,0:T(8,128)S(1)}, u32[]{:S(2)}, u32[]{:S(2)}) %collective-permute-start.1) | collective-permute-done | bytes 294944 | tf_op jit(solution)/shard_map/ppermute | solution.py:67
  14.5 0.6 copy-done.2
  15.2 0.7 %copy-done.3 = f32[192,128]{1,0:T(8,128)S(1)} copy-done((f32[192,128]{1,0:T(8,128)S(1)}, f32[192,128]{1,0:T(8,128)}, u32[]{:S(2)}) %copy-start.3) | copy-done | bytes 98328
  16.8 1.9 %collective-permute-start.2 = (f32[6,192,128]{2,1,0:T(8,128)S(1)}, f32[6,192,128]{2,1,0:T(8,128)S(1)}, u32[]{:S(2)}, u32[]{:S(2)}) collective-permute-start(f32[6,192,128]{2,1,0:T(8,128)S(1)} %maximum_select_fusion.3), channel_id=1, source_target_pairs={{0,1},{1,0},{2,3},{3,2},{4,5},{5,4},{6,7},{7,6},{8,9},{9,8},{10,11... | collective-permute-start | bytes 1769480 | tf_op jit(solution)/shard_map/ppermute | solution.py:92
  18.8 1.5 %collective-permute-done.2 = f32[6,192,128]{2,1,0:T(8,128)S(1)} collective-permute-done((f32[6,192,128]{2,1,0:T(8,128)S(1)}, f32[6,192,128]{2,1,0:T(8,128)S(1)}, u32[]{:S(2)}, u32[]{:S(2)}) %collective-permute-start.2) | collective-permute-done | bytes 589856 | tf_op jit(solution)/shard_map/ppermute | solution.py:92
  20.6 1.2 %convolution_bitcast_fusion.3 = f32[3,2,160,192,1]{3,2,1,4,0:T(8,128)S(1)} fusion(f32[3,2,192,64]{3,2,1,0:T(8,128)S(1)} %bitcast.464, f32[3,2,192,128]{3,2,1,0:T(8,128)S(1)} %bitcast.463, f32[2,2,192,192]{3,2,1,0:T(8,128)S(1)} %pad_maximum_fusion, pred[]{:T(512)S(6)} %eq.7), kind=kOutput, calls=%fused_computation.3 | convolution fusion | flops 425336832 | bytes 2572289 | tf_op jit(solution)/shard_map/dcab,icbj->idaj/dot_general | solution.py:152
  21.8 1.0 %convolution_bitcast_fusion.2 = f32[3,2,160,192]{3,2,1,0:T(8,128)S(1)} fusion(f32[3,2,160,192,1]{3,2,1,4,0:T(8,128)S(1)} %convolution_bitcast_fusion.3, f32[2,2,192,192]{3,2,1,0:T(8,128)S(1)} %pad_maximum_fusion), kind=kOutput, calls=%fused_computation.2 | convolution fusion | flops 424673280 | bytes 2064384 | tf_op jit(solution)/shard_map/dcyj,icxj->idxy/dot_general | solution.py:155
  22.8 3.2 %collective-permute-start.7 = (f32[2,64,128]{2,1,0:T(8,128)S(1)}, f32[2,64,128]{2,1,0:T(8,128)S(1)}, u32[]{:S(2)}, u32[]{:S(2)}) collective-permute-start(f32[2,64,128]{2,1,0:T(8,128)S(1)} %fusion.62), channel_id=1, source_target_pairs={{0,4},{4,8},{8,12},{1,5},{5,9},{9,13},{2,6},{6,10},{10,14},{3,7},{... | collective-permute-start | bytes 196616 | tf_op jit(solution)/shard_map/ppermute | solution.py:66
  26.0 2.1 %collective-permute-start.8 = (f32[2,64,128]{2,1,0:T(8,128)S(1)}, f32[2,64,128]{2,1,0:T(8,128)S(1)}, u32[]{:S(2)}, u32[]{:S(2)}) collective-permute-start(f32[2,64,128]{2,1,0:T(8,128)S(1)} %fusion.62), channel_id=1, source_target_pairs={{4,0},{8,4},{12,8},{5,1},{9,5},{13,9},{6,2},{10,6},{14,10},{7,3},{... | collective-permute-start | bytes 196616 | tf_op jit(solution)/shard_map/ppermute | solution.py:67
  28.6 1.0 %convolution_bitcast_fusion.7 = f32[3,2,144,192,1]{3,2,1,4,0:T(8,128)S(1)} fusion(f32[3,1,160,192]{3,2,1,0:T(8,128)S(1)} %get-tuple-element.20, f32[3,1,160,192]{3,2,1,0:T(8,128)S(1)} %get-tuple-element.19, f32[2,2,192,192]{3,2,1,0:T(8,128)S(1)} %pad_maximum_fusion), kind=kOutput, calls=%fused_computation.7 | convolution fusion | flops 318689280 | bytes 2236416 | tf_op jit(solution)/shard_map/dcab,icbj->idaj/dot_general | solution.py:152
  29.7 0.9 %convolution_bitcast_fusion.5 = f32[3,2,144,192]{3,2,1,0:T(8,128)S(1)} fusion(f32[3,2,144,192,1]{3,2,1,4,0:T(8,128)S(1)} %convolution_bitcast_fusion.7, f32[2,2,192,192]{3,2,1,0:T(8,128)S(1)} %pad_maximum_fusion), kind=kOutput, calls=%fused_computation.5 | convolution fusion | flops 382205952 | bytes 1916928 | tf_op jit(solution)/shard_map/dcyj,icxj->idxy/dot_general | solution.py:155
  31.1 0.7 %convolution_bitcast_fusion.9 = f32[3,2,96,192]{3,2,1,0:T(8,128)S(1)} fusion(f32[3,2,96,192,1]{3,2,1,4,0:T(8,128)S(1)} %convolution_bitcast_fusion.11, f32[2,2,192,192]{3,2,1,0:T(8,128)S(1)} %pad_maximum_fusion), kind=kOutput, calls=%fused_computation.9 | convolution fusion | flops 254803968 | bytes 1474560 | tf_op jit(solution)/shard_map/dcyj,icxj->idxy/dot_general | solution.py:155
  32.7 1.0 %collective-permute-start.9 = (f32[1,192,128]{2,1,0:T(8,128)S(1)}, f32[1,192,128]{2,1,0:T(8,128)S(1)}, u32[]{:S(2)}, u32[]{:S(2)}) collective-permute-start(f32[1,192,128]{2,1,0:T(8,128)S(1)} %maximum_select_fusion.6), channel_id=1, source_target_pairs={{0,1},{1,0},{2,3},{3,2},{4,5},{5,4},{6,7},{7,6},{8,9},{9,8},{10,11... | collective-permute-start | bytes 294920 | tf_op jit(solution)/shard_map/ppermute | solution.py:92
  34.1 1.3 %collective-permute-start.3 = (f32[6,64,128]{2,1,0:T(8,128)S(1)}, f32[6,64,128]{2,1,0:T(8,128)S(1)}, u32[]{:S(2)}, u32[]{:S(2)}) collective-permute-start(f32[6,64,128]{2,1,0:T(8,128)S(1)} %bitcast.460), channel_id=1, source_target_pairs={{0,6},{4,10},{8,14},{1,7},{5,11},{9,15},{16,22},{20,26},{24,30},{1... | collective-permute-start | bytes 589832 | tf_op jit(solution)/shard_map/ppermute | solution.py:182
  35.4 1.3 %collective-permute-start.4 = (f32[6,64,128]{2,1,0:T(8,128)S(1)}, f32[6,64,128]{2,1,0:T(8,128)S(1)}, u32[]{:S(2)}, u32[]{:S(2)}) collective-permute-start(f32[6,64,128]{2,1,0:T(8,128)S(1)} %bitcast.461), channel_id=1, source_target_pairs={{0,2},{4,6},{8,10},{12,14},{1,3},{5,7},{9,11},{13,15},{16,18},{20,... | collective-permute-start | bytes 589832 | tf_op jit(solution)/shard_map/ppermute | solution.py:183
  36.7 1.5 %collective-permute-start.5 = (f32[6,64,128]{2,1,0:T(8,128)S(1)}, f32[6,64,128]{2,1,0:T(8,128)S(1)}, u32[]{:S(2)}, u32[]{:S(2)}) collective-permute-start(f32[6,64,128]{2,1,0:T(8,128)S(1)} %bitcast.462), channel_id=1, source_target_pairs={{4,2},{8,6},{12,10},{5,3},{9,7},{13,11},{20,18},{24,22},{28,26},{2... | collective-permute-start | bytes 589832 | tf_op jit(solution)/shard_map/ppermute | solution.py:184
  38.3 6.0 %collective-permute-done.3 = f32[6,64,128]{2,1,0:T(8,128)S(1)} collective-permute-done((f32[6,64,128]{2,1,0:T(8,128)S(1)}, f32[6,64,128]{2,1,0:T(8,128)S(1)}, u32[]{:S(2)}, u32[]{:S(2)}) %collective-permute-start.3) | collective-permute-done | bytes 196640 | tf_op jit(solution)/shard_map/ppermute | solution.py:182
  44.3 7.9 %collective-permute-done.4 = f32[6,64,128]{2,1,0:T(8,128)S(1)} collective-permute-done((f32[6,64,128]{2,1,0:T(8,128)S(1)}, f32[6,64,128]{2,1,0:T(8,128)S(1)}, u32[]{:S(2)}, u32[]{:S(2)}) %collective-permute-start.4) | collective-permute-done | bytes 196640 | tf_op jit(solution)/shard_map/ppermute | solution.py:183
  53.4 1.0 %collective-permute-done.6 = f32[3,192,128]{2,1,0:T(8,128)S(1)} collective-permute-done((f32[3,192,128]{2,1,0:T(8,128)S(1)}, f32[3,192,128]{2,1,0:T(8,128)S(1)}, u32[]{:S(2)}, u32[]{:S(2)}) %collective-permute-start.6) | collective-permute-done | bytes 294944 | tf_op jit(solution)/shard_map/ppermute | solution.py:92
  55.1 1.0 %convolution_bitcast_fusion.1 = f32[3,2,160,192,1]{3,2,1,4,0:T(8,128)S(1)} fusion(f32[3,1,192,192]{3,2,1,0:T(8,128)S(1)} %get-tuple-element.16, f32[3,1,192,192]{3,2,1,0:T(8,128)S(1)} %get-tuple-element.15, f32[2,2,192,192]{3,2,1,0:T(8,128)S(1)} %pad_maximum_fusion), kind=kOutput, calls=%fused_computation.1 | convolution fusion | flops 424894464 | bytes 2572288 | tf_op jit(solution)/shard_map/dcab,icbj->idaj/dot_general | solution.py:152
  56.1 1.0 %convolution_bitcast_fusion = f32[3,2,160,192]{3,2,1,0:T(8,128)S(1)} fusion(f32[3,2,160,192,1]{3,2,1,4,0:T(8,128)S(1)} %convolution_bitcast_fusion.1, f32[2,2,192,192]{3,2,1,0:T(8,128)S(1)} %pad_maximum_fusion), kind=kOutput, calls=%fused_computation | convolution fusion | flops 424673280 | bytes 2064384 | tf_op jit(solution)/shard_map/dcyj,icxj->idxy/dot_general | solution.py:155
  57.2 1.0 %convolution_bitcast_fusion.6 = f32[3,2,144,192,1]{3,2,1,4,0:T(8,128)S(1)} fusion(f32[3,1,160,192]{3,2,1,0:T(8,128)S(1)} %get-tuple-element.18, f32[3,1,160,192]{3,2,1,0:T(8,128)S(1)} %get-tuple-element.17, f32[2,2,192,192]{3,2,1,0:T(8,128)S(1)} %pad_maximum_fusion), kind=kOutput, calls=%fused_computation.6 | convolution fusion | flops 318689280 | bytes 2236416 | tf_op jit(solution)/shard_map/dcab,icbj->idaj/dot_general | solution.py:152
  58.3 0.9 %convolution_bitcast_fusion.4 = f32[3,2,144,192]{3,2,1,0:T(8,128)S(1)} fusion(f32[3,2,144,192,1]{3,2,1,4,0:T(8,128)S(1)} %convolution_bitcast_fusion.6, f32[2,2,192,192]{3,2,1,0:T(8,128)S(1)} %pad_maximum_fusion), kind=kOutput, calls=%fused_computation.4 | convolution fusion | flops 382205952 | bytes 1916928 | tf_op jit(solution)/shard_map/dcyj,icxj->idxy/dot_general | solution.py:155
  59.7 0.7 %convolution_bitcast_fusion.8 = f32[3,2,96,192]{3,2,1,0:T(8,128)S(1)} fusion(f32[3,2,96,192,1]{3,2,1,4,0:T(8,128)S(1)} %convolution_bitcast_fusion.10, f32[2,2,192,192]{3,2,1,0:T(8,128)S(1)} %pad_maximum_fusion), kind=kOutput, calls=%fused_computation.8 | convolution fusion | flops 254803968 | bytes 1474560 | tf_op jit(solution)/shard_map/dcyj,icxj->idxy/dot_general | solution.py:155
  60.9 1.1 %fusion.10 = f32[1,3,2,64,128]{4,3,2,1,0:T(8,128)} fusion(f32[3,2,64,192,1]{3,2,1,4,0:T(8,128)S(1)} %convolution_bitcast_fusion.12, f32[3,64,2,128,1]{3,1,4,2,0:T(8,128)S(1)} %fusion.39, f32[2,2,192,192]{3,2,1,0:T(8,128)S(1)} %pad_maximum_fusion, pred[]{:T(512)S(6)} %eq.7, pred[]{:T(512)S(6)} %eq.8, pred[]{:T(512)S(6)} %eq.6), kind=kOutput, calls=%fused_computation.28 | convolution fusion | flops 113442816 | bytes 1835011 | tf_op jit(solution)/shard_map/dcyj,icxj->idxy/dot_general | solution.py:155
  (105 shorter events, 7.9 us)
Async XLA Ops:
  0.0 1.5 %copy-start = (f32[3,2,64,128]{3,2,1,0:T(8,128)S(1)}, f32[3,2,64,128]{3,2,1,0:T(8,128)}, u32[]{:S(2)}) copy-start(f32[3,2,64,128]{3,2,1,0:T(8,128)} %param.4) | copy-start | bytes 589828
  1.5 6.1 %copy-start.4 = (f32[2,33]{1,0:T(2,128)S(1)}, f32[2,33]{1,0:T(2,128)}, u32[]{:S(2)}) copy-start(f32[2,33]{1,0:T(2,128)} %param.7) | copy-start | bytes 796
  1.7 9.8 %collective-permute-start = (f32[9,64,128]{2,1,0:T(8,128)S(1)}, f32[9,64,128]{2,1,0:T(8,128)S(1)}, u32[]{:S(2)}, u32[]{:S(2)}) collective-permute-start(f32[9,64,128]{2,1,0:T(8,128)S(1)} %get-tuple-element.96), channel_id=1, source_target_pairs={{0,4},{4,8},{8,12},{1,5},{5,9},{9,13},{2,6},{6,10},{10,14},{3,7},{... | collective-permute-start | bytes 884744 | tf_op jit(solution)/shard_map/ppermute | solution.py:66
  4.9 9.5 %collective-permute-start.1 = (f32[9,64,128]{2,1,0:T(8,128)S(1)}, f32[9,64,128]{2,1,0:T(8,128)S(1)}, u32[]{:S(2)}, u32[]{:S(2)}) collective-permute-start(f32[9,64,128]{2,1,0:T(8,128)S(1)} %get-tuple-element.97), channel_id=1, source_target_pairs={{4,0},{8,4},{12,8},{5,1},{9,5},{13,9},{6,2},{10,6},{14,10},{7,3},{... | collective-permute-start | bytes 884744 | tf_op jit(solution)/shard_map/ppermute | solution.py:67
  10.7 0.9 %copy-start.1 = (f32[192,128]{1,0:T(8,128)S(1)}, f32[192,128]{1,0:T(8,128)}, u32[]{:S(2)}) copy-start(f32[192,128]{1,0:T(8,128)} %get-tuple-element.135) | copy-start | bytes 294916
  14.4 0.6 %copy-start.2 = (f32[192,128]{1,0:T(8,128)}, f32[192,128]{1,0:T(8,128)S(1)}, u32[]{:S(2)}) copy-start(f32[192,128]{1,0:T(8,128)S(1)} %constant_dynamic-update-slice_fusion.15) | copy-start | bytes 294916
  15.1 0.9 %copy-start.3 = (f32[192,128]{1,0:T(8,128)S(1)}, f32[192,128]{1,0:T(8,128)}, u32[]{:S(2)}) copy-start(f32[192,128]{1,0:T(8,128)} %copy-done.2) | copy-start | bytes 294916
  16.8 3.6 %collective-permute-start.2 = (f32[6,192,128]{2,1,0:T(8,128)S(1)}, f32[6,192,128]{2,1,0:T(8,128)S(1)}, u32[]{:S(2)}, u32[]{:S(2)}) collective-permute-start(f32[6,192,128]{2,1,0:T(8,128)S(1)} %maximum_select_fusion.3), channel_id=1, source_target_pairs={{0,1},{1,0},{2,3},{3,2},{4,5},{5,4},{6,7},{7,6},{8,9},{9,8},{10,11... | collective-permute-start | bytes 1769480 | tf_op jit(solution)/shard_map/ppermute | solution.py:92
  22.8 9.6 %collective-permute-start.7 = (f32[2,64,128]{2,1,0:T(8,128)S(1)}, f32[2,64,128]{2,1,0:T(8,128)S(1)}, u32[]{:S(2)}, u32[]{:S(2)}) collective-permute-start(f32[2,64,128]{2,1,0:T(8,128)S(1)} %fusion.62), channel_id=1, source_target_pairs={{0,4},{4,8},{8,12},{1,5},{5,9},{9,13},{2,6},{6,10},{10,14},{3,7},{... | collective-permute-start | bytes 196616 | tf_op jit(solution)/shard_map/ppermute | solution.py:66
  26.0 6.4 %collective-permute-start.8 = (f32[2,64,128]{2,1,0:T(8,128)S(1)}, f32[2,64,128]{2,1,0:T(8,128)S(1)}, u32[]{:S(2)}, u32[]{:S(2)}) collective-permute-start(f32[2,64,128]{2,1,0:T(8,128)S(1)} %fusion.62), channel_id=1, source_target_pairs={{4,0},{8,4},{12,8},{5,1},{9,5},{13,9},{6,2},{10,6},{14,10},{7,3},{... | collective-permute-start | bytes 196616 | tf_op jit(solution)/shard_map/ppermute | solution.py:67
  32.7 5.5 %collective-permute-start.9 = (f32[1,192,128]{2,1,0:T(8,128)S(1)}, f32[1,192,128]{2,1,0:T(8,128)S(1)}, u32[]{:S(2)}, u32[]{:S(2)}) collective-permute-start(f32[1,192,128]{2,1,0:T(8,128)S(1)} %maximum_select_fusion.6), channel_id=1, source_target_pairs={{0,1},{1,0},{2,3},{3,2},{4,5},{5,4},{6,7},{7,6},{8,9},{9,8},{10,11... | collective-permute-start | bytes 294920 | tf_op jit(solution)/shard_map/ppermute | solution.py:92
  34.1 10.2 %collective-permute-start.3 = (f32[6,64,128]{2,1,0:T(8,128)S(1)}, f32[6,64,128]{2,1,0:T(8,128)S(1)}, u32[]{:S(2)}, u32[]{:S(2)}) collective-permute-start(f32[6,64,128]{2,1,0:T(8,128)S(1)} %bitcast.460), channel_id=1, source_target_pairs={{0,6},{4,10},{8,14},{1,7},{5,11},{9,15},{16,22},{20,26},{24,30},{1... | collective-permute-start | bytes 589832 | tf_op jit(solution)/shard_map/ppermute | solution.py:182
  35.4 16.8 %collective-permute-start.4 = (f32[6,64,128]{2,1,0:T(8,128)S(1)}, f32[6,64,128]{2,1,0:T(8,128)S(1)}, u32[]{:S(2)}, u32[]{:S(2)}) collective-permute-start(f32[6,64,128]{2,1,0:T(8,128)S(1)} %bitcast.461), channel_id=1, source_target_pairs={{0,2},{4,6},{8,10},{12,14},{1,3},{5,7},{9,11},{13,15},{16,18},{20,... | collective-permute-start | bytes 589832 | tf_op jit(solution)/shard_map/ppermute | solution.py:183
  36.7 15.5 %collective-permute-start.5 = (f32[6,64,128]{2,1,0:T(8,128)S(1)}, f32[6,64,128]{2,1,0:T(8,128)S(1)}, u32[]{:S(2)}, u32[]{:S(2)}) collective-permute-start(f32[6,64,128]{2,1,0:T(8,128)S(1)} %bitcast.462), channel_id=1, source_target_pairs={{4,2},{8,6},{12,10},{5,3},{9,7},{13,11},{20,18},{24,22},{28,26},{2... | collective-permute-start | bytes 589832 | tf_op jit(solution)/shard_map/ppermute | solution.py:184
  52.7 1.7 %collective-permute-start.6 = (f32[3,192,128]{2,1,0:T(8,128)S(1)}, f32[3,192,128]{2,1,0:T(8,128)S(1)}, u32[]{:S(2)}, u32[]{:S(2)}) collective-permute-start(f32[3,192,128]{2,1,0:T(8,128)S(1)} %maximum_select_fusion.5), channel_id=1, source_target_pairs={{0,1},{1,0},{2,3},{3,2},{4,5},{5,4},{6,7},{7,6},{8,9},{9,8},{10,11... | collective-permute-start | bytes 884744 | tf_op jit(solution)/shard_map/ppermute | solution.py:92

commit v16 on v14

--- a/solution.py
+++ b/solution.py
@@ -73,22 +73,35 @@
             axis=0,
         )
     tall = jnp.stack(columns)
-    rider, tall = lax.optimization_barrier((rider, tall))
-    return widen(tall, halo, splits), rider
-
-
-def widen(tall, halo, splits):
+    early = pair_halves(stack, halo) if 2 * halo == cols else None
+    rider, early, tall = lax.optimization_barrier((rider, early, tall))
+    return widen(tall, halo, splits, early), rider
+
+
+def pair_halves(block, halo):
+    wave = lax.axis_index("wave")
+    if block.shape[0] % 2:
+        block = jnp.concatenate([block, jnp.zeros_like(block[:1])])
+    half = block.shape[0] // 2
+    return jnp.where(
+        wave == 0,
+        jnp.concatenate([block[:half, :, halo:], block[half:, :, halo:]], axis=-1),
+        jnp.concatenate([block[:half, :, :halo], block[half:, :, :halo]], axis=-1),
+    )
+
+
+def widen(tall, halo, splits, early=None):
     wave = lax.axis_index("wave")
     count, cols = tall.shape[0], tall.shape[-1]
     if 2 * halo == cols:
-        if count % 2:
-            tall = jnp.concatenate([tall, jnp.zeros_like(tall[:1])])
-        half = tall.shape[0] // 2
-        slabs = jnp.where(
-            wave == 0,
-            jnp.concatenate([tall[:half, :, halo:], tall[half:, :, halo:]], axis=-1),
-            jnp.concatenate([tall[:half, :, :halo], tall[half:, :, :halo]], axis=-1),
-        )
+        if early is None:
+            slabs = pair_halves(tall, halo)
+        else:
+            lines = tall.shape[1]
+            slabs = jnp.concatenate(
+                [pair_halves(tall[:, :halo], halo), early, pair_halves(tall[:, lines - halo:], halo)],
+                axis=1,
+            )
         got = lax.ppermute(slabs, "wave", [(0, 1), (1, 0)])
         parts = jnp.concatenate([got[..., :halo], got[..., halo:]], axis=0)
     else:

time: 56 us -> 61.9 us (1.11)
  local copies, waits for them, and re-layouts: 4.36 us -> 9.23 us
  other arithmetic: 5.65 us -> 7.75 us
  waiting for transfers between devices: 20.1 us -> 18.9 us
    unnamed x33 -> x38, local copies, waits for them, and re-layouts: 1.91 us -> 5.42 us
    unnamed x13, other arithmetic: 0.11 us -> 1.32 us
    ppermute x1, waiting for transfers between devices: 3.3 us -> 2.09 us  [grow(): lax.ppermute(sent_prev, 'tile', [(i, i + 1) for i in range(tiles - 1)])]
    squeeze x1, local copies, waits for them, and re-layouts: 0.02 us -> 0.9 us  [grow(): from_prev[n, at:at + needs[c]]]
    squeeze x2, local copies, waits for them, and re-layouts: 0.02 us -> 0.64 us  [grow(): stack[c]]
  transfers between devices with their start and end apart: 7 -> 7, of which waited for: 5 -> 5; matrix products, arithmetic and copies ran while one was open for 7% -> 15% of each run, Pallas kernels for 0% -> 0%
where the time goes in v16:
time: 61.9 us; the launch traced here: 61.4 us
  waiting for transfers between devices  18.9 us (31%)
  matrix products  12.3 us (20%)
  starting transfers between devices  11.8 us (19%)
  local copies, waits for them, and re-layouts  9.23 us (15%)
  other arithmetic  7.75 us (13%)
  between operations  1.39 us (2%)
    ppermute x1, waiting for transfers between devices, per_device(): mine = lax.ppermute(flat, grid, own_pairs)  9.1 us
    dot_general x8, matrix products, depth_section(): jnp.einsum('dcyj,icxj->idxy', last_band if s == slices - 1 else col_band,...  6.53 us
    dot_general x8, matrix products, depth_section(): jnp.einsum('dcab,icbj->idaj', row_bands[s], moved, precision=lax.Precisio...  5.8 us
    unnamed x38, local copies, waits for them, and re-layouts  5.42 us
    ppermute x1, waiting for transfers between devices, per_device(): from_prev = lax.ppermute(flat[:, rows - reach:], grid, prev_pairs)  4.87 us
    ppermute x1, starting transfers between devices, grow(): lax.ppermute(sent_prev, 'tile', [(i, i + 1) for i in range(tiles - 1)])  3.19 us
    ppermute x2, waiting for transfers between devices, widen(): got = lax.ppermute(slabs, 'wave', [(0, 1), (1, 0)])  2.88 us
    ppermute x2, starting transfers between devices, widen(): got = lax.ppermute(slabs, 'wave', [(0, 1), (1, 0)])  2.47 us
  transfers between devices with their start and end apart: 7, of which 5 were waited for; matrix products, arithmetic and copies ran while one was open for 15% of the time, Pallas kernels for 0%

profile of v16, /device:TPU:15, one launch (start us, length us, event | category | flops | bytes accessed | tf_op | source)
XLA Modules:
  0.0 61.4 jit_solution(8948122587826176553)
XLA Ops:
  0.0 1.4 %fusion.43 = (f32[4,1,64,128]{3,2,1,0:T(8,128)S(1)}, f32[4,1,64,128]{3,2,1,0:T(8,128)S(1)}) fusion(bf16[4,64,128]{2,1,0:T(8,128)(2,1)} %param.5, bf16[4,64,128]{2,1,0:T(8,128)(2,1)} %param.6), kind=kLoop, calls=%fused_computation.111 | loop fusion | flops 163840 | bytes 393216 | tf_op jit(solution)/shard_map/stack | solution.py:25
  1.5 0.7 %copy.55 = f32[11,64,128]{2,1,0:T(8,128)} copy(f32[11,64,128]{2,1,0:T(8,128)S(1)} %constant_dynamic-update-slice_fusion.8) | data formatting | bytes 720896
  2.3 2.1 %collective-permute-start.1 = (f32[11,64,128]{2,1,0:T(8,128)S(1)}, f32[11,64,128]{2,1,0:T(8,128)S(1)}, u32[]{:S(2)}, u32[]{:S(2)}) collective-permute-start(f32[11,64,128]{2,1,0:T(8,128)S(1)} %constant_dynamic-update-slice_fusion.5), channel_id=1, source_target_pairs={{4,0},{8,4},{12,8},{5,1},{9,5},{13,9},{6,2},{10,6},{14,10},{7,3},{... | collective-permute-start | bytes 1081352 | tf_op jit(solution)/shard_map/ppermute | solution.py:67
  4.4 0.6 %constant_dynamic-update-slice_fusion.2 = f32[11,64,128]{2,1,0:T(8,128)} fusion(f32[11,64,128]{2,1,0:T(8,128)} %copy.55, f32[16,128]{1,0:T(8,128)S(1)} %get-tuple-element.101, f32[48,128]{1,0:T(8,128)S(1)} %get-tuple-element.97), kind=kLoop, calls=%fused_computation.123 | loop fusion | flops 8192 | bytes 65536
  5.6 0.6 constant_dynamic-update-slice_fusion
  6.2 3.2 %collective-permute-start = (f32[11,64,128]{2,1,0:T(8,128)}, f32[11,64,128]{2,1,0:T(8,128)}, u32[]{:S(2)}, u32[]{:S(2)}) collective-permute-start(f32[11,64,128]{2,1,0:T(8,128)} %constant_dynamic-update-slice_fusion), channel_id=1, source_target_pairs={{0,4},{4,8},{8,12},{1,5},{5,9},{9,13},{2,6},{6,10},{10,14},{3,7},{... | collective-permute-start | bytes 1081352 | tf_op jit(solution)/shard_map/ppermute | solution.py:66
  9.6 0.6 %slice_bitcast_fusion.15 = (f32[64,128]{1,0:T(8,128)}, f32[64,128]{1,0:T(8,128)}) fusion(f32[8,64,128]{2,1,0:T(8,128)S(1)} %bitcast.469), kind=kLoop, calls=%fused_computation.197 | loop fusion | bytes 131072 | tf_op jit(solution)/shard_map/squeeze | solution.py:72
  14.0 0.8 %reshape.48 = f32[2,192,383]{2,1,0:T(8,128)S(1)} reshape(f32[2,73536]{1,0:T(2,128)S(1)} %slice.548) | data formatting | bytes 1176576 | tf_op jit(solution)/shard_map/reshape | solution.py:15
  15.3 2.1 %collective-permute-done = f32[11,64,128]{2,1,0:T(8,128)} collective-permute-done((f32[11,64,128]{2,1,0:T(8,128)}, f32[11,64,128]{2,1,0:T(8,128)}, u32[]{:S(2)}, u32[]{:S(2)}) %collective-permute-start) | collective-permute-done | bytes 360480 | tf_op jit(solution)/shard_map/ppermute | solution.py:66
  17.4 0.7 %constant_dynamic-update-slice_fusion.28 = (f32[192,128]{1,0:T(8,128)S(1)}, f32[192,128]{1,0:T(8,128)S(1)}) fusion(f32[192,128]{1,0:T(8,128)S(1)} %constant_dynamic-update-slice_fusion.29, f32[11,64,128]{2,1,0:T(8,128)} %collective-permute-done, f32[192,128]{1,0:T(8,128)S(1)} %copy-done.1), kind=kLoop, calls=%fused_computation.149 | loop fusion | bytes 65536
  18.1 0.8 %constant_dynamic-update-slice_fusion.18 = (f32[192,128]{1,0:T(8,128)S(1)}, f32[192,128]{1,0:T(8,128)S(1)}) fusion(f32[192,128]{1,0:T(8,128)S(1)} %copy-done.4, f32[11,64,128]{2,1,0:T(8,128)} %collective-permute-done, f32[192,128]{1,0:T(8,128)S(1)} %copy-done.5), kind=kLoop, calls=%fused_computation.139 | loop fusion | bytes 98304
  18.9 0.7 %constant_dynamic-update-slice_fusion.38 = (f32[192,128]{1,0:T(8,128)S(1)}, f32[192,128]{1,0:T(8,128)S(1)}) fusion(f32[192,128]{1,0:T(8,128)S(1)} %constant_dynamic-update-slice_fusion.39, f32[11,64,128]{2,1,0:T(8,128)} %collective-permute-done, f32[192,128]{1,0:T(8,128)S(1)} %constant_dynamic-update-slice_fusion.34), kind=kLoop, calls=%fused_computation.159 | loop fusion | bytes 32768
  19.8 0.9 %slice_bitcast_fusion.16 = (f32[64,128]{1,0:T(8,128)S(1)}, f32[64,128]{1,0:T(8,128)S(1)}, f32[64,128]{1,0:T(8,128)S(1)}, f32[64,128]{1,0:T(8,128)S(1)}, f32[64,1...) fusion(f32[11,64,128]{2,1,0:T(8,128)} %collective-permute-done), kind=kLoop, calls=%fused_computation.198 | loop fusion | bytes 524288 | tf_op jit(solution)/shard_map/squeeze | solution.py:72
  21.7 1.9 %collective-permute-start.2 = (f32[7,192,128]{2,1,0:T(8,128)S(1)}, f32[7,192,128]{2,1,0:T(8,128)S(1)}, u32[]{:S(2)}, u32[]{:S(2)}) collective-permute-start(f32[7,192,128]{2,1,0:T(8,128)S(1)} %pad_maximum_fusion.2), channel_id=1, source_target_pairs={{0,1},{1,0},{2,3},{3,2},{4,5},{5,4},{6,7},{7,6},{8,9},{9,8},{10,11... | collective-permute-start | bytes 2064392 | tf_op jit(solution)/shard_map/ppermute | solution.py:105
  23.7 1.7 %collective-permute-done.2 = f32[7,192,128]{2,1,0:T(8,128)S(1)} collective-permute-done((f32[7,192,128]{2,1,0:T(8,128)S(1)}, f32[7,192,128]{2,1,0:T(8,128)S(1)}, u32[]{:S(2)}, u32[]{:S(2)}) %collective-permute-start.2) | collective-permute-done | bytes 688160 | tf_op jit(solution)/shard_map/ppermute | solution.py:105
  27.3 1.0 %convolution_bitcast_fusion.3 = f32[3,2,160,192,1]{3,2,1,4,0:T(8,128)S(1)} fusion(f32[3,1,192,192]{3,2,1,0:T(8,128)S(1)} %get-tuple-element.20, f32[3,1,192,192]{3,2,1,0:T(8,128)S(1)} %get-tuple-element.19, f32[2,2,192,192]{3,2,1,0:T(8,128)S(1)} %pad_maximum_fusion.1), kind=kOutput, calls=%fused_computation.5 | convolution fusion | flops 424894464 | bytes 2572288 | tf_op jit(solution)/shard_map/dcab,icbj->idaj/dot_general | solution.py:159
  28.3 1.0 %convolution_bitcast_fusion.2 = f32[3,2,160,192]{3,2,1,0:T(8,128)S(1)} fusion(f32[3,2,160,192,1]{3,2,1,4,0:T(8,128)S(1)} %convolution_bitcast_fusion.3, f32[2,2,192,192]{3,2,1,0:T(8,128)S(1)} %pad_maximum_fusion.1), kind=kOutput, calls=%fused_computation.4 | convolution fusion | flops 424673280 | bytes 2064384 | tf_op jit(solution)/shard_map/dcyj,icxj->idxy/dot_general | solution.py:162
  29.4 1.0 %convolution_bitcast_fusion.7 = f32[3,2,144,192,1]{3,2,1,4,0:T(8,128)S(1)} fusion(f32[3,1,160,192]{3,2,1,0:T(8,128)S(1)} %get-tuple-element.34, f32[3,1,160,192]{3,2,1,0:T(8,128)S(1)} %get-tuple-element.33, f32[2,2,192,192]{3,2,1,0:T(8,128)S(1)} %pad_maximum_fusion.1), kind=kOutput, calls=%fused_computation.9 | convolution fusion | flops 318689280 | bytes 2236416 | tf_op jit(solution)/shard_map/dcab,icbj->idaj/dot_general | solution.py:159
  30.5 0.9 %convolution_bitcast_fusion.5 = f32[3,2,144,192]{3,2,1,0:T(8,128)S(1)} fusion(f32[3,2,144,192,1]{3,2,1,4,0:T(8,128)S(1)} %convolution_bitcast_fusion.7, f32[2,2,192,192]{3,2,1,0:T(8,128)S(1)} %pad_maximum_fusion.1), kind=kOutput, calls=%fused_computation.7 | convolution fusion | flops 382205952 | bytes 1916928 | tf_op jit(solution)/shard_map/dcyj,icxj->idxy/dot_general | solution.py:162
  31.9 0.7 %convolution_bitcast_fusion.9 = f32[3,2,96,192]{3,2,1,0:T(8,128)S(1)} fusion(f32[3,2,96,192,1]{3,2,1,4,0:T(8,128)S(1)} %convolution_bitcast_fusion.11, f32[2,2,192,192]{3,2,1,0:T(8,128)S(1)} %pad_maximum_fusion.1), kind=kOutput, calls=%fused_computation.11 | convolution fusion | flops 254803968 | bytes 1474560 | tf_op jit(solution)/shard_map/dcyj,icxj->idxy/dot_general | solution.py:162
  33.5 1.3 %collective-permute-start.3 = (f32[6,64,128]{2,1,0:T(8,128)S(1)}, f32[6,64,128]{2,1,0:T(8,128)S(1)}, u32[]{:S(2)}, u32[]{:S(2)}) collective-permute-start(f32[6,64,128]{2,1,0:T(8,128)S(1)} %bitcast.483), channel_id=1, source_target_pairs={{0,6},{4,10},{8,14},{1,7},{5,11},{9,15},{16,22},{20,26},{24,30},{1... | collective-permute-start | bytes 589832 | tf_op jit(solution)/shard_map/ppermute | solution.py:184
  34.8 1.3 %collective-permute-start.4 = (f32[6,64,128]{2,1,0:T(8,128)S(1)}, f32[6,64,128]{2,1,0:T(8,128)S(1)}, u32[]{:S(2)}, u32[]{:S(2)}) collective-permute-start(f32[6,64,128]{2,1,0:T(8,128)S(1)} %bitcast.484), channel_id=1, source_target_pairs={{0,2},{4,6},{8,10},{12,14},{1,3},{5,7},{9,11},{13,15},{16,18},{20,... | collective-permute-start | bytes 589832 | tf_op jit(solution)/shard_map/ppermute | solution.py:185
  36.1 1.5 %collective-permute-start.5 = (f32[6,64,128]{2,1,0:T(8,128)S(1)}, f32[6,64,128]{2,1,0:T(8,128)S(1)}, u32[]{:S(2)}, u32[]{:S(2)}) collective-permute-start(f32[6,64,128]{2,1,0:T(8,128)S(1)} %bitcast.485), channel_id=1, source_target_pairs={{4,2},{8,6},{12,10},{5,3},{9,7},{13,11},{20,18},{24,22},{28,26},{2... | collective-permute-start | bytes 589832 | tf_op jit(solution)/shard_map/ppermute | solution.py:186
  37.6 4.9 %collective-permute-done.3 = f32[6,64,128]{2,1,0:T(8,128)S(1)} collective-permute-done((f32[6,64,128]{2,1,0:T(8,128)S(1)}, f32[6,64,128]{2,1,0:T(8,128)S(1)}, u32[]{:S(2)}, u32[]{:S(2)}) %collective-permute-start.3) | collective-permute-done | bytes 196640 | tf_op jit(solution)/shard_map/ppermute | solution.py:184
  42.5 9.1 %collective-permute-done.4 = f32[6,64,128]{2,1,0:T(8,128)S(1)} collective-permute-done((f32[6,64,128]{2,1,0:T(8,128)S(1)}, f32[6,64,128]{2,1,0:T(8,128)S(1)}, u32[]{:S(2)}, u32[]{:S(2)}) %collective-permute-start.4) | collective-permute-done | bytes 196640 | tf_op jit(solution)/shard_map/ppermute | solution.py:185
  52.6 1.2 %collective-permute-done.6 = f32[3,192,128]{2,1,0:T(8,128)S(1)} collective-permute-done((f32[3,192,128]{2,1,0:T(8,128)S(1)}, f32[3,192,128]{2,1,0:T(8,128)S(1)}, u32[]{:S(2)}, u32[]{:S(2)}) %collective-permute-start.6) | collective-permute-done | bytes 294944 | tf_op jit(solution)/shard_map/ppermute | solution.py:105
  54.6 1.0 %convolution_bitcast_fusion.1 = f32[3,2,160,192,1]{3,2,1,4,0:T(8,128)S(1)} fusion(f32[3,1,192,192]{3,2,1,0:T(8,128)S(1)} %get-tuple-element.12, f32[3,1,192,192]{3,2,1,0:T(8,128)S(1)} %get-tuple-element.11, f32[2,2,192,192]{3,2,1,0:T(8,128)S(1)} %pad_maximum_fusion.1), kind=kOutput, calls=%fused_computation.3 | convolution fusion | flops 424894464 | bytes 2572288 | tf_op jit(solution)/shard_map/dcab,icbj->idaj/dot_general | solution.py:159
  55.6 1.0 %convolution_bitcast_fusion = f32[3,2,160,192]{3,2,1,0:T(8,128)S(1)} fusion(f32[3,2,160,192,1]{3,2,1,4,0:T(8,128)S(1)} %convolution_bitcast_fusion.1, f32[2,2,192,192]{3,2,1,0:T(8,128)S(1)} %pad_maximum_fusion.1), kind=kOutput, calls=%fused_computation.2 | convolution fusion | flops 424673280 | bytes 2064384 | tf_op jit(solution)/shard_map/dcyj,icxj->idxy/dot_general | solution.py:162
  56.6 1.0 %convolution_bitcast_fusion.6 = f32[3,2,144,192,1]{3,2,1,4,0:T(8,128)S(1)} fusion(f32[3,1,160,192]{3,2,1,0:T(8,128)S(1)} %get-tuple-element.32, f32[3,1,160,192]{3,2,1,0:T(8,128)S(1)} %get-tuple-element.31, f32[2,2,192,192]{3,2,1,0:T(8,128)S(1)} %pad_maximum_fusion.1), kind=kOutput, calls=%fused_computation.8 | convolution fusion | flops 318689280 | bytes 2236416 | tf_op jit(solution)/shard_map/dcab,icbj->idaj/dot_general | solution.py:159
  57.7 0.9 %convolution_bitcast_fusion.4 = f32[3,2,144,192]{3,2,1,0:T(8,128)S(1)} fusion(f32[3,2,144,192,1]{3,2,1,4,0:T(8,128)S(1)} %convolution_bitcast_fusion.6, f32[2,2,192,192]{3,2,1,0:T(8,128)S(1)} %pad_maximum_fusion.1), kind=kOutput, calls=%fused_computation.6 | convolution fusion | flops 382205952 | bytes 1916928 | tf_op jit(solution)/shard_map/dcyj,icxj->idxy/dot_general | solution.py:162
  59.1 0.7 %convolution_bitcast_fusion.8 = f32[3,2,96,192]{3,2,1,0:T(8,128)S(1)} fusion(f32[3,2,96,192,1]{3,2,1,4,0:T(8,128)S(1)} %convolution_bitcast_fusion.10, f32[2,2,192,192]{3,2,1,0:T(8,128)S(1)} %pad_maximum_fusion.1), kind=kOutput, calls=%fused_computation.10 | convolution fusion | flops 254803968 | bytes 1474560 | tf_op jit(solution)/shard_map/dcyj,icxj->idxy/dot_general | solution.py:162
  60.3 1.1 %fusion.5 = f32[1,3,2,64,128]{4,3,2,1,0:T(8,128)} fusion(f32[3,2,64,192,1]{3,2,1,4,0:T(8,128)S(1)} %convolution_bitcast_fusion.12, f32[3,64,2,128,1]{3,1,4,2,0:T(8,128)S(1)} %fusion.33, f32[2,2,192,192]{3,2,1,0:T(8,128)S(1)} %pad_maximum_fusion.1, pred[]{:T(512)S(6)} %eq.7, pred[]{:T(512)S(6)} %eq.8, pred[]{:T(512)S(6)} %eq.6), kind=kOutput, calls=%fused_computation.26 | convolution fusion | flops 113442816 | bytes 1835011 | tf_op jit(solution)/shard_map/dcyj,icxj->idxy/dot_general | solution.py:162
  (109 shorter events, 11.7 us)
Async XLA Ops:
  0.0 1.5 %copy-start = (f32[3,2,64,128]{3,2,1,0:T(8,128)S(1)}, f32[3,2,64,128]{3,2,1,0:T(8,128)}, u32[]{:S(2)}) copy-start(f32[3,2,64,128]{3,2,1,0:T(8,128)} %param.4) | copy-start | bytes 589828
  1.5 10.5 %copy-start.6 = (f32[2,33]{1,0:T(2,128)S(1)}, f32[2,33]{1,0:T(2,128)}, u32[]{:S(2)}) copy-start(f32[2,33]{1,0:T(2,128)} %param.7) | copy-start | bytes 796
  2.3 17.3 %collective-permute-start.1 = (f32[11,64,128]{2,1,0:T(8,128)S(1)}, f32[11,64,128]{2,1,0:T(8,128)S(1)}, u32[]{:S(2)}, u32[]{:S(2)}) collective-permute-start(f32[11,64,128]{2,1,0:T(8,128)S(1)} %constant_dynamic-update-slice_fusion.5), channel_id=1, source_target_pairs={{4,0},{8,4},{12,8},{5,1},{9,5},{13,9},{6,2},{10,6},{14,10},{7,3},{... | collective-permute-start | bytes 1081352 | tf_op jit(solution)/shard_map/ppermute | solution.py:67
  6.2 11.2 %collective-permute-start = (f32[11,64,128]{2,1,0:T(8,128)}, f32[11,64,128]{2,1,0:T(8,128)}, u32[]{:S(2)}, u32[]{:S(2)}) collective-permute-start(f32[11,64,128]{2,1,0:T(8,128)} %constant_dynamic-update-slice_fusion), channel_id=1, source_target_pairs={{0,4},{4,8},{8,12},{1,5},{5,9},{9,13},{2,6},{6,10},{10,14},{3,7},{... | collective-permute-start | bytes 1081352 | tf_op jit(solution)/shard_map/ppermute | solution.py:66
  15.0 2.4 %copy-start.1 = (f32[192,128]{1,0:T(8,128)S(1)}, f32[192,128]{1,0:T(8,128)}, u32[]{:S(2)}) copy-start(f32[192,128]{1,0:T(8,128)} %constant_dynamic-update-slice_fusion.24) | copy-start | bytes 294916
  15.0 3.1 %copy-start.4 = (f32[192,128]{1,0:T(8,128)S(1)}, f32[192,128]{1,0:T(8,128)}, u32[]{:S(2)}) copy-start(f32[192,128]{1,0:T(8,128)} %constant_dynamic-update-slice_fusion.19) | copy-start | bytes 294916
  15.0 3.1 %copy-start.5 = (f32[192,128]{1,0:T(8,128)S(1)}, f32[192,128]{1,0:T(8,128)}, u32[]{:S(2)}) copy-start(f32[192,128]{1,0:T(8,128)} %constant_dynamic-update-slice_fusion.14) | copy-start | bytes 294916
  19.6 1.2 %copy-start.3 = (f32[64,128]{1,0:T(8,128)S(1)}, f32[64,128]{1,0:T(8,128)}, u32[]{:S(2)}) copy-start(f32[64,128]{1,0:T(8,128)} %get-tuple-element.89) | copy-start | bytes 98308
  19.7 1.2 %copy-start.2 = (f32[64,128]{1,0:T(8,128)S(1)}, f32[64,128]{1,0:T(8,128)}, u32[]{:S(2)}) copy-start(f32[64,128]{1,0:T(8,128)} %get-tuple-element.88) | copy-start | bytes 98308
  21.7 3.7 %collective-permute-start.2 = (f32[7,192,128]{2,1,0:T(8,128)S(1)}, f32[7,192,128]{2,1,0:T(8,128)S(1)}, u32[]{:S(2)}, u32[]{:S(2)}) collective-permute-start(f32[7,192,128]{2,1,0:T(8,128)S(1)} %pad_maximum_fusion.2), channel_id=1, source_target_pairs={{0,1},{1,0},{2,3},{3,2},{4,5},{5,4},{6,7},{7,6},{8,9},{9,8},{10,11... | collective-permute-start | bytes 2064392 | tf_op jit(solution)/shard_map/ppermute | solution.py:105
  33.5 8.9 %collective-permute-start.3 = (f32[6,64,128]{2,1,0:T(8,128)S(1)}, f32[6,64,128]{2,1,0:T(8,128)S(1)}, u32[]{:S(2)}, u32[]{:S(2)}) collective-permute-start(f32[6,64,128]{2,1,0:T(8,128)S(1)} %bitcast.483), channel_id=1, source_target_pairs={{0,6},{4,10},{8,14},{1,7},{5,11},{9,15},{16,22},{20,26},{24,30},{1... | collective-permute-start | bytes 589832 | tf_op jit(solution)/shard_map/ppermute | solution.py:184
  34.8 16.8 %collective-permute-start.4 = (f32[6,64,128]{2,1,0:T(8,128)S(1)}, f32[6,64,128]{2,1,0:T(8,128)S(1)}, u32[]{:S(2)}, u32[]{:S(2)}) collective-permute-start(f32[6,64,128]{2,1,0:T(8,128)S(1)} %bitcast.484), channel_id=1, source_target_pairs={{0,2},{4,6},{8,10},{12,14},{1,3},{5,7},{9,11},{13,15},{16,18},{20,... | collective-permute-start | bytes 589832 | tf_op jit(solution)/shard_map/ppermute | solution.py:185
  36.1 15.5 %collective-permute-start.5 = (f32[6,64,128]{2,1,0:T(8,128)S(1)}, f32[6,64,128]{2,1,0:T(8,128)S(1)}, u32[]{:S(2)}, u32[]{:S(2)}) collective-permute-start(f32[6,64,128]{2,1,0:T(8,128)S(1)} %bitcast.485), channel_id=1, source_target_pairs={{4,2},{8,6},{12,10},{5,3},{9,7},{13,11},{20,18},{24,22},{28,26},{2... | collective-permute-start | bytes 589832 | tf_op jit(solution)/shard_map/ppermute | solution.py:186
  52.1 1.8 %collective-permute-start.6 = (f32[3,192,128]{2,1,0:T(8,128)S(1)}, f32[3,192,128]{2,1,0:T(8,128)S(1)}, u32[]{:S(2)}, u32[]{:S(2)}) collective-permute-start(f32[3,192,128]{2,1,0:T(8,128)S(1)} %maximum_select_fusion.4), channel_id=1, source_target_pairs={{0,1},{1,0},{2,3},{3,2},{4,5},{5,4},{6,7},{7,6},{8,9},{9,8},{10,11... | collective-permute-start | bytes 884744 | tf_op jit(solution)/shard_map/ppermute | solution.py:105
